TPU v7x, 32 devices: a whole 2x2x4 slice. The times are simulated.
32 devices in a mesh: tm: 4 (over z), row: 4 (over y, x), col: 2 (over core).
Axes of the slice: x: 2, y: 2, z: 4, core: 2. Of those that a mesh axis runs over, the one named last changes fastest.
Arguments:
- reflectance: bfloat16 [32, 12, 128, 512], P('tm', None, 'row', 'col'), may hold values from -6 to 6
- scene_class: int32 [32, 128, 512], P('tm', 'row', 'col'), may hold values from 0 to 11
- quality: float32 [32, 128, 512], P('tm', 'row', 'col'), may hold values from -8 to 304
- class_score: float32 [12], replicated, may hold values from -4 to 2
- encode_first: bfloat16 [3, 3, 32, 12], replicated, may hold values from -0.875 to 0.875
- encode_second: bfloat16 [3, 3, 32, 32], replicated, may hold values from -0.5 to 0.5
- middle_first: bfloat16 [3, 3, 64, 32], replicated, may hold values from -0.5 to 0.5
- middle_second: bfloat16 [3, 3, 64, 64], replicated, may hold values from -0.375 to 0.375
- decode_kernel: bfloat16 [3, 3, 32, 96], replicated, may hold values from -0.3125 to 0.3125
- head_weight: bfloat16 [11, 32], replicated, may hold values from -1.5 to 1.5
Outputs:
- logits: bfloat16 [11, 128, 512], P(None, 'row', 'col')
All inputs are finite; a program needn't handle non-finite values.
Results may differ from a plain program's by a relative error of at most 0.03.
Values may be sent and summed in bfloat16 or wider, within the bound.
No kernel may reach another device: no remote copies, remote signals or barrier semaphores. Data moves between devices by JAX's collectives and lax.ppermute only.
A program may use at most 64 MiB of HBM per device.

v0:
```python
import jax
import jax.numpy as jnp
from jax import lax
from jax.sharding import PartitionSpec as P


def with_halo(cells, sides, width):
    for axis, dim in sides:
        count = lax.axis_size(axis)
        ends = count - 1
        head = lax.slice_in_dim(cells, 0, width, axis=dim)
        tail = lax.slice_in_dim(cells, cells.shape[dim] - width, cells.shape[dim], axis=dim)
        cells = jnp.concatenate(
            [
                lax.ppermute(tail, axis, [(i, (i + 1) % count) for i in range(ends)]),
                cells,
                lax.ppermute(head, axis, [((i + 1) % count, i) for i in range(ends)]),
            ],
            axis=dim,
        )
    return cells


def valid_conv(padded, kernel):
    return lax.conv_general_dilated(
        padded[None],
        kernel,
        (1, 1),
        "VALID",
        dimension_numbers=("NCHW", "HWOI", "NCHW"),
        preferred_element_type=jnp.float32,
    )[0]


def convolve(field, kernel):
    padded = with_halo(field, (("row", 1), ("col", 2)), 1)
    return valid_conv(padded, kernel)


def relu_layer(field, kernel):
    return jnp.maximum(convolve(field, kernel), 0.0).astype(jnp.bfloat16)


def shards(
    reflectance,
    scene_class,
    quality,
    class_score,
    encode_first,
    encode_second,
    middle_first,
    middle_second,
    decode_kernel,
    head_weight,
):
    block_rows = quality.shape[1]
    width = quality.shape[2]
    looked = jnp.zeros(quality.shape, jnp.float32)
    for label in range(class_score.shape[0]):
        looked = jnp.where(scene_class == label, class_score[label], looked)
    scores = looked + quality
    local_top = jnp.max(scores, axis=0)
    top_score = lax.pmax(local_top.astype(jnp.bfloat16), "tm").astype(local_top.dtype)
    weights = jnp.exp(scores - top_score[None])
    part_sums = jnp.sum(weights[:, None] * reflectance, axis=0)
    part_total = jnp.sum(weights, axis=0)
    summed = (
        lax.psum(part_sums.astype(jnp.bfloat16), "tm").astype(jnp.float32),
        lax.psum(part_total.astype(jnp.bfloat16), "tm").astype(jnp.float32),
    )
    band_sums = summed[0]
    total_weight = summed[1]
    composite = (band_sums / total_weight[None]).astype(jnp.bfloat16)
    height = composite.shape[1]
    widened = with_halo(composite, (("row", 1), ("col", 2)), 2)
    first_map = jnp.maximum(valid_conv(widened, encode_first), 0.0)
    row_index = lax.axis_index("row") * block_rows - 1 + jnp.arange(height + 2, dtype=jnp.int32)
    col_index = lax.axis_index("col") * width - 1 + jnp.arange(width + 2, dtype=jnp.int32)
    row_inside = (row_index >= 0) & (row_index < block_rows * lax.axis_size("row"))
    col_inside = (col_index >= 0) & (col_index < width * lax.axis_size("col"))
    inside = row_inside[:, None] & col_inside[None, :]
    first_map = jnp.where(inside[None], first_map, 0.0).astype(jnp.bfloat16)
    skip = jnp.maximum(valid_conv(first_map, encode_second), 0.0).astype(jnp.bfloat16)
    channels = skip.shape[0]
    pooled = jnp.mean(
        skip.astype(jnp.float32).reshape(channels, height // 2, 2, width // 2, 2), axis=(2, 4)
    ).astype(jnp.bfloat16)
    deeper = relu_layer(relu_layer(pooled, middle_first), middle_second)
    upsampled = jnp.repeat(jnp.repeat(deeper, 2, axis=1), 2, axis=2)
    joined = jnp.concatenate([skip, upsampled], axis=0)
    decoded = relu_layer(joined, decode_kernel)
    return jnp.einsum(
        "oc,chw->ohw", head_weight, decoded, preferred_element_type=jnp.float32
    ).astype(jnp.bfloat16)


def solution(mesh):
    placed = (
        P("tm", None, "row", "col"),
        P("tm", "row", "col"),
        P("tm", "row", "col"),
        P(),
        P(),
        P(),
        P(),
        P(),
        P(),
        P(),
    )
    return jax.shard_map(
        shards, mesh=mesh, in_specs=placed, out_specs=P(None, "row", "col"), check_vma=False
    )
```

profile of v0, /device:TPU:0, one launch (start us, length us, event | category | flops | bytes accessed | tf_op | source)
XLA Modules:
  0.0 214.7 jit_solution(8139223746503246795)
XLA Ops:
  6.5 1.8 fusion.83
  8.3 8.9 %fusion.76 = (bf16[32,256]{1,0:T(8,128)(2,1)S(1)}, f32[8,32,256]{2,1,0:T(8,128)S(1)}) fusion(f32[8,32,256]{2,1,0:T(8,128)} %param.12, f32[]{:T(128)} %bitcast.11, s32[8,32,256]{2,1,0:T(8,128)} %param.11, f32[]{:T(128)} %bitcast.10, f32[]{:T(128)} %bitcast.9, f32[]{:T(128)} %bitcast.8, f32[]{:T(128)} %bitcast.7, f32[]{:T(128)} %bitcast.6, f32[]{:T(128)} %bitcast.5, ...), kind=kLoop, calls=%fused_computation.103 | loop fusion | flops 1695744 | bytes 802864 | tf_op jit(solution)/shard_map/reduce_max | solution.py:62
  17.3 20.5 %pmax.7 = bf16[32,256]{1,0:T(8,128)(2,1)S(1)} all-reduce(bf16[32,256]{1,0:T(8,128)(2,1)S(1)} %get-tuple-element.7), channel_id=1, replica_groups=mesh['tm'=4,'row'=4,'col'=2] {'tm'}, use_global_device_ids=true, to_apply=%region_1.2 | all-reduce | flops 8192 | bytes 32768 | tf_op jit(solution)/shard_map/pmax | solution.py:63
  37.8 2.5 %multiply_reduce_fusion = bf16[12,32,256]{2,1,0:T(8,128)(2,1)} fusion(bf16[8,12,32,256]{3,2,1,0:T(8,128)(2,1)} %param.10, f32[8,32,256]{2,1,0:T(8,128)S(1)} %get-tuple-element.6), kind=kLoop, calls=%fused_computation.9 | loop fusion | flops 2260992 | bytes 2031616 | tf_op jit(solution)/shard_map/reduce_sum | solution.py:65
  40.3 15.5 %psum.15 = bf16[32,256]{1,0:T(8,128)(2,1)S(1)} all-reduce(bf16[32,256]{1,0:T(8,128)(2,1)S(1)} %get-tuple-element.5), channel_id=1, replica_groups=mesh['tm'=4,'row'=4,'col'=2] {'tm'}, use_global_device_ids=true, to_apply=%region_5.6 | all-reduce | flops 8192 | bytes 32768 | tf_op jit(solution)/shard_map/psum | solution.py:69
  55.9 17.6 %all-reduce.2.cloned.1.call-done = bf16[12,32,256]{2,1,0:T(8,128)(2,1)} async-done(((bf16[12,32,256]{2,1,0:T(8,128)(2,1)}), bf16[12,32,256]{2,1,0:T(8,128)(2,1)}) %all-reduce.2.cloned.1.call-update) | async-done | bytes 196624 | tf_op jit(solution)/shard_map/psum | solution.py:68
  73.5 1.0 divide_convert_fusion
  74.5 3.4 %collective-permute-start = (bf16[12,2,256]{2,1,0:T(2,128)(2,1)S(1)}, bf16[12,2,256]{2,1,0:T(2,128)(2,1)S(1)}, u32[]{:S(2)}, u32[]{:S(2)}) collective-permute-start(bf16[12,2,256]{2,1,0:T(2,128)(2,1)S(1)} %get-tuple-element.23), channel_id=1, source_target_pairs={{0,2},{2,4},{4,6},{1,3},{3,5},{5,7},{8,10},{10,12},{12,14},{9,11},... | collective-permute-start | bytes 36872 | tf_op jit(solution)/shard_map/ppermute | solution.py:15
  77.9 1.3 collective-permute-start.1
  79.3 4.2 %collective-permute-done.1 = bf16[12,2,256]{2,1,0:T(2,128)(2,1)S(1)} collective-permute-done((bf16[12,2,256]{2,1,0:T(2,128)(2,1)S(1)}, bf16[12,2,256]{2,1,0:T(2,128)(2,1)S(1)}, u32[]{:S(2)}, u32[]{:S(2)}) %collective-permute-start.1) | collective-permute-done | bytes 12320 | tf_op jit(solution)/shard_map/ppermute | solution.py:17
  83.7 1.3 collective-permute-start.2
  85.0 1.3 collective-permute-start.3
  86.4 1.8 collective-permute-done.3
  88.7 0.8 reshape.73
  89.5 2.5 %copy.106 = bf16[12,36,1,8,33]{0,3,4,1,2:T(8,128)(2,1)S(1)} copy(bf16[12,36,1,8,33]{4,3,1,0,2:T(8,128)(2,1)S(1)} %reshape.73) | data formatting | bytes 456192 | tf_op jit(solution)/shard_map/conv_general_dilated | solution.py:25
  92.1 4.6 %select_maximum_fusion = bf16[34,8,33,32]{3,1,2,0:T(8,128)(2,1)} fusion(pred[8,33]{0,1:T(8,128)(4,1)S(1)} %copy-done.8, bf16[3,3,32,12]{2,3,1,0:T(8,128)(2,1)S(1)} %copy-done.5, bf16[12,36,1,7,2]{0,3,4,1,2:T(8,128)(2,1)S(1)} %slice.126, bf16[12,36,1,8,33]{0,3,4,1,2:T(8,128)(2,1)S(1)} %copy.106), kind=kOutput, calls=%fused_computation.6 | convolution fusion | flops 63629568 | bytes 821832 | tf_op jit(solution)/shard_map/conv_general_dilated | solution.py:25
  96.7 4.7 %copy.107 = bf16[34,8,33,32]{2,1,3,0:T(8,128)(2,1)S(1)} copy(bf16[34,8,33,32]{3,1,2,0:T(8,128)(2,1)} %select_maximum_fusion) | data formatting | bytes 1148928 | tf_op jit(solution)/shard_map/max | solution.py:76
  101.4 1.6 reshape.77
  103.3 1.9 reshape.80
  105.2 4.4 %copy.109 = bf16[32,34,1,8,33]{0,3,4,1,2:T(8,128)(2,1)} copy(bf16[32,34,1,8,33]{4,3,0,1,2:T(8,128)(2,1)S(1)} %reshape.80) | data formatting | bytes 1148928 | tf_op jit(solution)/shard_map/conv_general_dilated | solution.py:25
  109.6 0.9 slice.128
  110.6 5.7 %maximum_convert_fusion.1 = bf16[32,8,33,32]{3,1,2,0:T(8,128)(2,1)} fusion(pred[8,33]{0,1:T(8,128)(4,1)S(1)} %copy-done.6, bf16[3,3,32,32]{3,2,1,0:T(8,128)(2,1)S(1)} %copy-done.2, bf16[32,34,1,7,2]{0,3,4,1,2:T(8,128)(2,1)S(1)} %slice.128, bf16[32,34,1,8,33]{0,3,4,1,2:T(8,128)(2,1)} %copy.109), kind=kOutput, calls=%fused_computation.8 | convolution fusion | flops 158352384 | bytes 1164296 | tf_op jit(solution)/shard_map/conv_general_dilated | solution.py:25
  116.3 4.0 %copy.110 = bf16[32,8,33,32]{2,1,3,0:T(8,128)(2,1)S(1)} copy(bf16[32,8,33,32]{3,1,2,0:T(8,128)(2,1)} %maximum_convert_fusion.1) | data formatting | bytes 1081344 | tf_op jit(solution)/shard_map/convert_element_type | solution.py:83
  120.3 1.5 reshape.84
  121.9 2.6 %copy.111 = f32[1,32,32,256]{1,3,2,0:T(8,128)} copy(f32[1,32,32,256]{3,1,2,0:T(8,128)S(1)} %get-tuple-element.14) | data formatting | bytes 2097152 | tf_op jit(solution)/shard_map/convert_element_type | solution.py:86
  124.6 5.8 %reduce_sum.29 = f32[32,16,128]{0,2,1:T(8,128)S(1)} reduce(f32[32,16,2,128,2]{0,4,3,2,1:T(2,128)} %bitcast.108, f32[]{:T(128)} %constant.18.clone.1), dimensions={2,4}, to_apply=%region_6.7 | reduce | flops 196608 | bytes 1310724 | tf_op jit(solution)/shard_map/reduce_sum | solution.py:85
  130.5 4.3 %collective-permute-start.4 = (bf16[32,1,128]{0,2,1:T(8,128)(2,1)S(1)}, bf16[32,1,128]{0,2,1:T(8,128)(2,1)S(1)}, u32[]{:S(2)}, u32[]{:S(2)}) collective-permute-start(bf16[32,1,128]{0,2,1:T(8,128)(2,1)S(1)} %get-tuple-element.17), channel_id=1, source_target_pairs={{0,2},{2,4},{4,6},{1,3},{3,5},{5,7},{8,10},{10,12},{12,14},{9,11},... | collective-permute-start | bytes 24584 | tf_op jit(solution)/shard_map/ppermute | solution.py:15
  134.8 1.3 collective-permute-start.5
  136.4 4.2 %collective-permute-done.5 = bf16[32,1,128]{0,2,1:T(8,128)(2,1)S(1)} collective-permute-done((bf16[32,1,128]{0,2,1:T(8,128)(2,1)S(1)}, bf16[32,1,128]{0,2,1:T(8,128)(2,1)S(1)}, u32[]{:S(2)}, u32[]{:S(2)}) %collective-permute-start.5) | collective-permute-done | bytes 8224 | tf_op jit(solution)/shard_map/ppermute | solution.py:17
  140.8 1.4 collective-permute-start.6
  142.3 1.3 collective-permute-start.7
  143.6 2.0 collective-permute-done.7
  145.8 0.8 reshape.87
  146.7 1.2 copy.116
  147.9 1.1 fusion.31
  149.3 3.4 %collective-permute-start.8 = (bf16[64,1,128]{0,1,2:T(2,128)(2,1)S(1)}, bf16[64,1,128]{0,1,2:T(2,128)(2,1)S(1)}, u32[]{:S(2)}, u32[]{:S(2)}) collective-permute-start(bf16[64,1,128]{0,1,2:T(2,128)(2,1)S(1)} %get-tuple-element.15), channel_id=1, source_target_pairs={{0,2},{2,4},{4,6},{1,3},{3,5},{5,7},{8,10},{10,12},{12,14},{9,11},... | collective-permute-start | bytes 49160 | tf_op jit(solution)/shard_map/ppermute | solution.py:15
  152.7 1.3 collective-permute-start.9
  154.0 0.5 copy.119
  154.6 4.2 %collective-permute-done.9 = bf16[64,1,128]{0,1,2:T(2,128)(2,1)S(1)} collective-permute-done((bf16[64,1,128]{0,1,2:T(2,128)(2,1)S(1)}, bf16[64,1,128]{0,1,2:T(2,128)(2,1)S(1)}, u32[]{:S(2)}, u32[]{:S(2)}) %collective-permute-start.9) | collective-permute-done | bytes 16416 | tf_op jit(solution)/shard_map/ppermute | solution.py:17
  159.0 0.9 fusion.79
  159.9 1.3 collective-permute-start.10
  161.2 1.3 collective-permute-start.11
  162.5 3.2 %copy.125 = bf16[32,32,256]{0,1,2:T(8,128)(2,1)S(1)} copy(bf16[32,32,256]{2,0,1:T(8,128)(2,1)S(1)} %get-tuple-element.13) | data formatting | bytes 1048576 | tf_op jit(solution)/shard_map/convert_element_type | solution.py:83
  165.7 1.3 maximum_bitcast_fusion.1
  167.1 0.4 copy.134
  167.4 1.0 pad.6.clone
  168.4 1.4 reshape.94
  169.9 1.5 fusion.32
  171.5 0.7 broadcast_in_dim.92
  172.6 0.7 pad_maximum_fusion.4
  173.3 2.8 %collective-permute-start.12 = (bf16[96,1,256]{0,1,2:T(2,128)(2,1)S(1)}, bf16[96,1,256]{0,1,2:T(2,128)(2,1)S(1)}, u32[]{:S(2)}, u32[]{:S(2)}) collective-permute-start(bf16[96,1,256]{0,1,2:T(2,128)(2,1)S(1)} %get-tuple-element.11), channel_id=1, source_target_pairs={{0,2},{2,4},{4,6},{1,3},{3,5},{5,7},{8,10},{10,12},{12,14},{9,11},... | collective-permute-start | bytes 147464 | tf_op jit(solution)/shard_map/ppermute | solution.py:15
  176.2 1.3 collective-permute-start.13
  177.5 2.0 collective-permute-done.12
  179.4 4.7 %collective-permute-done.13 = bf16[96,1,256]{0,1,2:T(2,128)(2,1)S(1)} collective-permute-done((bf16[96,1,256]{0,1,2:T(2,128)(2,1)S(1)}, bf16[96,1,256]{0,1,2:T(2,128)(2,1)S(1)}, u32[]{:S(2)}, u32[]{:S(2)}) %collective-permute-start.13) | collective-permute-done | bytes 49184 | tf_op jit(solution)/shard_map/ppermute | solution.py:17
  184.2 2.0 collective-permute-start.14
  186.3 1.3 collective-permute-start.15
  187.6 1.8 collective-permute-done.15
  189.3 4.3 %maximum_bitcast_fusion = bf16[96,34,1,258]{0,1,3,2:T(8,128)(2,1)S(1)} fusion(bf16[96,34,1]{0,1,2:T(8,128)(2,1)S(1)} %collective-permute-done.15, bf16[96,1,256]{0,1,2:T(2,128)(2,1)S(1)} %collective-permute-done.13, bf16[64,32,256]{0,1,2:T(8,128)(2,1)S(1)} %bitcast.107, bf16[32,32,256]{0,1,2:T(8,128)(2,1)S(1)} %copy.125, ...), kind=kLoop, calls=%fused_computation.10 | loop fusion | flops 10105344 | bytes 3368448 | tf_op jit(solution)/shard_map/broadcast_in_dim | solution.py:26
  193.6 0.5 pad.8
  194.6 0.5 copy-done.4
  195.1 6.3 %maximum_convert_fusion = bf16[32,8,33,32]{3,1,2,0:T(8,128)(2,1)} fusion(pred[8,33]{0,1:T(8,128)(4,1)S(1)} %copy-done.7, bf16[3,3,32,96]{3,2,1,0:T(8,128)(2,1)S(1)} %copy-done.4, bf16[96,34,1,7,2]{0,3,4,1,2:T(8,128)(2,1)S(1)} %slice.142, bf16[96,34,1,8,33]{0,3,4,1,2:T(8,128)(2,1)S(1)} %copy.128), kind=kOutput, calls=%fused_computation.7 | convolution fusion | flops 473435136 | bytes 2411016 | tf_op jit(solution)/shard_map/conv_general_dilated | solution.py:25
  201.4 4.0 %copy.129 = bf16[32,8,33,32]{2,1,3,0:T(8,128)(2,1)S(1)} copy(bf16[32,8,33,32]{3,1,2,0:T(8,128)(2,1)} %maximum_convert_fusion) | data formatting | bytes 1081344 | tf_op jit(solution)/shard_map/convert_element_type | solution.py:41
  205.5 1.5 reshape.105
  207.2 0.7 copy.130
  (71 shorter events, 4.2 us)
Async XLA Ops:
  6.5 163.4 %copy-start = (bf16[3,3,64,64]{3,2,1,0:T(8,128)(2,1)S(1)}, bf16[3,3,64,64]{3,2,1,0:T(8,128)(2,1)}, u32[]{:S(2)}) copy-start(bf16[3,3,64,64]{3,2,1,0:T(8,128)(2,1)} %param.17) | copy-start | bytes 221188
  6.5 67.0 %all-reduce.2.cloned.1.call-start = ((), (), s32[]{:S(2)}) async-start(), calls=%async_computation | async-start | bytes 393216 | tf_op jit(solution)/shard_map/psum | solution.py:68
  74.5 4.8 %collective-permute-start = (bf16[12,2,256]{2,1,0:T(2,128)(2,1)S(1)}, bf16[12,2,256]{2,1,0:T(2,128)(2,1)S(1)}, u32[]{:S(2)}, u32[]{:S(2)}) collective-permute-start(bf16[12,2,256]{2,1,0:T(2,128)(2,1)S(1)} %get-tuple-element.23), channel_id=1, source_target_pairs={{0,2},{2,4},{4,6},{1,3},{3,5},{5,7},{8,10},{10,12},{12,14},{9,11},... | collective-permute-start | bytes 36872 | tf_op jit(solution)/shard_map/ppermute | solution.py:15
  77.9 5.6 %collective-permute-start.1 = (bf16[12,2,256]{2,1,0:T(2,128)(2,1)S(1)}, bf16[12,2,256]{2,1,0:T(2,128)(2,1)S(1)}, u32[]{:S(2)}, u32[]{:S(2)}) collective-permute-start(bf16[12,2,256]{2,1,0:T(2,128)(2,1)S(1)} %get-tuple-element.24), channel_id=1, source_target_pairs={{2,0},{4,2},{6,4},{3,1},{5,3},{7,5},{10,8},{12,10},{14,12},{11,9},... | collective-permute-start | bytes 36872 | tf_op jit(solution)/shard_map/ppermute | solution.py:17
  83.7 2.7 %collective-permute-start.2 = (bf16[12,36,2]{2,1,0:T(8,128)(2,1)S(1)}, bf16[12,36,2]{2,1,0:T(8,128)(2,1)S(1)}, u32[]{:S(2)}, u32[]{:S(2)}) collective-permute-start(bf16[12,36,2]{2,1,0:T(8,128)(2,1)S(1)} %get-tuple-element.21), channel_id=1, source_target_pairs={{0,1},{2,3},{4,5},{6,7},{8,9},{10,11},{12,13},{14,15},{16,17},{18,... | collective-permute-start | bytes 5192 | tf_op jit(solution)/shard_map/ppermute | solution.py:15
  85.0 3.2 %collective-permute-start.3 = (bf16[12,36,2]{2,1,0:T(8,128)(2,1)S(1)}, bf16[12,36,2]{2,1,0:T(8,128)(2,1)S(1)}, u32[]{:S(2)}, u32[]{:S(2)}) collective-permute-start(bf16[12,36,2]{2,1,0:T(8,128)(2,1)S(1)} %get-tuple-element.22), channel_id=1, source_target_pairs={{1,0},{3,2},{5,4},{7,6},{9,8},{11,10},{13,12},{15,14},{17,16},{19,... | collective-permute-start | bytes 5192 | tf_op jit(solution)/shard_map/ppermute | solution.py:17
  88.7 3.4 %copy-start.5 = (bf16[3,3,32,12]{2,3,1,0:T(8,128)(2,1)S(1)}, bf16[3,3,32,12]{2,3,1,0:T(8,128)(2,1)}, u32[]{:S(2)}) copy-start(bf16[3,3,32,12]{2,3,1,0:T(8,128)(2,1)} %param.14) | copy-start | bytes 20740
  88.7 3.4 %copy-start.8 = (pred[8,33]{0,1:T(8,128)(4,1)S(1)}, pred[8,33]{0,1:T(8,128)(4,1)}, u32[]{:S(2)}) copy-start(pred[8,33]{0,1:T(8,128)(4,1)} %constant.79) | copy-start | bytes 796
  105.2 5.4 %copy-start.2 = (bf16[3,3,32,32]{3,2,1,0:T(8,128)(2,1)S(1)}, bf16[3,3,32,32]{3,2,1,0:T(8,128)(2,1)}, u32[]{:S(2)}) copy-start(bf16[3,3,32,32]{3,2,1,0:T(8,128)(2,1)} %param.15) | copy-start | bytes 55300
  105.2 5.4 %copy-start.6 = (pred[8,33]{0,1:T(8,128)(4,1)S(1)}, pred[8,33]{0,1:T(8,128)(4,1)}, u32[]{:S(2)}) copy-start(pred[8,33]{0,1:T(8,128)(4,1)} %constant.77) | copy-start | bytes 796
  130.5 5.9 %collective-permute-start.4 = (bf16[32,1,128]{0,2,1:T(8,128)(2,1)S(1)}, bf16[32,1,128]{0,2,1:T(8,128)(2,1)S(1)}, u32[]{:S(2)}, u32[]{:S(2)}) collective-permute-start(bf16[32,1,128]{0,2,1:T(8,128)(2,1)S(1)} %get-tuple-element.17), channel_id=1, source_target_pairs={{0,2},{2,4},{4,6},{1,3},{3,5},{5,7},{8,10},{10,12},{12,14},{9,11},... | collective-permute-start | bytes 24584 | tf_op jit(solution)/shard_map/ppermute | solution.py:15
  134.8 5.8 %collective-permute-start.5 = (bf16[32,1,128]{0,2,1:T(8,128)(2,1)S(1)}, bf16[32,1,128]{0,2,1:T(8,128)(2,1)S(1)}, u32[]{:S(2)}, u32[]{:S(2)}) collective-permute-start(bf16[32,1,128]{0,2,1:T(8,128)(2,1)S(1)} %get-tuple-element.18), channel_id=1, source_target_pairs={{2,0},{4,2},{6,4},{3,1},{5,3},{7,5},{10,8},{12,10},{14,12},{11,9},... | collective-permute-start | bytes 24584 | tf_op jit(solution)/shard_map/ppermute | solution.py:17
  140.8 7.1 %copy-start.3 = (bf16[3,3,64,32]{2,3,1,0:T(8,128)(2,1)S(1)}, bf16[3,3,64,32]{2,3,1,0:T(8,128)(2,1)}, u32[]{:S(2)}) copy-start(bf16[3,3,64,32]{2,3,1,0:T(8,128)(2,1)} %param.16) | copy-start | bytes 110596
  140.8 7.1 %copy-start.9 = (pred[8,17]{0,1:T(8,128)(4,1)S(1)}, pred[8,17]{0,1:T(8,128)(4,1)}, u32[]{:S(2)}) copy-start(pred[8,17]{0,1:T(8,128)(4,1)} %constant.80) | copy-start | bytes 412
  140.8 2.7 %collective-permute-start.6 = (bf16[32,18,1]{2,0,1:T(8,128)(2,1)S(1)}, bf16[32,18,1]{2,0,1:T(8,128)(2,1)S(1)}, u32[]{:S(2)}, u32[]{:S(2)}) collective-permute-start(bf16[32,18,1]{2,0,1:T(8,128)(2,1)S(1)} %get-tuple-element.25), channel_id=1, source_target_pairs={{0,1},{2,3},{4,5},{6,7},{8,9},{10,11},{12,13},{14,15},{16,17},{18,... | collective-permute-start | bytes 3464 | tf_op jit(solution)/shard_map/ppermute | solution.py:15
  142.3 3.3 %collective-permute-start.7 = (bf16[32,18,1]{2,0,1:T(8,128)(2,1)S(1)}, bf16[32,18,1]{2,0,1:T(8,128)(2,1)S(1)}, u32[]{:S(2)}, u32[]{:S(2)}) collective-permute-start(bf16[32,18,1]{2,0,1:T(8,128)(2,1)S(1)} %get-tuple-element.26), channel_id=1, source_target_pairs={{1,0},{3,2},{5,4},{7,6},{9,8},{11,10},{13,12},{15,14},{17,16},{19,... | collective-permute-start | bytes 3464 | tf_op jit(solution)/shard_map/ppermute | solution.py:17
  149.3 5.3 %collective-permute-start.8 = (bf16[64,1,128]{0,1,2:T(2,128)(2,1)S(1)}, bf16[64,1,128]{0,1,2:T(2,128)(2,1)S(1)}, u32[]{:S(2)}, u32[]{:S(2)}) collective-permute-start(bf16[64,1,128]{0,1,2:T(2,128)(2,1)S(1)} %get-tuple-element.15), channel_id=1, source_target_pairs={{0,2},{2,4},{4,6},{1,3},{3,5},{5,7},{8,10},{10,12},{12,14},{9,11},... | collective-permute-start | bytes 49160 | tf_op jit(solution)/shard_map/ppermute | solution.py:15
  152.7 6.2 %collective-permute-start.9 = (bf16[64,1,128]{0,1,2:T(2,128)(2,1)S(1)}, bf16[64,1,128]{0,1,2:T(2,128)(2,1)S(1)}, u32[]{:S(2)}, u32[]{:S(2)}) collective-permute-start(bf16[64,1,128]{0,1,2:T(2,128)(2,1)S(1)} %get-tuple-element.16), channel_id=1, source_target_pairs={{2,0},{4,2},{6,4},{3,1},{5,3},{7,5},{10,8},{12,10},{14,12},{11,9},... | collective-permute-start | bytes 49160 | tf_op jit(solution)/shard_map/ppermute | solution.py:17
  159.9 5.8 %collective-permute-start.10 = (bf16[64,18,1]{2,0,1:T(8,128)(2,1)}, bf16[64,18,1]{2,0,1:T(8,128)(2,1)S(1)}, u32[]{:S(2)}, u32[]{:S(2)}) collective-permute-start(bf16[64,18,1]{2,0,1:T(8,128)(2,1)} %get-tuple-element.19), channel_id=1, source_target_pairs={{0,1},{2,3},{4,5},{6,7},{8,9},{10,11},{12,13},{14,15},{16,17},{18,... | collective-permute-start | bytes 6920 | tf_op jit(solution)/shard_map/ppermute | solution.py:15
  161.2 4.5 %collective-permute-start.11 = (bf16[64,18,1]{2,0,1:T(8,128)(2,1)}, bf16[64,18,1]{2,0,1:T(8,128)(2,1)}, u32[]{:S(2)}, u32[]{:S(2)}) collective-permute-start(bf16[64,18,1]{2,0,1:T(8,128)(2,1)} %get-tuple-element.20), channel_id=1, source_target_pairs={{1,0},{3,2},{5,4},{7,6},{9,8},{11,10},{13,12},{15,14},{17,16},{19,... | collective-permute-start | bytes 6920 | tf_op jit(solution)/shard_map/ppermute | solution.py:17
  167.4 2.5 %copy-start.10 = (pred[8,17]{0,1:T(8,128)(4,1)S(1)}, pred[8,17]{0,1:T(8,128)(4,1)}, u32[]{:S(2)}) copy-start(pred[8,17]{0,1:T(8,128)(4,1)} %constant.80) | copy-start | bytes 412
  173.3 6.1 %collective-permute-start.12 = (bf16[96,1,256]{0,1,2:T(2,128)(2,1)S(1)}, bf16[96,1,256]{0,1,2:T(2,128)(2,1)S(1)}, u32[]{:S(2)}, u32[]{:S(2)}) collective-permute-start(bf16[96,1,256]{0,1,2:T(2,128)(2,1)S(1)} %get-tuple-element.11), channel_id=1, source_target_pairs={{0,2},{2,4},{4,6},{1,3},{3,5},{5,7},{8,10},{10,12},{12,14},{9,11},... | collective-permute-start | bytes 147464 | tf_op jit(solution)/shard_map/ppermute | solution.py:15
  176.2 8.0 %collective-permute-start.13 = (bf16[96,1,256]{0,1,2:T(2,128)(2,1)S(1)}, bf16[96,1,256]{0,1,2:T(2,128)(2,1)S(1)}, u32[]{:S(2)}, u32[]{:S(2)}) collective-permute-start(bf16[96,1,256]{0,1,2:T(2,128)(2,1)S(1)} %get-tuple-element.12), channel_id=1, source_target_pairs={{2,0},{4,2},{6,4},{3,1},{5,3},{7,5},{10,8},{12,10},{14,12},{11,9},... | collective-permute-start | bytes 147464 | tf_op jit(solution)/shard_map/ppermute | solution.py:17
  184.2 3.3 %collective-permute-start.14 = (bf16[96,34,1]{0,1,2:T(8,128)(2,1)S(1)}, bf16[96,34,1]{0,1,2:T(8,128)(2,1)S(1)}, u32[]{:S(2)}, u32[]{:S(2)}) collective-permute-start(bf16[96,34,1]{0,1,2:T(8,128)(2,1)S(1)} %get-tuple-element.9), channel_id=1, source_target_pairs={{0,1},{2,3},{4,5},{6,7},{8,9},{10,11},{12,13},{14,15},{16,17},{18,... | collective-permute-start | bytes 19592 | tf_op jit(solution)/shard_map/ppermute | solution.py:15
  186.3 3.1 %collective-permute-start.15 = (bf16[96,34,1]{0,1,2:T(8,128)(2,1)S(1)}, bf16[96,34,1]{0,1,2:T(8,128)(2,1)S(1)}, u32[]{:S(2)}, u32[]{:S(2)}) collective-permute-start(bf16[96,34,1]{0,1,2:T(8,128)(2,1)S(1)} %get-tuple-element.10), channel_id=1, source_target_pairs={{1,0},{3,2},{5,4},{7,6},{9,8},{11,10},{13,12},{15,14},{17,16},{19,... | collective-permute-start | bytes 19592 | tf_op jit(solution)/shard_map/ppermute | solution.py:17
  194.2 0.9 copy-start.4
  194.2 0.9 copy-start.7
  205.4 1.5 copy-start.1
Sparse Core Ops, SparseCore 0:
  40.4 33.0 all-reduce.1
where the time goes:
time: 216 us; the launch traced here: 215 us
  local copies, waits for them, and re-layouts  46.3 us (21%)
  waiting for transfers between devices  42.7 us (20%)
  blocking collectives  36 us (17%)
  starting transfers between devices  30.2 us (14%)
  other arithmetic  25.9 us (12%)
  matrix products  19.4 us (9%)
  between operations  14.1 us (7%)
    ppermute x8, waiting for transfers between devices, with_halo(): lax.ppermute(head, axis, [((i + 1) % count, i) for i in range(ends)])  22.8 us
    pmax x1, blocking collectives, shards(): lax.pmax(local_top.astype(jnp.bfloat16), 'tm').astype(local_top.dtype)  20.5 us
    ppermute x8, starting transfers between devices, with_halo(): lax.ppermute(tail, axis, [(i, (i + 1) % count) for i in range(ends)])  19.9 us
    conv_general_dilated x5, matrix products, valid_conv(): lax.conv_general_dilated(padded[None], kernel, (1, 1), 'VALID', dimension...  19.2 us
    psum x1, waiting for transfers between devices, shards(): lax.psum(part_sums.astype(jnp.bfloat16), 'tm').astype(jnp.float32)  17.6 us
    psum x1, blocking collectives, shards(): lax.psum(part_total.astype(jnp.bfloat16), 'tm').astype(jnp.float32)  15.5 us
    conv_general_dilated x14, local copies, waits for them, and re-layouts, valid_conv(): lax.conv_general_dilated(padded[None], kernel, (1, 1), 'VALID', dimension...  14.4 us
    ppermute x8, starting transfers between devices, with_halo(): lax.ppermute(head, axis, [((i + 1) % count, i) for i in range(ends)])  10.3 us
  transfers between devices with their start and end apart: 17, of which 12 were waited for; matrix products, arithmetic and copies ran while one was open for 2% of the time, Pallas kernels for 0%

commit v1 on v0

v1 whole, which is shorter than its diff:
```python
import jax
import jax.numpy as jnp
from jax import lax
from jax.sharding import PartitionSpec as P

HALO = 8


def with_halo(cells, sides, width):
    for axis, dim in sides:
        count = lax.axis_size(axis)
        ends = count - 1
        head = lax.slice_in_dim(cells, 0, width, axis=dim)
        tail = lax.slice_in_dim(cells, cells.shape[dim] - width, cells.shape[dim], axis=dim)
        cells = jnp.concatenate(
            [
                lax.ppermute(tail, axis, [(i, (i + 1) % count) for i in range(ends)]),
                cells,
                lax.ppermute(head, axis, [((i + 1) % count, i) for i in range(ends)]),
            ],
            axis=dim,
        )
    return cells


def valid_conv(padded, kernel):
    return lax.conv_general_dilated(
        padded[None],
        kernel,
        (1, 1),
        "VALID",
        dimension_numbers=("NCHW", "HWOI", "NCHW"),
        preferred_element_type=jnp.float32,
    )[0]


def inside_mask(row_start, col_start, height, width, total_rows, total_cols):
    rows = row_start + jnp.arange(height, dtype=jnp.int32)
    cols = col_start + jnp.arange(width, dtype=jnp.int32)
    row_in = (rows >= 0) & (rows < total_rows)
    col_in = (cols >= 0) & (cols < total_cols)
    return (row_in[:, None] & col_in[None, :])[None]


def masked_layer(field, kernel, row_start, col_start, total_rows, total_cols):
    out = valid_conv(field, kernel)
    mask = inside_mask(row_start, col_start, out.shape[1], out.shape[2], total_rows, total_cols)
    return jnp.where(mask, jnp.maximum(out, 0.0), 0.0).astype(jnp.bfloat16)


def shards(
    reflectance,
    scene_class,
    quality,
    class_score,
    encode_first,
    encode_second,
    middle_first,
    middle_second,
    decode_kernel,
    head_weight,
):
    block_rows = quality.shape[1]
    block_cols = quality.shape[2]
    total_rows = block_rows * lax.axis_size("row")
    total_cols = block_cols * lax.axis_size("col")
    looked = jnp.zeros(quality.shape, jnp.float32)
    for label in range(class_score.shape[0]):
        looked = jnp.where(scene_class == label, class_score[label], looked)
    scores = looked + quality
    shift = jnp.max(scores, axis=0).astype(jnp.bfloat16).astype(jnp.float32)
    weights = jnp.exp(scores - shift[None])
    part_sums = jnp.sum(weights[:, None] * reflectance, axis=0)
    part_total = jnp.sum(weights, axis=0)
    packed = jnp.concatenate([part_sums, part_total[None], shift[None]], axis=0).astype(jnp.bfloat16)
    gathered = lax.all_gather(packed, "tm", axis=0).astype(jnp.float32)
    shifts = gathered[:, -1]
    scale = jnp.exp(shifts - jnp.max(shifts, axis=0)[None])
    band_sums = jnp.sum(scale[:, None] * gathered[:, :-2], axis=0)
    total_weight = jnp.sum(scale * gathered[:, -2], axis=0)
    composite = (band_sums / total_weight[None]).astype(jnp.bfloat16)

    row0 = lax.axis_index("row") * block_rows
    col0 = lax.axis_index("col") * block_cols
    widened = with_halo(composite, (("row", 1), ("col", 2)), HALO)
    first_map = masked_layer(widened, encode_first, row0 - HALO + 1, col0 - HALO + 1, total_rows, total_cols)
    skip_wide = masked_layer(first_map, encode_second, row0 - HALO + 2, col0 - HALO + 2, total_rows, total_cols)
    channels, wide_rows, wide_cols = skip_wide.shape
    pooled = jnp.mean(
        skip_wide.astype(jnp.float32).reshape(channels, wide_rows // 2, 2, wide_cols // 2, 2), axis=(2, 4)
    ).astype(jnp.bfloat16)
    coarse_halo = (HALO - 2) // 2
    crow0 = row0 // 2 - coarse_halo
    ccol0 = col0 // 2 - coarse_halo
    mid = masked_layer(pooled, middle_first, crow0 + 1, ccol0 + 1, total_rows // 2, total_cols // 2)
    deeper = masked_layer(mid, middle_second, crow0 + 2, ccol0 + 2, total_rows // 2, total_cols // 2)
    upsampled = jnp.repeat(jnp.repeat(deeper, 2, axis=1), 2, axis=2)
    up_halo = 2 * (coarse_halo - 2)
    upsampled = upsampled[:, up_halo - 1 : up_halo + block_rows + 1, up_halo - 1 : up_halo + block_cols + 1]
    skip_halo = HALO - 2
    skip = skip_wide[:, skip_halo - 1 : skip_halo + block_rows + 1, skip_halo - 1 : skip_halo + block_cols + 1]
    joined = jnp.concatenate([skip, upsampled], axis=0)
    decoded = jnp.maximum(valid_conv(joined, decode_kernel), 0.0).astype(jnp.bfloat16)
    return jnp.einsum(
        "oc,chw->ohw", head_weight, decoded, preferred_element_type=jnp.float32
    ).astype(jnp.bfloat16)


def solution(mesh):
    placed = (
        P("tm", None, "row", "col"),
        P("tm", "row", "col"),
        P("tm", "row", "col"),
        P(),
        P(),
        P(),
        P(),
        P(),
        P(),
        P(),
    )
    return jax.shard_map(
        shards, mesh=mesh, in_specs=placed, out_specs=P(None, "row", "col"), check_vma=False
    )
```

time: 216 us -> 165 us (0.76)
  waiting for transfers between devices: 42.7 us -> 4.56 us
  local copies, waits for them, and re-layouts: 46.3 us -> 74.5 us
  starting transfers between devices: 30.2 us -> 7.28 us
  between operations: 14.1 us -> 0.65 us
  blocking collectives: 36 us -> 22.8 us
  matrix products: 19.4 us -> 24.4 us
  other arithmetic: 25.9 us -> 30.2 us
    all_gather x0 -> x1, blocking collectives: none -> 22.8 us  [shards(): gathered = lax.all_gather(packed, 'tm', axis=0).astype(jnp.float32)]
    max x2 -> x10, local copies, waits for them, and re-layouts: 6.24 us -> 27.7 us  [masked_layer(): return jnp.where(mask, jnp.maximum(out, 0.0), 0.0).astype(jnp.bfloat16)]
    pmax x1 -> x0, blocking collectives: 20.5 us -> none  [shards(): lax.pmax(local_top.astype(jnp.bfloat16), 'tm').astype(local_top.dtype)]
    ppermute x8 -> x2, waiting for transfers between devices: 22.8 us -> 4.56 us  [with_halo(): lax.ppermute(head, axis, [((i + 1) % count, i) for i in range(ends)])]
    psum x1 -> x0, waiting for transfers between devices: 17.6 us -> none  [shards(): lax.psum(part_sums.astype(jnp.bfloat16), 'tm').astype(jnp.float32)]
    psum x1 -> x0, blocking collectives: 15.5 us -> none  [shards(): lax.psum(part_total.astype(jnp.bfloat16), 'tm').astype(jnp.float32)]
    ppermute x8 -> x2, starting transfers between devices: 19.9 us -> 4.7 us  [with_halo(): lax.ppermute(tail, axis, [(i, (i + 1) % count) for i in range(ends)])]
    convert_element_type x13 -> x5, local copies, waits for them, and re-layouts: 17.9 us -> 7.03 us  [the longest x2 5.52 us: shards(): jnp.maximum(valid_conv(joined, decode_kernel), 0.0).astype(jnp.bfloat16)]
  transfers between devices with their start and end apart: 17 -> 4, of which waited for: 12 -> 2; matrix products, arithmetic and copies ran while one was open for 2% -> 1% of each run, Pallas kernels for 0% -> 0%
where the time goes in v1:
time: 165 us; the launch traced here: 164 us
  local copies, waits for them, and re-layouts  74.5 us (45%)
  other arithmetic  30.2 us (18%)
  matrix products  24.4 us (15%)
  blocking collectives  22.8 us (14%)
  starting transfers between devices  7.28 us (4%)
  waiting for transfers between devices  4.56 us (3%)
    max x10, local copies, waits for them, and re-layouts, masked_layer(): return jnp.where(mask, jnp.maximum(out, 0.0), 0.0).astype(jnp.bfloat16)  27.7 us
    conv_general_dilated x5, matrix products, valid_conv(): lax.conv_general_dilated(padded[None], kernel, (1, 1), 'VALID', dimension...  24.2 us
    all_gather x1, blocking collectives, shards(): gathered = lax.all_gather(packed, 'tm', axis=0).astype(jnp.float32)  22.8 us
    conv_general_dilated x13, local copies, waits for them, and re-layouts, valid_conv(): lax.conv_general_dilated(padded[None], kernel, (1, 1), 'VALID', dimension...  20.5 us
    reduce_sum x1, other arithmetic, shards(): jnp.mean(skip_wide.astype(jnp.float32).reshape(channels, wide_rows // 2,...  11 us
    reduce_max x1, other arithmetic, shards(): shift = jnp.max(scores, axis=0).astype(jnp.bfloat16).astype(jnp.float32)  8.75 us
    reshape x2, local copies, waits for them, and re-layouts, shards(): upsampled = jnp.repeat(jnp.repeat(deeper, 2, axis=1), 2, axis=2)  5.97 us
    convert_element_type x2, local copies, waits for them, and re-layouts, shards(): jnp.maximum(valid_conv(joined, decode_kernel), 0.0).astype(jnp.bfloat16)  5.52 us
  transfers between devices with their start and end apart: 4, of which 2 were waited for; matrix products, arithmetic and copies ran while one was open for 1% of the time, Pallas kernels for 0%

profile of v1, /device:TPU:0, one launch (start us, length us, event | category | flops | bytes accessed | tf_op | source)
XLA Modules:
  0.0 164.4 jit_solution(2216221590525373773)
XLA Ops:
  0.0 1.8 %fusion.94 = (f32[1]{0:T(128)}, f32[1]{0:T(128)}, f32[1]{0:T(128)}, f32[1]{0:T(128)}, f32[1]{0:T(128)}, /*index=5*/f32[1]{0:T(128)}, f32[1]{0:T(128)}, f32[1]{0:...) fusion(f32[12]{0:T(128)} %param.13), kind=kLoop, calls=%fused_computation.136 | loop fusion | bytes 96 | tf_op jit(solution)/shard_map/slice | solution.py:69
  1.8 8.8 %fusion.91 = (bf16[32,256]{1,0:T(8,128)(2,1)S(1)}, f32[8,32,256]{2,1,0:T(8,128)S(1)}) fusion(f32[8,32,256]{2,1,0:T(8,128)} %param.12, f32[]{:T(128)} %bitcast.11, s32[8,32,256]{2,1,0:T(8,128)} %param.11, f32[]{:T(128)} %bitcast.10, f32[]{:T(128)} %bitcast.9, f32[]{:T(128)} %bitcast.8, f32[]{:T(128)} %bitcast.7, f32[]{:T(128)} %bitcast.6, f32[]{:T(128)} %bitcast.5, ...), kind=kLoop, calls=%fused_computation.133 | loop fusion | flops 1695744 | bytes 802864 | tf_op jit(solution)/shard_map/reduce_max | solution.py:71
  10.6 1.7 %multiply_reduce_fusion = bf16[12,32,256]{2,1,0:T(8,128)(2,1)S(1)} fusion(bf16[8,12,32,256]{3,2,1,0:T(8,128)(2,1)} %param.10, f32[8,32,256]{2,1,0:T(8,128)S(1)} %get-tuple-element.6), kind=kLoop, calls=%fused_computation.23 | loop fusion | flops 2260992 | bytes 2031616 | tf_op jit(solution)/shard_map/reduce_sum | solution.py:73
  12.4 22.8 %all_gather.4 = bf16[4,14,32,256]{3,2,1,0:T(8,128)(2,1)S(1)} all-gather(bf16[1,14,32,256]{3,2,1,0:T(8,128)(2,1)S(1)} %pad_maximum_fusion.2), channel_id=1, replica_groups=mesh['tm'=4,'row'=4,'col'=2] {'tm'}, dimensions={0}, use_global_device_ids=true | all-gather | bytes 1146880 | tf_op jit(solution)/shard_map/all_gather | solution.py:76
  35.2 0.2 convert_element_type.110
  35.5 0.2 fusion.34
  35.7 3.4 %collective-permute-start = (bf16[12,8,256]{2,1,0:T(8,128)(2,1)S(1)}, bf16[12,8,256]{2,1,0:T(8,128)(2,1)S(1)}, u32[]{:S(2)}, u32[]{:S(2)}) collective-permute-start(bf16[12,8,256]{2,1,0:T(8,128)(2,1)S(1)} %get-tuple-element.13), channel_id=1, source_target_pairs={{0,2},{2,4},{4,6},{1,3},{3,5},{5,7},{8,10},{10,12},{12,14},{9,11},... | collective-permute-start | bytes 147464 | tf_op jit(solution)/shard_map/ppermute | solution.py:17
  39.1 1.3 collective-permute-start.1
  40.6 0.1 copy.86
  40.8 1.3 broadcast_and_fusion
  42.3 2.8 %collective-permute-done.1 = bf16[12,8,256]{2,1,0:T(8,128)(2,1)S(1)} collective-permute-done((bf16[12,8,256]{2,1,0:T(8,128)(2,1)S(1)}, bf16[12,8,256]{2,1,0:T(8,128)(2,1)S(1)}, u32[]{:S(2)}, u32[]{:S(2)}) %collective-permute-start.1) | collective-permute-done | bytes 49184 | tf_op jit(solution)/shard_map/ppermute | solution.py:19
  45.1 0.1 fusion.92
  45.2 1.3 collective-permute-start.2
  46.5 1.3 collective-permute-start.3
  48.0 1.8 %collective-permute-done.3 = bf16[12,48,8]{2,1,0:T(8,128)(2,1)S(1)} collective-permute-done((bf16[12,48,8]{2,1,0:T(8,128)(2,1)S(1)}, bf16[12,48,8]{2,1,0:T(8,128)(2,1)S(1)}, u32[]{:S(2)}, u32[]{:S(2)}) %collective-permute-start.3) | collective-permute-done | bytes 9248 | tf_op jit(solution)/shard_map/ppermute | solution.py:19
  49.8 0.3 pad_maximum_fusion
  50.1 1.0 reshape.276
  51.1 4.4 %copy.81 = bf16[12,48,1,8,34]{0,3,4,1,2:T(8,128)(2,1)} copy(bf16[12,48,1,8,34]{4,3,1,0,2:T(8,128)(2,1)S(1)} %reshape.276) | data formatting | bytes 626688 | tf_op jit(solution)/shard_map/conv_general_dilated | solution.py:27
  55.4 1.0 slice.101
  56.5 7.9 %select_maximum_fusion = bf16[46,8,34,32]{3,1,2,0:T(8,128)(2,1)} fusion(pred[8,34]{0,1:T(8,128)(4,1)S(1)} %copy-done.9, bf16[3,3,32,12]{2,3,1,0:T(8,128)(2,1)S(1)} %copy-done.6, bf16[12,48,1,7,2]{0,3,4,1,2:T(8,128)(2,1)S(1)} %slice.101, bf16[12,48,1,8,34]{0,3,4,1,2:T(8,128)(2,1)} %copy.81), kind=kOutput, calls=%fused_computation.4 | convolution fusion | flops 88679424 | bytes 1137424 | tf_op jit(solution)/shard_map/conv_general_dilated | solution.py:27
  64.3 5.5 %copy.82 = bf16[46,8,34,32]{2,1,3,0:T(8,128)(2,1)S(1)} copy(bf16[46,8,34,32]{3,1,2,0:T(8,128)(2,1)} %select_maximum_fusion) | data formatting | bytes 1601536 | tf_op jit(solution)/shard_map/max | solution.py:48
  69.8 3.0 %reshape.280 = bf16[46,1,272,32]{2,3,0,1:T(8,128)(2,1)} reshape(bf16[46,8,34,32]{2,1,3,0:T(8,128)(2,1)S(1)} %copy.82) | data formatting | bytes 1601536 | tf_op jit(solution)/shard_map/max | solution.py:48
  72.8 1.6 fusion.43
  74.3 1.1 pad.1
  75.5 4.1 %reshape.283 = bf16[32,46,1,8,34]{4,3,0,1,2:T(8,128)(2,1)S(1)} reshape(bf16[32,46,1,272]{3,0,1,2:T(8,128)(2,1)} %pad.1) | data formatting | bytes 1601536 | tf_op jit(solution)/shard_map/conv_general_dilated | solution.py:27
  79.6 5.0 %copy.84 = bf16[32,46,1,8,34]{0,3,4,1,2:T(8,128)(2,1)} copy(bf16[32,46,1,8,34]{4,3,0,1,2:T(8,128)(2,1)S(1)} %reshape.283) | data formatting | bytes 1601536 | tf_op jit(solution)/shard_map/conv_general_dilated | solution.py:27
  84.6 1.0 slice.103
  85.6 7.0 %select_maximum_fusion.1 = bf16[44,8,34,32]{3,1,2,0:T(8,128)(2,1)} fusion(pred[8,34]{0,1:T(8,128)(4,1)S(1)} %copy-done.8, bf16[3,3,32,32]{3,2,1,0:T(8,128)(2,1)S(1)} %copy-done.3, bf16[32,46,1,7,2]{0,3,4,1,2:T(8,128)(2,1)S(1)} %slice.103, bf16[32,46,1,8,34]{0,3,4,1,2:T(8,128)(2,1)} %copy.84), kind=kOutput, calls=%fused_computation.5 | convolution fusion | flops 224286720 | bytes 1626640 | tf_op jit(solution)/shard_map/conv_general_dilated | solution.py:27
  92.6 4.5 %copy.85 = bf16[44,8,34,32]{2,1,3,0:T(8,128)(2,1)S(1)} copy(bf16[44,8,34,32]{3,1,2,0:T(8,128)(2,1)} %select_maximum_fusion.1) | data formatting | bytes 1531904 | tf_op jit(solution)/shard_map/max | solution.py:48
  97.1 2.8 %reshape.287 = bf16[44,1,272,32]{2,3,0,1:T(8,128)(2,1)} reshape(bf16[44,8,34,32]{2,1,3,0:T(8,128)(2,1)S(1)} %copy.85) | data formatting | bytes 1531904 | tf_op jit(solution)/shard_map/max | solution.py:48
  100.0 2.8 %slice_bitcast_fusion = (bf16[32,44,268]{2,0,1:T(8,128)(2,1)}, bf16[1,32,44,268]{3,1,2,0:T(8,128)(2,1)}) fusion(bf16[44,1,272,32]{2,3,0,1:T(8,128)(2,1)} %reshape.287), kind=kLoop, calls=%fused_computation.33 | loop fusion | bytes 2264064 | tf_op jit(solution)/shard_map/max | solution.py:48
  102.7 3.6 %copy.87 = bf16[1,32,44,268]{1,3,2,0:T(8,128)(2,1)S(1)} copy(bf16[1,32,44,268]{3,1,2,0:T(8,128)(2,1)} %get-tuple-element.10) | data formatting | bytes 1509376 | tf_op jit(solution)/shard_map/max | solution.py:48
  106.3 5.0 %max.59 = bf16[32,22,2,134,2]{0,4,3,2,1:T(2,128)(2,1)} reshape(bf16[1,32,44,268]{1,3,2,0:T(8,128)(2,1)S(1)} %copy.87) | data formatting | bytes 1509376 | tf_op jit(solution)/shard_map/max | solution.py:48
  111.3 11.0 %convert_reduce_fusion = f32[32,22,134]{0,2,1:T(8,128)S(1)} fusion(bf16[32,22,2,134,2]{0,4,3,2,1:T(2,128)(2,1)} %max.59, pred[22,2,134,2]{3,2,1,0:T(8,128)(4,1)} %broadcast_and_fusion), kind=kLoop, calls=%fused_computation.6 | loop fusion | flops 1037696 | bytes 1143824 | tf_op jit(solution)/shard_map/reduce_sum | solution.py:89
  122.3 0.1 fusion.57
  122.4 0.1 copy.104
  122.6 0.2 pad.3.clone
  122.9 0.4 copy-done.4
  123.3 1.3 fusion.36
  124.6 0.1 copy.91
  124.7 0.9 fusion.50
  125.6 0.2 pad.5
  126.0 1.6 fusion.37
  127.6 0.2 copy.94
  127.8 0.3 reshape.301
  128.1 0.4 copy.103
  128.5 0.1 fusion.41
  128.6 0.1 broadcast_in_dim.135
  128.7 1.6 copy.96
  130.3 2.5 %broadcast_in_dim.136 = bf16[64,36,130,2]{0,3,2,1:T(2,128)(2,1)S(1)} broadcast(bf16[64,36,130]{0,2,1:T(8,128)(2,1)} %copy.96), dimensions={0,1,2} | broadcast | bytes 1797120 | tf_op jit(solution)/shard_map/broadcast_in_dim | solution.py:97
  132.8 4.4 %reshape.273 = bf16[64,36,260]{0,2,1:T(8,128)(2,1)} reshape(bf16[64,36,130,2]{0,3,2,1:T(2,128)(2,1)S(1)} %broadcast_in_dim.136) | data formatting | bytes 2396160 | tf_op jit(solution)/shard_map/reshape | solution.py:97
  137.2 2.5 %slice.111 = bf16[64,34,258]{0,2,1:T(8,128)(2,1)S(1)} slice(bf16[64,36,260]{0,2,1:T(8,128)(2,1)} %reshape.273), slice={[0:64], [1:35], [1:259]} | slice | bytes 2245632 | tf_op jit(solution)/shard_map/slice | solution.py:99
  139.8 0.5 fusion.32
  140.3 2.0 %copy.97 = bf16[32,34,258]{0,2,1:T(8,128)(2,1)} copy(bf16[32,34,258]{2,0,1:T(8,128)(2,1)S(1)} %fusion.32) | data formatting | bytes 1122816 | tf_op jit(solution)/shard_map/slice | solution.py:101
  142.3 2.9 %maximum_bitcast_fusion = bf16[96,34,1,258]{0,3,1,2:T(8,128)(2,1)S(1)} fusion(bf16[64,34,258]{0,2,1:T(8,128)(2,1)S(1)} %slice.111, bf16[32,34,258]{0,2,1:T(8,128)(2,1)} %copy.97), kind=kLoop, calls=%fused_computation.30 | loop fusion | flops 3368448 | bytes 3368448 | tf_op jit(solution)/shard_map/broadcast_in_dim | solution.py:28
  145.2 1.8 %pad.7 = bf16[96,34,1,264]{0,3,1,2:T(8,128)(2,1)} pad(bf16[96,34,1,258]{0,3,1,2:T(8,128)(2,1)S(1)} %maximum_bitcast_fusion, bf16[]{:T(256)} %constant.107), padding=0_0x0_0x0_0x0_6 | pad | bytes 3407618 | tf_op jit(solution)/shard_map/broadcast_in_dim | solution.py:28
  147.0 3.6 %reshape.304 = bf16[96,34,1,8,33]{0,4,3,1,2:T(8,128)(2,1)S(1)} reshape(bf16[96,34,1,264]{0,3,1,2:T(8,128)(2,1)} %pad.7) | data formatting | bytes 3446784 | tf_op jit(solution)/shard_map/conv_general_dilated | solution.py:27
  150.6 0.3 copy.99
  151.0 0.5 copy-done.5
  151.5 6.4 %maximum_convert_fusion = bf16[32,8,33,32]{3,1,2,0:T(8,128)(2,1)} fusion(pred[8,33]{0,1:T(8,128)(4,1)S(1)} %copy-done.7, bf16[3,3,32,96]{3,2,1,0:T(8,128)(2,1)S(1)} %copy-done.5, bf16[96,34,1,7,2]{0,3,4,1,2:T(8,128)(2,1)S(1)} %slice.112, bf16[96,34,1,8,33]{0,3,4,1,2:T(8,128)(2,1)S(1)} %copy.99), kind=kOutput, calls=%fused_computation.10 | convolution fusion | flops 473435136 | bytes 2411016 | tf_op jit(solution)/shard_map/conv_general_dilated | solution.py:27
  157.9 4.0 %copy.100 = bf16[32,8,33,32]{2,1,3,0:T(8,128)(2,1)S(1)} copy(bf16[32,8,33,32]{3,1,2,0:T(8,128)(2,1)} %maximum_convert_fusion) | data formatting | bytes 1081344 | tf_op jit(solution)/shard_map/convert_element_type | solution.py:103
  161.9 1.5 reshape.308
  163.4 0.2 fusion.42
  163.6 0.7 copy.101
  (53 shorter events, 1.1 us)
Async XLA Ops:
  0.0 125.9 %copy-start = (bf16[3,3,64,64]{3,2,1,0:T(8,128)(2,1)S(1)}, bf16[3,3,64,64]{3,2,1,0:T(8,128)(2,1)}, u32[]{:S(2)}) copy-start(bf16[3,3,64,64]{3,2,1,0:T(8,128)(2,1)} %param.17) | copy-start | bytes 221188
  35.7 6.6 %collective-permute-start = (bf16[12,8,256]{2,1,0:T(8,128)(2,1)S(1)}, bf16[12,8,256]{2,1,0:T(8,128)(2,1)S(1)}, u32[]{:S(2)}, u32[]{:S(2)}) collective-permute-start(bf16[12,8,256]{2,1,0:T(8,128)(2,1)S(1)} %get-tuple-element.13), channel_id=1, source_target_pairs={{0,2},{2,4},{4,6},{1,3},{3,5},{5,7},{8,10},{10,12},{12,14},{9,11},... | collective-permute-start | bytes 147464 | tf_op jit(solution)/shard_map/ppermute | solution.py:17
  39.1 6.0 %collective-permute-start.1 = (bf16[12,8,256]{2,1,0:T(8,128)(2,1)S(1)}, bf16[12,8,256]{2,1,0:T(8,128)(2,1)S(1)}, u32[]{:S(2)}, u32[]{:S(2)}) collective-permute-start(bf16[12,8,256]{2,1,0:T(8,128)(2,1)S(1)} %get-tuple-element.14), channel_id=1, source_target_pairs={{2,0},{4,2},{6,4},{3,1},{5,3},{7,5},{10,8},{12,10},{14,12},{11,9},... | collective-permute-start | bytes 147464 | tf_op jit(solution)/shard_map/ppermute | solution.py:19
  45.2 2.8 %collective-permute-start.2 = (bf16[12,48,8]{2,1,0:T(8,128)(2,1)S(1)}, bf16[12,48,8]{2,1,0:T(8,128)(2,1)S(1)}, u32[]{:S(2)}, u32[]{:S(2)}) collective-permute-start(bf16[12,48,8]{2,1,0:T(8,128)(2,1)S(1)} %get-tuple-element.11), channel_id=1, source_target_pairs={{0,1},{2,3},{4,5},{6,7},{8,9},{10,11},{12,13},{14,15},{16,17},{18,... | collective-permute-start | bytes 27656 | tf_op jit(solution)/shard_map/ppermute | solution.py:17
  46.5 3.3 %collective-permute-start.3 = (bf16[12,48,8]{2,1,0:T(8,128)(2,1)S(1)}, bf16[12,48,8]{2,1,0:T(8,128)(2,1)S(1)}, u32[]{:S(2)}, u32[]{:S(2)}) collective-permute-start(bf16[12,48,8]{2,1,0:T(8,128)(2,1)S(1)} %get-tuple-element.12), channel_id=1, source_target_pairs={{1,0},{3,2},{5,4},{7,6},{9,8},{11,10},{13,12},{15,14},{17,16},{19,... | collective-permute-start | bytes 27656 | tf_op jit(solution)/shard_map/ppermute | solution.py:19
  51.1 5.4 %copy-start.6 = (bf16[3,3,32,12]{2,3,1,0:T(8,128)(2,1)S(1)}, bf16[3,3,32,12]{2,3,1,0:T(8,128)(2,1)}, u32[]{:S(2)}) copy-start(bf16[3,3,32,12]{2,3,1,0:T(8,128)(2,1)} %param.14) | copy-start | bytes 20740
  51.1 5.4 %copy-start.9 = (pred[8,34]{0,1:T(8,128)(4,1)S(1)}, pred[8,34]{0,1:T(8,128)(4,1)}, u32[]{:S(2)}) copy-start(pred[8,34]{0,1:T(8,128)(4,1)} %constant.128) | copy-start | bytes 820
  79.6 6.0 %copy-start.3 = (bf16[3,3,32,32]{3,2,1,0:T(8,128)(2,1)S(1)}, bf16[3,3,32,32]{3,2,1,0:T(8,128)(2,1)}, u32[]{:S(2)}) copy-start(bf16[3,3,32,32]{3,2,1,0:T(8,128)(2,1)} %param.15) | copy-start | bytes 55300
  79.6 6.0 %copy-start.8 = (pred[8,34]{0,1:T(8,128)(4,1)S(1)}, pred[8,34]{0,1:T(8,128)(4,1)}, u32[]{:S(2)}) copy-start(pred[8,34]{0,1:T(8,128)(4,1)} %constant.127) | copy-start | bytes 820
  122.4 0.9 copy-start.4
  122.4 0.9 copy-start.11
  124.7 1.2 copy-start.10
  137.2 2.5 %copy-start.1 = (bf16[32,44,268]{2,0,1:T(8,128)(2,1)S(1)}, bf16[32,44,268]{2,0,1:T(8,128)(2,1)}, u32[]{:S(2)}) copy-start(bf16[32,44,268]{2,0,1:T(8,128)(2,1)} %get-tuple-element.9) | copy-start | bytes 2264068
  150.6 0.9 copy-start.5
  150.6 0.9 copy-start.7
  161.9 1.5 copy-start.2

commit v2 on v1

--- a/solution.py
+++ b/solution.py
@@ -29,7 +29,7 @@
         kernel,
         (1, 1),
         "VALID",
-        dimension_numbers=("NCHW", "HWOI", "NCHW"),
+        dimension_numbers=("NHWC", "HWOI", "NHWC"),
         preferred_element_type=jnp.float32,
     )[0]
 
@@ -39,12 +39,12 @@
     cols = col_start + jnp.arange(width, dtype=jnp.int32)
     row_in = (rows >= 0) & (rows < total_rows)
     col_in = (cols >= 0) & (cols < total_cols)
-    return (row_in[:, None] & col_in[None, :])[None]
+    return (row_in[:, None] & col_in[None, :])[:, :, None]
 
 
 def masked_layer(field, kernel, row_start, col_start, total_rows, total_cols):
     out = valid_conv(field, kernel)
-    mask = inside_mask(row_start, col_start, out.shape[1], out.shape[2], total_rows, total_cols)
+    mask = inside_mask(row_start, col_start, out.shape[0], out.shape[1], total_rows, total_cols)
     return jnp.where(mask, jnp.maximum(out, 0.0), 0.0).astype(jnp.bfloat16)
 
 
@@ -82,27 +82,27 @@
 
     row0 = lax.axis_index("row") * block_rows
     col0 = lax.axis_index("col") * block_cols
-    widened = with_halo(composite, (("row", 1), ("col", 2)), HALO)
+    widened = with_halo(composite.transpose(1, 2, 0), (("row", 0), ("col", 1)), HALO)
     first_map = masked_layer(widened, encode_first, row0 - HALO + 1, col0 - HALO + 1, total_rows, total_cols)
     skip_wide = masked_layer(first_map, encode_second, row0 - HALO + 2, col0 - HALO + 2, total_rows, total_cols)
-    channels, wide_rows, wide_cols = skip_wide.shape
+    wide_rows, wide_cols, channels = skip_wide.shape
     pooled = jnp.mean(
-        skip_wide.astype(jnp.float32).reshape(channels, wide_rows // 2, 2, wide_cols // 2, 2), axis=(2, 4)
+        skip_wide.astype(jnp.float32).reshape(wide_rows // 2, 2, wide_cols // 2, 2, channels), axis=(1, 3)
     ).astype(jnp.bfloat16)
     coarse_halo = (HALO - 2) // 2
     crow0 = row0 // 2 - coarse_halo
     ccol0 = col0 // 2 - coarse_halo
     mid = masked_layer(pooled, middle_first, crow0 + 1, ccol0 + 1, total_rows // 2, total_cols // 2)
     deeper = masked_layer(mid, middle_second, crow0 + 2, ccol0 + 2, total_rows // 2, total_cols // 2)
-    upsampled = jnp.repeat(jnp.repeat(deeper, 2, axis=1), 2, axis=2)
+    upsampled = jnp.repeat(jnp.repeat(deeper, 2, axis=0), 2, axis=1)
     up_halo = 2 * (coarse_halo - 2)
-    upsampled = upsampled[:, up_halo - 1 : up_halo + block_rows + 1, up_halo - 1 : up_halo + block_cols + 1]
+    upsampled = upsampled[up_halo - 1 : up_halo + block_rows + 1, up_halo - 1 : up_halo + block_cols + 1]
     skip_halo = HALO - 2
-    skip = skip_wide[:, skip_halo - 1 : skip_halo + block_rows + 1, skip_halo - 1 : skip_halo + block_cols + 1]
-    joined = jnp.concatenate([skip, upsampled], axis=0)
+    skip = skip_wide[skip_halo - 1 : skip_halo + block_rows + 1, skip_halo - 1 : skip_halo + block_cols + 1]
+    joined = jnp.concatenate([skip, upsampled], axis=2)
     decoded = jnp.maximum(valid_conv(joined, decode_kernel), 0.0).astype(jnp.bfloat16)
     return jnp.einsum(
-        "oc,chw->ohw", head_weight, decoded, preferred_element_type=jnp.float32
+        "oc,hwc->ohw", head_weight, decoded, preferred_element_type=jnp.float32
     ).astype(jnp.bfloat16)
 
 

time: 165 us -> 163 us (0.988)
  local copies, waits for them, and re-layouts: 74.5 us -> 71.3 us
    reshape x2 -> x1, local copies, waits for them, and re-layouts: 5.97 us -> 4.4 us  [shards(): upsampled = jnp.repeat(jnp.repeat(deeper, 2, axis=0), 2, axis=1)]
where the time goes in v2:
time: 163 us; the launch traced here: 162 us
  local copies, waits for them, and re-layouts  71.3 us (44%)
  other arithmetic  30.6 us (19%)
  matrix products  24.4 us (15%)
  blocking collectives  22.8 us (14%)
  starting transfers between devices  7.28 us (4%)
  waiting for transfers between devices  4.56 us (3%)
    max x10, local copies, waits for them, and re-layouts, masked_layer(): return jnp.where(mask, jnp.maximum(out, 0.0), 0.0).astype(jnp.bfloat16)  27.7 us
    conv_general_dilated x5, matrix products, valid_conv(): lax.conv_general_dilated(padded[None], kernel, (1, 1), 'VALID', dimension...  24.2 us
    all_gather x1, blocking collectives, shards(): gathered = lax.all_gather(packed, 'tm', axis=0).astype(jnp.float32)  22.8 us
    conv_general_dilated x13, local copies, waits for them, and re-layouts, valid_conv(): lax.conv_general_dilated(padded[None], kernel, (1, 1), 'VALID', dimension...  20.5 us
    reduce_sum x1, other arithmetic, shards(): jnp.mean(skip_wide.astype(jnp.float32).reshape(wide_rows // 2, 2, wide_co...  11 us
    reduce_max x1, other arithmetic, shards(): shift = jnp.max(scores, axis=0).astype(jnp.bfloat16).astype(jnp.float32)  8.75 us
    convert_element_type x2, local copies, waits for them, and re-layouts, shards(): jnp.maximum(valid_conv(joined, decode_kernel), 0.0).astype(jnp.bfloat16)  5.52 us
    ppermute x2, starting transfers between devices, with_halo(): lax.ppermute(tail, axis, [(i, (i + 1) % count) for i in range(ends)])  4.7 us
  transfers between devices with their start and end apart: 4, of which 2 were waited for; matrix products, arithmetic and copies ran while one was open for 1% of the time, Pallas kernels for 0%

profile of v2, /device:TPU:0, one launch (start us, length us, event | category | flops | bytes accessed | tf_op | source)
XLA Modules:
  0.0 161.6 jit_solution(4553221266921278933)
XLA Ops:
  0.0 1.8 %fusion.94 = (f32[1]{0:T(128)}, f32[1]{0:T(128)}, f32[1]{0:T(128)}, f32[1]{0:T(128)}, f32[1]{0:T(128)}, /*index=5*/f32[1]{0:T(128)}, f32[1]{0:T(128)}, f32[1]{0:...) fusion(f32[12]{0:T(128)} %param.13), kind=kLoop, calls=%fused_computation.135 | loop fusion | bytes 96 | tf_op jit(solution)/shard_map/slice | solution.py:69
  1.8 8.8 %fusion.91 = (bf16[32,256]{1,0:T(8,128)(2,1)S(1)}, f32[8,32,256]{2,1,0:T(8,128)S(1)}) fusion(f32[8,32,256]{2,1,0:T(8,128)} %param.12, f32[]{:T(128)} %bitcast.11, s32[8,32,256]{2,1,0:T(8,128)} %param.11, f32[]{:T(128)} %bitcast.10, f32[]{:T(128)} %bitcast.9, f32[]{:T(128)} %bitcast.8, f32[]{:T(128)} %bitcast.7, f32[]{:T(128)} %bitcast.6, f32[]{:T(128)} %bitcast.5, ...), kind=kLoop, calls=%fused_computation.132 | loop fusion | flops 1695744 | bytes 802864 | tf_op jit(solution)/shard_map/reduce_max | solution.py:71
  10.6 1.7 %multiply_reduce_fusion = bf16[12,32,256]{2,1,0:T(8,128)(2,1)S(1)} fusion(bf16[8,12,32,256]{3,2,1,0:T(8,128)(2,1)} %param.10, f32[8,32,256]{2,1,0:T(8,128)S(1)} %get-tuple-element.6), kind=kLoop, calls=%fused_computation.23 | loop fusion | flops 2260992 | bytes 2031616 | tf_op jit(solution)/shard_map/reduce_sum | solution.py:73
  12.4 22.8 %all_gather.4 = bf16[4,14,32,256]{3,2,1,0:T(8,128)(2,1)S(1)} all-gather(bf16[1,14,32,256]{3,2,1,0:T(8,128)(2,1)S(1)} %pad_maximum_fusion.2), channel_id=1, replica_groups=mesh['tm'=4,'row'=4,'col'=2] {'tm'}, dimensions={0}, use_global_device_ids=true | all-gather | bytes 1146880 | tf_op jit(solution)/shard_map/all_gather | solution.py:76
  35.2 0.2 convert_element_type.114
  35.5 0.2 fusion.34
  35.7 3.4 %collective-permute-start = (bf16[8,256,12]{1,0,2:T(8,128)(2,1)S(1)}, bf16[8,256,12]{1,0,2:T(8,128)(2,1)S(1)}, u32[]{:S(2)}, u32[]{:S(2)}) collective-permute-start(bf16[8,256,12]{1,0,2:T(8,128)(2,1)S(1)} %get-tuple-element.13), channel_id=1, source_target_pairs={{0,2},{2,4},{4,6},{1,3},{3,5},{5,7},{8,10},{10,12},{12,14},{9,11},... | collective-permute-start | bytes 147464 | tf_op jit(solution)/shard_map/ppermute | solution.py:17
  39.1 1.3 collective-permute-start.1
  40.6 0.1 copy.80
  40.8 1.3 broadcast_and_fusion
  42.3 2.8 %collective-permute-done.1 = bf16[8,256,12]{1,0,2:T(8,128)(2,1)S(1)} collective-permute-done((bf16[8,256,12]{1,0,2:T(8,128)(2,1)S(1)}, bf16[8,256,12]{1,0,2:T(8,128)(2,1)S(1)}, u32[]{:S(2)}, u32[]{:S(2)}) %collective-permute-start.1) | collective-permute-done | bytes 49184 | tf_op jit(solution)/shard_map/ppermute | solution.py:19
  45.1 0.1 fusion.92
  45.2 1.3 collective-permute-start.2
  46.5 1.3 collective-permute-start.3
  48.0 1.8 %collective-permute-done.3 = bf16[48,8,12]{1,0,2:T(8,128)(2,1)S(1)} collective-permute-done((bf16[48,8,12]{1,0,2:T(8,128)(2,1)S(1)}, bf16[48,8,12]{1,0,2:T(8,128)(2,1)S(1)}, u32[]{:S(2)}, u32[]{:S(2)}) %collective-permute-start.3) | collective-permute-done | bytes 9248 | tf_op jit(solution)/shard_map/ppermute | solution.py:19
  49.8 0.3 pad_maximum_fusion
  50.1 1.0 reshape.276
  51.1 4.4 %copy.75 = bf16[48,1,8,34,12]{4,2,3,0,1:T(8,128)(2,1)} copy(bf16[48,1,8,34,12]{3,2,0,4,1:T(8,128)(2,1)S(1)} %reshape.276) | data formatting | bytes 626688 | tf_op jit(solution)/shard_map/conv_general_dilated | solution.py:27
  55.4 1.0 slice.101
  56.5 7.9 %select_maximum_fusion = bf16[46,8,34,32]{3,1,2,0:T(8,128)(2,1)} fusion(pred[8,34]{0,1:T(8,128)(4,1)S(1)} %copy-done.9, bf16[3,3,32,12]{2,3,1,0:T(8,128)(2,1)S(1)} %copy-done.6, bf16[48,1,7,2,12]{4,2,3,0,1:T(8,128)(2,1)S(1)} %slice.101, bf16[48,1,8,34,12]{4,2,3,0,1:T(8,128)(2,1)} %copy.75), kind=kOutput, calls=%fused_computation.4 | convolution fusion | flops 88679424 | bytes 1137424 | tf_op jit(solution)/shard_map/conv_general_dilated | solution.py:27
  64.3 5.5 %copy.76 = bf16[46,8,34,32]{2,1,3,0:T(8,128)(2,1)S(1)} copy(bf16[46,8,34,32]{3,1,2,0:T(8,128)(2,1)} %select_maximum_fusion) | data formatting | bytes 1601536 | tf_op jit(solution)/shard_map/max | solution.py:48
  69.8 3.0 %reshape.280 = bf16[46,1,272,32]{2,3,0,1:T(8,128)(2,1)} reshape(bf16[46,8,34,32]{2,1,3,0:T(8,128)(2,1)S(1)} %copy.76) | data formatting | bytes 1601536 | tf_op jit(solution)/shard_map/max | solution.py:48
  72.8 1.6 fusion.24
  74.3 1.1 pad.1
  75.5 4.1 %reshape.283 = bf16[46,1,8,34,32]{3,2,4,0,1:T(8,128)(2,1)S(1)} reshape(bf16[46,1,272,32]{2,3,0,1:T(8,128)(2,1)} %pad.1) | data formatting | bytes 1601536 | tf_op jit(solution)/shard_map/conv_general_dilated | solution.py:27
  79.6 5.0 %copy.78 = bf16[46,1,8,34,32]{4,2,3,0,1:T(8,128)(2,1)} copy(bf16[46,1,8,34,32]{3,2,4,0,1:T(8,128)(2,1)S(1)} %reshape.283) | data formatting | bytes 1601536 | tf_op jit(solution)/shard_map/conv_general_dilated | solution.py:27
  84.6 1.0 slice.103
  85.6 7.0 %select_maximum_fusion.1 = bf16[44,8,34,32]{3,1,2,0:T(8,128)(2,1)} fusion(pred[8,34]{0,1:T(8,128)(4,1)S(1)} %copy-done.8, bf16[3,3,32,32]{3,2,1,0:T(8,128)(2,1)S(1)} %copy-done.3, bf16[46,1,7,2,32]{4,2,3,0,1:T(8,128)(2,1)S(1)} %slice.103, bf16[46,1,8,34,32]{4,2,3,0,1:T(8,128)(2,1)} %copy.78), kind=kOutput, calls=%fused_computation.5 | convolution fusion | flops 224286720 | bytes 1626640 | tf_op jit(solution)/shard_map/conv_general_dilated | solution.py:27
  92.6 4.5 %copy.79 = bf16[44,8,34,32]{2,1,3,0:T(8,128)(2,1)S(1)} copy(bf16[44,8,34,32]{3,1,2,0:T(8,128)(2,1)} %select_maximum_fusion.1) | data formatting | bytes 1531904 | tf_op jit(solution)/shard_map/max | solution.py:48
  97.1 2.8 %reshape.287 = bf16[44,1,272,32]{2,3,0,1:T(8,128)(2,1)} reshape(bf16[44,8,34,32]{2,1,3,0:T(8,128)(2,1)S(1)} %copy.79) | data formatting | bytes 1531904 | tf_op jit(solution)/shard_map/max | solution.py:48
  100.0 2.8 %slice_bitcast_fusion.4 = (bf16[44,268,32]{1,2,0:T(8,128)(2,1)}, bf16[44,1,268,32]{2,3,0,1:T(8,128)(2,1)}) fusion(bf16[44,1,272,32]{2,3,0,1:T(8,128)(2,1)} %reshape.287), kind=kLoop, calls=%fused_computation.130 | loop fusion | bytes 2264064 | tf_op jit(solution)/shard_map/max | solution.py:48
  102.7 3.6 %copy.81 = bf16[44,1,268,32]{3,2,0,1:T(8,128)(2,1)S(1)} copy(bf16[44,1,268,32]{2,3,0,1:T(8,128)(2,1)} %get-tuple-element.10) | data formatting | bytes 1509376 | tf_op jit(solution)/shard_map/max | solution.py:48
  106.3 5.0 %max.59 = bf16[22,2,134,2,32]{4,3,2,1,0:T(2,128)(2,1)} reshape(bf16[44,1,268,32]{3,2,0,1:T(8,128)(2,1)S(1)} %copy.81) | data formatting | bytes 1509376 | tf_op jit(solution)/shard_map/max | solution.py:48
  111.3 11.0 %convert_reduce_fusion = f32[22,134,32]{2,1,0:T(8,128)S(1)} fusion(bf16[22,2,134,2,32]{4,3,2,1,0:T(2,128)(2,1)} %max.59, pred[22,2,134,2]{3,2,1,0:T(8,128)(4,1)} %broadcast_and_fusion), kind=kLoop, calls=%fused_computation.6 | loop fusion | flops 1037696 | bytes 1143824 | tf_op jit(solution)/shard_map/reduce_sum | solution.py:89
  122.3 0.1 fusion.56
  122.5 0.1 copy.95
  122.6 0.2 pad.3.clone
  122.8 0.1 copy.84
  122.9 0.4 copy-done.4
  123.3 1.3 fusion.36
  124.6 0.1 copy.85
  124.8 0.9 fusion.33
  125.6 0.2 pad.5
  125.8 0.1 copy.87
  126.0 1.6 %fusion.37 = bf16[18,8,17,64]{3,1,2,0:T(8,128)(2,1)S(1)} fusion(bf16[3,3,64,64]{3,2,1,0:T(8,128)(2,1)S(1)} %copy-done, bf16[20,1,7,2,64]{4,2,3,0,1:T(8,128)(2,1)S(1)} %slice.109, bf16[20,1,8,17,64]{4,2,3,0,1:T(8,128)(2,1)S(1)} %copy.87, pred[8,17]{0,1:T(8,128)(4,1)S(1)} %copy-done.10), kind=kOutput, calls=%fused_computation.50 | convolution fusion | flops 182123520 | bytes 771208 | tf_op jit(solution)/shard_map/conv_general_dilated | solution.py:27
  127.6 0.2 copy.88
  127.8 0.3 reshape.301
  128.1 0.5 fusion.41
  128.7 0.2 broadcast_in_dim.135
  128.8 1.2 broadcast_in_dim.136
  130.1 4.4 %reshape.273 = bf16[36,260,64]{2,1,0:T(8,128)(2,1)} reshape(bf16[36,130,2,64]{3,2,1,0:T(2,128)(2,1)S(1)} %broadcast_in_dim.136) | data formatting | bytes 2396160 | tf_op jit(solution)/shard_map/reshape | solution.py:97
  134.5 2.5 %slice.111 = bf16[34,258,64]{2,1,0:T(8,128)(2,1)S(1)} slice(bf16[36,260,64]{2,1,0:T(8,128)(2,1)} %reshape.273), slice={[1:35], [1:259], [0:64]} | slice | bytes 2245632 | tf_op jit(solution)/shard_map/slice | solution.py:99
  137.0 0.5 fusion.32
  137.5 2.0 %copy.89 = bf16[34,258,32]{2,1,0:T(8,128)(2,1)} copy(bf16[34,258,32]{1,2,0:T(8,128)(2,1)S(1)} %fusion.32) | data formatting | bytes 1122816 | tf_op jit(solution)/shard_map/slice | solution.py:101
  139.5 2.9 %maximum_bitcast_fusion = bf16[34,1,258,96]{3,2,0,1:T(8,128)(2,1)S(1)} fusion(bf16[34,258,64]{2,1,0:T(8,128)(2,1)S(1)} %slice.111, bf16[34,258,32]{2,1,0:T(8,128)(2,1)} %copy.89), kind=kLoop, calls=%fused_computation.30 | loop fusion | flops 3368448 | bytes 3368448 | tf_op jit(solution)/shard_map/broadcast_in_dim | solution.py:28
  142.4 1.8 %pad.7 = bf16[34,1,264,96]{3,2,0,1:T(8,128)(2,1)} pad(bf16[34,1,258,96]{3,2,0,1:T(8,128)(2,1)S(1)} %maximum_bitcast_fusion, bf16[]{:T(256)} %constant.107), padding=0_0x0_0x0_6x0_0 | pad | bytes 3407618 | tf_op jit(solution)/shard_map/broadcast_in_dim | solution.py:28
  144.3 3.6 %reshape.304 = bf16[34,1,8,33,96]{4,3,2,0,1:T(8,128)(2,1)S(1)} reshape(bf16[34,1,264,96]{3,2,0,1:T(8,128)(2,1)} %pad.7) | data formatting | bytes 3446784 | tf_op jit(solution)/shard_map/conv_general_dilated | solution.py:27
  147.9 0.3 copy.91
  148.2 0.5 copy-done.5
  148.7 6.4 %maximum_convert_fusion = bf16[32,8,33,32]{3,1,2,0:T(8,128)(2,1)} fusion(pred[8,33]{0,1:T(8,128)(4,1)S(1)} %copy-done.7, bf16[3,3,32,96]{3,2,1,0:T(8,128)(2,1)S(1)} %copy-done.5, bf16[34,1,7,2,96]{4,2,3,0,1:T(8,128)(2,1)S(1)} %slice.112, bf16[34,1,8,33,96]{4,2,3,0,1:T(8,128)(2,1)S(1)} %copy.91), kind=kOutput, calls=%fused_computation.10 | convolution fusion | flops 473435136 | bytes 2411016 | tf_op jit(solution)/shard_map/conv_general_dilated | solution.py:27
  155.1 4.0 %copy.92 = bf16[32,8,33,32]{2,1,3,0:T(8,128)(2,1)S(1)} copy(bf16[32,8,33,32]{3,1,2,0:T(8,128)(2,1)} %maximum_convert_fusion) | data formatting | bytes 1081344 | tf_op jit(solution)/shard_map/convert_element_type | solution.py:103
  159.2 1.5 reshape.308
  160.7 0.2 fusion.43
  160.9 0.7 copy.93
  (51 shorter events, 0.9 us)
Async XLA Ops:
  0.0 126.0 %copy-start = (bf16[3,3,64,64]{3,2,1,0:T(8,128)(2,1)S(1)}, bf16[3,3,64,64]{3,2,1,0:T(8,128)(2,1)}, u32[]{:S(2)}) copy-start(bf16[3,3,64,64]{3,2,1,0:T(8,128)(2,1)} %param.17) | copy-start | bytes 221188
  35.7 6.6 %collective-permute-start = (bf16[8,256,12]{1,0,2:T(8,128)(2,1)S(1)}, bf16[8,256,12]{1,0,2:T(8,128)(2,1)S(1)}, u32[]{:S(2)}, u32[]{:S(2)}) collective-permute-start(bf16[8,256,12]{1,0,2:T(8,128)(2,1)S(1)} %get-tuple-element.13), channel_id=1, source_target_pairs={{0,2},{2,4},{4,6},{1,3},{3,5},{5,7},{8,10},{10,12},{12,14},{9,11},... | collective-permute-start | bytes 147464 | tf_op jit(solution)/shard_map/ppermute | solution.py:17
  39.1 6.0 %collective-permute-start.1 = (bf16[8,256,12]{1,0,2:T(8,128)(2,1)S(1)}, bf16[8,256,12]{1,0,2:T(8,128)(2,1)S(1)}, u32[]{:S(2)}, u32[]{:S(2)}) collective-permute-start(bf16[8,256,12]{1,0,2:T(8,128)(2,1)S(1)} %get-tuple-element.14), channel_id=1, source_target_pairs={{2,0},{4,2},{6,4},{3,1},{5,3},{7,5},{10,8},{12,10},{14,12},{11,9},... | collective-permute-start | bytes 147464 | tf_op jit(solution)/shard_map/ppermute | solution.py:19
  45.2 2.8 %collective-permute-start.2 = (bf16[48,8,12]{1,0,2:T(8,128)(2,1)S(1)}, bf16[48,8,12]{1,0,2:T(8,128)(2,1)S(1)}, u32[]{:S(2)}, u32[]{:S(2)}) collective-permute-start(bf16[48,8,12]{1,0,2:T(8,128)(2,1)S(1)} %get-tuple-element.11), channel_id=1, source_target_pairs={{0,1},{2,3},{4,5},{6,7},{8,9},{10,11},{12,13},{14,15},{16,17},{18,... | collective-permute-start | bytes 27656 | tf_op jit(solution)/shard_map/ppermute | solution.py:17
  46.5 3.3 %collective-permute-start.3 = (bf16[48,8,12]{1,0,2:T(8,128)(2,1)S(1)}, bf16[48,8,12]{1,0,2:T(8,128)(2,1)S(1)}, u32[]{:S(2)}, u32[]{:S(2)}) collective-permute-start(bf16[48,8,12]{1,0,2:T(8,128)(2,1)S(1)} %get-tuple-element.12), channel_id=1, source_target_pairs={{1,0},{3,2},{5,4},{7,6},{9,8},{11,10},{13,12},{15,14},{17,16},{19,... | collective-permute-start | bytes 27656 | tf_op jit(solution)/shard_map/ppermute | solution.py:19
  51.1 5.4 %copy-start.6 = (bf16[3,3,32,12]{2,3,1,0:T(8,128)(2,1)S(1)}, bf16[3,3,32,12]{2,3,1,0:T(8,128)(2,1)}, u32[]{:S(2)}) copy-start(bf16[3,3,32,12]{2,3,1,0:T(8,128)(2,1)} %param.14) | copy-start | bytes 20740
  51.1 5.4 %copy-start.9 = (pred[8,34]{0,1:T(8,128)(4,1)S(1)}, pred[8,34]{0,1:T(8,128)(4,1)}, u32[]{:S(2)}) copy-start(pred[8,34]{0,1:T(8,128)(4,1)} %constant.128) | copy-start | bytes 820
  79.6 6.0 %copy-start.3 = (bf16[3,3,32,32]{3,2,1,0:T(8,128)(2,1)S(1)}, bf16[3,3,32,32]{3,2,1,0:T(8,128)(2,1)}, u32[]{:S(2)}) copy-start(bf16[3,3,32,32]{3,2,1,0:T(8,128)(2,1)} %param.15) | copy-start | bytes 55300
  79.6 6.0 %copy-start.8 = (pred[8,34]{0,1:T(8,128)(4,1)S(1)}, pred[8,34]{0,1:T(8,128)(4,1)}, u32[]{:S(2)}) copy-start(pred[8,34]{0,1:T(8,128)(4,1)} %constant.127) | copy-start | bytes 820
  122.5 0.9 copy-start.4
  122.5 0.9 copy-start.11
  124.8 1.2 copy-start.10
  134.5 2.5 %copy-start.1 = (bf16[44,268,32]{1,2,0:T(8,128)(2,1)S(1)}, bf16[44,268,32]{1,2,0:T(8,128)(2,1)}, u32[]{:S(2)}) copy-start(bf16[44,268,32]{1,2,0:T(8,128)(2,1)} %get-tuple-element.9) | copy-start | bytes 2264068
  147.8 0.9 copy-start.5
  147.9 0.9 copy-start.7
  159.2 1.5 copy-start.2

commit v3 on v1

--- a/solution.py
+++ b/solution.py
@@ -24,14 +24,21 @@
 
 
 def valid_conv(padded, kernel):
-    return lax.conv_general_dilated(
-        padded[None],
-        kernel,
-        (1, 1),
-        "VALID",
-        dimension_numbers=("NCHW", "HWOI", "NCHW"),
-        preferred_element_type=jnp.float32,
-    )[0]
+    taps, _, outs, ins = kernel.shape[0], kernel.shape[1], kernel.shape[2], kernel.shape[3]
+    height = padded.shape[1] - taps + 1
+    width = padded.shape[2] - taps + 1
+    patches = jnp.concatenate(
+        [padded[:, a : a + height, e : e + width] for a in range(taps) for e in range(taps)], axis=0
+    )
+    flat = kernel.transpose(2, 0, 1, 3).reshape(outs, taps * taps * ins)
+    return jnp.einsum("ok,khw->ohw", flat, patches, preferred_element_type=jnp.float32)
+
+
+def pair_matrix(count, spread):
+    wide = jnp.arange(count * 2, dtype=jnp.int32) // 2
+    narrow = jnp.arange(count, dtype=jnp.int32)
+    ones = (narrow[:, None] == wide[None, :]).astype(jnp.bfloat16)
+    return ones if spread else ones.T
 
 
 def inside_mask(row_start, col_start, height, width, total_rows, total_cols):
@@ -86,15 +93,24 @@
     first_map = masked_layer(widened, encode_first, row0 - HALO + 1, col0 - HALO + 1, total_rows, total_cols)
     skip_wide = masked_layer(first_map, encode_second, row0 - HALO + 2, col0 - HALO + 2, total_rows, total_cols)
     channels, wide_rows, wide_cols = skip_wide.shape
-    pooled = jnp.mean(
-        skip_wide.astype(jnp.float32).reshape(channels, wide_rows // 2, 2, wide_cols // 2, 2), axis=(2, 4)
+    col_pairs = jnp.einsum(
+        "chw,wv->chv", skip_wide, pair_matrix(wide_cols // 2, False), preferred_element_type=jnp.float32
+    )
+    pooled = (
+        jnp.sum(col_pairs.reshape(channels, wide_rows // 2, 2, wide_cols // 2), axis=2) * 0.25
     ).astype(jnp.bfloat16)
     coarse_halo = (HALO - 2) // 2
     crow0 = row0 // 2 - coarse_halo
     ccol0 = col0 // 2 - coarse_halo
     mid = masked_layer(pooled, middle_first, crow0 + 1, ccol0 + 1, total_rows // 2, total_cols // 2)
     deeper = masked_layer(mid, middle_second, crow0 + 2, ccol0 + 2, total_rows // 2, total_cols // 2)
-    upsampled = jnp.repeat(jnp.repeat(deeper, 2, axis=1), 2, axis=2)
+    deep_ch, deep_rows, deep_cols = deeper.shape
+    spread = jnp.einsum(
+        "chv,vw->chw", deeper, pair_matrix(deep_cols, True), preferred_element_type=jnp.float32
+    ).astype(jnp.bfloat16)
+    upsampled = jnp.broadcast_to(spread[:, :, None], (deep_ch, deep_rows, 2, 2 * deep_cols)).reshape(
+        deep_ch, 2 * deep_rows, 2 * deep_cols
+    )
     up_halo = 2 * (coarse_halo - 2)
     upsampled = upsampled[:, up_halo - 1 : up_halo + block_rows + 1, up_halo - 1 : up_halo + block_cols + 1]
     skip_halo = HALO - 2

time: 165 us -> 173 us (1.048)
  local copies, waits for them, and re-layouts: 74.5 us -> 87.3 us
  matrix products: 24.4 us -> 18.6 us
  waiting for transfers between devices: 4.56 us -> 2.73 us
    slice x0 -> x11, local copies, waits for them, and re-layouts: none -> 40.7 us  [valid_conv(): padded[:, a:a + height, e:e + width]]
    concatenate x0 -> x4, local copies, waits for them, and re-layouts: none -> 34.3 us  [valid_conv(): jnp.concatenate([padded[:, a:a + height, e:e + width] for a in range(taps...]
    max x10 -> x0, local copies, waits for them, and re-layouts: 27.7 us -> none  [masked_layer(): return jnp.where(mask, jnp.maximum(out, 0.0), 0.0).astype(jnp.bfloat16)]
    conv_general_dilated x5 -> x0, matrix products: 24.2 us -> none  [valid_conv(): lax.conv_general_dilated(padded[None], kernel, (1, 1), 'VALID', dimension...]
    conv_general_dilated x13 -> x0, local copies, waits for them, and re-layouts: 20.5 us -> none  [valid_conv(): lax.conv_general_dilated(padded[None], kernel, (1, 1), 'VALID', dimension...]
    unnamed x0 -> x8, other arithmetic: none -> 14.5 us
    dot_general x0 -> x5, matrix products: none -> 11 us  [the longest x3 6.37 us: valid_conv(): jnp.einsum('ok,khw->ohw', flat, patches, preferred_element_type=jnp.float32)]
    reduce_sum x1, other arithmetic: 11 us -> 0.2 us  [shards(): jnp.sum(col_pairs.reshape(channels, wide_rows // 2, 2, wide_cols // 2), a...]
  transfers between devices with their start and end apart: 4 -> 4, of which waited for: 2 -> 2; matrix products, arithmetic and copies ran while one was open for 1% -> 2% of each run, Pallas kernels for 0% -> 0%
where the time goes in v3:
time: 173 us; the launch traced here: 171 us
  local copies, waits for them, and re-layouts  87.3 us (50%)
  other arithmetic  31.6 us (18%)
  blocking collectives  22.8 us (13%)
  matrix products  18.6 us (11%)
  starting transfers between devices  7.28 us (4%)
  waiting for transfers between devices  2.73 us (2%)
    slice x11, local copies, waits for them, and re-layouts, valid_conv(): padded[:, a:a + height, e:e + width]  40.7 us
    concatenate x4, local copies, waits for them, and re-layouts, valid_conv(): jnp.concatenate([padded[:, a:a + height, e:e + width] for a in range(taps...  34.3 us
    all_gather x1, blocking collectives, shards(): gathered = lax.all_gather(packed, 'tm', axis=0).astype(jnp.float32)  22.8 us
    unnamed x8, other arithmetic  14.5 us
    reduce_max x1, other arithmetic, shards(): shift = jnp.max(scores, axis=0).astype(jnp.bfloat16).astype(jnp.float32)  8.75 us
    dot_general x1, matrix products, shards(): jnp.einsum('oc,chw->ohw', head_weight, decoded, preferred_element_type=jn...  7.68 us
    unnamed x38, local copies, waits for them, and re-layouts  7.16 us
    dot_general x3, matrix products, valid_conv(): jnp.einsum('ok,khw->ohw', flat, patches, preferred_element_type=jnp.float32)  6.37 us
  transfers between devices with their start and end apart: 4, of which 2 were waited for; matrix products, arithmetic and copies ran while one was open for 2% of the time, Pallas kernels for 0%

profile of v3, /device:TPU:0, one launch (start us, length us, event | category | flops | bytes accessed | tf_op | source)
XLA Modules:
  0.0 170.9 jit_solution(5357430983880363031)
XLA Ops:
  0.0 1.8 %fusion.68 = (f32[1]{0:T(128)}, f32[1]{0:T(128)}, f32[1]{0:T(128)}, f32[1]{0:T(128)}, f32[1]{0:T(128)}, /*index=5*/f32[1]{0:T(128)}, f32[1]{0:T(128)}, f32[1]{0:...) fusion(f32[12]{0:T(128)} %param.13), kind=kLoop, calls=%fused_computation.146 | loop fusion | bytes 96 | tf_op jit(solution)/shard_map/slice | solution.py:76
  1.8 8.8 %fusion.63 = (bf16[32,256]{1,0:T(8,128)(2,1)S(1)}, f32[8,32,256]{2,1,0:T(8,128)S(1)}) fusion(f32[8,32,256]{2,1,0:T(8,128)} %param.12, f32[]{:T(128)} %bitcast.11, s32[8,32,256]{2,1,0:T(8,128)} %param.11, f32[]{:T(128)} %bitcast.10, f32[]{:T(128)} %bitcast.9, f32[]{:T(128)} %bitcast.8, f32[]{:T(128)} %bitcast.7, f32[]{:T(128)} %bitcast.6, f32[]{:T(128)} %bitcast.5, ...), kind=kLoop, calls=%fused_computation.141 | loop fusion | flops 1695744 | bytes 802864 | tf_op jit(solution)/shard_map/reduce_max | solution.py:78
  10.6 1.7 %multiply_reduce_fusion = bf16[12,32,256]{2,1,0:T(8,128)(2,1)S(1)} fusion(bf16[8,12,32,256]{3,2,1,0:T(8,128)(2,1)} %param.10, f32[8,32,256]{2,1,0:T(8,128)S(1)} %get-tuple-element.6), kind=kLoop, calls=%fused_computation.16 | loop fusion | flops 2260992 | bytes 2031616 | tf_op jit(solution)/shard_map/reduce_sum | solution.py:80
  12.4 22.8 %all_gather.4 = bf16[4,14,32,256]{3,2,1,0:T(8,128)(2,1)S(1)} all-gather(bf16[1,14,32,256]{3,2,1,0:T(8,128)(2,1)S(1)} %pad_maximum_fusion.3), channel_id=1, replica_groups=mesh['tm'=4,'row'=4,'col'=2] {'tm'}, dimensions={0}, use_global_device_ids=true | all-gather | bytes 1146880 | tf_op jit(solution)/shard_map/all_gather | solution.py:83
  35.8 3.4 %collective-permute-start = (bf16[12,8,256]{2,1,0:T(8,128)(2,1)S(1)}, bf16[12,8,256]{2,1,0:T(8,128)(2,1)S(1)}, u32[]{:S(2)}, u32[]{:S(2)}) collective-permute-start(bf16[12,8,256]{2,1,0:T(8,128)(2,1)S(1)} %get-tuple-element.29), channel_id=1, source_target_pairs={{0,2},{2,4},{4,6},{1,3},{3,5},{5,7},{8,10},{10,12},{12,14},{9,11},... | collective-permute-start | bytes 147464 | tf_op jit(solution)/shard_map/ppermute | solution.py:17
  39.2 1.3 collective-permute-start.1
  40.6 0.7 broadcast_and_fusion
  41.4 0.7 broadcast_and_fusion.2
  42.1 0.7 broadcast_and_fusion.3
  42.7 0.5 add_select_fusion.1
  43.3 1.9 %collective-permute-done.1 = bf16[12,8,256]{2,1,0:T(8,128)(2,1)S(1)} collective-permute-done((bf16[12,8,256]{2,1,0:T(8,128)(2,1)S(1)}, bf16[12,8,256]{2,1,0:T(8,128)(2,1)S(1)}, u32[]{:S(2)}, u32[]{:S(2)}) %collective-permute-start.1) | collective-permute-done | bytes 49184 | tf_op jit(solution)/shard_map/ppermute | solution.py:19
  45.3 1.3 collective-permute-start.2
  46.6 1.3 collective-permute-start.3
  47.9 0.5 add_select_fusion
  49.0 0.9 collective-permute-done.3
  49.9 0.3 pad_maximum_fusion.1
  50.1 2.9 %fusion.65 = (bf16[12,46,270]{2,1,0:T(8,128)(2,1)}, bf16[12,46,270]{2,1,0:T(8,128)(2,1)}, bf16[12,46,270]{2,1,0:T(8,128)(2,1)}, bf16[12,46,270]{2,1,0:T(8,128)(2...) fusion(bf16[12,48,272]{2,1,0:T(8,128)(2,1)S(1)} %pad_maximum_fu, ...), kind=kLoop, calls=%fused_computation.143 | loop fusion | bytes 5365440 | tf_op jit(solution)/shard_map/slice | solution.py:31
  53.0 3.5 %copy.30 = bf16[12,46,270]{0,2,1:T(8,128)(2,1)S(1)} copy(bf16[12,46,270]{2,1,0:T(8,128)(2,1)} %get-tuple-element.26) | data formatting | bytes 596160 | tf_op jit(solution)/shard_map/slice | solution.py:31
  56.6 3.9 %copy.31 = bf16[12,46,270]{0,2,1:T(8,128)(2,1)} copy(bf16[12,46,270]{2,1,0:T(8,128)(2,1)} %get-tuple-element.25) | data formatting | bytes 596160 | tf_op jit(solution)/shard_map/slice | solution.py:31
  60.5 3.9 %copy.32 = bf16[12,46,270]{0,2,1:T(8,128)(2,1)} copy(bf16[12,46,270]{2,1,0:T(8,128)(2,1)} %get-tuple-element.24) | data formatting | bytes 596160 | tf_op jit(solution)/shard_map/slice | solution.py:31
  64.4 4.0 %copy.33 = bf16[12,46,270]{0,2,1:T(8,128)(2,1)} copy(bf16[12,46,270]{2,1,0:T(8,128)(2,1)} %get-tuple-element.23) | data formatting | bytes 596160 | tf_op jit(solution)/shard_map/slice | solution.py:31
  68.4 3.9 %copy.34 = bf16[12,46,270]{0,2,1:T(8,128)(2,1)} copy(bf16[12,46,270]{2,1,0:T(8,128)(2,1)} %get-tuple-element.22) | data formatting | bytes 596160 | tf_op jit(solution)/shard_map/slice | solution.py:31
  72.3 3.9 %copy.35 = bf16[12,46,270]{0,2,1:T(8,128)(2,1)} copy(bf16[12,46,270]{2,1,0:T(8,128)(2,1)} %get-tuple-element.21) | data formatting | bytes 596160 | tf_op jit(solution)/shard_map/slice | solution.py:31
  76.2 3.9 %copy.36 = bf16[12,46,270]{0,2,1:T(8,128)(2,1)} copy(bf16[12,46,270]{2,1,0:T(8,128)(2,1)} %get-tuple-element.20) | data formatting | bytes 596160 | tf_op jit(solution)/shard_map/slice | solution.py:31
  80.1 3.9 %copy.37 = bf16[12,46,270]{0,2,1:T(8,128)(2,1)} copy(bf16[12,46,270]{2,1,0:T(8,128)(2,1)} %get-tuple-element.19) | data formatting | bytes 596160 | tf_op jit(solution)/shard_map/slice | solution.py:31
  84.0 4.0 %copy.38 = bf16[12,46,270]{0,2,1:T(8,128)(2,1)} copy(bf16[12,46,270]{2,1,0:T(8,128)(2,1)} %get-tuple-element.18) | data formatting | bytes 596160 | tf_op jit(solution)/shard_map/slice | solution.py:31
  88.0 25.7 %concatenate.47 = bf16[108,46,270]{0,2,1:T(8,128)(2,1)} concatenate(bf16[12,46,270]{0,2,1:T(8,128)(2,1)S(1)} %copy.30, bf16[12,46,270]{0,2,1:T(8,128)(2,1)} %copy.31, bf16[12,46,270]{0,2,1:T(8,128)(2,1)} %copy.32, bf16[12,46,270]{0,2,1:T(8,128)(2,1)} %copy.33, bf16[12,46,270]{0,2,1:T(8,128)(2,1)} %copy.34, bf16[12,46,270]{0,2,1:T(8,128)(2,1)} %copy.35, ...), dimensions={0} | concatenate | bytes 5365440 | tf_op jit(solution)/shard_map/concatenate | solution.py:30
  113.7 3.4 %fusion.20 = bf16[32,46,270]{2,0,1:T(8,128)(2,1)S(1)} fusion(bf16[108,46,270]{0,2,1:T(8,128)(2,1)} %concatenate.47, pred[46,270]{1,0:T(8,128)(4,1)} %broadcast_and_fusion, bf16[32,108]{0,1:T(8,128)(2,1)S(1)} %reshape.274), kind=kOutput, calls=%fused_computation.45 | convolution fusion | flops 87039360 | bytes 3496932 | tf_op jit(solution)/shard_map/ok,khw->ohw/dot_general | solution.py:34
  117.3 0.6 slice_dynamic-update-slice_fusion.7
  117.8 0.6 slice_dynamic-update-slice_fusion.6
  118.4 0.2 slice_dynamic-update-slice_fusion.5
  118.6 0.6 slice_dynamic-update-slice_fusion.4
  119.2 0.6 slice_dynamic-update-slice_fusion.3
  119.7 0.2 slice_dynamic-update-slice_fusion.2
  120.0 0.6 slice_dynamic-update-slice_fusion.1
  120.5 0.6 slice_dynamic-update-slice_fusion
  121.1 1.9 %fusion.21 = bf16[32,44,268]{2,0,1:T(8,128)(2,1)S(1)} fusion(bf16[288,44,268]{2,0,1:T(8,128)(2,1)S(1)} %slice_dynamic-update-slice_fusion, bf16[32,288,1]{1,0,2:T(8,128)(2,1)S(1)} %reshape.282, pred[44,268]{1,0:T(8,128)(4,1)S(1)} %broadcast_and_fusion.1), kind=kOutput, calls=%fused_computation.46 | convolution fusion | flops 218482176 | bytes 7577104 | tf_op jit(solution)/shard_map/ok,khw->ohw/dot_general | solution.py:34
  123.0 0.4 slice.289
  123.4 0.6 fusion.35
  124.2 0.5 copy.44
  124.9 2.8 %fusion.64 = (bf16[32,20,132]{0,2,1:T(8,128)(2,1)}, bf16[32,20,132]{0,2,1:T(8,128)(2,1)}, bf16[32,20,132]{0,2,1:T(8,128)(2,1)}, bf16[32,20,132]{0,2,1:T(8,128)(2...) fusion(bf16[32,22,134]{0,2,1:T(8,128)(2,1)S(1)} %multiply_conve, ...), kind=kLoop, calls=%fused_computation.142 | loop fusion | bytes 3041280 | tf_op jit(solution)/shard_map/slice | solution.py:31
  127.6 7.8 %concatenate.49 = bf16[288,20,132]{0,2,1:T(8,128)(2,1)S(1)} concatenate(bf16[32,20,132]{0,2,1:T(8,128)(2,1)} %get-tuple-element.17, bf16[32,20,132]{0,2,1:T(8,128)(2,1)} %get-tuple-element.16, bf16[32,20,132]{0,2,1:T(8,128)(2,1)} %get-tuple-element.15, bf16[32,20,132]{0,2,1:T(8,128)(2,1)} %get-tuple-element.14, bf16[32,20,132]{0,2,1:T(8,128)(2,1)} %get-tuple-element.13, ...), dimensions={0} | concatenate | bytes 3041280 | tf_op jit(solution)/shard_map/concatenate | solution.py:30
  135.5 1.1 fusion.25
  136.7 0.3 slice_dynamic-update-slice_fusion.16
  136.9 0.3 slice_dynamic-update-slice_fusion.15
  137.3 0.3 slice_dynamic-update-slice_fusion.13
  137.5 0.3 slice_dynamic-update-slice_fusion.12
  137.9 0.3 slice_dynamic-update-slice_fusion.10
  138.1 0.3 slice_dynamic-update-slice_fusion.9
  138.4 2.3 %copy-done.4 = bf16[576,18,130]{2,0,1:T(8,128)(2,1)} copy-done((bf16[576,18,130]{2,0,1:T(8,128)(2,1)}, bf16[576,18,130]{2,0,1:T(8,128)(2,1)S(1)}, u32[]{:S(2)}) %copy-start.4) | copy-done | bytes 2695704
  140.7 4.0 %convolution_convert_fusion = bf16[64,18,260]{2,0,1:T(8,128)(2,1)S(1)} fusion(bf16[576,18,130]{2,0,1:T(8,128)(2,1)} %copy-done.4, bf16[64,576,1]{0,1,2:T(8,128)(2,1)S(1)} %bitcast.107, pred[18,130]{1,0:T(8,128)(4,1)S(1)} %copy-done.8, s32[260]{0:T(512)S(1)} %copy-done.10), kind=kOutput, calls=%fused_computation.40 | convolution fusion | flops 251181312 | bytes 3371828 | tf_op jit(solution)/shard_map/chv,vw->chw/dot_general | solution.py:108
  144.8 0.3 broadcast_in_dim.126
  145.1 0.8 slice.308
  145.8 1.4 fusion.3
  147.2 2.1 %fusion.5 = bf16[864,32,256]{2,0,1:T(8,128)(2,1)} fusion(bf16[864,32,256]{2,0,1:T(8,128)(2,1)} %fusion.3, bf16[64,34,258]{2,0,1:T(8,128)(2,1)S(1)} %slice.308, bf16[32,34,258]{2,0,1:T(8,128)(2,1)S(1)} %slice.289), kind=kLoop, calls=%fused_computation.24 | loop fusion | flops 3145728 | bytes 3257088
  149.3 2.2 %fusion.7 = bf16[864,32,256]{2,0,1:T(8,128)(2,1)} fusion(bf16[864,32,256]{2,0,1:T(8,128)(2,1)} %fusion.5, bf16[64,34,258]{2,0,1:T(8,128)(2,1)S(1)} %slice.308, bf16[32,34,258]{2,0,1:T(8,128)(2,1)S(1)} %slice.289), kind=kLoop, calls=%fused_computation.26 | loop fusion | flops 3145728 | bytes 3257088
  151.4 1.3 fusion.9
  152.7 2.1 %fusion.11 = bf16[864,32,256]{2,0,1:T(8,128)(2,1)} fusion(bf16[864,32,256]{2,0,1:T(8,128)(2,1)} %fusion.9, bf16[64,34,258]{2,0,1:T(8,128)(2,1)S(1)} %slice.308, bf16[32,34,258]{2,0,1:T(8,128)(2,1)S(1)} %slice.289), kind=kLoop, calls=%fused_computation.30 | loop fusion | flops 3145728 | bytes 3257088
  154.9 2.1 %fusion.13 = bf16[864,32,256]{2,0,1:T(8,128)(2,1)} fusion(bf16[864,32,256]{2,0,1:T(8,128)(2,1)} %fusion.11, bf16[64,34,258]{2,0,1:T(8,128)(2,1)S(1)} %slice.308, bf16[32,34,258]{2,0,1:T(8,128)(2,1)S(1)} %slice.289), kind=kLoop, calls=%fused_computation.32 | loop fusion | flops 3145728 | bytes 3257088
  156.9 1.3 fusion.15
  158.2 2.1 %fusion.1 = bf16[864,32,256]{2,0,1:T(8,128)(2,1)} fusion(bf16[864,32,256]{2,0,1:T(8,128)(2,1)} %fusion.15, bf16[64,34,258]{2,0,1:T(8,128)(2,1)S(1)} %slice.308, bf16[32,34,258]{2,0,1:T(8,128)(2,1)S(1)} %slice.289), kind=kLoop, calls=%fused_computation.20 | loop fusion | flops 3145728 | bytes 3257088
  160.3 2.1 %fusion.16 = bf16[864,32,256]{2,0,1:T(8,128)(2,1)} fusion(bf16[864,32,256]{2,0,1:T(8,128)(2,1)} %fusion.1, bf16[64,34,258]{2,0,1:T(8,128)(2,1)S(1)} %slice.308, bf16[32,34,258]{2,0,1:T(8,128)(2,1)S(1)} %slice.289), kind=kLoop, calls=%fused_computation.36 | loop fusion | flops 3145728 | bytes 3257088 | tf_op jit(solution)/shard_map/concatenate | solution.py:30
  162.5 7.7 %fusion.30 = bf16[11,32,256]{2,0,1:T(8,128)(2,1)S(1)} fusion(bf16[32,864,1]{1,0,2:T(8,128)(2,1)S(1)} %reshape.287, bf16[864,32,256]{2,0,1:T(8,128)(2,1)} %fusion.16, bf16[11,32]{1,0:T(8,128)(2,1)S(1)} %copy-done.9), kind=kOutput, calls=%fused_computation.56 | convolution fusion | flops 459366400 | bytes 14392000 | tf_op jit(solution)/shard_map/oc,chw->ohw/dot_general | solution.py:120
  170.2 0.7 copy.50
  (56 shorter events, 2.0 us)
Async XLA Ops:
  0.0 135.5 %copy-start = (bf16[3,3,64,32]{2,3,1,0:T(8,128)(2,1)S(1)}, bf16[3,3,64,32]{2,3,1,0:T(8,128)(2,1)}, u32[]{:S(2)}) copy-start(bf16[3,3,64,32]{2,3,1,0:T(8,128)(2,1)} %param.16) | copy-start | bytes 110596
  35.4 13.1 %copy-start.5 = (bf16[3,3,32,12]{2,3,1,0:T(8,128)(2,1)S(1)}, bf16[3,3,32,12]{2,3,1,0:T(8,128)(2,1)}, u32[]{:S(2)}) copy-start(bf16[3,3,32,12]{2,3,1,0:T(8,128)(2,1)} %param.14) | copy-start | bytes 20740
  35.4 13.1 %copy-start.2 = (bf16[3,3,32,32]{3,2,1,0:T(8,128)(2,1)S(1)}, bf16[3,3,32,32]{3,2,1,0:T(8,128)(2,1)}, u32[]{:S(2)}) copy-start(bf16[3,3,32,32]{3,2,1,0:T(8,128)(2,1)} %param.15) | copy-start | bytes 55300
  35.4 13.2 %copy-start.1 = (bf16[3,3,64,64]{3,2,1,0:T(8,128)(2,1)S(1)}, bf16[3,3,64,64]{3,2,1,0:T(8,128)(2,1)}, u32[]{:S(2)}) copy-start(bf16[3,3,64,64]{3,2,1,0:T(8,128)(2,1)} %param.17) | copy-start | bytes 221188
  35.4 13.4 %copy-start.3 = (bf16[3,3,32,96]{3,2,1,0:T(8,128)(2,1)S(1)}, bf16[3,3,32,96]{3,2,1,0:T(8,128)(2,1)}, u32[]{:S(2)}) copy-start(bf16[3,3,32,96]{3,2,1,0:T(8,128)(2,1)} %param.18) | copy-start | bytes 165892
  35.8 7.5 %collective-permute-start = (bf16[12,8,256]{2,1,0:T(8,128)(2,1)S(1)}, bf16[12,8,256]{2,1,0:T(8,128)(2,1)S(1)}, u32[]{:S(2)}, u32[]{:S(2)}) collective-permute-start(bf16[12,8,256]{2,1,0:T(8,128)(2,1)S(1)} %get-tuple-element.29), channel_id=1, source_target_pairs={{0,2},{2,4},{4,6},{1,3},{3,5},{5,7},{8,10},{10,12},{12,14},{9,11},... | collective-permute-start | bytes 147464 | tf_op jit(solution)/shard_map/ppermute | solution.py:17
  39.2 6.0 %collective-permute-start.1 = (bf16[12,8,256]{2,1,0:T(8,128)(2,1)S(1)}, bf16[12,8,256]{2,1,0:T(8,128)(2,1)S(1)}, u32[]{:S(2)}, u32[]{:S(2)}) collective-permute-start(bf16[12,8,256]{2,1,0:T(8,128)(2,1)S(1)} %get-tuple-element.30), channel_id=1, source_target_pairs={{2,0},{4,2},{6,4},{3,1},{5,3},{7,5},{10,8},{12,10},{14,12},{11,9},... | collective-permute-start | bytes 147464 | tf_op jit(solution)/shard_map/ppermute | solution.py:19
  45.3 3.7 %collective-permute-start.2 = (bf16[12,48,8]{2,1,0:T(8,128)(2,1)S(1)}, bf16[12,48,8]{2,1,0:T(8,128)(2,1)S(1)}, u32[]{:S(2)}, u32[]{:S(2)}) collective-permute-start(bf16[12,48,8]{2,1,0:T(8,128)(2,1)S(1)} %get-tuple-element.27), channel_id=1, source_target_pairs={{0,1},{2,3},{4,5},{6,7},{8,9},{10,11},{12,13},{14,15},{16,17},{18,... | collective-permute-start | bytes 27656 | tf_op jit(solution)/shard_map/ppermute | solution.py:17
  46.6 3.3 %collective-permute-start.3 = (bf16[12,48,8]{2,1,0:T(8,128)(2,1)S(1)}, bf16[12,48,8]{2,1,0:T(8,128)(2,1)S(1)}, u32[]{:S(2)}, u32[]{:S(2)}) collective-permute-start(bf16[12,48,8]{2,1,0:T(8,128)(2,1)S(1)} %get-tuple-element.28), channel_id=1, source_target_pairs={{1,0},{3,2},{5,4},{7,6},{9,8},{11,10},{13,12},{15,14},{17,16},{19,... | collective-permute-start | bytes 27656 | tf_op jit(solution)/shard_map/ppermute | solution.py:19
  121.1 2.3 %copy-start.7 = (s32[268]{0:T(512)S(1)}, s32[268]{0:T(512)}, u32[]{:S(2)}) copy-start(s32[268]{0:T(512)} %add_select_fusion.1) | copy-start | bytes 3220
  127.6 7.9 %copy-start.6 = (pred[20,132]{1,0:T(8,128)(4,1)S(1)}, pred[20,132]{1,0:T(8,128)(4,1)}, u32[]{:S(2)}) copy-start(pred[20,132]{1,0:T(8,128)(4,1)} %broadcast_and_fusion.2) | copy-start | bytes 7924
  137.3 3.5 %copy-start.8 = (pred[18,130]{1,0:T(8,128)(4,1)S(1)}, pred[18,130]{1,0:T(8,128)(4,1)}, u32[]{:S(2)}) copy-start(pred[18,130]{1,0:T(8,128)(4,1)} %broadcast_and_fusion.3) | copy-start | bytes 7024
  137.3 3.5 %copy-start.10 = (s32[260]{0:T(512)S(1)}, s32[260]{0:T(512)}, u32[]{:S(2)}) copy-start(s32[260]{0:T(512)} %add_select_fusion) | copy-start | bytes 3124
  138.4 2.3 %copy-start.4 = (bf16[576,18,130]{2,0,1:T(8,128)(2,1)}, bf16[576,18,130]{2,0,1:T(8,128)(2,1)S(1)}, u32[]{:S(2)}) copy-start(bf16[576,18,130]{2,0,1:T(8,128)(2,1)S(1)} %slice_dynamic-update-slice_fusion.9) | copy-start | bytes 8087044
  158.2 4.3 %copy-start.9 = (bf16[11,32]{1,0:T(8,128)(2,1)S(1)}, bf16[11,32]{1,0:T(8,128)(2,1)}, u32[]{:S(2)}) copy-start(bf16[11,32]{1,0:T(8,128)(2,1)} %param.19) | copy-start | bytes 2116

commit v4 on v2

--- a/solution.py
+++ b/solution.py
@@ -24,14 +24,20 @@
 
 
 def valid_conv(padded, kernel):
-    return lax.conv_general_dilated(
-        padded[None],
-        kernel,
-        (1, 1),
-        "VALID",
-        dimension_numbers=("NHWC", "HWOI", "NHWC"),
-        preferred_element_type=jnp.float32,
-    )[0]
+    taps = kernel.shape[0]
+    height = padded.shape[0] - taps + 1
+    width = padded.shape[1] - taps + 1
+    total = None
+    for a in range(taps):
+        for e in range(taps):
+            term = jnp.einsum(
+                "hwc,oc->hwo",
+                padded[a : a + height, e : e + width],
+                kernel[a, e],
+                preferred_element_type=jnp.float32,
+            )
+            total = term if total is None else total + term
+    return total
 
 
 def inside_mask(row_start, col_start, height, width, total_rows, total_cols):

time: 163 us -> 113 us (0.69)
  local copies, waits for them, and re-layouts: 71.3 us -> 29.7 us
  other arithmetic: 30.6 us -> 19.8 us
  waiting for transfers between devices: 4.56 us -> 6.41 us
    max x10 -> x0, local copies, waits for them, and re-layouts: 27.7 us -> none  [masked_layer(): return jnp.where(mask, jnp.maximum(out, 0.0), 0.0).astype(jnp.bfloat16)]
    conv_general_dilated x5 -> x0, matrix products: 24.2 us -> none  [valid_conv(): lax.conv_general_dilated(padded[None], kernel, (1, 1), 'VALID', dimension...]
    dot_general x0 -> x44, matrix products: none -> 23.3 us  [valid_conv(): jnp.einsum('hwc,oc->hwo', padded[a:a + height, e:e + width], kernel[a, e]...]
    conv_general_dilated x13 -> x0, local copies, waits for them, and re-layouts: 20.5 us -> none  [valid_conv(): lax.conv_general_dilated(padded[None], kernel, (1, 1), 'VALID', dimension...]
    reshape x0 -> x2, local copies, waits for them, and re-layouts: none -> 11.5 us  [shards(): skip_wide.astype(jnp.float32)]
    convert_element_type x3 -> x0, local copies, waits for them, and re-layouts: 5.7 us -> none  [the longest x2 5.52 us: shards(): jnp.maximum(valid_conv(joined, decode_kernel), 0.0).astype(jnp.bfloat16)]
    convert_element_type x4 -> x0, other arithmetic: 3.51 us -> none  [masked_layer(): return jnp.where(mask, jnp.maximum(out, 0.0), 0.0).astype(jnp.bfloat16)]
    reduce_sum x1, other arithmetic: 11 us -> 7.66 us  [shards(): jnp.mean(skip_wide.astype(jnp.float32).reshape(wide_rows // 2, 2, wide_co...]
  transfers between devices with their start and end apart: 4 -> 4, of which waited for: 2 -> 3; matrix products, arithmetic and copies ran while one was open for 1% -> 0% of each run, Pallas kernels for 0% -> 0%
where the time goes in v4:
time: 113 us; the launch traced here: 112 us
  local copies, waits for them, and re-layouts  29.7 us (26%)
  matrix products  25.5 us (23%)
  blocking collectives  22.8 us (20%)
  other arithmetic  19.8 us (18%)
  starting transfers between devices  7.28 us (6%)
  waiting for transfers between devices  6.41 us (6%)
    dot_general x44, matrix products, valid_conv(): jnp.einsum('hwc,oc->hwo', padded[a:a + height, e:e + width], kernel[a, e]...  23.3 us
    all_gather x1, blocking collectives, shards(): gathered = lax.all_gather(packed, 'tm', axis=0).astype(jnp.float32)  22.8 us
    reshape x2, local copies, waits for them, and re-layouts, shards(): skip_wide.astype(jnp.float32)  11.5 us
    reduce_max x1, other arithmetic, shards(): shift = jnp.max(scores, axis=0).astype(jnp.bfloat16).astype(jnp.float32)  8.74 us
    reduce_sum x1, other arithmetic, shards(): jnp.mean(skip_wide.astype(jnp.float32).reshape(wide_rows // 2, 2, wide_co...  7.66 us
    ppermute x2, waiting for transfers between devices, with_halo(): lax.ppermute(head, axis, [((i + 1) % count, i) for i in range(ends)])  6.23 us
    ppermute x2, starting transfers between devices, with_halo(): lax.ppermute(tail, axis, [(i, (i + 1) % count) for i in range(ends)])  4.7 us
    reshape x1, local copies, waits for them, and re-layouts, shards(): upsampled = jnp.repeat(jnp.repeat(deeper, 2, axis=0), 2, axis=1)  4.44 us
  transfers between devices with their start and end apart: 4, of which 3 were waited for; matrix products, arithmetic and copies ran while one was open for 0% of the time, Pallas kernels for 0%

profile of v4, /device:TPU:0, one launch (start us, length us, event | category | flops | bytes accessed | tf_op | source)
XLA Modules:
  0.0 112.0 jit_solution(6037263394461252852)
XLA Ops:
  0.0 1.8 %fusion.239 = (f32[1]{0:T(128)}, f32[1]{0:T(128)}, f32[1]{0:T(128)}, f32[1]{0:T(128)}, f32[1]{0:T(128)}, /*index=5*/f32[1]{0:T(128)}, f32[1]{0:T(128)}, f32[1]{0...) fusion(f32[12]{0:T(128)} %param.13), kind=kLoop, calls=%fused_computation.276 | loop fusion | bytes 96 | tf_op jit(solution)/shard_map/slice | solution.py:75
  1.8 8.7 %fusion.236 = (bf16[32,256]{1,0:T(8,128)(2,1)S(1)}, f32[8,32,256]{2,1,0:T(8,128)S(1)}) fusion(f32[8,32,256]{2,1,0:T(8,128)} %param.12, f32[]{:T(128)} %bitcast.11, s32[8,32,256]{2,1,0:T(8,128)} %param.11, f32[]{:T(128)} %bitcast.10, f32[]{:T(128)} %bitcast.9, f32[]{:T(128)} %bitcast.8, f32[]{:T(128)} %bitcast.7, f32[]{:T(128)} %bitcast.6, f32[]{:T(128)} %bitcast.5, ...), kind=kLoop, calls=%fused_computation.273 | loop fusion | flops 1695744 | bytes 802864 | tf_op jit(solution)/shard_map/reduce_max | solution.py:77
  10.6 1.7 %multiply_reduce_fusion = bf16[12,32,256]{2,1,0:T(8,128)(2,1)S(1)} fusion(bf16[8,12,32,256]{3,2,1,0:T(8,128)(2,1)} %param.10, f32[8,32,256]{2,1,0:T(8,128)S(1)} %get-tuple-element.6), kind=kLoop, calls=%fused_computation.16 | loop fusion | flops 2260992 | bytes 2031616 | tf_op jit(solution)/shard_map/reduce_sum | solution.py:79
  12.4 22.8 %all_gather.4 = bf16[4,14,32,256]{3,2,1,0:T(8,128)(2,1)S(1)} all-gather(bf16[1,14,32,256]{3,2,1,0:T(8,128)(2,1)S(1)} %pad_maximum_fusion.16), channel_id=1, replica_groups=mesh['tm'=4,'row'=4,'col'=2] {'tm'}, dimensions={0}, use_global_device_ids=true | all-gather | bytes 1146880 | tf_op jit(solution)/shard_map/all_gather | solution.py:82
  35.9 3.4 %collective-permute-start = (bf16[8,256,12]{1,2,0:T(8,128)(2,1)S(1)}, bf16[8,256,12]{1,2,0:T(8,128)(2,1)S(1)}, u32[]{:S(2)}, u32[]{:S(2)}) collective-permute-start(bf16[8,256,12]{1,2,0:T(8,128)(2,1)S(1)} %get-tuple-element.11), channel_id=1, source_target_pairs={{0,2},{2,4},{4,6},{1,3},{3,5},{5,7},{8,10},{10,12},{12,14},{9,11},... | collective-permute-start | bytes 147464 | tf_op jit(solution)/shard_map/ppermute | solution.py:17
  39.3 1.3 %collective-permute-start.1 = (bf16[8,256,12]{1,2,0:T(8,128)(2,1)S(1)}, bf16[8,256,12]{1,2,0:T(8,128)(2,1)S(1)}, u32[]{:S(2)}, u32[]{:S(2)}) collective-permute-start(bf16[8,256,12]{1,2,0:T(8,128)(2,1)S(1)} %get-tuple-element.12), channel_id=1, source_target_pairs={{2,0},{4,2},{6,4},{3,1},{5,3},{7,5},{10,8},{12,10},{14,12},{11,9},... | collective-permute-start | bytes 147464 | tf_op jit(solution)/shard_map/ppermute | solution.py:19
  41.2 4.3 %collective-permute-done.1 = bf16[8,256,12]{1,2,0:T(8,128)(2,1)S(1)} collective-permute-done((bf16[8,256,12]{1,2,0:T(8,128)(2,1)S(1)}, bf16[8,256,12]{1,2,0:T(8,128)(2,1)S(1)}, u32[]{:S(2)}, u32[]{:S(2)}) %collective-permute-start.1) | collective-permute-done | bytes 49184 | tf_op jit(solution)/shard_map/ppermute | solution.py:19
  45.7 1.3 %collective-permute-start.2 = (bf16[48,8,12]{1,2,0:T(8,128)(2,1)S(1)}, bf16[48,8,12]{1,2,0:T(8,128)(2,1)S(1)}, u32[]{:S(2)}, u32[]{:S(2)}) collective-permute-start(bf16[48,8,12]{1,2,0:T(8,128)(2,1)S(1)} %get-tuple-element.9), channel_id=1, source_target_pairs={{0,1},{2,3},{4,5},{6,7},{8,9},{10,11},{12,13},{14,15},{16,17},{18,... | collective-permute-start | bytes 27656 | tf_op jit(solution)/shard_map/ppermute | solution.py:17
  47.0 1.3 %collective-permute-start.3 = (bf16[48,8,12]{1,2,0:T(8,128)(2,1)S(1)}, bf16[48,8,12]{1,2,0:T(8,128)(2,1)S(1)}, u32[]{:S(2)}, u32[]{:S(2)}) collective-permute-start(bf16[48,8,12]{1,2,0:T(8,128)(2,1)S(1)} %get-tuple-element.10), channel_id=1, source_target_pairs={{1,0},{3,2},{5,4},{7,6},{9,8},{11,10},{13,12},{15,14},{17,16},{19,... | collective-permute-start | bytes 27656 | tf_op jit(solution)/shard_map/ppermute | solution.py:19
  48.4 2.0 %collective-permute-done.3 = bf16[48,8,12]{1,2,0:T(8,128)(2,1)S(1)} collective-permute-done((bf16[48,8,12]{1,2,0:T(8,128)(2,1)S(1)}, bf16[48,8,12]{1,2,0:T(8,128)(2,1)S(1)}, u32[]{:S(2)}, u32[]{:S(2)}) %collective-permute-start.3) | collective-permute-done | bytes 9248 | tf_op jit(solution)/shard_map/ppermute | solution.py:19
  50.3 0.3 pad_maximum_fusion.14
  50.7 0.5 fusion.101
  51.2 0.5 fusion.103
  51.7 0.5 fusion.105
  52.2 0.5 fusion.91
  52.7 0.5 fusion.93
  53.2 0.5 fusion.95
  53.7 0.5 fusion.97
  54.2 0.5 fusion.99
  54.8 1.3 %select_convert_fusion = bf16[46,270,32]{1,2,0:T(8,128)(2,1)S(1)} fusion(f32[46,270,32]{1,2,0:T(8,128)S(1)} %fusion.91, f32[46,270,32]{1,2,0:T(8,128)S(1)} %fusion.93, f32[46,270,32]{1,2,0:T(8,128)S(1)} %fusion.95, f32[46,270,32]{1,2,0:T(8,128)S(1)} %fusion.97, f32[46,270,32]{1,2,0:T(8,128)S(1)} %fusion.99, f32[46,270,32]{1,2,0:T(8,128)S(1)} %fusion.101, ...), kind=kOutput, calls=%fused_computation.17 | convolution fusion | flops 13910400 | bytes 19470592 | tf_op jit(solution)/shard_map/hwc,oc->hwo/dot_general | solution.py:33
  56.1 0.5 fusion.61
  56.6 0.4 fusion.63
  57.1 0.5 fusion.65
  57.6 0.5 fusion.67
  58.1 0.4 fusion.69
  58.6 0.5 fusion.71
  59.1 0.5 fusion.73
  59.6 0.4 fusion.75
  60.0 1.6 %select_convert_fusion.1 = bf16[44,268,32]{1,2,0:T(8,128)(2,1)S(1)} fusion(f32[44,268,32]{1,2,0:T(8,128)S(1)} %fusion.61, f32[44,268,32]{1,2,0:T(8,128)S(1)} %fusion.63, f32[44,268,32]{1,2,0:T(8,128)S(1)} %fusion.65, f32[44,268,32]{1,2,0:T(8,128)S(1)} %fusion.67, f32[44,268,32]{1,2,0:T(8,128)S(1)} %fusion.69, f32[44,268,32]{1,2,0:T(8,128)S(1)} %fusion.71, ...), kind=kOutput, calls=%fused_computation.18 | convolution fusion | flops 28300800 | bytes 19164160 | tf_op jit(solution)/shard_map/hwc,oc->hwo/dot_general | solution.py:33
  61.6 3.5 %copy.28 = f32[44,268,32]{2,1,0:T(8,128)} copy(bf16[44,268,32]{1,2,0:T(8,128)(2,1)S(1)} %select_convert_fusion.1) | data formatting | bytes 2264064 | tf_op jit(solution)/shard_map/reshape | solution.py:96
  65.2 0.4 slice.469
  65.6 7.9 %reshape.243 = f32[22,2,134,2,32]{4,3,2,1,0:T(2,128)} reshape(f32[44,268,32]{2,1,0:T(8,128)} %copy.28) | data formatting | bytes 3018752 | tf_op jit(solution)/shard_map/reshape | solution.py:96
  73.5 7.7 %reduce_sum.49 = f32[22,134,32]{2,1,0:T(8,128)S(1)} reduce(f32[22,2,134,2,32]{4,3,2,1,0:T(2,128)} %reshape.243, f32[]{:T(128)} %constant.99.clone.1), dimensions={1,3}, to_apply=%region_6.7 | reduce | flops 283008 | bytes 1886724 | tf_op jit(solution)/shard_map/reduce_sum | solution.py:95
  81.2 0.8 copy.29
  82.1 0.4 fusion.117
  82.4 0.4 convolution_add_fusion.7
  82.9 0.4 convolution_add_fusion.6
  83.3 0.4 convolution_add_fusion.5
  83.7 0.4 convolution_add_fusion.4
  84.1 0.4 convolution_add_fusion.3
  84.5 0.4 convolution_add_fusion.2
  84.9 0.4 convolution_add_fusion.1
  85.3 0.4 fusion.54
  85.8 0.4 copy-done.1
  86.5 0.4 convolution_add_fusion.15
  86.9 0.4 convolution_add_fusion.14
  87.6 0.4 convolution_add_fusion.12
  88.0 0.4 convolution_add_fusion.11
  88.7 0.4 convolution_add_fusion.9
  89.1 0.4 fusion.55
  89.5 0.6 copy.30
  90.3 1.2 %broadcast_in_dim.123 = bf16[36,130,2,64]{3,2,1,0:T(2,128)(2,1)S(1)} broadcast(bf16[36,130,64]{2,1,0:T(8,128)(2,1)S(1)} %bitcast.277), dimensions={0,1,3} | broadcast | bytes 1797120 | tf_op jit(solution)/shard_map/broadcast_in_dim | solution.py:103
  91.5 4.4 %reshape.241 = bf16[36,260,64]{2,1,0:T(8,128)(2,1)} reshape(bf16[36,130,2,64]{3,2,1,0:T(2,128)(2,1)S(1)} %broadcast_in_dim.123) | data formatting | bytes 2396160 | tf_op jit(solution)/shard_map/reshape | solution.py:103
  95.9 3.8 %slice.488 = bf16[34,258,64]{2,1,0:T(8,128)(2,1)} slice(bf16[36,260,64]{2,1,0:T(8,128)(2,1)} %reshape.241), slice={[1:35], [1:259], [0:64]} | slice | bytes 2245632 | tf_op jit(solution)/shard_map/slice | solution.py:105
  99.8 3.6 %copy.34 = bf16[34,258,64]{1,2,0:T(8,128)(2,1)S(1)} copy(bf16[34,258,64]{2,1,0:T(8,128)(2,1)} %slice.488) | data formatting | bytes 2245632
  103.8 0.7 fusion.1
  104.4 0.7 fusion.51
  105.2 0.7 fusion.48
  105.9 0.4 fusion.45
  106.3 0.7 fusion.42
  107.0 0.7 fusion.39
  107.7 1.4 %fusion.36 = f32[32,256,32]{1,2,0:T(8,128)} fusion(f32[32,256,32]{1,2,0:T(8,128)S(1)} %fusion.1, f32[32,256,32]{1,2,0:T(8,128)S(1)} %fusion.39, bf16[34,258,64]{1,2,0:T(8,128)(2,1)S(1)} %copy.34, bf16[34,258,32]{1,2,0:T(8,128)(2,1)S(1)} %slice.469, bf16[3,3,32,96]{3,2,1,0:T(8,128)(2,1)S(1)} %copy-done.4), kind=kOutput, calls=%fused_computation.63 | convolution fusion | flops 54001664 | bytes 5660672 | tf_op jit(solution)/shard_map/hwc,oc->hwo/dot_general | solution.py:33
  109.1 2.2 %fusion.59 = bf16[11,32,256]{2,0,1:T(8,128)(2,1)S(1)} fusion(f32[32,256,32]{1,2,0:T(8,128)} %fusion.36, bf16[34,258,64]{1,2,0:T(8,128)(2,1)S(1)} %copy.34, bf16[34,258,32]{1,2,0:T(8,128)(2,1)S(1)} %slice.469, bf16[3,3,32,96]{3,2,1,0:T(8,128)(2,1)S(1)} %copy-done.4, bf16[11,32]{1,0:T(8,128)(2,1)S(1)} %copy-done), kind=kOutput, calls=%fused_computation.74 | convolution fusion | flops 60121088 | bytes 3747840 | tf_op jit(solution)/shard_map/oc,hwc->ohw/dot_general | solution.py:110
  111.2 0.7 copy.32
  (43 shorter events, 3.1 us)
Async XLA Ops:
  0.0 109.1 %copy-start = (bf16[11,32]{1,0:T(8,128)(2,1)S(1)}, bf16[11,32]{1,0:T(8,128)(2,1)}, u32[]{:S(2)}) copy-start(bf16[11,32]{1,0:T(8,128)(2,1)} %param.19) | copy-start | bytes 2116
  35.9 14.8 %copy-start.5 = (bf16[3,3,32,12]{2,3,1,0:T(8,128)(2,1)S(1)}, bf16[3,3,32,12]{2,3,1,0:T(8,128)(2,1)}, u32[]{:S(2)}) copy-start(bf16[3,3,32,12]{2,3,1,0:T(8,128)(2,1)} %param.14) | copy-start | bytes 20740
  35.9 5.3 %collective-permute-start = (bf16[8,256,12]{1,2,0:T(8,128)(2,1)S(1)}, bf16[8,256,12]{1,2,0:T(8,128)(2,1)S(1)}, u32[]{:S(2)}, u32[]{:S(2)}) collective-permute-start(bf16[8,256,12]{1,2,0:T(8,128)(2,1)S(1)} %get-tuple-element.11), channel_id=1, source_target_pairs={{0,2},{2,4},{4,6},{1,3},{3,5},{5,7},{8,10},{10,12},{12,14},{9,11},... | collective-permute-start | bytes 147464 | tf_op jit(solution)/shard_map/ppermute | solution.py:17
  39.3 6.2 %collective-permute-start.1 = (bf16[8,256,12]{1,2,0:T(8,128)(2,1)S(1)}, bf16[8,256,12]{1,2,0:T(8,128)(2,1)S(1)}, u32[]{:S(2)}, u32[]{:S(2)}) collective-permute-start(bf16[8,256,12]{1,2,0:T(8,128)(2,1)S(1)} %get-tuple-element.12), channel_id=1, source_target_pairs={{2,0},{4,2},{6,4},{3,1},{5,3},{7,5},{10,8},{12,10},{14,12},{11,9},... | collective-permute-start | bytes 147464 | tf_op jit(solution)/shard_map/ppermute | solution.py:19
  45.7 2.7 %collective-permute-start.2 = (bf16[48,8,12]{1,2,0:T(8,128)(2,1)S(1)}, bf16[48,8,12]{1,2,0:T(8,128)(2,1)S(1)}, u32[]{:S(2)}, u32[]{:S(2)}) collective-permute-start(bf16[48,8,12]{1,2,0:T(8,128)(2,1)S(1)} %get-tuple-element.9), channel_id=1, source_target_pairs={{0,1},{2,3},{4,5},{6,7},{8,9},{10,11},{12,13},{14,15},{16,17},{18,... | collective-permute-start | bytes 27656 | tf_op jit(solution)/shard_map/ppermute | solution.py:17
  47.0 3.3 %collective-permute-start.3 = (bf16[48,8,12]{1,2,0:T(8,128)(2,1)S(1)}, bf16[48,8,12]{1,2,0:T(8,128)(2,1)S(1)}, u32[]{:S(2)}, u32[]{:S(2)}) collective-permute-start(bf16[48,8,12]{1,2,0:T(8,128)(2,1)S(1)} %get-tuple-element.10), channel_id=1, source_target_pairs={{1,0},{3,2},{5,4},{7,6},{9,8},{11,10},{13,12},{15,14},{17,16},{19,... | collective-permute-start | bytes 27656 | tf_op jit(solution)/shard_map/ppermute | solution.py:19
  54.8 1.4 %copy-start.2 = (bf16[3,3,32,32]{3,2,1,0:T(8,128)(2,1)S(1)}, bf16[3,3,32,32]{3,2,1,0:T(8,128)(2,1)}, u32[]{:S(2)}) copy-start(bf16[3,3,32,32]{3,2,1,0:T(8,128)(2,1)} %param.15) | copy-start | bytes 55300
  81.2 0.9 copy-start.3
  85.3 0.9 copy-start.1
  99.8 3.6 %copy-start.4 = (bf16[3,3,32,96]{3,2,1,0:T(8,128)(2,1)S(1)}, bf16[3,3,32,96]{3,2,1,0:T(8,128)(2,1)}, u32[]{:S(2)}) copy-start(bf16[3,3,32,96]{3,2,1,0:T(8,128)(2,1)} %param.18) | copy-start | bytes 165892

commit v5 on v4

--- a/solution.py
+++ b/solution.py
@@ -38,6 +38,11 @@
             )
             total = term if total is None else total + term
     return total
+
+
+def pair_matrix(narrow, wide, offset):
+    pick = (jnp.arange(wide, dtype=jnp.int32) + offset) // 2
+    return (jnp.arange(narrow, dtype=jnp.int32)[:, None] == pick[None, :]).astype(jnp.bfloat16)
 
 
 def inside_mask(row_start, col_start, height, width, total_rows, total_cols):
@@ -92,17 +97,28 @@
     first_map = masked_layer(widened, encode_first, row0 - HALO + 1, col0 - HALO + 1, total_rows, total_cols)
     skip_wide = masked_layer(first_map, encode_second, row0 - HALO + 2, col0 - HALO + 2, total_rows, total_cols)
     wide_rows, wide_cols, channels = skip_wide.shape
-    pooled = jnp.mean(
-        skip_wide.astype(jnp.float32).reshape(wide_rows // 2, 2, wide_cols // 2, 2, channels), axis=(1, 3)
+    col_pairs = jnp.einsum(
+        "vw,hwc->hvc", pair_matrix(wide_cols // 2, wide_cols, 0), skip_wide, preferred_element_type=jnp.float32
+    )
+    pooled = (
+        jnp.sum(col_pairs.reshape(wide_rows // 2, 2, wide_cols // 2, channels), axis=1) * 0.25
     ).astype(jnp.bfloat16)
     coarse_halo = (HALO - 2) // 2
     crow0 = row0 // 2 - coarse_halo
     ccol0 = col0 // 2 - coarse_halo
     mid = masked_layer(pooled, middle_first, crow0 + 1, ccol0 + 1, total_rows // 2, total_cols // 2)
     deeper = masked_layer(mid, middle_second, crow0 + 2, ccol0 + 2, total_rows // 2, total_cols // 2)
-    upsampled = jnp.repeat(jnp.repeat(deeper, 2, axis=0), 2, axis=1)
     up_halo = 2 * (coarse_halo - 2)
-    upsampled = upsampled[up_halo - 1 : up_halo + block_rows + 1, up_halo - 1 : up_halo + block_cols + 1]
+    deep_rows, deep_cols, deep_ch = deeper.shape
+    spread = jnp.einsum(
+        "wv,hvc->hwc",
+        pair_matrix(deep_cols, block_cols + 2, up_halo - 1).T,
+        deeper,
+        preferred_element_type=jnp.float32,
+    ).astype(jnp.bfloat16)
+    upsampled = jnp.broadcast_to(spread[:, None], (deep_rows, 2, block_cols + 2, deep_ch)).reshape(
+        2 * deep_rows, block_cols + 2, deep_ch
+    )[up_halo - 1 : up_halo + block_rows + 1]
     skip_halo = HALO - 2
     skip = skip_wide[skip_halo - 1 : skip_halo + block_rows + 1, skip_halo - 1 : skip_halo + block_cols + 1]
     joined = jnp.concatenate([skip, upsampled], axis=2)

time: 113 us -> 83.9 us (0.74)
  local copies, waits for them, and re-layouts: 29.7 us -> 6.46 us
  other arithmetic: 19.8 us -> 12.4 us
  matrix products: 25.5 us -> 27.5 us
    reshape x3 -> x0, local copies, waits for them, and re-layouts: 15.9 us -> none  [the longest x2 11.5 us: shards(): skip_wide.astype(jnp.float32)]
    reduce_sum x1, other arithmetic: 7.66 us -> 0.21 us  [shards(): jnp.sum(col_pairs.reshape(wide_rows // 2, 2, wide_cols // 2, channels), a...]
    slice x1, local copies, waits for them, and re-layouts: 3.82 us -> 0.17 us  [shards(): jnp.broadcast_to(spread[:, None], (deep_rows, 2, block_cols + 2, deep_ch))]
    unnamed x13 -> x12, local copies, waits for them, and re-layouts: 4.1 us -> 1.75 us
    dot_general x0 -> x2, matrix products: none -> 2.23 us  [the longest x1 1.68 us: shards(): jnp.einsum('wv,hvc->hwc', pair_matrix(deep_cols, block_cols + 2, up_halo...]
    dot_general x44 -> x43, matrix products: 23.3 us -> 23.1 us  [valid_conv(): jnp.einsum('hwc,oc->hwo', padded[a:a + height, e:e + width], kernel[a, e]...]
where the time goes in v5:
time: 83.9 us; the launch traced here: 83.3 us
  matrix products  27.5 us (33%)
  blocking collectives  22.8 us (27%)
  other arithmetic  12.4 us (15%)
  starting transfers between devices  7.46 us (9%)
  local copies, waits for them, and re-layouts  6.46 us (8%)
  waiting for transfers between devices  6.2 us (7%)
    dot_general x43, matrix products, valid_conv(): jnp.einsum('hwc,oc->hwo', padded[a:a + height, e:e + width], kernel[a, e]...  23.1 us
    all_gather x1, blocking collectives, shards(): gathered = lax.all_gather(packed, 'tm', axis=0).astype(jnp.float32)  22.8 us
    reduce_max x1, other arithmetic, shards(): shift = jnp.max(scores, axis=0).astype(jnp.bfloat16).astype(jnp.float32)  8.74 us
    ppermute x2, waiting for transfers between devices, with_halo(): lax.ppermute(head, axis, [((i + 1) % count, i) for i in range(ends)])  6.11 us
    ppermute x2, starting transfers between devices, with_halo(): lax.ppermute(tail, axis, [(i, (i + 1) % count) for i in range(ends)])  4.7 us
    ppermute x2, starting transfers between devices, with_halo(): lax.ppermute(head, axis, [((i + 1) % count, i) for i in range(ends)])  2.76 us
    dot_general x1, matrix products, shards(): jnp.einsum('oc,hwc->ohw', head_weight, decoded, preferred_element_type=jn...  2.15 us
    slice x1, local copies, waits for them, and re-layouts, shards(): looked = jnp.where(scene_class == label, class_score[label], looked)  1.8 us
  transfers between devices with their start and end apart: 4, of which 3 were waited for; matrix products, arithmetic and copies ran while one was open for 0% of the time, Pallas kernels for 0%

profile of v5, /device:TPU:0, one launch (start us, length us, event | category | flops | bytes accessed | tf_op | source)
XLA Modules:
  0.0 83.3 jit_solution(13364385540088145018)
XLA Ops:
  0.0 1.8 %fusion.259 = (f32[1]{0:T(128)}, f32[1]{0:T(128)}, f32[1]{0:T(128)}, f32[1]{0:T(128)}, f32[1]{0:T(128)}, /*index=5*/f32[1]{0:T(128)}, f32[1]{0:T(128)}, f32[1]{0...) fusion(f32[12]{0:T(128)} %param.13), kind=kLoop, calls=%fused_computation.304 | loop fusion | bytes 96 | tf_op jit(solution)/shard_map/slice | solution.py:80
  1.8 8.7 %fusion.256 = (bf16[32,256]{1,0:T(8,128)(2,1)S(1)}, f32[8,32,256]{2,1,0:T(8,128)S(1)}) fusion(f32[8,32,256]{2,1,0:T(8,128)} %param.12, f32[]{:T(128)} %bitcast.11, s32[8,32,256]{2,1,0:T(8,128)} %param.11, f32[]{:T(128)} %bitcast.10, f32[]{:T(128)} %bitcast.9, f32[]{:T(128)} %bitcast.8, f32[]{:T(128)} %bitcast.7, f32[]{:T(128)} %bitcast.6, f32[]{:T(128)} %bitcast.5, ...), kind=kLoop, calls=%fused_computation.301 | loop fusion | flops 1695744 | bytes 802864 | tf_op jit(solution)/shard_map/reduce_max | solution.py:82
  10.6 1.7 %multiply_reduce_fusion = bf16[12,32,256]{2,1,0:T(8,128)(2,1)S(1)} fusion(bf16[8,12,32,256]{3,2,1,0:T(8,128)(2,1)} %param.10, f32[8,32,256]{2,1,0:T(8,128)S(1)} %get-tuple-element.6), kind=kLoop, calls=%fused_computation.16 | loop fusion | flops 2260992 | bytes 2031616 | tf_op jit(solution)/shard_map/reduce_sum | solution.py:84
  12.4 22.8 %all_gather.4 = bf16[4,14,32,256]{3,2,1,0:T(8,128)(2,1)S(1)} all-gather(bf16[1,14,32,256]{3,2,1,0:T(8,128)(2,1)S(1)} %pad_maximum_fusion.16), channel_id=1, replica_groups=mesh['tm'=4,'row'=4,'col'=2] {'tm'}, dimensions={0}, use_global_device_ids=true | all-gather | bytes 1146880 | tf_op jit(solution)/shard_map/all_gather | solution.py:87
  35.7 0.2 fusion.123
  35.9 3.4 %collective-permute-start = (bf16[8,256,12]{1,2,0:T(8,128)(2,1)S(1)}, bf16[8,256,12]{1,2,0:T(8,128)(2,1)S(1)}, u32[]{:S(2)}, u32[]{:S(2)}) collective-permute-start(bf16[8,256,12]{1,2,0:T(8,128)(2,1)S(1)} %get-tuple-element.11), channel_id=1, source_target_pairs={{0,2},{2,4},{4,6},{1,3},{3,5},{5,7},{8,10},{10,12},{12,14},{9,11},... | collective-permute-start | bytes 147464 | tf_op jit(solution)/shard_map/ppermute | solution.py:17
  39.3 1.3 %collective-permute-start.1 = (bf16[8,256,12]{1,2,0:T(8,128)(2,1)S(1)}, bf16[8,256,12]{1,2,0:T(8,128)(2,1)S(1)}, u32[]{:S(2)}, u32[]{:S(2)}) collective-permute-start(bf16[8,256,12]{1,2,0:T(8,128)(2,1)S(1)} %get-tuple-element.12), channel_id=1, source_target_pairs={{2,0},{4,2},{6,4},{3,1},{5,3},{7,5},{10,8},{12,10},{14,12},{11,9},... | collective-permute-start | bytes 147464 | tf_op jit(solution)/shard_map/ppermute | solution.py:19
  41.2 4.3 %collective-permute-done.1 = bf16[8,256,12]{1,2,0:T(8,128)(2,1)S(1)} collective-permute-done((bf16[8,256,12]{1,2,0:T(8,128)(2,1)S(1)}, bf16[8,256,12]{1,2,0:T(8,128)(2,1)S(1)}, u32[]{:S(2)}, u32[]{:S(2)}) %collective-permute-start.1) | collective-permute-done | bytes 49184 | tf_op jit(solution)/shard_map/ppermute | solution.py:19
  45.7 1.3 %collective-permute-start.2 = (bf16[48,8,12]{1,2,0:T(8,128)(2,1)S(1)}, bf16[48,8,12]{1,2,0:T(8,128)(2,1)S(1)}, u32[]{:S(2)}, u32[]{:S(2)}) collective-permute-start(bf16[48,8,12]{1,2,0:T(8,128)(2,1)S(1)} %get-tuple-element.9), channel_id=1, source_target_pairs={{0,1},{2,3},{4,5},{6,7},{8,9},{10,11},{12,13},{14,15},{16,17},{18,... | collective-permute-start | bytes 27656 | tf_op jit(solution)/shard_map/ppermute | solution.py:17
  47.0 1.5 %collective-permute-start.3 = (bf16[48,8,12]{1,2,0:T(8,128)(2,1)S(1)}, bf16[48,8,12]{1,2,0:T(8,128)(2,1)S(1)}, u32[]{:S(2)}, u32[]{:S(2)}) collective-permute-start(bf16[48,8,12]{1,2,0:T(8,128)(2,1)S(1)} %get-tuple-element.10), channel_id=1, source_target_pairs={{1,0},{3,2},{5,4},{7,6},{9,8},{11,10},{13,12},{15,14},{17,16},{19,... | collective-permute-start | bytes 27656 | tf_op jit(solution)/shard_map/ppermute | solution.py:19
  48.5 1.8 %collective-permute-done.3 = bf16[48,8,12]{1,2,0:T(8,128)(2,1)S(1)} collective-permute-done((bf16[48,8,12]{1,2,0:T(8,128)(2,1)S(1)}, bf16[48,8,12]{1,2,0:T(8,128)(2,1)S(1)}, u32[]{:S(2)}, u32[]{:S(2)}) %collective-permute-start.3) | collective-permute-done | bytes 9248 | tf_op jit(solution)/shard_map/ppermute | solution.py:19
  50.3 0.3 pad_maximum_fusion.14
  50.7 0.5 fusion.101
  51.2 0.5 fusion.103
  51.7 0.5 fusion.105
  52.2 0.5 fusion.107
  52.7 0.5 fusion.109
  53.2 0.5 fusion.95
  53.7 0.5 fusion.97
  54.3 0.5 fusion.99
  54.8 1.3 %select_convert_fusion = bf16[46,270,32]{1,2,0:T(8,128)(2,1)S(1)} fusion(f32[46,270,32]{1,2,0:T(8,128)S(1)} %fusion.95, f32[46,270,32]{1,2,0:T(8,128)S(1)} %fusion.97, f32[46,270,32]{1,2,0:T(8,128)S(1)} %fusion.99, f32[46,270,32]{1,2,0:T(8,128)S(1)} %fusion.101, f32[46,270,32]{1,2,0:T(8,128)S(1)} %fusion.103, f32[46,270,32]{1,2,0:T(8,128)S(1)} %fusion.105, ...), kind=kOutput, calls=%fused_computation.17 | convolution fusion | flops 13910400 | bytes 19470592 | tf_op jit(solution)/shard_map/hwc,oc->hwo/dot_general | solution.py:33
  56.1 0.5 fusion.62
  56.7 0.4 fusion.64
  57.1 0.5 fusion.66
  57.6 0.5 fusion.68
  58.2 0.4 fusion.70
  58.6 0.5 fusion.72
  59.1 0.5 fusion.74
  59.6 0.4 fusion.76
  60.1 1.6 %select_convert_fusion.1 = bf16[44,268,32]{1,2,0:T(8,128)(2,1)S(1)} fusion(f32[44,268,32]{1,2,0:T(8,128)S(1)} %fusion.62, f32[44,268,32]{1,2,0:T(8,128)S(1)} %fusion.64, f32[44,268,32]{1,2,0:T(8,128)S(1)} %fusion.66, f32[44,268,32]{1,2,0:T(8,128)S(1)} %fusion.68, f32[44,268,32]{1,2,0:T(8,128)S(1)} %fusion.70, f32[44,268,32]{1,2,0:T(8,128)S(1)} %fusion.72, ...), kind=kOutput, calls=%fused_computation.18 | convolution fusion | flops 28300800 | bytes 19164160 | tf_op jit(solution)/shard_map/hwc,oc->hwo/dot_general | solution.py:33
  61.6 0.4 slice.469
  62.1 0.6 fusion.125
  62.9 0.6 copy-done.3
  63.5 0.4 fusion.121
  63.9 0.6 convolution_add_fusion.7
  64.5 0.4 convolution_add_fusion.6
  65.0 0.4 convolution_add_fusion.5
  65.3 0.4 convolution_add_fusion.4
  65.8 0.4 convolution_add_fusion.3
  66.2 0.4 convolution_add_fusion.2
  66.6 0.4 convolution_add_fusion.1
  67.0 0.4 fusion.54
  67.5 0.4 copy-done.1
  67.9 0.3 fusion.87
  68.2 0.4 convolution_add_fusion.15
  68.6 0.4 convolution_add_fusion.14
  69.0 0.3 convolution_add_fusion.13
  69.3 0.4 convolution_add_fusion.12
  69.7 0.4 convolution_add_fusion.11
  70.0 0.3 convolution_add_fusion.10
  70.4 0.4 convolution_add_fusion.9
  70.7 1.7 %fusion.56 = bf16[18,258,64]{1,2,0:T(8,128)(2,1)} fusion(f32[18,130,64]{1,2,0:T(8,128)S(1)} %convolution_add_fusion.9, bf16[20,132,64]{1,2,0:T(8,128)(2,1)S(1)} %fusion.54, pred[18,130]{1,0:T(8,128)(4,1)S(1)} %broadcast_and_fusion.3, s32[258]{0:T(512)S(1)} %add_select_fusion, bf16[3,3,64,64]{3,2,1,0:T(8,128)(2,1)S(1)} %copy-done.1), kind=kOutput, calls=%fused_computation.72 | convolution fusion | flops 97375232 | bytes 2388480 | tf_op jit(solution)/shard_map/wv,hvc->hwc/dot_general | solution.py:113
  72.4 1.4 %broadcast_in_dim.126 = bf16[18,2,258,64]{2,3,1,0:T(8,128)(2,1)S(1)} broadcast(bf16[18,258,64]{1,2,0:T(8,128)(2,1)} %fusion.56), dimensions={0,2,3} | broadcast | bytes 1783296 | tf_op jit(solution)/shard_map/broadcast_in_dim | solution.py:119
  74.1 0.7 copy-done.4
  74.8 0.3 fusion.4
  75.1 0.7 fusion.1
  75.8 0.7 fusion.51
  76.5 0.7 fusion.48
  77.2 0.4 fusion.45
  77.6 0.7 fusion.42
  78.3 0.7 fusion.39
  79.1 1.4 %fusion.36 = f32[32,256,32]{1,2,0:T(8,128)} fusion(f32[32,256,32]{1,2,0:T(8,128)S(1)} %fusion.1, f32[32,256,32]{1,2,0:T(8,128)S(1)} %fusion.39, bf16[34,258,64]{1,2,0:T(8,128)(2,1)S(1)} %slice.488, bf16[34,258,32]{1,2,0:T(8,128)(2,1)S(1)} %slice.469, bf16[3,3,32,96]{3,2,1,0:T(8,128)(2,1)S(1)} %copy-done.4), kind=kOutput, calls=%fused_computation.64 | convolution fusion | flops 54001664 | bytes 5660672 | tf_op jit(solution)/shard_map/hwc,oc->hwo/dot_general | solution.py:33
  80.4 2.2 %fusion.60 = bf16[11,32,256]{2,0,1:T(8,128)(2,1)S(1)} fusion(f32[32,256,32]{1,2,0:T(8,128)} %fusion.36, bf16[34,258,64]{1,2,0:T(8,128)(2,1)S(1)} %slice.488, bf16[34,258,32]{1,2,0:T(8,128)(2,1)S(1)} %slice.469, bf16[3,3,32,96]{3,2,1,0:T(8,128)(2,1)S(1)} %copy-done.4, bf16[11,32]{1,0:T(8,128)(2,1)S(1)} %copy-done), kind=kOutput, calls=%fused_computation.76 | convolution fusion | flops 60121088 | bytes 3747840 | tf_op jit(solution)/shard_map/oc,hwc->ohw/dot_general | solution.py:126
  82.6 0.7 copy.21
  (39 shorter events, 1.7 us)
Async XLA Ops:
  0.0 80.4 %copy-start = (bf16[11,32]{1,0:T(8,128)(2,1)S(1)}, bf16[11,32]{1,0:T(8,128)(2,1)}, u32[]{:S(2)}) copy-start(bf16[11,32]{1,0:T(8,128)(2,1)} %param.19) | copy-start | bytes 2116
  35.9 14.8 %copy-start.5 = (bf16[3,3,32,12]{2,3,1,0:T(8,128)(2,1)S(1)}, bf16[3,3,32,12]{2,3,1,0:T(8,128)(2,1)}, u32[]{:S(2)}) copy-start(bf16[3,3,32,12]{2,3,1,0:T(8,128)(2,1)} %param.14) | copy-start | bytes 20740
  35.9 5.3 %collective-permute-start = (bf16[8,256,12]{1,2,0:T(8,128)(2,1)S(1)}, bf16[8,256,12]{1,2,0:T(8,128)(2,1)S(1)}, u32[]{:S(2)}, u32[]{:S(2)}) collective-permute-start(bf16[8,256,12]{1,2,0:T(8,128)(2,1)S(1)} %get-tuple-element.11), channel_id=1, source_target_pairs={{0,2},{2,4},{4,6},{1,3},{3,5},{5,7},{8,10},{10,12},{12,14},{9,11},... | collective-permute-start | bytes 147464 | tf_op jit(solution)/shard_map/ppermute | solution.py:17
  39.3 6.2 %collective-permute-start.1 = (bf16[8,256,12]{1,2,0:T(8,128)(2,1)S(1)}, bf16[8,256,12]{1,2,0:T(8,128)(2,1)S(1)}, u32[]{:S(2)}, u32[]{:S(2)}) collective-permute-start(bf16[8,256,12]{1,2,0:T(8,128)(2,1)S(1)} %get-tuple-element.12), channel_id=1, source_target_pairs={{2,0},{4,2},{6,4},{3,1},{5,3},{7,5},{10,8},{12,10},{14,12},{11,9},... | collective-permute-start | bytes 147464 | tf_op jit(solution)/shard_map/ppermute | solution.py:19
  45.7 2.8 %collective-permute-start.2 = (bf16[48,8,12]{1,2,0:T(8,128)(2,1)S(1)}, bf16[48,8,12]{1,2,0:T(8,128)(2,1)S(1)}, u32[]{:S(2)}, u32[]{:S(2)}) collective-permute-start(bf16[48,8,12]{1,2,0:T(8,128)(2,1)S(1)} %get-tuple-element.9), channel_id=1, source_target_pairs={{0,1},{2,3},{4,5},{6,7},{8,9},{10,11},{12,13},{14,15},{16,17},{18,... | collective-permute-start | bytes 27656 | tf_op jit(solution)/shard_map/ppermute | solution.py:17
  47.0 3.3 %collective-permute-start.3 = (bf16[48,8,12]{1,2,0:T(8,128)(2,1)S(1)}, bf16[48,8,12]{1,2,0:T(8,128)(2,1)S(1)}, u32[]{:S(2)}, u32[]{:S(2)}) collective-permute-start(bf16[48,8,12]{1,2,0:T(8,128)(2,1)S(1)} %get-tuple-element.10), channel_id=1, source_target_pairs={{1,0},{3,2},{5,4},{7,6},{9,8},{11,10},{13,12},{15,14},{17,16},{19,... | collective-permute-start | bytes 27656 | tf_op jit(solution)/shard_map/ppermute | solution.py:19
  54.8 1.4 %copy-start.2 = (bf16[3,3,32,32]{3,2,1,0:T(8,128)(2,1)S(1)}, bf16[3,3,32,32]{3,2,1,0:T(8,128)(2,1)}, u32[]{:S(2)}) copy-start(bf16[3,3,32,32]{3,2,1,0:T(8,128)(2,1)} %param.15) | copy-start | bytes 55300
  62.6 0.9 %copy-start.3 = (bf16[3,3,64,32]{2,3,1,0:T(8,128)(2,1)S(1)}, bf16[3,3,64,32]{2,3,1,0:T(8,128)(2,1)}, u32[]{:S(2)}) copy-start(bf16[3,3,64,32]{2,3,1,0:T(8,128)(2,1)} %param.16) | copy-start | bytes 110596
  67.0 0.9 %copy-start.1 = (bf16[3,3,64,64]{3,2,1,0:T(8,128)(2,1)S(1)}, bf16[3,3,64,64]{3,2,1,0:T(8,128)(2,1)}, u32[]{:S(2)}) copy-start(bf16[3,3,64,64]{3,2,1,0:T(8,128)(2,1)} %param.17) | copy-start | bytes 221188
  73.9 0.9 %copy-start.4 = (bf16[3,3,32,96]{3,2,1,0:T(8,128)(2,1)S(1)}, bf16[3,3,32,96]{3,2,1,0:T(8,128)(2,1)}, u32[]{:S(2)}) copy-start(bf16[3,3,32,96]{3,2,1,0:T(8,128)(2,1)} %param.18) | copy-start | bytes 165892

commit v6 on v5

--- a/solution.py
+++ b/solution.py
@@ -1,6 +1,8 @@
 import jax
 import jax.numpy as jnp
 from jax import lax
+from jax.experimental import pallas as pl
+from jax.experimental.pallas import tpu as pltpu
 from jax.sharding import PartitionSpec as P
 
 HALO = 8
@@ -45,6 +47,49 @@
     return (jnp.arange(narrow, dtype=jnp.int32)[:, None] == pick[None, :]).astype(jnp.bfloat16)
 
 
+def weight_kernel(score_ref, class_ref, quality_ref, weight_ref, shift_ref):
+    dates, rows, _ = class_ref.shape
+    classes = score_ref.shape[0]
+    step = 8
+
+    def chunk(index, carry):
+        at = pl.ds(pl.multiple_of(index * step, step), step)
+
+        def score(date):
+            label = class_ref[date, at, :]
+            looked = jnp.zeros(label.shape, jnp.float32)
+            for k in range(classes):
+                looked = jnp.where(label == k, score_ref[k], looked)
+            return looked + quality_ref[date, at, :]
+
+        top = lax.fori_loop(1, dates, lambda date, top: jnp.maximum(top, score(date)), score(0))
+        shift = top.astype(jnp.bfloat16).astype(jnp.float32)
+        shift_ref[at, :] = shift
+
+        def one_date(date, inner):
+            weight_ref[date, at, :] = jnp.exp(score(date) - shift)
+            return inner
+
+        lax.fori_loop(0, dates, one_date, 0)
+        return carry
+
+    lax.fori_loop(0, rows // step, chunk, 0)
+
+
+def shifted_weights(class_score, scene_class, quality):
+    dates, rows, cols = quality.shape
+    vmem = pl.BlockSpec(memory_space=pltpu.VMEM)
+    return pl.pallas_call(
+        weight_kernel,
+        out_shape=(
+            jax.ShapeDtypeStruct((dates, rows, cols), jnp.float32),
+            jax.ShapeDtypeStruct((rows, cols), jnp.float32),
+        ),
+        in_specs=[pl.BlockSpec(memory_space=pltpu.SMEM), vmem, vmem],
+        out_specs=(vmem, vmem),
+    )(class_score, scene_class, quality)
+
+
 def inside_mask(row_start, col_start, height, width, total_rows, total_cols):
     rows = row_start + jnp.arange(height, dtype=jnp.int32)
     cols = col_start + jnp.arange(width, dtype=jnp.int32)
@@ -75,12 +120,7 @@
     block_cols = quality.shape[2]
     total_rows = block_rows * lax.axis_size("row")
     total_cols = block_cols * lax.axis_size("col")
-    looked = jnp.zeros(quality.shape, jnp.float32)
-    for label in range(class_score.shape[0]):
-        looked = jnp.where(scene_class == label, class_score[label], looked)
-    scores = looked + quality
-    shift = jnp.max(scores, axis=0).astype(jnp.bfloat16).astype(jnp.float32)
-    weights = jnp.exp(scores - shift[None])
+    weights, shift = shifted_weights(class_score, scene_class, quality)
     part_sums = jnp.sum(weights[:, None] * reflectance, axis=0)
     part_total = jnp.sum(weights, axis=0)
     packed = jnp.concatenate([part_sums, part_total[None], shift[None]], axis=0).astype(jnp.bfloat16)

time: 83.9 us -> 76.1 us (0.907)
  other arithmetic: 12.4 us -> 3.66 us
  Pallas kernels: 0 us -> 2.83 us
  local copies, waits for them, and re-layouts: 6.46 us -> 4.68 us
    reduce_max x1 -> x0, other arithmetic: 8.74 us -> none  [shards(): shift = jnp.max(scores, axis=0).astype(jnp.bfloat16).astype(jnp.float32)]
    pallas_call x0 -> x1, Pallas kernels: none -> 2.83 us  [shifted_weights(): pl.pallas_call(weight_kernel, out_shape=(jax.ShapeDtypeStruct((dates, row...]
    slice x1 -> x0, local copies, waits for them, and re-layouts: 1.8 us -> none  [shards(): looked = jnp.where(scene_class == label, class_score[label], looked)]
    unnamed x12 -> x16, local copies, waits for them, and re-layouts: 1.75 us -> 1.76 us
  transfers between devices with their start and end apart: 4 -> 4, of which waited for: 3 -> 3; matrix products, arithmetic and copies ran while one was open for 0% -> 1% of each run, Pallas kernels for 0% -> 0%
where the time goes in v6:
time: 76.1 us; the launch traced here: 75.6 us
  matrix products  27.5 us (36%)
  blocking collectives  22.8 us (30%)
  starting transfers between devices  7.28 us (10%)
  waiting for transfers between devices  6.38 us (8%)
  local copies, waits for them, and re-layouts  4.68 us (6%)
  other arithmetic  3.66 us (5%)
  Pallas kernels  2.83 us (4%)
    dot_general x43, matrix products, valid_conv(): jnp.einsum('hwc,oc->hwo', padded[a:a + height, e:e + width], kernel[a, e]...  23.1 us
    all_gather x1, blocking collectives, shards(): gathered = lax.all_gather(packed, 'tm', axis=0).astype(jnp.float32)  22.8 us
    ppermute x2, waiting for transfers between devices, with_halo(): lax.ppermute(head, axis, [((i + 1) % count, i) for i in range(ends)])  6.29 us
    ppermute x2, starting transfers between devices, with_halo(): lax.ppermute(tail, axis, [(i, (i + 1) % count) for i in range(ends)])  4.7 us
    pallas_call x1, Pallas kernels, shifted_weights(): pl.pallas_call(weight_kernel, out_shape=(jax.ShapeDtypeStruct((dates, row...  2.83 us
    ppermute x2, starting transfers between devices, with_halo(): lax.ppermute(head, axis, [((i + 1) % count, i) for i in range(ends)])  2.58 us
    dot_general x1, matrix products, shards(): jnp.einsum('oc,hwc->ohw', head_weight, decoded, preferred_element_type=jn...  2.15 us
    reduce_sum x1, other arithmetic, shards(): part_sums = jnp.sum(weights[:, None] * reflectance, axis=0)  1.79 us
  transfers between devices with their start and end apart: 4, of which 3 were waited for; matrix products, arithmetic and copies ran while one was open for 1% of the time, Pallas kernels for 0%

profile of v6, /device:TPU:0, one launch (start us, length us, event | category | flops | bytes accessed | tf_op | source)
XLA Modules:
  0.0 75.6 jit_solution(9605018217734737801)
XLA Ops:
  0.0 2.8 %shard_map.100 = (f32[8,32,256]{2,1,0:T(8,128)}, f32[32,256]{1,0:T(8,128)}) custom-call(f32[12]{0:T(128)} %score_ref.1, s32[8,32,256]{2,1,0:T(8,128)} %class_ref.1, f32[8,32,256]{2,1,0:T(8,128)} %quality_ref.1), custom_call_target="tpu_custom_call" | custom-call | tf_op jit(solution)/shard_map/pallas_call | solution.py:82
  2.8 1.8 %multiply_reduce_fusion = bf16[12,32,256]{2,1,0:T(8,128)(2,1)S(1)} fusion(bf16[8,12,32,256]{3,2,1,0:T(8,128)(2,1)} %param.10, f32[8,32,256]{2,1,0:T(8,128)} %get-tuple-element.7), kind=kLoop, calls=%fused_computation.16 | loop fusion | flops 2260992 | bytes 2031616 | tf_op jit(solution)/shard_map/reduce_sum | solution.py:124
  4.7 22.8 %all_gather.4 = bf16[4,14,32,256]{3,2,1,0:T(8,128)(2,1)S(1)} all-gather(bf16[1,14,32,256]{3,2,1,0:T(8,128)(2,1)S(1)} %pad_maximum_fusion.16), channel_id=1, replica_groups=mesh['tm'=4,'row'=4,'col'=2] {'tm'}, dimensions={0}, use_global_device_ids=true | all-gather | bytes 1146880 | tf_op jit(solution)/shard_map/all_gather | solution.py:127
  28.0 0.2 fusion.123
  28.3 3.4 %collective-permute-start = (bf16[8,256,12]{1,2,0:T(8,128)(2,1)S(1)}, bf16[8,256,12]{1,2,0:T(8,128)(2,1)S(1)}, u32[]{:S(2)}, u32[]{:S(2)}) collective-permute-start(bf16[8,256,12]{1,2,0:T(8,128)(2,1)S(1)} %get-tuple-element.11), channel_id=1, source_target_pairs={{0,2},{2,4},{4,6},{1,3},{3,5},{5,7},{8,10},{10,12},{12,14},{9,11},... | collective-permute-start | bytes 147464 | tf_op jit(solution)/shard_map/ppermute | solution.py:19
  31.7 1.3 %collective-permute-start.1 = (bf16[8,256,12]{1,2,0:T(8,128)(2,1)S(1)}, bf16[8,256,12]{1,2,0:T(8,128)(2,1)S(1)}, u32[]{:S(2)}, u32[]{:S(2)}) collective-permute-start(bf16[8,256,12]{1,2,0:T(8,128)(2,1)S(1)} %get-tuple-element.12), channel_id=1, source_target_pairs={{2,0},{4,2},{6,4},{3,1},{5,3},{7,5},{10,8},{12,10},{14,12},{11,9},... | collective-permute-start | bytes 147464 | tf_op jit(solution)/shard_map/ppermute | solution.py:21
  33.6 4.3 %collective-permute-done.1 = bf16[8,256,12]{1,2,0:T(8,128)(2,1)S(1)} collective-permute-done((bf16[8,256,12]{1,2,0:T(8,128)(2,1)S(1)}, bf16[8,256,12]{1,2,0:T(8,128)(2,1)S(1)}, u32[]{:S(2)}, u32[]{:S(2)}) %collective-permute-start.1) | collective-permute-done | bytes 49184 | tf_op jit(solution)/shard_map/ppermute | solution.py:21
  38.0 1.3 %collective-permute-start.2 = (bf16[48,8,12]{1,2,0:T(8,128)(2,1)S(1)}, bf16[48,8,12]{1,2,0:T(8,128)(2,1)S(1)}, u32[]{:S(2)}, u32[]{:S(2)}) collective-permute-start(bf16[48,8,12]{1,2,0:T(8,128)(2,1)S(1)} %get-tuple-element.9), channel_id=1, source_target_pairs={{0,1},{2,3},{4,5},{6,7},{8,9},{10,11},{12,13},{14,15},{16,17},{18,... | collective-permute-start | bytes 27656 | tf_op jit(solution)/shard_map/ppermute | solution.py:19
  39.3 1.3 %collective-permute-start.3 = (bf16[48,8,12]{1,2,0:T(8,128)(2,1)S(1)}, bf16[48,8,12]{1,2,0:T(8,128)(2,1)S(1)}, u32[]{:S(2)}, u32[]{:S(2)}) collective-permute-start(bf16[48,8,12]{1,2,0:T(8,128)(2,1)S(1)} %get-tuple-element.10), channel_id=1, source_target_pairs={{1,0},{3,2},{5,4},{7,6},{9,8},{11,10},{13,12},{15,14},{17,16},{19,... | collective-permute-start | bytes 27656 | tf_op jit(solution)/shard_map/ppermute | solution.py:21
  40.7 2.0 %collective-permute-done.3 = bf16[48,8,12]{1,2,0:T(8,128)(2,1)S(1)} collective-permute-done((bf16[48,8,12]{1,2,0:T(8,128)(2,1)S(1)}, bf16[48,8,12]{1,2,0:T(8,128)(2,1)S(1)}, u32[]{:S(2)}, u32[]{:S(2)}) %collective-permute-start.3) | collective-permute-done | bytes 9248 | tf_op jit(solution)/shard_map/ppermute | solution.py:21
  42.7 0.3 pad_maximum_fusion.14
  43.0 0.5 fusion.101
  43.5 0.5 fusion.103
  44.1 0.5 fusion.105
  44.6 0.5 fusion.107
  45.1 0.5 fusion.109
  45.6 0.5 fusion.95
  46.1 0.5 fusion.97
  46.6 0.5 fusion.99
  47.1 1.3 %select_convert_fusion = bf16[46,270,32]{1,2,0:T(8,128)(2,1)S(1)} fusion(f32[46,270,32]{1,2,0:T(8,128)S(1)} %fusion.95, f32[46,270,32]{1,2,0:T(8,128)S(1)} %fusion.97, f32[46,270,32]{1,2,0:T(8,128)S(1)} %fusion.99, f32[46,270,32]{1,2,0:T(8,128)S(1)} %fusion.101, f32[46,270,32]{1,2,0:T(8,128)S(1)} %fusion.103, f32[46,270,32]{1,2,0:T(8,128)S(1)} %fusion.105, ...), kind=kOutput, calls=%fused_computation.17 | convolution fusion | flops 13910400 | bytes 19470592 | tf_op jit(solution)/shard_map/hwc,oc->hwo/dot_general | solution.py:35
  48.5 0.5 fusion.62
  49.0 0.4 fusion.64
  49.4 0.5 fusion.66
  50.0 0.5 fusion.68
  50.5 0.4 fusion.70
  50.9 0.5 fusion.72
  51.5 0.5 fusion.74
  52.0 0.4 fusion.76
  52.4 1.6 %select_convert_fusion.1 = bf16[44,268,32]{1,2,0:T(8,128)(2,1)S(1)} fusion(f32[44,268,32]{1,2,0:T(8,128)S(1)} %fusion.62, f32[44,268,32]{1,2,0:T(8,128)S(1)} %fusion.64, f32[44,268,32]{1,2,0:T(8,128)S(1)} %fusion.66, f32[44,268,32]{1,2,0:T(8,128)S(1)} %fusion.68, f32[44,268,32]{1,2,0:T(8,128)S(1)} %fusion.70, f32[44,268,32]{1,2,0:T(8,128)S(1)} %fusion.72, ...), kind=kOutput, calls=%fused_computation.18 | convolution fusion | flops 28300800 | bytes 19164160 | tf_op jit(solution)/shard_map/hwc,oc->hwo/dot_general | solution.py:35
  54.0 0.4 slice.421
  54.4 0.6 fusion.125
  55.0 0.2 reduce_sum.49
  55.3 0.6 copy-done.4
  55.9 0.4 fusion.121
  56.2 0.6 convolution_add_fusion.7
  56.8 0.4 convolution_add_fusion.6
  57.2 0.4 convolution_add_fusion.5
  57.6 0.4 convolution_add_fusion.4
  58.1 0.4 convolution_add_fusion.3
  58.5 0.4 convolution_add_fusion.2
  58.9 0.4 convolution_add_fusion.1
  59.3 0.4 fusion.54
  59.8 0.4 copy-done.2
  60.2 0.3 fusion.87
  60.5 0.4 convolution_add_fusion.15
  60.9 0.4 convolution_add_fusion.14
  61.3 0.3 convolution_add_fusion.13
  61.6 0.4 convolution_add_fusion.12
  62.0 0.4 convolution_add_fusion.11
  62.3 0.3 convolution_add_fusion.10
  62.7 0.4 convolution_add_fusion.9
  63.0 1.7 %fusion.56 = bf16[18,258,64]{1,2,0:T(8,128)(2,1)} fusion(f32[18,130,64]{1,2,0:T(8,128)S(1)} %convolution_add_fusion.9, bf16[20,132,64]{1,2,0:T(8,128)(2,1)S(1)} %fusion.54, pred[18,130]{1,0:T(8,128)(4,1)S(1)} %broadcast_and_fusion.3, s32[258]{0:T(512)S(1)} %add_select_fusion, bf16[3,3,64,64]{3,2,1,0:T(8,128)(2,1)S(1)} %copy-done.2), kind=kOutput, calls=%fused_computation.72 | convolution fusion | flops 97375232 | bytes 2388480 | tf_op jit(solution)/shard_map/wv,hvc->hwc/dot_general | solution.py:153
  64.7 1.4 %broadcast_in_dim.42 = bf16[18,2,258,64]{2,3,1,0:T(8,128)(2,1)S(1)} broadcast(bf16[18,258,64]{1,2,0:T(8,128)(2,1)} %fusion.56), dimensions={0,2,3} | broadcast | bytes 1783296 | tf_op jit(solution)/shard_map/broadcast_in_dim | solution.py:159
  66.4 0.7 copy-done.5
  67.1 0.3 fusion.4
  67.4 0.7 fusion.1
  68.1 0.7 fusion.51
  68.8 0.7 fusion.48
  69.5 0.4 fusion.45
  69.9 0.7 fusion.42
  70.6 0.7 fusion.39
  71.4 1.4 %fusion.36 = f32[32,256,32]{1,2,0:T(8,128)} fusion(f32[32,256,32]{1,2,0:T(8,128)S(1)} %fusion.1, f32[32,256,32]{1,2,0:T(8,128)S(1)} %fusion.39, bf16[34,258,64]{1,2,0:T(8,128)(2,1)S(1)} %slice.440, bf16[34,258,32]{1,2,0:T(8,128)(2,1)S(1)} %slice.421, bf16[3,3,32,96]{3,2,1,0:T(8,128)(2,1)S(1)} %copy-done.5), kind=kOutput, calls=%fused_computation.64 | convolution fusion | flops 54001664 | bytes 5660672 | tf_op jit(solution)/shard_map/hwc,oc->hwo/dot_general | solution.py:35
  72.7 2.2 %fusion.60 = bf16[11,32,256]{2,0,1:T(8,128)(2,1)S(1)} fusion(f32[32,256,32]{1,2,0:T(8,128)} %fusion.36, bf16[34,258,64]{1,2,0:T(8,128)(2,1)S(1)} %slice.440, bf16[34,258,32]{1,2,0:T(8,128)(2,1)S(1)} %slice.421, bf16[3,3,32,96]{3,2,1,0:T(8,128)(2,1)S(1)} %copy-done.5, bf16[11,32]{1,0:T(8,128)(2,1)S(1)} %copy-done), kind=kOutput, calls=%fused_computation.76 | convolution fusion | flops 60121088 | bytes 3747840 | tf_op jit(solution)/shard_map/oc,hwc->ohw/dot_general | solution.py:166
  74.9 0.7 copy.21
  (42 shorter events, 1.5 us)
Async XLA Ops:
  0.0 72.7 %copy-start = (bf16[11,32]{1,0:T(8,128)(2,1)S(1)}, bf16[11,32]{1,0:T(8,128)(2,1)}, u32[]{:S(2)}) copy-start(bf16[11,32]{1,0:T(8,128)(2,1)} %param.19) | copy-start | bytes 2116
  2.8 1.8 %copy-start.1 = (f32[8,32,256]{2,1,0:T(8,128)S(1)}, f32[8,32,256]{2,1,0:T(8,128)}, u32[]{:S(2)}) copy-start(f32[8,32,256]{2,1,0:T(8,128)} %get-tuple-element.7) | copy-start | bytes 786436
  2.8 1.8 %copy-start.7 = (f32[32,256]{1,0:T(8,128)S(1)}, f32[32,256]{1,0:T(8,128)}, u32[]{:S(2)}) copy-start(f32[32,256]{1,0:T(8,128)} %get-tuple-element.8) | copy-start | bytes 98308
  28.3 14.8 %copy-start.6 = (bf16[3,3,32,12]{2,3,1,0:T(8,128)(2,1)S(1)}, bf16[3,3,32,12]{2,3,1,0:T(8,128)(2,1)}, u32[]{:S(2)}) copy-start(bf16[3,3,32,12]{2,3,1,0:T(8,128)(2,1)} %param.14) | copy-start | bytes 20740
  28.3 5.3 %collective-permute-start = (bf16[8,256,12]{1,2,0:T(8,128)(2,1)S(1)}, bf16[8,256,12]{1,2,0:T(8,128)(2,1)S(1)}, u32[]{:S(2)}, u32[]{:S(2)}) collective-permute-start(bf16[8,256,12]{1,2,0:T(8,128)(2,1)S(1)} %get-tuple-element.11), channel_id=1, source_target_pairs={{0,2},{2,4},{4,6},{1,3},{3,5},{5,7},{8,10},{10,12},{12,14},{9,11},... | collective-permute-start | bytes 147464 | tf_op jit(solution)/shard_map/ppermute | solution.py:19
  31.7 6.2 %collective-permute-start.1 = (bf16[8,256,12]{1,2,0:T(8,128)(2,1)S(1)}, bf16[8,256,12]{1,2,0:T(8,128)(2,1)S(1)}, u32[]{:S(2)}, u32[]{:S(2)}) collective-permute-start(bf16[8,256,12]{1,2,0:T(8,128)(2,1)S(1)} %get-tuple-element.12), channel_id=1, source_target_pairs={{2,0},{4,2},{6,4},{3,1},{5,3},{7,5},{10,8},{12,10},{14,12},{11,9},... | collective-permute-start | bytes 147464 | tf_op jit(solution)/shard_map/ppermute | solution.py:21
  38.0 2.6 %collective-permute-start.2 = (bf16[48,8,12]{1,2,0:T(8,128)(2,1)S(1)}, bf16[48,8,12]{1,2,0:T(8,128)(2,1)S(1)}, u32[]{:S(2)}, u32[]{:S(2)}) collective-permute-start(bf16[48,8,12]{1,2,0:T(8,128)(2,1)S(1)} %get-tuple-element.9), channel_id=1, source_target_pairs={{0,1},{2,3},{4,5},{6,7},{8,9},{10,11},{12,13},{14,15},{16,17},{18,... | collective-permute-start | bytes 27656 | tf_op jit(solution)/shard_map/ppermute | solution.py:19
  39.3 3.3 %collective-permute-start.3 = (bf16[48,8,12]{1,2,0:T(8,128)(2,1)S(1)}, bf16[48,8,12]{1,2,0:T(8,128)(2,1)S(1)}, u32[]{:S(2)}, u32[]{:S(2)}) collective-permute-start(bf16[48,8,12]{1,2,0:T(8,128)(2,1)S(1)} %get-tuple-element.10), channel_id=1, source_target_pairs={{1,0},{3,2},{5,4},{7,6},{9,8},{11,10},{13,12},{15,14},{17,16},{19,... | collective-permute-start | bytes 27656 | tf_op jit(solution)/shard_map/ppermute | solution.py:21
  47.1 1.4 %copy-start.3 = (bf16[3,3,32,32]{3,2,1,0:T(8,128)(2,1)S(1)}, bf16[3,3,32,32]{3,2,1,0:T(8,128)(2,1)}, u32[]{:S(2)}) copy-start(bf16[3,3,32,32]{3,2,1,0:T(8,128)(2,1)} %param.15) | copy-start | bytes 55300
  55.0 0.9 %copy-start.4 = (bf16[3,3,64,32]{2,3,1,0:T(8,128)(2,1)S(1)}, bf16[3,3,64,32]{2,3,1,0:T(8,128)(2,1)}, u32[]{:S(2)}) copy-start(bf16[3,3,64,32]{2,3,1,0:T(8,128)(2,1)} %param.16) | copy-start | bytes 110596
  59.3 0.9 %copy-start.2 = (bf16[3,3,64,64]{3,2,1,0:T(8,128)(2,1)S(1)}, bf16[3,3,64,64]{3,2,1,0:T(8,128)(2,1)}, u32[]{:S(2)}) copy-start(bf16[3,3,64,64]{3,2,1,0:T(8,128)(2,1)} %param.17) | copy-start | bytes 221188
  66.2 0.9 %copy-start.5 = (bf16[3,3,32,96]{3,2,1,0:T(8,128)(2,1)S(1)}, bf16[3,3,32,96]{3,2,1,0:T(8,128)(2,1)}, u32[]{:S(2)}) copy-start(bf16[3,3,32,96]{3,2,1,0:T(8,128)(2,1)} %param.18) | copy-start | bytes 165892

commit v7 on v6

--- a/solution.py
+++ b/solution.py
@@ -14,6 +14,14 @@
         ends = count - 1
         head = lax.slice_in_dim(cells, 0, width, axis=dim)
         tail = lax.slice_in_dim(cells, cells.shape[dim] - width, cells.shape[dim], axis=dim)
+        if count == 2:
+            first = lax.axis_index(axis) == 0
+            got = lax.ppermute(jnp.where(first, tail, head), axis, [(0, 1), (1, 0)])
+            empty = jnp.zeros_like(got)
+            cells = jnp.concatenate(
+                [jnp.where(first, empty, got), cells, jnp.where(first, got, empty)], axis=dim
+            )
+            continue
         cells = jnp.concatenate(
             [
                 lax.ppermute(tail, axis, [(i, (i + 1) % count) for i in range(ends)]),

time: 76.1 us -> 72.7 us (0.955)
  starting transfers between devices: 7.28 us -> 4.76 us
    ppermute x2 -> x1, waiting for transfers between devices: 6.29 us -> 4.27 us  [with_halo(): lax.ppermute(head, axis, [((i + 1) % count, i) for i in range(ends)])]
    ppermute x0 -> x1, waiting for transfers between devices: none -> 1.42 us  [with_halo(): got = lax.ppermute(jnp.where(first, tail, head), axis, [(0, 1), (1, 0)])]
    ppermute x2 -> x1, starting transfers between devices: 4.7 us -> 3.4 us  [with_halo(): lax.ppermute(tail, axis, [(i, (i + 1) % count) for i in range(ends)])]
    ppermute x2 -> x1, starting transfers between devices: 2.58 us -> 1.29 us  [with_halo(): lax.ppermute(head, axis, [((i + 1) % count, i) for i in range(ends)])]
  transfers between devices with their start and end apart: 4 -> 3, of which waited for: 3 -> 3; matrix products, arithmetic and copies ran while one was open for 1% -> 1% of each run, Pallas kernels for 0% -> 0%
where the time goes in v7:
time: 72.7 us; the launch traced here: 72.3 us
  matrix products  27.3 us (38%)
  blocking collectives  22.8 us (31%)
  waiting for transfers between devices  5.78 us (8%)
  starting transfers between devices  4.76 us (7%)
  local copies, waits for them, and re-layouts  4.37 us (6%)
  other arithmetic  3.99 us (5%)
  Pallas kernels  2.83 us (4%)
    dot_general x43, matrix products, valid_conv(): jnp.einsum('hwc,oc->hwo', padded[a:a + height, e:e + width], kernel[a, e]...  22.9 us
    all_gather x1, blocking collectives, shards(): gathered = lax.all_gather(packed, 'tm', axis=0).astype(jnp.float32)  22.8 us
    ppermute x1, waiting for transfers between devices, with_halo(): lax.ppermute(head, axis, [((i + 1) % count, i) for i in range(ends)])  4.27 us
    ppermute x1, starting transfers between devices, with_halo(): lax.ppermute(tail, axis, [(i, (i + 1) % count) for i in range(ends)])  3.4 us
    pallas_call x1, Pallas kernels, shifted_weights(): pl.pallas_call(weight_kernel, out_shape=(jax.ShapeDtypeStruct((dates, row...  2.83 us
    dot_general x1, matrix products, shards(): jnp.einsum('oc,hwc->ohw', head_weight, decoded, preferred_element_type=jn...  2.15 us
    reduce_sum x1, other arithmetic, shards(): part_sums = jnp.sum(weights[:, None] * reflectance, axis=0)  1.79 us
    dot_general x1, matrix products, shards(): jnp.einsum('wv,hvc->hwc', pair_matrix(deep_cols, block_cols + 2, up_halo...  1.68 us
  transfers between devices with their start and end apart: 3, of which 3 were waited for; matrix products, arithmetic and copies ran while one was open for 1% of the time, Pallas kernels for 0%

profile of v7, /device:TPU:0, one launch (start us, length us, event | category | flops | bytes accessed | tf_op | source)
XLA Modules:
  0.0 72.3 jit_solution(6840958119955718671)
XLA Ops:
  0.0 2.8 %shard_map.100 = (f32[8,32,256]{2,1,0:T(8,128)}, f32[32,256]{1,0:T(8,128)}) custom-call(f32[12]{0:T(128)} %score_ref.1, s32[8,32,256]{2,1,0:T(8,128)} %class_ref.1, f32[8,32,256]{2,1,0:T(8,128)} %quality_ref.1), custom_call_target="tpu_custom_call" | custom-call | tf_op jit(solution)/shard_map/pallas_call | solution.py:90
  2.8 1.8 %multiply_reduce_fusion = bf16[12,32,256]{2,1,0:T(8,128)(2,1)S(1)} fusion(bf16[8,12,32,256]{3,2,1,0:T(8,128)(2,1)} %param.10, f32[8,32,256]{2,1,0:T(8,128)} %get-tuple-element.7), kind=kLoop, calls=%fused_computation.16 | loop fusion | flops 2260992 | bytes 2031616 | tf_op jit(solution)/shard_map/reduce_sum | solution.py:132
  4.7 22.8 %all_gather.4 = bf16[4,14,32,256]{3,2,1,0:T(8,128)(2,1)S(1)} all-gather(bf16[1,14,32,256]{3,2,1,0:T(8,128)(2,1)S(1)} %pad_maximum_fusion.16), channel_id=1, replica_groups=mesh['tm'=4,'row'=4,'col'=2] {'tm'}, dimensions={0}, use_global_device_ids=true | all-gather | bytes 1146880 | tf_op jit(solution)/shard_map/all_gather | solution.py:135
  27.5 0.2 convert_element_type.54
  27.8 0.2 fusion.26
  28.0 0.2 fusion.120
  28.3 3.4 %collective-permute-start = (bf16[8,256,12]{1,2,0:T(8,128)(2,1)S(1)}, bf16[8,256,12]{1,2,0:T(8,128)(2,1)S(1)}, u32[]{:S(2)}, u32[]{:S(2)}) collective-permute-start(bf16[8,256,12]{1,2,0:T(8,128)(2,1)S(1)} %get-tuple-element.9), channel_id=1, source_target_pairs={{0,2},{2,4},{4,6},{1,3},{3,5},{5,7},{8,10},{10,12},{12,14},{9,11},... | collective-permute-start | bytes 147464 | tf_op jit(solution)/shard_map/ppermute | solution.py:27
  31.7 1.3 %collective-permute-start.1 = (bf16[8,256,12]{1,2,0:T(8,128)(2,1)S(1)}, bf16[8,256,12]{1,2,0:T(8,128)(2,1)S(1)}, u32[]{:S(2)}, u32[]{:S(2)}) collective-permute-start(bf16[8,256,12]{1,2,0:T(8,128)(2,1)S(1)} %get-tuple-element.10), channel_id=1, source_target_pairs={{2,0},{4,2},{6,4},{3,1},{5,3},{7,5},{10,8},{12,10},{14,12},{11,9},... | collective-permute-start | bytes 147464 | tf_op jit(solution)/shard_map/ppermute | solution.py:29
  33.5 4.3 %collective-permute-done.1 = bf16[8,256,12]{1,2,0:T(8,128)(2,1)S(1)} collective-permute-done((bf16[8,256,12]{1,2,0:T(8,128)(2,1)S(1)}, bf16[8,256,12]{1,2,0:T(8,128)(2,1)S(1)}, u32[]{:S(2)}, u32[]{:S(2)}) %collective-permute-start.1) | collective-permute-done | bytes 49184 | tf_op jit(solution)/shard_map/ppermute | solution.py:29
  38.1 1.4 %collective-permute-done.2 = bf16[48,8,12]{1,2,0:T(8,128)(2,1)S(1)} collective-permute-done((bf16[48,8,12]{1,2,0:T(8,128)(2,1)S(1)}, bf16[48,8,12]{1,2,0:T(8,128)(2,1)S(1)}, u32[]{:S(2)}, u32[]{:S(2)}) %collective-permute-start.2) | collective-permute-done | bytes 9248 | tf_op jit(solution)/shard_map/ppermute | solution.py:19
  39.6 0.4 pad_maximum_fusion.14
  39.9 0.5 fusion.100
  40.4 0.5 fusion.102
  40.9 0.5 fusion.104
  41.4 0.5 fusion.106
  41.9 0.5 fusion.92
  42.5 0.5 fusion.94
  43.0 0.5 fusion.96
  43.5 0.5 fusion.98
  44.0 1.3 %select_convert_fusion = bf16[46,270,32]{1,2,0:T(8,128)(2,1)S(1)} fusion(f32[46,270,32]{1,2,0:T(8,128)S(1)} %fusion.92, f32[46,270,32]{1,2,0:T(8,128)S(1)} %fusion.94, f32[46,270,32]{1,2,0:T(8,128)S(1)} %fusion.96, f32[46,270,32]{1,2,0:T(8,128)S(1)} %fusion.98, f32[46,270,32]{1,2,0:T(8,128)S(1)} %fusion.100, f32[46,270,32]{1,2,0:T(8,128)S(1)} %fusion.102, ...), kind=kOutput, calls=%fused_computation.17 | convolution fusion | flops 13910400 | bytes 19470592 | tf_op jit(solution)/shard_map/hwc,oc->hwo/dot_general | solution.py:43
  45.3 0.5 fusion.62
  45.9 0.4 fusion.64
  46.3 0.5 fusion.66
  46.8 0.5 fusion.68
  47.4 0.4 fusion.70
  47.8 0.5 fusion.72
  48.3 0.5 fusion.74
  48.9 0.4 fusion.76
  49.3 1.6 %select_convert_fusion.1 = bf16[44,268,32]{1,2,0:T(8,128)(2,1)S(1)} fusion(f32[44,268,32]{1,2,0:T(8,128)S(1)} %fusion.62, f32[44,268,32]{1,2,0:T(8,128)S(1)} %fusion.64, f32[44,268,32]{1,2,0:T(8,128)S(1)} %fusion.66, f32[44,268,32]{1,2,0:T(8,128)S(1)} %fusion.68, f32[44,268,32]{1,2,0:T(8,128)S(1)} %fusion.70, f32[44,268,32]{1,2,0:T(8,128)S(1)} %fusion.72, ...), kind=kOutput, calls=%fused_computation.18 | convolution fusion | flops 28300800 | bytes 19164160 | tf_op jit(solution)/shard_map/hwc,oc->hwo/dot_general | solution.py:43
  50.8 0.4 slice.421
  51.3 0.6 fusion.122
  51.9 0.4 reduce_sum.49
  52.3 0.4 copy-done.4
  52.7 0.4 fusion.118
  53.1 0.4 convolution_add_fusion.7
  53.5 0.4 convolution_add_fusion.6
  53.9 0.4 convolution_add_fusion.5
  54.3 0.4 convolution_add_fusion.4
  54.8 0.4 convolution_add_fusion.3
  55.2 0.4 convolution_add_fusion.2
  55.6 0.4 convolution_add_fusion.1
  56.0 0.4 fusion.54
  56.5 0.4 copy-done.2
  56.9 0.3 fusion.87
  57.2 0.4 convolution_add_fusion.15
  57.6 0.4 convolution_add_fusion.14
  58.0 0.3 convolution_add_fusion.13
  58.3 0.4 convolution_add_fusion.12
  58.7 0.4 convolution_add_fusion.11
  59.0 0.3 convolution_add_fusion.10
  59.4 0.4 convolution_add_fusion.9
  59.7 1.7 %fusion.56 = bf16[18,258,64]{1,2,0:T(8,128)(2,1)} fusion(f32[18,130,64]{1,2,0:T(8,128)S(1)} %convolution_add_fusion.9, bf16[20,132,64]{1,2,0:T(8,128)(2,1)S(1)} %fusion.54, pred[18,130]{1,0:T(8,128)(4,1)S(1)} %broadcast_and_fusion.3, s32[258]{0:T(512)S(1)} %add_select_fusion, bf16[3,3,64,64]{3,2,1,0:T(8,128)(2,1)S(1)} %copy-done.2), kind=kOutput, calls=%fused_computation.72 | convolution fusion | flops 97375232 | bytes 2388480 | tf_op jit(solution)/shard_map/wv,hvc->hwc/dot_general | solution.py:161
  61.4 1.4 %broadcast_in_dim.45 = bf16[18,2,258,64]{2,3,1,0:T(8,128)(2,1)S(1)} broadcast(bf16[18,258,64]{1,2,0:T(8,128)(2,1)} %fusion.56), dimensions={0,2,3} | broadcast | bytes 1783296 | tf_op jit(solution)/shard_map/broadcast_in_dim | solution.py:167
  63.1 0.7 copy-done.5
  63.8 0.3 fusion.4
  64.1 0.7 fusion.1
  64.8 0.7 %fusion.51 = f32[32,256,32]{1,2,0:T(8,128)S(1)} fusion(f32[32,256,32]{1,2,0:T(8,128)S(1)} %fusion.4, bf16[34,258,64]{1,2,0:T(8,128)(2,1)S(1)} %slice.440, bf16[34,258,32]{1,2,0:T(8,128)(2,1)S(1)} %slice.421, bf16[3,3,32,96]{3,2,1,0:T(8,128)(2,1)S(1)} %copy-done.5), kind=kOutput, calls=%fused_computation.69 | convolution fusion | flops 53739520 | bytes 4612096 | tf_op jit(solution)/shard_map/hwc,oc->hwo/dot_general | solution.py:43
  65.5 0.7 fusion.48
  66.2 0.4 fusion.45
  66.6 0.7 fusion.42
  67.3 0.7 fusion.39
  68.1 1.4 %fusion.36 = f32[32,256,32]{1,2,0:T(8,128)} fusion(f32[32,256,32]{1,2,0:T(8,128)S(1)} %fusion.1, f32[32,256,32]{1,2,0:T(8,128)S(1)} %fusion.39, bf16[34,258,64]{1,2,0:T(8,128)(2,1)S(1)} %slice.440, bf16[34,258,32]{1,2,0:T(8,128)(2,1)S(1)} %slice.421, bf16[3,3,32,96]{3,2,1,0:T(8,128)(2,1)S(1)} %copy-done.5), kind=kOutput, calls=%fused_computation.64 | convolution fusion | flops 54001664 | bytes 5660672 | tf_op jit(solution)/shard_map/hwc,oc->hwo/dot_general | solution.py:43
  69.4 2.2 %fusion.60 = bf16[11,32,256]{2,0,1:T(8,128)(2,1)S(1)} fusion(f32[32,256,32]{1,2,0:T(8,128)} %fusion.36, bf16[34,258,64]{1,2,0:T(8,128)(2,1)S(1)} %slice.440, bf16[34,258,32]{1,2,0:T(8,128)(2,1)S(1)} %slice.421, bf16[3,3,32,96]{3,2,1,0:T(8,128)(2,1)S(1)} %copy-done.5, bf16[11,32]{1,0:T(8,128)(2,1)S(1)} %copy-done), kind=kOutput, calls=%fused_computation.76 | convolution fusion | flops 60121088 | bytes 3747840 | tf_op jit(solution)/shard_map/oc,hwc->ohw/dot_general | solution.py:174
  71.6 0.7 %copy.21 = bf16[11,32,256]{2,1,0:T(8,128)(2,1)} copy(bf16[11,32,256]{2,0,1:T(8,128)(2,1)S(1)} %fusion.60) | data formatting | bytes 360448 | tf_op jit(solution)/shard_map/convert_element_type | solution.py:176
  (41 shorter events, 1.2 us)
Async XLA Ops:
  0.0 69.4 %copy-start = (bf16[11,32]{1,0:T(8,128)(2,1)S(1)}, bf16[11,32]{1,0:T(8,128)(2,1)}, u32[]{:S(2)}) copy-start(bf16[11,32]{1,0:T(8,128)(2,1)} %param.19) | copy-start | bytes 2116
  2.8 1.8 %copy-start.1 = (f32[8,32,256]{2,1,0:T(8,128)S(1)}, f32[8,32,256]{2,1,0:T(8,128)}, u32[]{:S(2)}) copy-start(f32[8,32,256]{2,1,0:T(8,128)} %get-tuple-element.7) | copy-start | bytes 786436
  2.8 1.8 %copy-start.7 = (f32[32,256]{1,0:T(8,128)S(1)}, f32[32,256]{1,0:T(8,128)}, u32[]{:S(2)}) copy-start(f32[32,256]{1,0:T(8,128)} %get-tuple-element.8) | copy-start | bytes 98308
  28.3 5.3 %collective-permute-start = (bf16[8,256,12]{1,2,0:T(8,128)(2,1)S(1)}, bf16[8,256,12]{1,2,0:T(8,128)(2,1)S(1)}, u32[]{:S(2)}, u32[]{:S(2)}) collective-permute-start(bf16[8,256,12]{1,2,0:T(8,128)(2,1)S(1)} %get-tuple-element.9), channel_id=1, source_target_pairs={{0,2},{2,4},{4,6},{1,3},{3,5},{5,7},{8,10},{10,12},{12,14},{9,11},... | collective-permute-start | bytes 147464 | tf_op jit(solution)/shard_map/ppermute | solution.py:27
  31.7 6.2 %collective-permute-start.1 = (bf16[8,256,12]{1,2,0:T(8,128)(2,1)S(1)}, bf16[8,256,12]{1,2,0:T(8,128)(2,1)S(1)}, u32[]{:S(2)}, u32[]{:S(2)}) collective-permute-start(bf16[8,256,12]{1,2,0:T(8,128)(2,1)S(1)} %get-tuple-element.10), channel_id=1, source_target_pairs={{2,0},{4,2},{6,4},{3,1},{5,3},{7,5},{10,8},{12,10},{14,12},{11,9},... | collective-permute-start | bytes 147464 | tf_op jit(solution)/shard_map/ppermute | solution.py:29
  33.5 6.5 %copy-start.6 = (bf16[3,3,32,12]{2,3,1,0:T(8,128)(2,1)S(1)}, bf16[3,3,32,12]{2,3,1,0:T(8,128)(2,1)}, u32[]{:S(2)}) copy-start(bf16[3,3,32,12]{2,3,1,0:T(8,128)(2,1)} %param.14) | copy-start | bytes 20740
  38.0 1.5 %collective-permute-start.2 = (bf16[48,8,12]{1,2,0:T(8,128)(2,1)S(1)}, bf16[48,8,12]{1,2,0:T(8,128)(2,1)S(1)}, u32[]{:S(2)}, u32[]{:S(2)}) collective-permute-start(bf16[48,8,12]{1,2,0:T(8,128)(2,1)S(1)} %slice_select_fusion), channel_id=1, source_target_pairs={{0,1},{1,0},{2,3},{3,2},{4,5},{5,4},{6,7},{7,6},{8,9},{9,8},{10,11... | collective-permute-start | bytes 27656 | tf_op jit(solution)/shard_map/ppermute | solution.py:19
  44.0 1.4 %copy-start.3 = (bf16[3,3,32,32]{3,2,1,0:T(8,128)(2,1)S(1)}, bf16[3,3,32,32]{3,2,1,0:T(8,128)(2,1)}, u32[]{:S(2)}) copy-start(bf16[3,3,32,32]{3,2,1,0:T(8,128)(2,1)} %param.15) | copy-start | bytes 55300
  51.8 0.9 %copy-start.4 = (bf16[3,3,64,32]{2,3,1,0:T(8,128)(2,1)S(1)}, bf16[3,3,64,32]{2,3,1,0:T(8,128)(2,1)}, u32[]{:S(2)}) copy-start(bf16[3,3,64,32]{2,3,1,0:T(8,128)(2,1)} %param.16) | copy-start | bytes 110596
  56.0 0.9 %copy-start.2 = (bf16[3,3,64,64]{3,2,1,0:T(8,128)(2,1)S(1)}, bf16[3,3,64,64]{3,2,1,0:T(8,128)(2,1)}, u32[]{:S(2)}) copy-start(bf16[3,3,64,64]{3,2,1,0:T(8,128)(2,1)} %param.17) | copy-start | bytes 221188
  62.9 0.9 %copy-start.5 = (bf16[3,3,32,96]{3,2,1,0:T(8,128)(2,1)S(1)}, bf16[3,3,32,96]{3,2,1,0:T(8,128)(2,1)}, u32[]{:S(2)}) copy-start(bf16[3,3,32,96]{3,2,1,0:T(8,128)(2,1)} %param.18) | copy-start | bytes 165892

commit v8 on v7

--- a/solution.py
+++ b/solution.py
@@ -34,20 +34,15 @@
 
 
 def valid_conv(padded, kernel):
-    taps = kernel.shape[0]
+    taps, _, outs, ins = kernel.shape
     height = padded.shape[0] - taps + 1
     width = padded.shape[1] - taps + 1
-    total = None
-    for a in range(taps):
-        for e in range(taps):
-            term = jnp.einsum(
-                "hwc,oc->hwo",
-                padded[a : a + height, e : e + width],
-                kernel[a, e],
-                preferred_element_type=jnp.float32,
-            )
-            total = term if total is None else total + term
-    return total
+    stacked = jnp.stack(
+        [padded[a : a + height, e : e + width] for a in range(taps) for e in range(taps)], axis=0
+    )
+    return jnp.einsum(
+        "thwc,toc->hwo", stacked, kernel.reshape(taps * taps, outs, ins), preferred_element_type=jnp.float32
+    )
 
 
 def pair_matrix(narrow, wide, offset):

time: 72.7 us -> 82.4 us (1.13)
  local copies, waits for them, and re-layouts: 4.37 us -> 17.7 us
  matrix products: 27.3 us -> 16 us
  other arithmetic: 3.99 us -> 11.5 us
    dot_general x43 -> x3, matrix products: 22.9 us -> 3.61 us  [valid_conv(): jnp.einsum('thwc,toc->hwo', stacked, kernel.reshape(taps * taps, outs, in...]
    unnamed x16 -> x48, local copies, waits for them, and re-layouts: 1.58 us -> 14.9 us
    dot_general x1, matrix products: 2.15 us -> 7.76 us  [shards(): jnp.einsum('oc,hwc->ohw', head_weight, decoded, preferred_element_type=jn...]
    unnamed x0 -> x8, other arithmetic: none -> 5.1 us
    dot_general x1, matrix products: 1.68 us -> 4.03 us  [shards(): jnp.einsum('wv,hvc->hwc', pair_matrix(deep_cols, block_cols + 2, up_halo...]
    another operation x0 -> x4, local copies, waits for them, and re-layouts: none -> 1.26 us  [valid_conv(): jnp.stack([padded[a:a + height, e:e + width] for a in range(taps) for e i...]
    broadcast_in_dim x1, local copies, waits for them, and re-layouts: 1.44 us -> 0.28 us  [shards(): jnp.broadcast_to(spread[:, None], (deep_rows, 2, block_cols + 2, deep_ch))]
    reduce_sum x1, other arithmetic: 0.02 us -> 0.97 us  [shards(): part_total = jnp.sum(weights, axis=0)]
  transfers between devices with their start and end apart: 3 -> 3, of which waited for: 3 -> 3; matrix products, arithmetic and copies ran while one was open for 1% -> 0% of each run, Pallas kernels for 0% -> 0%
where the time goes in v8:
time: 82.4 us; the launch traced here: 82 us
  blocking collectives  22.8 us (28%)
  local copies, waits for them, and re-layouts  17.7 us (21%)
  matrix products  16 us (19%)
  other arithmetic  11.5 us (14%)
  waiting for transfers between devices  5.77 us (7%)
  starting transfers between devices  4.76 us (6%)
  Pallas kernels  2.85 us (3%)
    all_gather x1, blocking collectives, shards(): gathered = lax.all_gather(packed, 'tm', axis=0).astype(jnp.float32)  22.8 us
    unnamed x48, local copies, waits for them, and re-layouts  14.9 us
    dot_general x1, matrix products, shards(): jnp.einsum('oc,hwc->ohw', head_weight, decoded, preferred_element_type=jn...  7.76 us
    unnamed x8, other arithmetic  5.1 us
    ppermute x1, waiting for transfers between devices, with_halo(): lax.ppermute(head, axis, [((i + 1) % count, i) for i in range(ends)])  4.27 us
    dot_general x1, matrix products, shards(): jnp.einsum('wv,hvc->hwc', pair_matrix(deep_cols, block_cols + 2, up_halo...  4.03 us
    dot_general x3, matrix products, valid_conv(): jnp.einsum('thwc,toc->hwo', stacked, kernel.reshape(taps * taps, outs, in...  3.61 us
    ppermute x1, starting transfers between devices, with_halo(): lax.ppermute(tail, axis, [(i, (i + 1) % count) for i in range(ends)])  3.4 us
  transfers between devices with their start and end apart: 3, of which 3 were waited for; matrix products, arithmetic and copies ran while one was open for 0% of the time, Pallas kernels for 0%

profile of v8, /device:TPU:0, one launch (start us, length us, event | category | flops | bytes accessed | tf_op | source)
XLA Modules:
  0.0 82.0 jit_solution(5306198348128309681)
XLA Ops:
  0.0 2.9 %shard_map.100 = (f32[8,32,256]{2,1,0:T(8,128)}, f32[32,256]{1,0:T(8,128)}) custom-call(f32[12]{0:T(128)} %score_ref.1, s32[8,32,256]{2,1,0:T(8,128)} %class_ref.1, f32[8,32,256]{2,1,0:T(8,128)} %quality_ref.1), custom_call_target="tpu_custom_call" | custom-call | tf_op jit(solution)/shard_map/pallas_call | solution.py:85
  2.9 0.8 convert_bitcast_fusion.1
  3.6 1.0 %reduce_sum.46 = bf16[32,256]{1,0:T(8,128)(2,1)S(1)} reduce(f32[8,32,256]{2,1,0:T(8,128)} %get-tuple-element.7, f32[]{:T(128)} %constant.98.clone.1), dimensions={0}, to_apply=%region_1.0 | reduce | flops 57344 | bytes 278532 | tf_op jit(solution)/shard_map/reduce_sum | solution.py:128
  4.6 1.8 %multiply_reduce_fusion = bf16[12,32,256]{2,1,0:T(8,128)(2,1)S(1)} fusion(bf16[8,12,32,256]{3,2,1,0:T(8,128)(2,1)} %param.10, f32[8,32,256]{2,1,0:T(8,128)} %get-tuple-element.7), kind=kLoop, calls=%fused_computation.16 | loop fusion | flops 2260992 | bytes 2031616 | tf_op jit(solution)/shard_map/reduce_sum | solution.py:127
  6.4 22.8 %all_gather.4 = bf16[4,14,32,256]{3,2,1,0:T(8,128)(2,1)S(1)} all-gather(bf16[1,14,32,256]{3,2,1,0:T(8,128)(2,1)S(1)} %pad_maximum_fusion.3), channel_id=1, replica_groups=mesh['tm'=4,'row'=4,'col'=2] {'tm'}, dimensions={0}, use_global_device_ids=true | all-gather | bytes 1146880 | tf_op jit(solution)/shard_map/all_gather | solution.py:130
  29.1 0.2 convert_element_type.54
  29.4 0.2 fusion.30
  29.6 0.2 fusion.83
  29.9 3.4 %collective-permute-start = (bf16[8,256,12]{1,2,0:T(8,128)(2,1)S(1)}, bf16[8,256,12]{1,2,0:T(8,128)(2,1)S(1)}, u32[]{:S(2)}, u32[]{:S(2)}) collective-permute-start(bf16[8,256,12]{1,2,0:T(8,128)(2,1)S(1)} %get-tuple-element.9), channel_id=1, source_target_pairs={{0,2},{2,4},{4,6},{1,3},{3,5},{5,7},{8,10},{10,12},{12,14},{9,11},... | collective-permute-start | bytes 147464 | tf_op jit(solution)/shard_map/ppermute | solution.py:27
  33.3 1.3 %collective-permute-start.1 = (bf16[8,256,12]{1,2,0:T(8,128)(2,1)S(1)}, bf16[8,256,12]{1,2,0:T(8,128)(2,1)S(1)}, u32[]{:S(2)}, u32[]{:S(2)}) collective-permute-start(bf16[8,256,12]{1,2,0:T(8,128)(2,1)S(1)} %get-tuple-element.10), channel_id=1, source_target_pairs={{2,0},{4,2},{6,4},{3,1},{5,3},{7,5},{10,8},{12,10},{14,12},{11,9},... | collective-permute-start | bytes 147464 | tf_op jit(solution)/shard_map/ppermute | solution.py:29
  35.2 4.3 %collective-permute-done.1 = bf16[8,256,12]{1,2,0:T(8,128)(2,1)S(1)} collective-permute-done((bf16[8,256,12]{1,2,0:T(8,128)(2,1)S(1)}, bf16[8,256,12]{1,2,0:T(8,128)(2,1)S(1)}, u32[]{:S(2)}, u32[]{:S(2)}) %collective-permute-start.1) | collective-permute-done | bytes 49184 | tf_op jit(solution)/shard_map/ppermute | solution.py:29
  39.5 0.1 slice_select_fusion
  39.7 1.4 %collective-permute-done.2 = bf16[48,8,12]{1,2,0:T(8,128)(2,1)S(1)} collective-permute-done((bf16[48,8,12]{1,2,0:T(8,128)(2,1)S(1)}, bf16[48,8,12]{1,2,0:T(8,128)(2,1)S(1)}, u32[]{:S(2)}, u32[]{:S(2)}) %collective-permute-start.2) | collective-permute-done | bytes 9248 | tf_op jit(solution)/shard_map/ppermute | solution.py:19
  41.2 0.3 pad_maximum_fusion.1
  41.6 0.3 fusion.70
  41.9 0.3 fusion.69
  42.2 0.1 fusion.68
  42.3 0.3 fusion.67
  42.6 0.3 fusion.66
  43.0 0.3 fusion.64
  43.2 0.3 fusion.63
  43.5 0.9 %fusion.1 = bf16[46,270,32]{1,2,0:T(8,128)(2,1)S(1)} fusion(bf16[9,46,270,12]{2,3,0,1:T(8,128)(2,1)S(1)} %fusion.63, bf16[9,32,12,1]{1,2,0,3:T(8,128)(2,1)S(1)} %bitcast.343, pred[46,270]{1,0:T(8,128)(4,1)S(1)} %broadcast_and_fusion), kind=kOutput, calls=%fused_computation.19 | convolution fusion | flops 87039360 | bytes 3496932 | tf_op jit(solution)/shard_map/thwc,toc->hwo/dot_general | solution.py:43
  44.4 0.1 fusion.51
  44.6 0.6 fusion.50
  45.1 0.6 fusion.49
  45.7 0.2 fusion.48
  45.9 0.6 fusion.47
  46.5 0.6 fusion.46
  47.0 0.2 fusion.45
  47.3 0.6 fusion.44
  47.8 0.6 fusion.43
  48.4 1.9 %fusion.3 = bf16[44,268,32]{1,2,0:T(8,128)(2,1)S(1)} fusion(bf16[9,44,268,32]{2,3,1,0:T(8,128)(2,1)S(1)} %fusion.43, bf16[9,32,32,1]{2,1,3,0:T(8,128)(2,1)S(1)} %bitcast.344, pred[44,268]{1,0:T(8,128)(4,1)S(1)} %broadcast_and_fusion.1), kind=kOutput, calls=%fused_computation.22 | convolution fusion | flops 218482176 | bytes 7577104 | tf_op jit(solution)/shard_map/thwc,toc->hwo/dot_general | solution.py:43
  50.3 0.4 slice.241
  50.7 0.6 fusion.85
  51.3 0.2 reduce_sum.49
  51.6 0.2 fusion.81
  51.8 0.2 fusion.80
  52.0 0.2 fusion.78
  52.2 0.2 fusion.77
  52.4 0.2 fusion.75
  52.5 0.2 fusion.74
  52.7 0.8 fusion.36
  53.6 0.3 fusion.59
  53.9 0.3 fusion.58
  54.2 0.4 fusion.56
  54.6 0.3 fusion.55
  55.0 0.3 fusion.53
  55.2 0.3 fusion.52
  55.5 2.3 %copy-done.3 = bf16[9,18,130,64]{2,3,1,0:T(8,128)(2,1)} copy-done((bf16[9,18,130,64]{2,3,1,0:T(8,128)(2,1)}, bf16[9,18,130,64]{2,3,1,0:T(8,128)(2,1)S(1)}, u32[]{:S(2)}) %copy-start.3) | copy-done | bytes 2695704
  57.8 4.0 %fusion.38 = bf16[18,258,64]{1,2,0:T(8,128)(2,1)S(1)} fusion(bf16[9,18,130,64]{2,3,1,0:T(8,128)(2,1)} %copy-done.3, bf16[9,64,64,1]{2,1,3,0:T(8,128)(2,1)S(1)} %bitcast.337, pred[18,130]{1,0:T(8,128)(4,1)S(1)} %broadcast_and_fusion.3, s32[258]{0:T(512)S(1)} %add_select_fusion), kind=kOutput, calls=%fused_computation.63 | convolution fusion | flops 250579712 | bytes 3367212 | tf_op jit(solution)/shard_map/wv,hvc->hwc/dot_general | solution.py:156
  61.9 0.3 broadcast_in_dim.45
  62.2 0.2 slice.260
  62.3 0.1 fusion.9
  62.5 0.9 %fusion.12 = bf16[9,32,256,96]{2,3,1,0:T(8,128)(2,1)S(1)} fusion(bf16[9,32,256,96]{2,3,1,0:T(8,128)(2,1)S(1)} %fusion.9, bf16[34,258,64]{1,2,0:T(8,128)(2,1)S(1)} %slice.260, bf16[34,258,32]{1,2,0:T(8,128)(2,1)S(1)} %slice.241), kind=kLoop, calls=%fused_computation.31 | loop fusion | flops 3145728 | bytes 4079616
  63.4 0.9 %fusion.15 = bf16[9,32,256,96]{2,3,1,0:T(8,128)(2,1)S(1)} fusion(bf16[9,32,256,96]{2,3,1,0:T(8,128)(2,1)S(1)} %fusion.12, bf16[34,258,64]{1,2,0:T(8,128)(2,1)S(1)} %slice.260, bf16[34,258,32]{1,2,0:T(8,128)(2,1)S(1)} %slice.241), kind=kLoop, calls=%fused_computation.34 | loop fusion | flops 3145728 | bytes 4079616
  64.4 0.1 fusion.18
  64.5 0.9 %fusion.21 = bf16[9,32,256,96]{2,3,1,0:T(8,128)(2,1)S(1)} fusion(bf16[9,32,256,96]{2,3,1,0:T(8,128)(2,1)S(1)} %fusion.18, bf16[34,258,64]{1,2,0:T(8,128)(2,1)S(1)} %slice.260, bf16[34,258,32]{1,2,0:T(8,128)(2,1)S(1)} %slice.241), kind=kLoop, calls=%fused_computation.40 | loop fusion | flops 3145728 | bytes 4079616
  65.5 0.9 %fusion.24 = bf16[9,32,256,96]{2,3,1,0:T(8,128)(2,1)S(1)} fusion(bf16[9,32,256,96]{2,3,1,0:T(8,128)(2,1)S(1)} %fusion.21, bf16[34,258,64]{1,2,0:T(8,128)(2,1)S(1)} %slice.260, bf16[34,258,32]{1,2,0:T(8,128)(2,1)S(1)} %slice.241), kind=kLoop, calls=%fused_computation.43 | loop fusion | flops 3145728 | bytes 4079616
  66.4 0.1 fusion.27
  66.6 0.9 %fusion.6 = bf16[9,32,256,96]{2,3,1,0:T(8,128)(2,1)S(1)} fusion(bf16[9,32,256,96]{2,3,1,0:T(8,128)(2,1)S(1)} %fusion.27, bf16[34,258,64]{1,2,0:T(8,128)(2,1)S(1)} %slice.260, bf16[34,258,32]{1,2,0:T(8,128)(2,1)S(1)} %slice.241), kind=kLoop, calls=%fused_computation.25 | loop fusion | flops 3145728 | bytes 4079616
  67.5 0.9 %fusion.29 = bf16[9,32,256,96]{2,3,1,0:T(8,128)(2,1)S(1)} fusion(bf16[9,32,256,96]{2,3,1,0:T(8,128)(2,1)S(1)} %fusion.6, bf16[34,258,64]{1,2,0:T(8,128)(2,1)S(1)} %slice.260, bf16[34,258,32]{1,2,0:T(8,128)(2,1)S(1)} %slice.241), kind=kLoop, calls=%fused_computation.49 | loop fusion | flops 3145728 | bytes 4079616 | tf_op jit(solution)/shard_map/stack | solution.py:40
  68.5 5.0 %copy-done.1 = bf16[9,32,256,96]{2,3,1,0:T(8,128)(2,1)} copy-done((bf16[9,32,256,96]{2,3,1,0:T(8,128)(2,1)}, bf16[9,32,256,96]{2,3,1,0:T(8,128)(2,1)S(1)}, u32[]{:S(2)}) %copy-start.1) | copy-done | bytes 14155800
  73.5 7.8 %fusion.42 = bf16[11,32,256]{2,0,1:T(8,128)(2,1)S(1)} fusion(bf16[9,32,96,1]{2,1,3,0:T(8,128)(2,1)S(1)} %bitcast.341, bf16[9,32,256,96]{2,3,1,0:T(8,128)(2,1)} %copy-done.1, bf16[11,32]{1,0:T(8,128)(2,1)S(1)} %copy-done.5), kind=kOutput, calls=%fused_computation.67 | convolution fusion | flops 459366400 | bytes 14392000 | tf_op jit(solution)/shard_map/oc,hwc->ohw/dot_general | solution.py:169
  81.3 0.7 copy.71
  (46 shorter events, 1.2 us)
Async XLA Ops:
  0.0 57.8 %copy-start = (bf16[3,3,64,64]{3,2,1,0:T(8,128)(2,1)S(1)}, bf16[3,3,64,64]{3,2,1,0:T(8,128)(2,1)}, u32[]{:S(2)}) copy-start(bf16[3,3,64,64]{3,2,1,0:T(8,128)(2,1)} %param.17) | copy-start | bytes 221188
  29.9 5.3 %collective-permute-start = (bf16[8,256,12]{1,2,0:T(8,128)(2,1)S(1)}, bf16[8,256,12]{1,2,0:T(8,128)(2,1)S(1)}, u32[]{:S(2)}, u32[]{:S(2)}) collective-permute-start(bf16[8,256,12]{1,2,0:T(8,128)(2,1)S(1)} %get-tuple-element.9), channel_id=1, source_target_pairs={{0,2},{2,4},{4,6},{1,3},{3,5},{5,7},{8,10},{10,12},{12,14},{9,11},... | collective-permute-start | bytes 147464 | tf_op jit(solution)/shard_map/ppermute | solution.py:27
  33.3 6.2 %collective-permute-start.1 = (bf16[8,256,12]{1,2,0:T(8,128)(2,1)S(1)}, bf16[8,256,12]{1,2,0:T(8,128)(2,1)S(1)}, u32[]{:S(2)}, u32[]{:S(2)}) collective-permute-start(bf16[8,256,12]{1,2,0:T(8,128)(2,1)S(1)} %get-tuple-element.10), channel_id=1, source_target_pairs={{2,0},{4,2},{6,4},{3,1},{5,3},{7,5},{10,8},{12,10},{14,12},{11,9},... | collective-permute-start | bytes 147464 | tf_op jit(solution)/shard_map/ppermute | solution.py:29
  39.7 1.5 %collective-permute-start.2 = (bf16[48,8,12]{1,2,0:T(8,128)(2,1)S(1)}, bf16[48,8,12]{1,2,0:T(8,128)(2,1)S(1)}, u32[]{:S(2)}, u32[]{:S(2)}) collective-permute-start(bf16[48,8,12]{1,2,0:T(8,128)(2,1)S(1)} %slice_select_fusion), channel_id=1, source_target_pairs={{0,1},{1,0},{2,3},{3,2},{4,5},{5,4},{6,7},{7,6},{8,9},{9,8},{10,11... | collective-permute-start | bytes 27656 | tf_op jit(solution)/shard_map/ppermute | solution.py:19
  42.2 1.3 %copy-start.4 = (bf16[3,3,32,12]{2,3,1,0:T(8,128)(2,1)S(1)}, bf16[3,3,32,12]{2,3,1,0:T(8,128)(2,1)}, u32[]{:S(2)}) copy-start(bf16[3,3,32,12]{2,3,1,0:T(8,128)(2,1)} %param.14) | copy-start | bytes 20740
  47.0 1.4 %copy-start.6 = (bf16[3,3,32,32]{3,2,1,0:T(8,128)(2,1)S(1)}, bf16[3,3,32,32]{3,2,1,0:T(8,128)(2,1)}, u32[]{:S(2)}) copy-start(bf16[3,3,32,32]{3,2,1,0:T(8,128)(2,1)} %param.15) | copy-start | bytes 55300
  51.6 1.1 %copy-start.7 = (bf16[3,3,64,32]{2,3,1,0:T(8,128)(2,1)S(1)}, bf16[3,3,64,32]{2,3,1,0:T(8,128)(2,1)}, u32[]{:S(2)}) copy-start(bf16[3,3,64,32]{2,3,1,0:T(8,128)(2,1)} %param.16) | copy-start | bytes 110596
  55.5 2.3 %copy-start.3 = (bf16[9,18,130,64]{2,3,1,0:T(8,128)(2,1)}, bf16[9,18,130,64]{2,3,1,0:T(8,128)(2,1)S(1)}, u32[]{:S(2)}) copy-start(bf16[9,18,130,64]{2,3,1,0:T(8,128)(2,1)S(1)} %fusion.52) | copy-start | bytes 8087044
  66.6 7.0 %copy-start.2 = (bf16[3,3,32,96]{3,2,1,0:T(8,128)(2,1)S(1)}, bf16[3,3,32,96]{3,2,1,0:T(8,128)(2,1)}, u32[]{:S(2)}) copy-start(bf16[3,3,32,96]{3,2,1,0:T(8,128)(2,1)} %param.18) | copy-start | bytes 165892
  66.6 7.0 %copy-start.5 = (bf16[11,32]{1,0:T(8,128)(2,1)S(1)}, bf16[11,32]{1,0:T(8,128)(2,1)}, u32[]{:S(2)}) copy-start(bf16[11,32]{1,0:T(8,128)(2,1)} %param.19) | copy-start | bytes 2116
  68.5 5.1 %copy-start.1 = (bf16[9,32,256,96]{2,3,1,0:T(8,128)(2,1)}, bf16[9,32,256,96]{2,3,1,0:T(8,128)(2,1)S(1)}, u32[]{:S(2)}) copy-start(bf16[9,32,256,96]{2,3,1,0:T(8,128)(2,1)S(1)} %fusion.29) | copy-start | bytes 42467332

commit v9 on v7

--- a/solution.py
+++ b/solution.py
@@ -58,24 +58,27 @@
 def weight_kernel(score_ref, class_ref, quality_ref, weight_ref, shift_ref):
     dates, rows, _ = class_ref.shape
     classes = score_ref.shape[0]
-    step = 8
+    step = 16
 
     def chunk(index, carry):
         at = pl.ds(pl.multiple_of(index * step, step), step)
 
-        def score(date):
+        def score(date, top):
             label = class_ref[date, at, :]
             looked = jnp.zeros(label.shape, jnp.float32)
             for k in range(classes):
                 looked = jnp.where(label == k, score_ref[k], looked)
-            return looked + quality_ref[date, at, :]
+            value = looked + quality_ref[date, at, :]
+            weight_ref[date, at, :] = value
+            return jnp.maximum(top, value)
 
-        top = lax.fori_loop(1, dates, lambda date, top: jnp.maximum(top, score(date)), score(0))
+        start = jnp.full((step, weight_ref.shape[2]), -jnp.inf, jnp.float32)
+        top = lax.fori_loop(0, dates, score, start)
         shift = top.astype(jnp.bfloat16).astype(jnp.float32)
         shift_ref[at, :] = shift
 
         def one_date(date, inner):
-            weight_ref[date, at, :] = jnp.exp(score(date) - shift)
+            weight_ref[date, at, :] = jnp.exp(weight_ref[date, at, :] - shift)
             return inner
 
         lax.fori_loop(0, dates, one_date, 0)

time: 72.7 us -> 72.2 us (level)
  no operation moved by 1% of the time
where the time goes in v9:
time: 72.2 us; the launch traced here: 71.8 us
  matrix products  27.3 us (38%)
  blocking collectives  22.8 us (32%)
  waiting for transfers between devices  5.78 us (8%)
  starting transfers between devices  4.76 us (7%)
  local copies, waits for them, and re-layouts  4.37 us (6%)
  other arithmetic  3.99 us (6%)
  Pallas kernels  2.32 us (3%)
    dot_general x43, matrix products, valid_conv(): jnp.einsum('hwc,oc->hwo', padded[a:a + height, e:e + width], kernel[a, e]...  22.9 us
    all_gather x1, blocking collectives, shards(): gathered = lax.all_gather(packed, 'tm', axis=0).astype(jnp.float32)  22.8 us
    ppermute x1, waiting for transfers between devices, with_halo(): lax.ppermute(head, axis, [((i + 1) % count, i) for i in range(ends)])  4.27 us
    ppermute x1, starting transfers between devices, with_halo(): lax.ppermute(tail, axis, [(i, (i + 1) % count) for i in range(ends)])  3.4 us
    pallas_call x1, Pallas kernels, shifted_weights(): pl.pallas_call(weight_kernel, out_shape=(jax.ShapeDtypeStruct((dates, row...  2.32 us
    dot_general x1, matrix products, shards(): jnp.einsum('oc,hwc->ohw', head_weight, decoded, preferred_element_type=jn...  2.15 us
    reduce_sum x1, other arithmetic, shards(): part_sums = jnp.sum(weights[:, None] * reflectance, axis=0)  1.79 us
    dot_general x1, matrix products, shards(): jnp.einsum('wv,hvc->hwc', pair_matrix(deep_cols, block_cols + 2, up_halo...  1.68 us
  transfers between devices with their start and end apart: 3, of which 3 were waited for; matrix products, arithmetic and copies ran while one was open for 1% of the time, Pallas kernels for 0%

profile of v9, /device:TPU:0, one launch (start us, length us, event | category | flops | bytes accessed | tf_op | source)
XLA Modules:
  0.0 71.8 jit_solution(14390000643453241096)
XLA Ops:
  0.0 2.3 %shard_map.100 = (f32[8,32,256]{2,1,0:T(8,128)}, f32[32,256]{1,0:T(8,128)}) custom-call(f32[12]{0:T(128)} %score_ref.1, s32[8,32,256]{2,1,0:T(8,128)} %class_ref.1, f32[8,32,256]{2,1,0:T(8,128)} %quality_ref.1), custom_call_target="tpu_custom_call" | custom-call | tf_op jit(solution)/shard_map/pallas_call | solution.py:93
  2.3 1.8 %multiply_reduce_fusion = bf16[12,32,256]{2,1,0:T(8,128)(2,1)S(1)} fusion(bf16[8,12,32,256]{3,2,1,0:T(8,128)(2,1)} %param.10, f32[8,32,256]{2,1,0:T(8,128)} %get-tuple-element.7), kind=kLoop, calls=%fused_computation.16 | loop fusion | flops 2260992 | bytes 2031616 | tf_op jit(solution)/shard_map/reduce_sum | solution.py:135
  4.2 22.8 %all_gather.4 = bf16[4,14,32,256]{3,2,1,0:T(8,128)(2,1)S(1)} all-gather(bf16[1,14,32,256]{3,2,1,0:T(8,128)(2,1)S(1)} %pad_maximum_fusion.16), channel_id=1, replica_groups=mesh['tm'=4,'row'=4,'col'=2] {'tm'}, dimensions={0}, use_global_device_ids=true | all-gather | bytes 1146880 | tf_op jit(solution)/shard_map/all_gather | solution.py:138
  27.0 0.2 convert_element_type.54
  27.3 0.2 fusion.26
  27.5 0.2 fusion.120
  27.7 3.4 %collective-permute-start = (bf16[8,256,12]{1,2,0:T(8,128)(2,1)S(1)}, bf16[8,256,12]{1,2,0:T(8,128)(2,1)S(1)}, u32[]{:S(2)}, u32[]{:S(2)}) collective-permute-start(bf16[8,256,12]{1,2,0:T(8,128)(2,1)S(1)} %get-tuple-element.9), channel_id=1, source_target_pairs={{0,2},{2,4},{4,6},{1,3},{3,5},{5,7},{8,10},{10,12},{12,14},{9,11},... | collective-permute-start | bytes 147464 | tf_op jit(solution)/shard_map/ppermute | solution.py:27
  31.1 1.3 %collective-permute-start.1 = (bf16[8,256,12]{1,2,0:T(8,128)(2,1)S(1)}, bf16[8,256,12]{1,2,0:T(8,128)(2,1)S(1)}, u32[]{:S(2)}, u32[]{:S(2)}) collective-permute-start(bf16[8,256,12]{1,2,0:T(8,128)(2,1)S(1)} %get-tuple-element.10), channel_id=1, source_target_pairs={{2,0},{4,2},{6,4},{3,1},{5,3},{7,5},{10,8},{12,10},{14,12},{11,9},... | collective-permute-start | bytes 147464 | tf_op jit(solution)/shard_map/ppermute | solution.py:29
  33.0 4.3 %collective-permute-done.1 = bf16[8,256,12]{1,2,0:T(8,128)(2,1)S(1)} collective-permute-done((bf16[8,256,12]{1,2,0:T(8,128)(2,1)S(1)}, bf16[8,256,12]{1,2,0:T(8,128)(2,1)S(1)}, u32[]{:S(2)}, u32[]{:S(2)}) %collective-permute-start.1) | collective-permute-done | bytes 49184 | tf_op jit(solution)/shard_map/ppermute | solution.py:29
  37.6 1.4 %collective-permute-done.2 = bf16[48,8,12]{1,2,0:T(8,128)(2,1)S(1)} collective-permute-done((bf16[48,8,12]{1,2,0:T(8,128)(2,1)S(1)}, bf16[48,8,12]{1,2,0:T(8,128)(2,1)S(1)}, u32[]{:S(2)}, u32[]{:S(2)}) %collective-permute-start.2) | collective-permute-done | bytes 9248 | tf_op jit(solution)/shard_map/ppermute | solution.py:19
  39.0 0.4 pad_maximum_fusion.14
  39.4 0.5 fusion.100
  39.9 0.5 fusion.102
  40.4 0.5 fusion.104
  40.9 0.5 fusion.106
  41.4 0.5 fusion.92
  42.0 0.5 fusion.94
  42.4 0.5 fusion.96
  43.0 0.5 fusion.98
  43.5 1.3 %select_convert_fusion = bf16[46,270,32]{1,2,0:T(8,128)(2,1)S(1)} fusion(f32[46,270,32]{1,2,0:T(8,128)S(1)} %fusion.92, f32[46,270,32]{1,2,0:T(8,128)S(1)} %fusion.94, f32[46,270,32]{1,2,0:T(8,128)S(1)} %fusion.96, f32[46,270,32]{1,2,0:T(8,128)S(1)} %fusion.98, f32[46,270,32]{1,2,0:T(8,128)S(1)} %fusion.100, f32[46,270,32]{1,2,0:T(8,128)S(1)} %fusion.102, ...), kind=kOutput, calls=%fused_computation.17 | convolution fusion | flops 13910400 | bytes 19470592 | tf_op jit(solution)/shard_map/hwc,oc->hwo/dot_general | solution.py:43
  44.8 0.5 fusion.62
  45.4 0.4 fusion.64
  45.8 0.5 fusion.66
  46.3 0.5 fusion.68
  46.9 0.4 fusion.70
  47.3 0.5 fusion.72
  47.8 0.5 fusion.74
  48.4 0.4 fusion.76
  48.8 1.6 %select_convert_fusion.1 = bf16[44,268,32]{1,2,0:T(8,128)(2,1)S(1)} fusion(f32[44,268,32]{1,2,0:T(8,128)S(1)} %fusion.62, f32[44,268,32]{1,2,0:T(8,128)S(1)} %fusion.64, f32[44,268,32]{1,2,0:T(8,128)S(1)} %fusion.66, f32[44,268,32]{1,2,0:T(8,128)S(1)} %fusion.68, f32[44,268,32]{1,2,0:T(8,128)S(1)} %fusion.70, f32[44,268,32]{1,2,0:T(8,128)S(1)} %fusion.72, ...), kind=kOutput, calls=%fused_computation.18 | convolution fusion | flops 28300800 | bytes 19164160 | tf_op jit(solution)/shard_map/hwc,oc->hwo/dot_general | solution.py:43
  50.3 0.4 slice.421
  50.8 0.6 fusion.122
  51.4 0.4 reduce_sum.49
  51.8 0.4 copy-done.4
  52.2 0.4 fusion.118
  52.6 0.4 convolution_add_fusion.7
  53.0 0.4 convolution_add_fusion.6
  53.5 0.4 convolution_add_fusion.5
  53.8 0.4 convolution_add_fusion.4
  54.3 0.4 convolution_add_fusion.3
  54.7 0.4 convolution_add_fusion.2
  55.1 0.4 convolution_add_fusion.1
  55.5 0.4 fusion.54
  56.0 0.4 copy-done.2
  56.4 0.3 fusion.87
  56.7 0.4 convolution_add_fusion.15
  57.1 0.4 convolution_add_fusion.14
  57.5 0.3 convolution_add_fusion.13
  57.8 0.4 convolution_add_fusion.12
  58.2 0.4 convolution_add_fusion.11
  58.6 0.3 convolution_add_fusion.10
  58.9 0.4 convolution_add_fusion.9
  59.2 1.7 %fusion.56 = bf16[18,258,64]{1,2,0:T(8,128)(2,1)} fusion(f32[18,130,64]{1,2,0:T(8,128)S(1)} %convolution_add_fusion.9, bf16[20,132,64]{1,2,0:T(8,128)(2,1)S(1)} %fusion.54, pred[18,130]{1,0:T(8,128)(4,1)S(1)} %broadcast_and_fusion.3, s32[258]{0:T(512)S(1)} %add_select_fusion, bf16[3,3,64,64]{3,2,1,0:T(8,128)(2,1)S(1)} %copy-done.2), kind=kOutput, calls=%fused_computation.72 | convolution fusion | flops 97375232 | bytes 2388480 | tf_op jit(solution)/shard_map/wv,hvc->hwc/dot_general | solution.py:164
  60.9 1.4 %broadcast_in_dim.45 = bf16[18,2,258,64]{2,3,1,0:T(8,128)(2,1)S(1)} broadcast(bf16[18,258,64]{1,2,0:T(8,128)(2,1)} %fusion.56), dimensions={0,2,3} | broadcast | bytes 1783296 | tf_op jit(solution)/shard_map/broadcast_in_dim | solution.py:170
  62.6 0.7 copy-done.5
  63.3 0.3 fusion.4
  63.6 0.7 fusion.1
  64.3 0.7 %fusion.51 = f32[32,256,32]{1,2,0:T(8,128)S(1)} fusion(f32[32,256,32]{1,2,0:T(8,128)S(1)} %fusion.4, bf16[34,258,64]{1,2,0:T(8,128)(2,1)S(1)} %slice.440, bf16[34,258,32]{1,2,0:T(8,128)(2,1)S(1)} %slice.421, bf16[3,3,32,96]{3,2,1,0:T(8,128)(2,1)S(1)} %copy-done.5), kind=kOutput, calls=%fused_computation.69 | convolution fusion | flops 53739520 | bytes 4612096 | tf_op jit(solution)/shard_map/hwc,oc->hwo/dot_general | solution.py:43
  65.0 0.7 %fusion.48 = f32[32,256,32]{1,2,0:T(8,128)S(1)} fusion(f32[32,256,32]{1,2,0:T(8,128)S(1)} %fusion.51, bf16[34,258,64]{1,2,0:T(8,128)(2,1)S(1)} %slice.440, bf16[34,258,32]{1,2,0:T(8,128)(2,1)S(1)} %slice.421, bf16[3,3,32,96]{3,2,1,0:T(8,128)(2,1)S(1)} %copy-done.5), kind=kOutput, calls=%fused_computation.68 | convolution fusion | flops 53739520 | bytes 4612096 | tf_op jit(solution)/shard_map/hwc,oc->hwo/dot_general | solution.py:43
  65.8 0.4 fusion.45
  66.1 0.7 fusion.42
  66.8 0.7 %fusion.39 = f32[32,256,32]{1,2,0:T(8,128)S(1)} fusion(f32[32,256,32]{1,2,0:T(8,128)S(1)} %fusion.42, bf16[34,258,64]{1,2,0:T(8,128)(2,1)S(1)} %slice.440, bf16[34,258,32]{1,2,0:T(8,128)(2,1)S(1)} %slice.421, bf16[3,3,32,96]{3,2,1,0:T(8,128)(2,1)S(1)} %copy-done.5), kind=kOutput, calls=%fused_computation.65 | convolution fusion | flops 53739520 | bytes 4612096 | tf_op jit(solution)/shard_map/hwc,oc->hwo/dot_general | solution.py:43
  67.6 1.4 %fusion.36 = f32[32,256,32]{1,2,0:T(8,128)} fusion(f32[32,256,32]{1,2,0:T(8,128)S(1)} %fusion.1, f32[32,256,32]{1,2,0:T(8,128)S(1)} %fusion.39, bf16[34,258,64]{1,2,0:T(8,128)(2,1)S(1)} %slice.440, bf16[34,258,32]{1,2,0:T(8,128)(2,1)S(1)} %slice.421, bf16[3,3,32,96]{3,2,1,0:T(8,128)(2,1)S(1)} %copy-done.5), kind=kOutput, calls=%fused_computation.64 | convolution fusion | flops 54001664 | bytes 5660672 | tf_op jit(solution)/shard_map/hwc,oc->hwo/dot_general | solution.py:43
  68.9 2.2 %fusion.60 = bf16[11,32,256]{2,0,1:T(8,128)(2,1)S(1)} fusion(f32[32,256,32]{1,2,0:T(8,128)} %fusion.36, bf16[34,258,64]{1,2,0:T(8,128)(2,1)S(1)} %slice.440, bf16[34,258,32]{1,2,0:T(8,128)(2,1)S(1)} %slice.421, bf16[3,3,32,96]{3,2,1,0:T(8,128)(2,1)S(1)} %copy-done.5, bf16[11,32]{1,0:T(8,128)(2,1)S(1)} %copy-done), kind=kOutput, calls=%fused_computation.76 | convolution fusion | flops 60121088 | bytes 3747840 | tf_op jit(solution)/shard_map/oc,hwc->ohw/dot_general | solution.py:177
  71.1 0.7 %copy.21 = bf16[11,32,256]{2,1,0:T(8,128)(2,1)} copy(bf16[11,32,256]{2,0,1:T(8,128)(2,1)S(1)} %fusion.60) | data formatting | bytes 360448 | tf_op jit(solution)/shard_map/convert_element_type | solution.py:179
  (41 shorter events, 1.2 us)
Async XLA Ops:
  0.0 68.9 %copy-start = (bf16[11,32]{1,0:T(8,128)(2,1)S(1)}, bf16[11,32]{1,0:T(8,128)(2,1)}, u32[]{:S(2)}) copy-start(bf16[11,32]{1,0:T(8,128)(2,1)} %param.19) | copy-start | bytes 2116
  2.3 1.8 %copy-start.1 = (f32[8,32,256]{2,1,0:T(8,128)S(1)}, f32[8,32,256]{2,1,0:T(8,128)}, u32[]{:S(2)}) copy-start(f32[8,32,256]{2,1,0:T(8,128)} %get-tuple-element.7) | copy-start | bytes 786436
  2.3 1.8 %copy-start.7 = (f32[32,256]{1,0:T(8,128)S(1)}, f32[32,256]{1,0:T(8,128)}, u32[]{:S(2)}) copy-start(f32[32,256]{1,0:T(8,128)} %get-tuple-element.8) | copy-start | bytes 98308
  27.7 5.3 %collective-permute-start = (bf16[8,256,12]{1,2,0:T(8,128)(2,1)S(1)}, bf16[8,256,12]{1,2,0:T(8,128)(2,1)S(1)}, u32[]{:S(2)}, u32[]{:S(2)}) collective-permute-start(bf16[8,256,12]{1,2,0:T(8,128)(2,1)S(1)} %get-tuple-element.9), channel_id=1, source_target_pairs={{0,2},{2,4},{4,6},{1,3},{3,5},{5,7},{8,10},{10,12},{12,14},{9,11},... | collective-permute-start | bytes 147464 | tf_op jit(solution)/shard_map/ppermute | solution.py:27
  31.1 6.2 %collective-permute-start.1 = (bf16[8,256,12]{1,2,0:T(8,128)(2,1)S(1)}, bf16[8,256,12]{1,2,0:T(8,128)(2,1)S(1)}, u32[]{:S(2)}, u32[]{:S(2)}) collective-permute-start(bf16[8,256,12]{1,2,0:T(8,128)(2,1)S(1)} %get-tuple-element.10), channel_id=1, source_target_pairs={{2,0},{4,2},{6,4},{3,1},{5,3},{7,5},{10,8},{12,10},{14,12},{11,9},... | collective-permute-start | bytes 147464 | tf_op jit(solution)/shard_map/ppermute | solution.py:29
  32.9 6.5 %copy-start.6 = (bf16[3,3,32,12]{2,3,1,0:T(8,128)(2,1)S(1)}, bf16[3,3,32,12]{2,3,1,0:T(8,128)(2,1)}, u32[]{:S(2)}) copy-start(bf16[3,3,32,12]{2,3,1,0:T(8,128)(2,1)} %param.14) | copy-start | bytes 20740
  37.5 1.5 %collective-permute-start.2 = (bf16[48,8,12]{1,2,0:T(8,128)(2,1)S(1)}, bf16[48,8,12]{1,2,0:T(8,128)(2,1)S(1)}, u32[]{:S(2)}, u32[]{:S(2)}) collective-permute-start(bf16[48,8,12]{1,2,0:T(8,128)(2,1)S(1)} %slice_select_fusion), channel_id=1, source_target_pairs={{0,1},{1,0},{2,3},{3,2},{4,5},{5,4},{6,7},{7,6},{8,9},{9,8},{10,11... | collective-permute-start | bytes 27656 | tf_op jit(solution)/shard_map/ppermute | solution.py:19
  43.5 1.4 %copy-start.3 = (bf16[3,3,32,32]{3,2,1,0:T(8,128)(2,1)S(1)}, bf16[3,3,32,32]{3,2,1,0:T(8,128)(2,1)}, u32[]{:S(2)}) copy-start(bf16[3,3,32,32]{3,2,1,0:T(8,128)(2,1)} %param.15) | copy-start | bytes 55300
  51.3 0.9 %copy-start.4 = (bf16[3,3,64,32]{2,3,1,0:T(8,128)(2,1)S(1)}, bf16[3,3,64,32]{2,3,1,0:T(8,128)(2,1)}, u32[]{:S(2)}) copy-start(bf16[3,3,64,32]{2,3,1,0:T(8,128)(2,1)} %param.16) | copy-start | bytes 110596
  55.5 0.9 %copy-start.2 = (bf16[3,3,64,64]{3,2,1,0:T(8,128)(2,1)S(1)}, bf16[3,3,64,64]{3,2,1,0:T(8,128)(2,1)}, u32[]{:S(2)}) copy-start(bf16[3,3,64,64]{3,2,1,0:T(8,128)(2,1)} %param.17) | copy-start | bytes 221188
  62.4 0.9 %copy-start.5 = (bf16[3,3,32,96]{3,2,1,0:T(8,128)(2,1)S(1)}, bf16[3,3,32,96]{3,2,1,0:T(8,128)(2,1)}, u32[]{:S(2)}) copy-start(bf16[3,3,32,96]{3,2,1,0:T(8,128)(2,1)} %param.18) | copy-start | bytes 165892

commit v10 on v9

--- a/solution.py
+++ b/solution.py
@@ -50,6 +50,17 @@
     return total
 
 
+def native_conv(padded, kernel):
+    return lax.conv_general_dilated(
+        padded[None],
+        kernel,
+        (1, 1),
+        "VALID",
+        dimension_numbers=("NHWC", "HWOI", "NHWC"),
+        preferred_element_type=jnp.float32,
+    )[0]
+
+
 def pair_matrix(narrow, wide, offset):
     pick = (jnp.arange(wide, dtype=jnp.int32) + offset) // 2
     return (jnp.arange(narrow, dtype=jnp.int32)[:, None] == pick[None, :]).astype(jnp.bfloat16)
@@ -109,8 +120,8 @@
     return (row_in[:, None] & col_in[None, :])[:, :, None]
 
 
-def masked_layer(field, kernel, row_start, col_start, total_rows, total_cols):
-    out = valid_conv(field, kernel)
+def masked_layer(field, kernel, row_start, col_start, total_rows, total_cols, conv=valid_conv):
+    out = conv(field, kernel)
     mask = inside_mask(row_start, col_start, out.shape[0], out.shape[1], total_rows, total_cols)
     return jnp.where(mask, jnp.maximum(out, 0.0), 0.0).astype(jnp.bfloat16)
 
@@ -157,8 +168,9 @@
     coarse_halo = (HALO - 2) // 2
     crow0 = row0 // 2 - coarse_halo
     ccol0 = col0 // 2 - coarse_halo
-    mid = masked_layer(pooled, middle_first, crow0 + 1, ccol0 + 1, total_rows // 2, total_cols // 2)
-    deeper = masked_layer(mid, middle_second, crow0 + 2, ccol0 + 2, total_rows // 2, total_cols // 2)
+    coarse = (total_rows // 2, total_cols // 2, native_conv)
+    mid = masked_layer(pooled, middle_first, crow0 + 1, ccol0 + 1, *coarse)
+    deeper = masked_layer(mid, middle_second, crow0 + 2, ccol0 + 2, *coarse)
     up_halo = 2 * (coarse_halo - 2)
     deep_rows, deep_cols, deep_ch = deeper.shape
     spread = jnp.einsum(

time: 72.2 us -> 69.5 us (0.963)
  matrix products: 27.3 us -> 22.6 us
  local copies, waits for them, and re-layouts: 4.37 us -> 5.46 us
  other arithmetic: 3.99 us -> 4.83 us
    dot_general x43 -> x26, matrix products: 22.9 us -> 16.6 us  [valid_conv(): jnp.einsum('hwc,oc->hwo', padded[a:a + height, e:e + width], kernel[a, e]...]
    conv_general_dilated x0 -> x2, matrix products: none -> 2.89 us  [native_conv(): lax.conv_general_dilated(padded[None], kernel, (1, 1), 'VALID', dimension...]
    dot_general x1, matrix products: 1.68 us -> 0.48 us  [shards(): jnp.einsum('wv,hvc->hwc', pair_matrix(deep_cols, block_cols + 2, up_halo...]
    broadcast_in_dim x1, local copies, waits for them, and re-layouts: 1.44 us -> 0.27 us  [shards(): jnp.broadcast_to(spread[:, None], (deep_rows, 2, block_cols + 2, deep_ch))]
    unnamed x16 -> x22, local copies, waits for them, and re-layouts: 1.58 us -> 2.63 us
    convert_element_type x0 -> x1, other arithmetic: none -> 0.87 us  [masked_layer(): return jnp.where(mask, jnp.maximum(out, 0.0), 0.0).astype(jnp.bfloat16)]
where the time goes in v10:
time: 69.5 us; the launch traced here: 69.1 us
  blocking collectives  22.8 us (33%)
  matrix products  22.6 us (33%)
  waiting for transfers between devices  5.76 us (8%)
  local copies, waits for them, and re-layouts  5.46 us (8%)
  other arithmetic  4.83 us (7%)
  starting transfers between devices  4.76 us (7%)
  Pallas kernels  2.34 us (3%)
    all_gather x1, blocking collectives, shards(): gathered = lax.all_gather(packed, 'tm', axis=0).astype(jnp.float32)  22.8 us
    dot_general x26, matrix products, valid_conv(): jnp.einsum('hwc,oc->hwo', padded[a:a + height, e:e + width], kernel[a, e]...  16.6 us
    ppermute x1, waiting for transfers between devices, with_halo(): lax.ppermute(head, axis, [((i + 1) % count, i) for i in range(ends)])  4.27 us
    ppermute x1, starting transfers between devices, with_halo(): lax.ppermute(tail, axis, [(i, (i + 1) % count) for i in range(ends)])  3.4 us
    conv_general_dilated x2, matrix products, native_conv(): lax.conv_general_dilated(padded[None], kernel, (1, 1), 'VALID', dimension...  2.89 us
    unnamed x22, local copies, waits for them, and re-layouts  2.63 us
    pallas_call x1, Pallas kernels, shifted_weights(): pl.pallas_call(weight_kernel, out_shape=(jax.ShapeDtypeStruct((dates, row...  2.34 us
    dot_general x1, matrix products, shards(): jnp.einsum('oc,hwc->ohw', head_weight, decoded, preferred_element_type=jn...  2.15 us
  transfers between devices with their start and end apart: 3, of which 3 were waited for; matrix products, arithmetic and copies ran while one was open for 1% of the time, Pallas kernels for 0%

profile of v10, /device:TPU:0, one launch (start us, length us, event | category | flops | bytes accessed | tf_op | source)
XLA Modules:
  0.0 69.1 jit_solution(7870561368942918548)
XLA Ops:
  0.0 2.3 %shard_map.100 = (f32[8,32,256]{2,1,0:T(8,128)}, f32[32,256]{1,0:T(8,128)}) custom-call(f32[12]{0:T(128)} %score_ref.1, s32[8,32,256]{2,1,0:T(8,128)} %class_ref.1, f32[8,32,256]{2,1,0:T(8,128)} %quality_ref.1), custom_call_target="tpu_custom_call" | custom-call | tf_op jit(solution)/shard_map/pallas_call | solution.py:104
  2.3 1.8 %multiply_reduce_fusion = bf16[12,32,256]{2,1,0:T(8,128)(2,1)S(1)} fusion(bf16[8,12,32,256]{3,2,1,0:T(8,128)(2,1)} %param.10, f32[8,32,256]{2,1,0:T(8,128)} %get-tuple-element.7), kind=kLoop, calls=%fused_computation.16 | loop fusion | flops 2260992 | bytes 2031616 | tf_op jit(solution)/shard_map/reduce_sum | solution.py:146
  4.2 22.8 %all_gather.4 = bf16[4,14,32,256]{3,2,1,0:T(8,128)(2,1)S(1)} all-gather(bf16[1,14,32,256]{3,2,1,0:T(8,128)(2,1)S(1)} %pad_maximum_fusion.16), channel_id=1, replica_groups=mesh['tm'=4,'row'=4,'col'=2] {'tm'}, dimensions={0}, use_global_device_ids=true | all-gather | bytes 1146880 | tf_op jit(solution)/shard_map/all_gather | solution.py:149
  27.0 0.2 convert_element_type.65
  27.3 0.2 fusion.28
  27.5 0.2 fusion.115
  27.8 3.4 %collective-permute-start = (bf16[8,256,12]{1,2,0:T(8,128)(2,1)S(1)}, bf16[8,256,12]{1,2,0:T(8,128)(2,1)S(1)}, u32[]{:S(2)}, u32[]{:S(2)}) collective-permute-start(bf16[8,256,12]{1,2,0:T(8,128)(2,1)S(1)} %get-tuple-element.9), channel_id=1, source_target_pairs={{0,2},{2,4},{4,6},{1,3},{3,5},{5,7},{8,10},{10,12},{12,14},{9,11},... | collective-permute-start | bytes 147464 | tf_op jit(solution)/shard_map/ppermute | solution.py:27
  31.2 1.3 %collective-permute-start.1 = (bf16[8,256,12]{1,2,0:T(8,128)(2,1)S(1)}, bf16[8,256,12]{1,2,0:T(8,128)(2,1)S(1)}, u32[]{:S(2)}, u32[]{:S(2)}) collective-permute-start(bf16[8,256,12]{1,2,0:T(8,128)(2,1)S(1)} %get-tuple-element.10), channel_id=1, source_target_pairs={{2,0},{4,2},{6,4},{3,1},{5,3},{7,5},{10,8},{12,10},{14,12},{11,9},... | collective-permute-start | bytes 147464 | tf_op jit(solution)/shard_map/ppermute | solution.py:29
  32.6 0.1 broadcast_and_fusion
  32.7 0.1 broadcast_and_fusion.1
  32.8 0.1 broadcast_and_fusion.2
  33.1 4.3 %collective-permute-done.1 = bf16[8,256,12]{1,2,0:T(8,128)(2,1)S(1)} collective-permute-done((bf16[8,256,12]{1,2,0:T(8,128)(2,1)S(1)}, bf16[8,256,12]{1,2,0:T(8,128)(2,1)S(1)}, u32[]{:S(2)}, u32[]{:S(2)}) %collective-permute-start.1) | collective-permute-done | bytes 49184 | tf_op jit(solution)/shard_map/ppermute | solution.py:29
  37.4 0.1 slice_select_fusion.1
  37.6 1.4 %collective-permute-done.2 = bf16[48,8,12]{1,2,0:T(8,128)(2,1)S(1)} collective-permute-done((bf16[48,8,12]{1,2,0:T(8,128)(2,1)S(1)}, bf16[48,8,12]{1,2,0:T(8,128)(2,1)S(1)}, u32[]{:S(2)}, u32[]{:S(2)}) %collective-permute-start.2) | collective-permute-done | bytes 9248 | tf_op jit(solution)/shard_map/ppermute | solution.py:19
  39.1 0.3 pad_maximum_fusion.14
  39.4 0.5 fusion.100
  39.9 0.5 fusion.102
  40.4 0.5 fusion.104
  40.9 0.5 fusion.106
  41.5 0.5 fusion.108
  41.9 0.5 fusion.94
  42.5 0.5 fusion.96
  43.0 0.5 fusion.98
  43.5 1.3 %select_convert_fusion = bf16[46,270,32]{1,2,0:T(8,128)(2,1)S(1)} fusion(f32[46,270,32]{1,2,0:T(8,128)S(1)} %fusion.94, f32[46,270,32]{1,2,0:T(8,128)S(1)} %fusion.96, f32[46,270,32]{1,2,0:T(8,128)S(1)} %fusion.98, f32[46,270,32]{1,2,0:T(8,128)S(1)} %fusion.100, f32[46,270,32]{1,2,0:T(8,128)S(1)} %fusion.102, f32[46,270,32]{1,2,0:T(8,128)S(1)} %fusion.104, ...), kind=kOutput, calls=%fused_computation.17 | convolution fusion | flops 13910400 | bytes 19470592 | tf_op jit(solution)/shard_map/hwc,oc->hwo/dot_general | solution.py:43
  44.8 0.5 fusion.62
  45.4 0.4 fusion.64
  45.8 0.5 fusion.66
  46.3 0.5 fusion.68
  46.9 0.4 fusion.70
  47.3 0.5 fusion.72
  47.8 0.5 fusion.74
  48.4 0.4 fusion.76
  48.8 1.6 %select_convert_fusion.1 = bf16[44,268,32]{1,2,0:T(8,128)(2,1)S(1)} fusion(f32[44,268,32]{1,2,0:T(8,128)S(1)} %fusion.62, f32[44,268,32]{1,2,0:T(8,128)S(1)} %fusion.64, f32[44,268,32]{1,2,0:T(8,128)S(1)} %fusion.66, f32[44,268,32]{1,2,0:T(8,128)S(1)} %fusion.68, f32[44,268,32]{1,2,0:T(8,128)S(1)} %fusion.70, f32[44,268,32]{1,2,0:T(8,128)S(1)} %fusion.72, ...), kind=kOutput, calls=%fused_computation.18 | convolution fusion | flops 28300800 | bytes 19164160 | tf_op jit(solution)/shard_map/hwc,oc->hwo/dot_general | solution.py:43
  50.4 0.4 slice.281
  50.8 0.6 fusion.117
  51.4 0.4 reduce_sum.49
  51.8 0.6 copy.60
  52.5 0.2 pad.clone
  52.7 0.1 copy.51
  52.8 0.5 copy-done.7
  53.3 1.3 %fusion.30 = bf16[20,8,17,64]{3,1,2,0:T(8,128)(2,1)S(1)} fusion(bf16[3,3,64,32]{2,3,1,0:T(8,128)(2,1)S(1)} %copy-done.7, bf16[22,1,7,2,32]{4,2,3,0,1:T(8,128)(2,1)S(1)} %slice.282, bf16[22,1,8,17,32]{4,2,3,0,1:T(8,128)(2,1)S(1)} %copy.51, pred[8,17]{0,1:T(8,128)(4,1)S(1)} %copy-done.9), kind=kOutput, calls=%fused_computation.47 | convolution fusion | flops 101434368 | bytes 596360 | tf_op jit(solution)/shard_map/conv_general_dilated | solution.py:54
  54.6 0.1 copy.52
  54.8 0.9 %fusion.1 = bf16[20,1,132,64]{3,0,2,1:T(8,128)(2,1)S(1)} fusion(bf16[20,1,136,64]{3,0,2,1:T(8,128)(2,1)S(1)} %bitcast.209, pred[20,132]{0,1:T(8,128)(4,1)S(1)} %broadcast_and_fusion.2), kind=kLoop, calls=%fused_computation.22 | loop fusion | flops 168960 | bytes 678480 | tf_op jit(solution)/shard_map/convert_element_type | solution.py:126
  55.6 0.2 pad.2
  55.8 0.1 copy.54
  56.0 0.3 copy-done.8
  56.3 1.6 %fusion.31 = bf16[18,8,17,64]{3,1,2,0:T(8,128)(2,1)S(1)} fusion(bf16[3,3,64,64]{3,2,1,0:T(8,128)(2,1)S(1)} %copy-done, bf16[20,1,7,2,64]{4,2,3,0,1:T(8,128)(2,1)S(1)} %slice.284, bf16[20,1,8,17,64]{4,2,3,0,1:T(8,128)(2,1)S(1)} %copy.54, pred[8,17]{0,1:T(8,128)(4,1)S(1)} %copy-done.8), kind=kOutput, calls=%fused_computation.50 | convolution fusion | flops 182123520 | bytes 771208 | tf_op jit(solution)/shard_map/conv_general_dilated | solution.py:54
  57.9 0.2 copy.55
  58.1 0.3 reshape.283
  58.4 0.4 copy.59
  58.8 0.5 fusion.55
  59.3 0.3 broadcast_in_dim.45
  59.6 0.2 slice.286
  59.8 0.7 %copy-done.3 = bf16[3,3,32,96]{3,2,1,0:T(8,128)(2,1)S(1)} copy-done((bf16[3,3,32,96]{3,2,1,0:T(8,128)(2,1)S(1)}, bf16[3,3,32,96]{3,2,1,0:T(8,128)(2,1)}, u32[]{:S(2)}) %copy-start.3) | copy-done | bytes 55320
  60.5 0.3 fusion.6
  60.8 0.7 %fusion.3 = f32[32,256,32]{1,2,0:T(8,128)S(1)} fusion(bf16[34,258,64]{1,2,0:T(8,128)(2,1)S(1)} %slice.286, bf16[34,258,32]{1,2,0:T(8,128)(2,1)S(1)} %slice.281, bf16[3,3,32,96]{3,2,1,0:T(8,128)(2,1)S(1)} %copy-done.3), kind=kOutput, calls=%fused_computation.24 | convolution fusion | flops 53477376 | bytes 3563520 | tf_op jit(solution)/shard_map/hwc,oc->hwo/dot_general | solution.py:43
  61.5 0.7 %fusion.52 = f32[32,256,32]{1,2,0:T(8,128)S(1)} fusion(f32[32,256,32]{1,2,0:T(8,128)S(1)} %fusion.6, bf16[34,258,64]{1,2,0:T(8,128)(2,1)S(1)} %slice.286, bf16[34,258,32]{1,2,0:T(8,128)(2,1)S(1)} %slice.281, bf16[3,3,32,96]{3,2,1,0:T(8,128)(2,1)S(1)} %copy-done.3), kind=kOutput, calls=%fused_computation.59 | convolution fusion | flops 53739520 | bytes 4612096 | tf_op jit(solution)/shard_map/hwc,oc->hwo/dot_general | solution.py:43
  62.3 0.7 %fusion.49 = f32[32,256,32]{1,2,0:T(8,128)S(1)} fusion(f32[32,256,32]{1,2,0:T(8,128)S(1)} %fusion.52, bf16[34,258,64]{1,2,0:T(8,128)(2,1)S(1)} %slice.286, bf16[34,258,32]{1,2,0:T(8,128)(2,1)S(1)} %slice.281, bf16[3,3,32,96]{3,2,1,0:T(8,128)(2,1)S(1)} %copy-done.3), kind=kOutput, calls=%fused_computation.58 | convolution fusion | flops 53739520 | bytes 4612096 | tf_op jit(solution)/shard_map/hwc,oc->hwo/dot_general | solution.py:43
  63.0 0.4 fusion.46
  63.4 0.7 %fusion.43 = f32[32,256,32]{1,2,0:T(8,128)S(1)} fusion(f32[32,256,32]{1,2,0:T(8,128)S(1)} %fusion.46, bf16[34,258,64]{1,2,0:T(8,128)(2,1)S(1)} %slice.286, bf16[34,258,32]{1,2,0:T(8,128)(2,1)S(1)} %slice.281, bf16[3,3,32,96]{3,2,1,0:T(8,128)(2,1)S(1)} %copy-done.3), kind=kOutput, calls=%fused_computation.56 | convolution fusion | flops 53739520 | bytes 4612096 | tf_op jit(solution)/shard_map/hwc,oc->hwo/dot_general | solution.py:43
  64.1 0.7 %fusion.40 = f32[32,256,32]{1,2,0:T(8,128)S(1)} fusion(f32[32,256,32]{1,2,0:T(8,128)S(1)} %fusion.43, bf16[34,258,64]{1,2,0:T(8,128)(2,1)S(1)} %slice.286, bf16[34,258,32]{1,2,0:T(8,128)(2,1)S(1)} %slice.281, bf16[3,3,32,96]{3,2,1,0:T(8,128)(2,1)S(1)} %copy-done.3), kind=kOutput, calls=%fused_computation.55 | convolution fusion | flops 53739520 | bytes 4612096 | tf_op jit(solution)/shard_map/hwc,oc->hwo/dot_general | solution.py:43
  64.9 1.4 %fusion.37 = f32[32,256,32]{1,2,0:T(8,128)} fusion(f32[32,256,32]{1,2,0:T(8,128)S(1)} %fusion.3, f32[32,256,32]{1,2,0:T(8,128)S(1)} %fusion.40, bf16[34,258,64]{1,2,0:T(8,128)(2,1)S(1)} %slice.286, bf16[34,258,32]{1,2,0:T(8,128)(2,1)S(1)} %slice.281, bf16[3,3,32,96]{3,2,1,0:T(8,128)(2,1)S(1)} %copy-done.3), kind=kOutput, calls=%fused_computation.54 | convolution fusion | flops 54001664 | bytes 5660672 | tf_op jit(solution)/shard_map/hwc,oc->hwo/dot_general | solution.py:43
  66.2 2.2 %fusion.60 = bf16[11,32,256]{2,0,1:T(8,128)(2,1)S(1)} fusion(f32[32,256,32]{1,2,0:T(8,128)} %fusion.37, bf16[34,258,64]{1,2,0:T(8,128)(2,1)S(1)} %slice.286, bf16[34,258,32]{1,2,0:T(8,128)(2,1)S(1)} %slice.281, bf16[3,3,32,96]{3,2,1,0:T(8,128)(2,1)S(1)} %copy-done.3, bf16[11,32]{1,0:T(8,128)(2,1)S(1)} %copy-done.6), kind=kOutput, calls=%fused_computation.66 | convolution fusion | flops 60121088 | bytes 3747840 | tf_op jit(solution)/shard_map/oc,hwc->ohw/dot_general | solution.py:189
  68.4 0.7 %copy.57 = bf16[11,32,256]{2,1,0:T(8,128)(2,1)} copy(bf16[11,32,256]{2,0,1:T(8,128)(2,1)S(1)} %fusion.60) | data formatting | bytes 360448 | tf_op jit(solution)/shard_map/convert_element_type | solution.py:191
  (42 shorter events, 0.7 us)
Async XLA Ops:
  0.0 56.0 %copy-start = (bf16[3,3,64,64]{3,2,1,0:T(8,128)(2,1)S(1)}, bf16[3,3,64,64]{3,2,1,0:T(8,128)(2,1)}, u32[]{:S(2)}) copy-start(bf16[3,3,64,64]{3,2,1,0:T(8,128)(2,1)} %param.17) | copy-start | bytes 221188
  2.3 1.8 %copy-start.1 = (f32[8,32,256]{2,1,0:T(8,128)S(1)}, f32[8,32,256]{2,1,0:T(8,128)}, u32[]{:S(2)}) copy-start(f32[8,32,256]{2,1,0:T(8,128)} %get-tuple-element.7) | copy-start | bytes 786436
  2.3 1.8 %copy-start.5 = (f32[32,256]{1,0:T(8,128)S(1)}, f32[32,256]{1,0:T(8,128)}, u32[]{:S(2)}) copy-start(f32[32,256]{1,0:T(8,128)} %get-tuple-element.8) | copy-start | bytes 98308
  27.8 5.3 %collective-permute-start = (bf16[8,256,12]{1,2,0:T(8,128)(2,1)S(1)}, bf16[8,256,12]{1,2,0:T(8,128)(2,1)S(1)}, u32[]{:S(2)}, u32[]{:S(2)}) collective-permute-start(bf16[8,256,12]{1,2,0:T(8,128)(2,1)S(1)} %get-tuple-element.9), channel_id=1, source_target_pairs={{0,2},{2,4},{4,6},{1,3},{3,5},{5,7},{8,10},{10,12},{12,14},{9,11},... | collective-permute-start | bytes 147464 | tf_op jit(solution)/shard_map/ppermute | solution.py:27
  31.2 6.2 %collective-permute-start.1 = (bf16[8,256,12]{1,2,0:T(8,128)(2,1)S(1)}, bf16[8,256,12]{1,2,0:T(8,128)(2,1)S(1)}, u32[]{:S(2)}, u32[]{:S(2)}) collective-permute-start(bf16[8,256,12]{1,2,0:T(8,128)(2,1)S(1)} %get-tuple-element.10), channel_id=1, source_target_pairs={{2,0},{4,2},{6,4},{3,1},{5,3},{7,5},{10,8},{12,10},{14,12},{11,9},... | collective-permute-start | bytes 147464 | tf_op jit(solution)/shard_map/ppermute | solution.py:29
  32.6 6.8 %copy-start.4 = (bf16[3,3,32,12]{2,3,1,0:T(8,128)(2,1)S(1)}, bf16[3,3,32,12]{2,3,1,0:T(8,128)(2,1)}, u32[]{:S(2)}) copy-start(bf16[3,3,32,12]{2,3,1,0:T(8,128)(2,1)} %param.14) | copy-start | bytes 20740
  37.5 1.5 %collective-permute-start.2 = (bf16[48,8,12]{1,2,0:T(8,128)(2,1)S(1)}, bf16[48,8,12]{1,2,0:T(8,128)(2,1)S(1)}, u32[]{:S(2)}, u32[]{:S(2)}) collective-permute-start(bf16[48,8,12]{1,2,0:T(8,128)(2,1)S(1)} %slice_select_fusion.1), channel_id=1, source_target_pairs={{0,1},{1,0},{2,3},{3,2},{4,5},{5,4},{6,7},{7,6},{8,9},{9,8},{10,11... | collective-permute-start | bytes 27656 | tf_op jit(solution)/shard_map/ppermute | solution.py:19
  43.5 1.4 %copy-start.2 = (bf16[3,3,32,32]{3,2,1,0:T(8,128)(2,1)S(1)}, bf16[3,3,32,32]{3,2,1,0:T(8,128)(2,1)}, u32[]{:S(2)}) copy-start(bf16[3,3,32,32]{3,2,1,0:T(8,128)(2,1)} %param.15) | copy-start | bytes 55300
  52.5 0.9 %copy-start.7 = (bf16[3,3,64,32]{2,3,1,0:T(8,128)(2,1)S(1)}, bf16[3,3,64,32]{2,3,1,0:T(8,128)(2,1)}, u32[]{:S(2)}) copy-start(bf16[3,3,64,32]{2,3,1,0:T(8,128)(2,1)} %param.16) | copy-start | bytes 110596
  52.5 0.9 %copy-start.9 = (pred[8,17]{0,1:T(8,128)(4,1)S(1)}, pred[8,17]{0,1:T(8,128)(4,1)}, u32[]{:S(2)}) copy-start(pred[8,17]{0,1:T(8,128)(4,1)} %constant.114) | copy-start | bytes 412
  55.6 0.7 copy-start.8
  59.6 0.9 %copy-start.3 = (bf16[3,3,32,96]{3,2,1,0:T(8,128)(2,1)S(1)}, bf16[3,3,32,96]{3,2,1,0:T(8,128)(2,1)}, u32[]{:S(2)}) copy-start(bf16[3,3,32,96]{3,2,1,0:T(8,128)(2,1)} %param.18) | copy-start | bytes 165892
  64.9 1.4 %copy-start.6 = (bf16[11,32]{1,0:T(8,128)(2,1)S(1)}, bf16[11,32]{1,0:T(8,128)(2,1)}, u32[]{:S(2)}) copy-start(bf16[11,32]{1,0:T(8,128)(2,1)} %param.19) | copy-start | bytes 2116

commit v11 on v10

--- a/solution.py
+++ b/solution.py
@@ -146,16 +146,25 @@
     part_sums = jnp.sum(weights[:, None] * reflectance, axis=0)
     part_total = jnp.sum(weights, axis=0)
     packed = jnp.concatenate([part_sums, part_total[None], shift[None]], axis=0).astype(jnp.bfloat16)
-    gathered = lax.all_gather(packed, "tm", axis=0).astype(jnp.float32)
-    shifts = gathered[:, -1]
-    scale = jnp.exp(shifts - jnp.max(shifts, axis=0)[None])
-    band_sums = jnp.sum(scale[:, None] * gathered[:, :-2], axis=0)
-    total_weight = jnp.sum(scale * gathered[:, -2], axis=0)
-    composite = (band_sums / total_weight[None]).astype(jnp.bfloat16)
+    def combine(part):
+        gathered = lax.all_gather(part, "tm", axis=0).astype(jnp.float32)
+        shifts = gathered[:, -1]
+        scale = jnp.exp(shifts - jnp.max(shifts, axis=0)[None])
+        band_sums = jnp.sum(scale[:, None] * gathered[:, :-2], axis=0)
+        total_weight = jnp.sum(scale * gathered[:, -2], axis=0)
+        return (band_sums / total_weight[None]).astype(jnp.bfloat16).transpose(1, 2, 0)
+
+    half = block_rows // 2
+    upper = combine(packed[:, :half])
+    ends = lax.axis_size("row") - 1
+    from_below = lax.ppermute(upper[:HALO], "row", [(i + 1, i) for i in range(ends)])
+    lower = combine(packed[:, half:])
+    from_above = lax.ppermute(lower[half - HALO :], "row", [(i, i + 1) for i in range(ends)])
+    stacked = jnp.concatenate([from_above, upper, lower, from_below], axis=0)
 
     row0 = lax.axis_index("row") * block_rows
     col0 = lax.axis_index("col") * block_cols
-    widened = with_halo(composite.transpose(1, 2, 0), (("row", 0), ("col", 1)), HALO)
+    widened = with_halo(stacked, (("col", 1),), HALO)
     first_map = masked_layer(widened, encode_first, row0 - HALO + 1, col0 - HALO + 1, total_rows, total_cols)
     skip_wide = masked_layer(first_map, encode_second, row0 - HALO + 2, col0 - HALO + 2, total_rows, total_cols)
     wide_rows, wide_cols, channels = skip_wide.shape

time: 69.5 us -> 79.6 us (1.15)
  blocking collectives: 22.8 us -> 32.4 us
    all_gather x1 -> x2, blocking collectives: 22.8 us -> 32.4 us  [combine(): gathered = lax.all_gather(part, 'tm', axis=0).astype(jnp.float32)]
  transfers between devices with their start and end apart: 3 -> 3, of which waited for: 3 -> 2; matrix products, arithmetic and copies ran while one was open for 1% -> 1% of each run, Pallas kernels for 0% -> 0%
where the time goes in v11:
time: 79.6 us; the launch traced here: 78.9 us
  blocking collectives  32.4 us (41%)
  matrix products  22.7 us (29%)
  waiting for transfers between devices  5.76 us (7%)
  local copies, waits for them, and re-layouts  5.48 us (7%)
  other arithmetic  4.87 us (6%)
  starting transfers between devices  4.76 us (6%)
  Pallas kernels  2.34 us (3%)
    all_gather x2, blocking collectives, combine(): gathered = lax.all_gather(part, 'tm', axis=0).astype(jnp.float32)  32.4 us
    dot_general x26, matrix products, valid_conv(): jnp.einsum('hwc,oc->hwo', padded[a:a + height, e:e + width], kernel[a, e]...  16.6 us
    ppermute x1, waiting for transfers between devices, shards(): lax.ppermute(upper[:HALO], 'row', [(i + 1, i) for i in range(ends)])  4.34 us
    ppermute x1, starting transfers between devices, shards(): lax.ppermute(lower[half - HALO:], 'row', [(i, i + 1) for i in range(ends)])  3.4 us
    conv_general_dilated x2, matrix products, native_conv(): lax.conv_general_dilated(padded[None], kernel, (1, 1), 'VALID', dimension...  2.89 us
    unnamed x22, local copies, waits for them, and re-layouts  2.62 us
    pallas_call x1, Pallas kernels, shifted_weights(): pl.pallas_call(weight_kernel, out_shape=(jax.ShapeDtypeStruct((dates, row...  2.34 us
    dot_general x1, matrix products, shards(): jnp.einsum('oc,hwc->ohw', head_weight, decoded, preferred_element_type=jn...  2.15 us
  transfers between devices with their start and end apart: 3, of which 2 were waited for; matrix products, arithmetic and copies ran while one was open for 1% of the time, Pallas kernels for 0%

profile of v11, /device:TPU:0, one launch (start us, length us, event | category | flops | bytes accessed | tf_op | source)
XLA Modules:
  0.0 78.9 jit_solution(17285874442755972055)
XLA Ops:
  0.0 2.3 %shard_map.100 = (f32[8,32,256]{2,1,0:T(8,128)}, f32[32,256]{1,0:T(8,128)}) custom-call(f32[12]{0:T(128)} %score_ref.1, s32[8,32,256]{2,1,0:T(8,128)} %class_ref.1, f32[8,32,256]{2,1,0:T(8,128)} %quality_ref.1), custom_call_target="tpu_custom_call" | custom-call | tf_op jit(solution)/shard_map/pallas_call | solution.py:104
  2.3 1.8 %multiply_reduce_fusion = bf16[12,32,256]{2,1,0:T(8,128)(2,1)S(1)} fusion(bf16[8,12,32,256]{3,2,1,0:T(8,128)(2,1)} %param.10, f32[8,32,256]{2,1,0:T(8,128)} %get-tuple-element.7), kind=kLoop, calls=%fused_computation.16 | loop fusion | flops 2260992 | bytes 2031616 | tf_op jit(solution)/shard_map/reduce_sum | solution.py:146
  4.3 16.8 %all-gather = bf16[56,16,256]{2,1,0:T(8,128)(2,1)S(1)} all-gather(bf16[14,16,256]{2,1,0:T(8,128)(2,1)S(1)} %get-tuple-element.9), channel_id=2, replica_groups=mesh['tm'=4,'row'=4,'col'=2] {'tm'}, dimensions={0}, use_global_device_ids=true | all-gather | bytes 573440 | tf_op jit(solution)/shard_map/all_gather | solution.py:150
  21.1 0.1 convert.14
  21.3 0.1 fusion.84
  21.3 0.1 fusion.122
  21.5 3.4 %collective-permute-start = (bf16[8,256,12]{1,2,0:T(8,128)(2,1)S(1)}, bf16[8,256,12]{1,2,0:T(8,128)(2,1)S(1)}, u32[]{:S(2)}, u32[]{:S(2)}) collective-permute-start(bf16[8,256,12]{1,2,0:T(8,128)(2,1)S(1)} %slice.280), channel_id=1, source_target_pairs={{0,2},{2,4},{4,6},{1,3},{3,5},{5,7},{8,10},{10,12},{12,14},{9,11},... | collective-permute-start | bytes 147464 | tf_op jit(solution)/shard_map/ppermute | solution.py:162
  24.9 15.6 %all-gather.1 = bf16[56,16,256]{2,1,0:T(8,128)(2,1)S(1)} all-gather(bf16[14,16,256]{2,1,0:T(8,128)(2,1)S(1)} %get-tuple-element.10), channel_id=3, replica_groups=mesh['tm'=4,'row'=4,'col'=2] {'tm'}, dimensions={0}, use_global_device_ids=true | all-gather | bytes 573440 | tf_op jit(solution)/shard_map/all_gather | solution.py:150
  40.5 0.1 convert.15
  40.8 0.1 fusion.123
  40.9 1.3 %collective-permute-start.1 = (bf16[8,256,12]{1,2,0:T(8,128)(2,1)S(1)}, bf16[8,256,12]{1,2,0:T(8,128)(2,1)S(1)}, u32[]{:S(2)}, u32[]{:S(2)}) collective-permute-start(bf16[8,256,12]{1,2,0:T(8,128)(2,1)S(1)} %slice.285), channel_id=1, source_target_pairs={{2,0},{4,2},{6,4},{3,1},{5,3},{7,5},{10,8},{12,10},{14,12},{11,9},... | collective-permute-start | bytes 147464 | tf_op jit(solution)/shard_map/ppermute | solution.py:160
  42.8 4.3 %collective-permute-done.1 = bf16[8,256,12]{1,2,0:T(8,128)(2,1)S(1)} collective-permute-done((bf16[8,256,12]{1,2,0:T(8,128)(2,1)S(1)}, bf16[8,256,12]{1,2,0:T(8,128)(2,1)S(1)}, u32[]{:S(2)}, u32[]{:S(2)}) %collective-permute-start.1) | collective-permute-done | bytes 49184 | tf_op jit(solution)/shard_map/ppermute | solution.py:160
  47.2 0.1 slice_select_fusion.1
  47.4 1.4 %collective-permute-done.2 = bf16[48,8,12]{1,2,0:T(8,128)(2,1)S(1)} collective-permute-done((bf16[48,8,12]{1,2,0:T(8,128)(2,1)S(1)}, bf16[48,8,12]{1,2,0:T(8,128)(2,1)S(1)}, u32[]{:S(2)}, u32[]{:S(2)}) %collective-permute-start.2) | collective-permute-done | bytes 9248 | tf_op jit(solution)/shard_map/ppermute | solution.py:19
  48.8 0.3 pad_maximum_fusion.14
  49.2 0.5 fusion.101
  49.7 0.5 fusion.103
  50.2 0.5 fusion.105
  50.7 0.5 fusion.107
  51.2 0.5 fusion.109
  51.7 0.5 fusion.95
  52.3 0.5 fusion.97
  52.8 0.5 fusion.99
  53.3 1.3 %select_convert_fusion = bf16[46,270,32]{1,2,0:T(8,128)(2,1)S(1)} fusion(f32[46,270,32]{1,2,0:T(8,128)S(1)} %fusion.95, f32[46,270,32]{1,2,0:T(8,128)S(1)} %fusion.97, f32[46,270,32]{1,2,0:T(8,128)S(1)} %fusion.99, f32[46,270,32]{1,2,0:T(8,128)S(1)} %fusion.101, f32[46,270,32]{1,2,0:T(8,128)S(1)} %fusion.103, f32[46,270,32]{1,2,0:T(8,128)S(1)} %fusion.105, ...), kind=kOutput, calls=%fused_computation.17 | convolution fusion | flops 13910400 | bytes 19470592 | tf_op jit(solution)/shard_map/hwc,oc->hwo/dot_general | solution.py:43
  54.6 0.5 fusion.61
  55.2 0.4 fusion.63
  55.6 0.5 fusion.65
  56.1 0.5 fusion.67
  56.7 0.4 fusion.69
  57.1 0.5 fusion.71
  57.6 0.5 fusion.73
  58.2 0.4 fusion.75
  58.6 1.6 %select_convert_fusion.1 = bf16[44,268,32]{1,2,0:T(8,128)(2,1)S(1)} fusion(f32[44,268,32]{1,2,0:T(8,128)S(1)} %fusion.61, f32[44,268,32]{1,2,0:T(8,128)S(1)} %fusion.63, f32[44,268,32]{1,2,0:T(8,128)S(1)} %fusion.65, f32[44,268,32]{1,2,0:T(8,128)S(1)} %fusion.67, f32[44,268,32]{1,2,0:T(8,128)S(1)} %fusion.69, f32[44,268,32]{1,2,0:T(8,128)S(1)} %fusion.71, ...), kind=kOutput, calls=%fused_computation.18 | convolution fusion | flops 28300800 | bytes 19164160 | tf_op jit(solution)/shard_map/hwc,oc->hwo/dot_general | solution.py:43
  60.2 0.4 slice.306
  60.6 0.6 fusion.118
  61.2 0.4 reduce_sum.69
  61.6 0.6 copy.68
  62.3 0.2 pad.clone
  62.5 0.1 copy.58
  62.6 0.5 copy-done.7
  63.1 1.3 %fusion.29 = bf16[20,8,17,64]{3,1,2,0:T(8,128)(2,1)S(1)} fusion(bf16[3,3,64,32]{2,3,1,0:T(8,128)(2,1)S(1)} %copy-done.7, bf16[22,1,7,2,32]{4,2,3,0,1:T(8,128)(2,1)S(1)} %slice.307, bf16[22,1,8,17,32]{4,2,3,0,1:T(8,128)(2,1)S(1)} %copy.58, pred[8,17]{0,1:T(8,128)(4,1)S(1)} %copy-done.9), kind=kOutput, calls=%fused_computation.45 | convolution fusion | flops 101434368 | bytes 596360 | tf_op jit(solution)/shard_map/conv_general_dilated | solution.py:54
  64.4 0.1 copy.59
  64.6 0.9 %fusion.1 = bf16[20,1,132,64]{3,0,2,1:T(8,128)(2,1)S(1)} fusion(bf16[20,1,136,64]{3,0,2,1:T(8,128)(2,1)S(1)} %bitcast.234, pred[20,132]{0,1:T(8,128)(4,1)S(1)} %broadcast_and_fusion.2), kind=kLoop, calls=%fused_computation.22 | loop fusion | flops 168960 | bytes 678480 | tf_op jit(solution)/shard_map/convert_element_type | solution.py:126
  65.5 0.2 pad.2
  65.6 0.1 copy.61
  65.8 0.3 copy-done.8
  66.1 1.6 %fusion.30 = bf16[18,8,17,64]{3,1,2,0:T(8,128)(2,1)S(1)} fusion(bf16[3,3,64,64]{3,2,1,0:T(8,128)(2,1)S(1)} %copy-done, bf16[20,1,7,2,64]{4,2,3,0,1:T(8,128)(2,1)S(1)} %slice.309, bf16[20,1,8,17,64]{4,2,3,0,1:T(8,128)(2,1)S(1)} %copy.61, pred[8,17]{0,1:T(8,128)(4,1)S(1)} %copy-done.8), kind=kOutput, calls=%fused_computation.48 | convolution fusion | flops 182123520 | bytes 771208 | tf_op jit(solution)/shard_map/conv_general_dilated | solution.py:54
  67.8 0.2 copy.62
  67.9 0.3 reshape.238
  68.2 0.4 copy.67
  68.6 0.5 fusion.54
  69.1 0.3 broadcast_in_dim.53
  69.4 0.2 slice.311
  69.6 0.7 copy-done.3
  70.3 0.3 fusion.6
  70.6 0.7 fusion.3
  71.3 0.7 fusion.51
  72.1 0.7 fusion.48
  72.8 0.4 fusion.45
  73.2 0.7 fusion.42
  73.9 0.7 fusion.39
  74.7 1.4 %fusion.36 = f32[32,256,32]{1,2,0:T(8,128)} fusion(f32[32,256,32]{1,2,0:T(8,128)S(1)} %fusion.3, f32[32,256,32]{1,2,0:T(8,128)S(1)} %fusion.39, bf16[34,258,64]{1,2,0:T(8,128)(2,1)S(1)} %slice.311, bf16[34,258,32]{1,2,0:T(8,128)(2,1)S(1)} %slice.306, bf16[3,3,32,96]{3,2,1,0:T(8,128)(2,1)S(1)} %copy-done.3), kind=kOutput, calls=%fused_computation.52 | convolution fusion | flops 54001664 | bytes 5660672 | tf_op jit(solution)/shard_map/hwc,oc->hwo/dot_general | solution.py:43
  76.0 2.2 %fusion.59 = bf16[11,32,256]{2,0,1:T(8,128)(2,1)S(1)} fusion(f32[32,256,32]{1,2,0:T(8,128)} %fusion.36, bf16[34,258,64]{1,2,0:T(8,128)(2,1)S(1)} %slice.311, bf16[34,258,32]{1,2,0:T(8,128)(2,1)S(1)} %slice.306, bf16[3,3,32,96]{3,2,1,0:T(8,128)(2,1)S(1)} %copy-done.3, bf16[11,32]{1,0:T(8,128)(2,1)S(1)} %copy-done.6), kind=kOutput, calls=%fused_computation.64 | convolution fusion | flops 60121088 | bytes 3747840 | tf_op jit(solution)/shard_map/oc,hwc->ohw/dot_general | solution.py:198
  78.2 0.7 copy.64
  (51 shorter events, 1.0 us)
Async XLA Ops:
  0.0 65.8 %copy-start = (bf16[3,3,64,64]{3,2,1,0:T(8,128)(2,1)S(1)}, bf16[3,3,64,64]{3,2,1,0:T(8,128)(2,1)}, u32[]{:S(2)}) copy-start(bf16[3,3,64,64]{3,2,1,0:T(8,128)(2,1)} %param.17) | copy-start | bytes 221188
  2.3 1.8 %copy-start.1 = (f32[8,32,256]{2,1,0:T(8,128)S(1)}, f32[8,32,256]{2,1,0:T(8,128)}, u32[]{:S(2)}) copy-start(f32[8,32,256]{2,1,0:T(8,128)} %get-tuple-element.7) | copy-start | bytes 786436
  2.3 1.8 %copy-start.5 = (f32[32,256]{1,0:T(8,128)S(1)}, f32[32,256]{1,0:T(8,128)}, u32[]{:S(2)}) copy-start(f32[32,256]{1,0:T(8,128)} %get-tuple-element.8) | copy-start | bytes 98308
  21.5 21.3 %collective-permute-start = (bf16[8,256,12]{1,2,0:T(8,128)(2,1)S(1)}, bf16[8,256,12]{1,2,0:T(8,128)(2,1)S(1)}, u32[]{:S(2)}, u32[]{:S(2)}) collective-permute-start(bf16[8,256,12]{1,2,0:T(8,128)(2,1)S(1)} %slice.280), channel_id=1, source_target_pairs={{0,2},{2,4},{4,6},{1,3},{3,5},{5,7},{8,10},{10,12},{12,14},{9,11},... | collective-permute-start | bytes 147464 | tf_op jit(solution)/shard_map/ppermute | solution.py:162
  40.9 6.2 %collective-permute-start.1 = (bf16[8,256,12]{1,2,0:T(8,128)(2,1)S(1)}, bf16[8,256,12]{1,2,0:T(8,128)(2,1)S(1)}, u32[]{:S(2)}, u32[]{:S(2)}) collective-permute-start(bf16[8,256,12]{1,2,0:T(8,128)(2,1)S(1)} %slice.285), channel_id=1, source_target_pairs={{2,0},{4,2},{6,4},{3,1},{5,3},{7,5},{10,8},{12,10},{14,12},{11,9},... | collective-permute-start | bytes 147464 | tf_op jit(solution)/shard_map/ppermute | solution.py:160
  42.7 6.5 %copy-start.4 = (bf16[3,3,32,12]{2,3,1,0:T(8,128)(2,1)S(1)}, bf16[3,3,32,12]{2,3,1,0:T(8,128)(2,1)}, u32[]{:S(2)}) copy-start(bf16[3,3,32,12]{2,3,1,0:T(8,128)(2,1)} %param.14) | copy-start | bytes 20740
  47.3 1.5 %collective-permute-start.2 = (bf16[48,8,12]{1,2,0:T(8,128)(2,1)S(1)}, bf16[48,8,12]{1,2,0:T(8,128)(2,1)S(1)}, u32[]{:S(2)}, u32[]{:S(2)}) collective-permute-start(bf16[48,8,12]{1,2,0:T(8,128)(2,1)S(1)} %slice_select_fusion.1), channel_id=1, source_target_pairs={{0,1},{1,0},{2,3},{3,2},{4,5},{5,4},{6,7},{7,6},{8,9},{9,8},{10,11... | collective-permute-start | bytes 27656 | tf_op jit(solution)/shard_map/ppermute | solution.py:19
  53.3 1.4 %copy-start.2 = (bf16[3,3,32,32]{3,2,1,0:T(8,128)(2,1)S(1)}, bf16[3,3,32,32]{3,2,1,0:T(8,128)(2,1)}, u32[]{:S(2)}) copy-start(bf16[3,3,32,32]{3,2,1,0:T(8,128)(2,1)} %param.15) | copy-start | bytes 55300
  62.3 0.9 %copy-start.7 = (bf16[3,3,64,32]{2,3,1,0:T(8,128)(2,1)S(1)}, bf16[3,3,64,32]{2,3,1,0:T(8,128)(2,1)}, u32[]{:S(2)}) copy-start(bf16[3,3,64,32]{2,3,1,0:T(8,128)(2,1)} %param.16) | copy-start | bytes 110596
  62.3 0.9 %copy-start.9 = (pred[8,17]{0,1:T(8,128)(4,1)S(1)}, pred[8,17]{0,1:T(8,128)(4,1)}, u32[]{:S(2)}) copy-start(pred[8,17]{0,1:T(8,128)(4,1)} %constant.114) | copy-start | bytes 412
  65.4 0.7 copy-start.8
  69.4 0.9 %copy-start.3 = (bf16[3,3,32,96]{3,2,1,0:T(8,128)(2,1)S(1)}, bf16[3,3,32,96]{3,2,1,0:T(8,128)(2,1)}, u32[]{:S(2)}) copy-start(bf16[3,3,32,96]{3,2,1,0:T(8,128)(2,1)} %param.18) | copy-start | bytes 165892
  74.7 1.4 %copy-start.6 = (bf16[11,32]{1,0:T(8,128)(2,1)S(1)}, bf16[11,32]{1,0:T(8,128)(2,1)}, u32[]{:S(2)}) copy-start(bf16[11,32]{1,0:T(8,128)(2,1)} %param.19) | copy-start | bytes 2116

commit v12 on v10

--- a/solution.py
+++ b/solution.py
@@ -146,8 +146,19 @@
     part_sums = jnp.sum(weights[:, None] * reflectance, axis=0)
     part_total = jnp.sum(weights, axis=0)
     packed = jnp.concatenate([part_sums, part_total[None], shift[None]], axis=0).astype(jnp.bfloat16)
-    gathered = lax.all_gather(packed, "tm", axis=0).astype(jnp.float32)
-    shifts = gathered[:, -1]
+    count = lax.axis_size("tm")
+    me = lax.axis_index("tm")
+    slots = [packed]
+    valid = [me >= 0]
+    rising = packed
+    falling = packed
+    for step in range(1, count):
+        rising = lax.ppermute(rising, "tm", [(i, i + 1) for i in range(count - 1)])
+        falling = lax.ppermute(falling, "tm", [(i + 1, i) for i in range(count - 1)])
+        slots += [rising, falling]
+        valid += [me - step >= 0, me + step <= count - 1]
+    gathered = jnp.stack(slots, axis=0).astype(jnp.float32)
+    shifts = jnp.where(jnp.stack(valid)[:, None, None], gathered[:, -1], -jnp.inf)
     scale = jnp.exp(shifts - jnp.max(shifts, axis=0)[None])
     band_sums = jnp.sum(scale[:, None] * gathered[:, :-2], axis=0)
     total_weight = jnp.sum(scale * gathered[:, -2], axis=0)

time: 69.5 us -> 78 us (1.12)
  blocking collectives: 22.8 us -> 0 us
  starting transfers between devices: 4.76 us -> 22.5 us
  waiting for transfers between devices: 5.76 us -> 18.1 us
    all_gather x1 -> x0, blocking collectives: 22.8 us -> none  [shards(): gathered = lax.all_gather(packed, 'tm', axis=0).astype(jnp.float32)]
    ppermute x0 -> x6, starting transfers between devices: none -> 17.6 us  [the longest x3 13.7 us: shards(): rising = lax.ppermute(rising, 'tm', [(i, i + 1) for i in range(count - 1)])]
    ppermute x0 -> x6, waiting for transfers between devices: none -> 12.1 us  [the longest x3 7.63 us: shards(): rising = lax.ppermute(rising, 'tm', [(i, i + 1) for i in range(count - 1)])]
    unnamed x22 -> x27, local copies, waits for them, and re-layouts: 2.63 us -> 2.93 us
  transfers between devices with their start and end apart: 3 -> 9, of which waited for: 3 -> 7; matrix products, arithmetic and copies ran while one was open for 1% -> 1% of each run, Pallas kernels for 0% -> 0%
where the time goes in v12:
time: 78 us; the launch traced here: 77.5 us
  matrix products  22.6 us (29%)
  starting transfers between devices  22.5 us (29%)
  waiting for transfers between devices  18.1 us (23%)
  local copies, waits for them, and re-layouts  5.88 us (8%)
  other arithmetic  5.27 us (7%)
  Pallas kernels  2.34 us (3%)
    dot_general x26, matrix products, valid_conv(): jnp.einsum('hwc,oc->hwo', padded[a:a + height, e:e + width], kernel[a, e]...  16.6 us
    ppermute x3, starting transfers between devices, shards(): rising = lax.ppermute(rising, 'tm', [(i, i + 1) for i in range(count - 1)])  13.7 us
    ppermute x3, waiting for transfers between devices, shards(): rising = lax.ppermute(rising, 'tm', [(i, i + 1) for i in range(count - 1)])  7.63 us
    ppermute x3, waiting for transfers between devices, shards(): lax.ppermute(falling, 'tm', [(i + 1, i) for i in range(count - 1)])  4.43 us
    ppermute x1, waiting for transfers between devices, with_halo(): lax.ppermute(head, axis, [((i + 1) % count, i) for i in range(ends)])  4.27 us
    ppermute x3, starting transfers between devices, shards(): lax.ppermute(falling, 'tm', [(i + 1, i) for i in range(count - 1)])  3.88 us
    ppermute x1, starting transfers between devices, with_halo(): lax.ppermute(tail, axis, [(i, (i + 1) % count) for i in range(ends)])  3.4 us
    unnamed x27, local copies, waits for them, and re-layouts  2.93 us
  transfers between devices with their start and end apart: 9, of which 7 were waited for; matrix products, arithmetic and copies ran while one was open for 1% of the time, Pallas kernels for 0%

profile of v12, /device:TPU:0, one launch (start us, length us, event | category | flops | bytes accessed | tf_op | source)
XLA Modules:
  0.0 77.5 jit_solution(4442382506600690915)
XLA Ops:
  0.0 2.3 %shard_map.100 = (f32[8,32,256]{2,1,0:T(8,128)}, f32[32,256]{1,0:T(8,128)}) custom-call(f32[12]{0:T(128)} %score_ref.1, s32[8,32,256]{2,1,0:T(8,128)} %class_ref.1, f32[8,32,256]{2,1,0:T(8,128)} %quality_ref.1), custom_call_target="tpu_custom_call" | custom-call | tf_op jit(solution)/shard_map/pallas_call | solution.py:104
  2.3 1.8 %multiply_reduce_fusion = bf16[12,32,256]{2,1,0:T(8,128)(2,1)S(1)} fusion(bf16[8,12,32,256]{3,2,1,0:T(8,128)(2,1)} %param.10, f32[8,32,256]{2,1,0:T(8,128)} %get-tuple-element.7), kind=kLoop, calls=%fused_computation.16 | loop fusion | flops 2260992 | bytes 2031616 | tf_op jit(solution)/shard_map/reduce_sum | solution.py:146
  4.3 4.9 %collective-permute-start = (bf16[14,32,256]{2,1,0:T(8,128)(2,1)S(1)}, bf16[14,32,256]{2,1,0:T(8,128)(2,1)S(1)}, u32[]{:S(2)}, u32[]{:S(2)}) collective-permute-start(bf16[14,32,256]{2,1,0:T(8,128)(2,1)S(1)} %pad_maximum_fusion.16), channel_id=1, source_target_pairs={{0,8},{8,16},{16,24},{1,9},{9,17},{17,25},{2,10},{10,18},{18,26},{... | collective-permute-start | bytes 688136 | tf_op jit(solution)/shard_map/ppermute | solution.py:156
  9.2 1.3 %collective-permute-start.1 = (bf16[14,32,256]{2,1,0:T(8,128)(2,1)S(1)}, bf16[14,32,256]{2,1,0:T(8,128)(2,1)S(1)}, u32[]{:S(2)}, u32[]{:S(2)}) collective-permute-start(bf16[14,32,256]{2,1,0:T(8,128)(2,1)S(1)} %pad_maximum_fusion.16), channel_id=1, source_target_pairs={{8,0},{16,8},{24,16},{9,1},{17,9},{25,17},{10,2},{18,10},{26,18},{... | collective-permute-start | bytes 688136 | tf_op jit(solution)/shard_map/ppermute | solution.py:157
  11.1 2.9 %collective-permute-done = bf16[14,32,256]{2,1,0:T(8,128)(2,1)S(1)} collective-permute-done((bf16[14,32,256]{2,1,0:T(8,128)(2,1)S(1)}, bf16[14,32,256]{2,1,0:T(8,128)(2,1)S(1)}, u32[]{:S(2)}, u32[]{:S(2)}) %collective-permute-start) | collective-permute-done | bytes 229408 | tf_op jit(solution)/shard_map/ppermute | solution.py:156
  14.0 4.4 %collective-permute-start.2 = (bf16[14,32,256]{2,1,0:T(8,128)(2,1)S(1)}, bf16[14,32,256]{2,1,0:T(8,128)(2,1)S(1)}, u32[]{:S(2)}, u32[]{:S(2)}) collective-permute-start(bf16[14,32,256]{2,1,0:T(8,128)(2,1)S(1)} %collective-permute-done), channel_id=1, source_target_pairs={{0,8},{8,16},{16,24},{1,9},{9,17},{17,25},{2,10},{10,18},{18,26},{... | collective-permute-start | bytes 688136 | tf_op jit(solution)/shard_map/ppermute | solution.py:156
  18.5 1.3 %collective-permute-start.3 = (bf16[14,32,256]{2,1,0:T(8,128)(2,1)S(1)}, bf16[14,32,256]{2,1,0:T(8,128)(2,1)S(1)}, u32[]{:S(2)}, u32[]{:S(2)}) collective-permute-start(bf16[14,32,256]{2,1,0:T(8,128)(2,1)S(1)} %collective-permute-done.1), channel_id=1, source_target_pairs={{8,0},{16,8},{24,16},{9,1},{17,9},{25,17},{10,2},{18,10},{26,18},{... | collective-permute-start | bytes 688136 | tf_op jit(solution)/shard_map/ppermute | solution.py:157
  19.8 2.6 %collective-permute-done.2 = bf16[14,32,256]{2,1,0:T(8,128)(2,1)S(1)} collective-permute-done((bf16[14,32,256]{2,1,0:T(8,128)(2,1)S(1)}, bf16[14,32,256]{2,1,0:T(8,128)(2,1)S(1)}, u32[]{:S(2)}, u32[]{:S(2)}) %collective-permute-start.2) | collective-permute-done | bytes 229408 | tf_op jit(solution)/shard_map/ppermute | solution.py:156
  22.4 4.4 %collective-permute-start.4 = (bf16[14,32,256]{2,1,0:T(8,128)(2,1)S(1)}, bf16[14,32,256]{2,1,0:T(8,128)(2,1)S(1)}, u32[]{:S(2)}, u32[]{:S(2)}) collective-permute-start(bf16[14,32,256]{2,1,0:T(8,128)(2,1)S(1)} %collective-permute-done.2), channel_id=1, source_target_pairs={{0,8},{8,16},{16,24},{1,9},{9,17},{17,25},{2,10},{10,18},{18,26},{... | collective-permute-start | bytes 688136 | tf_op jit(solution)/shard_map/ppermute | solution.py:156
  26.8 1.3 %collective-permute-start.5 = (bf16[14,32,256]{2,1,0:T(8,128)(2,1)S(1)}, bf16[14,32,256]{2,1,0:T(8,128)(2,1)S(1)}, u32[]{:S(2)}, u32[]{:S(2)}) collective-permute-start(bf16[14,32,256]{2,1,0:T(8,128)(2,1)S(1)} %collective-permute-done.3), channel_id=1, source_target_pairs={{8,0},{16,8},{24,16},{9,1},{17,9},{25,17},{10,2},{18,10},{26,18},{... | collective-permute-start | bytes 688136 | tf_op jit(solution)/shard_map/ppermute | solution.py:157
  28.1 2.1 %collective-permute-done.4 = bf16[14,32,256]{2,1,0:T(8,128)(2,1)S(1)} collective-permute-done((bf16[14,32,256]{2,1,0:T(8,128)(2,1)S(1)}, bf16[14,32,256]{2,1,0:T(8,128)(2,1)S(1)}, u32[]{:S(2)}, u32[]{:S(2)}) %collective-permute-start.4) | collective-permute-done | bytes 229408 | tf_op jit(solution)/shard_map/ppermute | solution.py:156
  30.3 4.4 %collective-permute-done.5 = bf16[14,32,256]{2,1,0:T(8,128)(2,1)S(1)} collective-permute-done((bf16[14,32,256]{2,1,0:T(8,128)(2,1)S(1)}, bf16[14,32,256]{2,1,0:T(8,128)(2,1)S(1)}, u32[]{:S(2)}, u32[]{:S(2)}) %collective-permute-start.5) | collective-permute-done | bytes 229408 | tf_op jit(solution)/shard_map/ppermute | solution.py:157
  34.8 0.4 convert_element_type.65
  35.5 0.3 fusion
  35.9 0.2 fusion.115
  36.1 3.4 %collective-permute-start.6 = (bf16[8,256,12]{1,2,0:T(8,128)(2,1)S(1)}, bf16[8,256,12]{1,2,0:T(8,128)(2,1)S(1)}, u32[]{:S(2)}, u32[]{:S(2)}) collective-permute-start(bf16[8,256,12]{1,2,0:T(8,128)(2,1)S(1)} %get-tuple-element.9), channel_id=1, source_target_pairs={{0,2},{2,4},{4,6},{1,3},{3,5},{5,7},{8,10},{10,12},{12,14},{9,11},... | collective-permute-start | bytes 147464 | tf_op jit(solution)/shard_map/ppermute | solution.py:27
  39.5 1.5 %collective-permute-start.7 = (bf16[8,256,12]{1,2,0:T(8,128)(2,1)S(1)}, bf16[8,256,12]{1,2,0:T(8,128)(2,1)S(1)}, u32[]{:S(2)}, u32[]{:S(2)}) collective-permute-start(bf16[8,256,12]{1,2,0:T(8,128)(2,1)S(1)} %get-tuple-element.10), channel_id=1, source_target_pairs={{2,0},{4,2},{6,4},{3,1},{5,3},{7,5},{10,8},{12,10},{14,12},{11,9},... | collective-permute-start | bytes 147464 | tf_op jit(solution)/shard_map/ppermute | solution.py:29
  41.0 0.4 collective-permute-done.6
  41.4 4.3 %collective-permute-done.7 = bf16[8,256,12]{1,2,0:T(8,128)(2,1)S(1)} collective-permute-done((bf16[8,256,12]{1,2,0:T(8,128)(2,1)S(1)}, bf16[8,256,12]{1,2,0:T(8,128)(2,1)S(1)}, u32[]{:S(2)}, u32[]{:S(2)}) %collective-permute-start.7) | collective-permute-done | bytes 49184 | tf_op jit(solution)/shard_map/ppermute | solution.py:29
  46.0 1.4 %collective-permute-done.8 = bf16[48,8,12]{1,2,0:T(8,128)(2,1)S(1)} collective-permute-done((bf16[48,8,12]{1,2,0:T(8,128)(2,1)S(1)}, bf16[48,8,12]{1,2,0:T(8,128)(2,1)S(1)}, u32[]{:S(2)}, u32[]{:S(2)}) %collective-permute-start.8) | collective-permute-done | bytes 9248 | tf_op jit(solution)/shard_map/ppermute | solution.py:19
  47.4 0.3 pad_maximum_fusion.14
  47.8 0.5 fusion.100
  48.3 0.5 fusion.102
  48.8 0.5 fusion.104
  49.3 0.5 fusion.106
  49.8 0.5 fusion.108
  50.3 0.5 fusion.94
  50.8 0.5 fusion.96
  51.3 0.5 fusion.98
  51.9 1.3 %select_convert_fusion = bf16[46,270,32]{1,2,0:T(8,128)(2,1)S(1)} fusion(f32[46,270,32]{1,2,0:T(8,128)S(1)} %fusion.94, f32[46,270,32]{1,2,0:T(8,128)S(1)} %fusion.96, f32[46,270,32]{1,2,0:T(8,128)S(1)} %fusion.98, f32[46,270,32]{1,2,0:T(8,128)S(1)} %fusion.100, f32[46,270,32]{1,2,0:T(8,128)S(1)} %fusion.102, f32[46,270,32]{1,2,0:T(8,128)S(1)} %fusion.104, ...), kind=kOutput, calls=%fused_computation.19 | convolution fusion | flops 13910400 | bytes 19470592 | tf_op jit(solution)/shard_map/hwc,oc->hwo/dot_general | solution.py:43
  53.2 0.5 fusion.62
  53.7 0.4 fusion.64
  54.2 0.5 fusion.66
  54.7 0.5 fusion.68
  55.2 0.4 fusion.70
  55.7 0.5 fusion.72
  56.2 0.5 fusion.74
  56.7 0.4 fusion.76
  57.2 1.6 %select_convert_fusion.1 = bf16[44,268,32]{1,2,0:T(8,128)(2,1)S(1)} fusion(f32[44,268,32]{1,2,0:T(8,128)S(1)} %fusion.62, f32[44,268,32]{1,2,0:T(8,128)S(1)} %fusion.64, f32[44,268,32]{1,2,0:T(8,128)S(1)} %fusion.66, f32[44,268,32]{1,2,0:T(8,128)S(1)} %fusion.68, f32[44,268,32]{1,2,0:T(8,128)S(1)} %fusion.70, f32[44,268,32]{1,2,0:T(8,128)S(1)} %fusion.72, ...), kind=kOutput, calls=%fused_computation.20 | convolution fusion | flops 28300800 | bytes 19164160 | tf_op jit(solution)/shard_map/hwc,oc->hwo/dot_general | solution.py:43
  58.8 0.4 slice.281
  59.2 0.6 fusion.121
  59.7 0.2 reduce_sum.49
  60.0 0.8 %copy.87 = bf16[22,1,134,32]{3,0,2,1:T(8,128)(2,1)S(1)} copy(bf16[22,1,134,32]{2,3,0,1:T(8,128)(2,1)S(1)} %fusion.114) | data formatting | bytes 377344
  60.9 0.2 pad.clone
  61.2 0.5 copy-done.7
  61.8 1.3 %fusion.30 = bf16[20,8,17,64]{3,1,2,0:T(8,128)(2,1)S(1)} fusion(bf16[3,3,64,32]{2,3,1,0:T(8,128)(2,1)S(1)} %copy-done.7, bf16[22,1,7,2,32]{4,2,3,0,1:T(8,128)(2,1)S(1)} %slice.282, bf16[22,1,8,17,32]{4,2,3,0,1:T(8,128)(2,1)S(1)} %copy.79, pred[8,17]{0,1:T(8,128)(4,1)S(1)} %copy-done.9), kind=kOutput, calls=%fused_computation.47 | convolution fusion | flops 101434368 | bytes 596360 | tf_op jit(solution)/shard_map/conv_general_dilated | solution.py:54
  63.2 0.9 %fusion.2 = bf16[20,1,132,64]{3,0,2,1:T(8,128)(2,1)S(1)} fusion(bf16[20,1,136,64]{3,0,2,1:T(8,128)(2,1)S(1)} %bitcast.237, pred[20,132]{0,1:T(8,128)(4,1)S(1)} %broadcast_and_fusion.2), kind=kLoop, calls=%fused_computation.24 | loop fusion | flops 168960 | bytes 678480 | tf_op jit(solution)/shard_map/convert_element_type | solution.py:126
  64.4 0.3 copy-done.8
  64.7 1.6 %fusion.31 = bf16[18,8,17,64]{3,1,2,0:T(8,128)(2,1)S(1)} fusion(bf16[3,3,64,64]{3,2,1,0:T(8,128)(2,1)S(1)} %copy-done, bf16[20,1,7,2,64]{4,2,3,0,1:T(8,128)(2,1)S(1)} %slice.284, bf16[20,1,8,17,64]{4,2,3,0,1:T(8,128)(2,1)S(1)} %copy.82, pred[8,17]{0,1:T(8,128)(4,1)S(1)} %copy-done.8), kind=kOutput, calls=%fused_computation.50 | convolution fusion | flops 182123520 | bytes 771208 | tf_op jit(solution)/shard_map/conv_general_dilated | solution.py:54
  66.5 0.3 reshape.284
  66.8 0.4 copy.86
  67.3 0.5 fusion.55
  67.7 0.3 broadcast_in_dim.107
  68.2 0.7 copy-done.3
  68.9 0.3 fusion.7
  69.3 0.7 fusion.4
  69.9 0.7 fusion.52
  70.7 0.7 fusion.49
  71.4 0.4 fusion.46
  71.8 0.7 fusion.43
  72.5 0.7 fusion.40
  73.3 1.4 %fusion.37 = f32[32,256,32]{1,2,0:T(8,128)} fusion(f32[32,256,32]{1,2,0:T(8,128)S(1)} %fusion.4, f32[32,256,32]{1,2,0:T(8,128)S(1)} %fusion.40, bf16[34,258,64]{1,2,0:T(8,128)(2,1)S(1)} %slice.286, bf16[34,258,32]{1,2,0:T(8,128)(2,1)S(1)} %slice.281, bf16[3,3,32,96]{3,2,1,0:T(8,128)(2,1)S(1)} %copy-done.3), kind=kOutput, calls=%fused_computation.54 | convolution fusion | flops 54001664 | bytes 5660672 | tf_op jit(solution)/shard_map/hwc,oc->hwo/dot_general | solution.py:43
  74.6 2.2 %fusion.60 = bf16[11,32,256]{2,0,1:T(8,128)(2,1)S(1)} fusion(f32[32,256,32]{1,2,0:T(8,128)} %fusion.37, bf16[34,258,64]{1,2,0:T(8,128)(2,1)S(1)} %slice.286, bf16[34,258,32]{1,2,0:T(8,128)(2,1)S(1)} %slice.281, bf16[3,3,32,96]{3,2,1,0:T(8,128)(2,1)S(1)} %copy-done.3, bf16[11,32]{1,0:T(8,128)(2,1)S(1)} %copy-done.6), kind=kOutput, calls=%fused_computation.66 | convolution fusion | flops 60121088 | bytes 3747840 | tf_op jit(solution)/shard_map/oc,hwc->ohw/dot_general | solution.py:200
  76.8 0.7 copy.85
  (61 shorter events, 2.3 us)
Async XLA Ops:
  0.0 64.4 %copy-start = (bf16[3,3,64,64]{3,2,1,0:T(8,128)(2,1)S(1)}, bf16[3,3,64,64]{3,2,1,0:T(8,128)(2,1)}, u32[]{:S(2)}) copy-start(bf16[3,3,64,64]{3,2,1,0:T(8,128)(2,1)} %param.17) | copy-start | bytes 221188
  2.3 1.8 %copy-start.1 = (f32[8,32,256]{2,1,0:T(8,128)S(1)}, f32[8,32,256]{2,1,0:T(8,128)}, u32[]{:S(2)}) copy-start(f32[8,32,256]{2,1,0:T(8,128)} %get-tuple-element.7) | copy-start | bytes 786436
  2.3 1.8 %copy-start.5 = (f32[32,256]{1,0:T(8,128)S(1)}, f32[32,256]{1,0:T(8,128)}, u32[]{:S(2)}) copy-start(f32[32,256]{1,0:T(8,128)} %get-tuple-element.8) | copy-start | bytes 98308
  4.3 9.8 %collective-permute-start = (bf16[14,32,256]{2,1,0:T(8,128)(2,1)S(1)}, bf16[14,32,256]{2,1,0:T(8,128)(2,1)S(1)}, u32[]{:S(2)}, u32[]{:S(2)}) collective-permute-start(bf16[14,32,256]{2,1,0:T(8,128)(2,1)S(1)} %pad_maximum_fusion.16), channel_id=1, source_target_pairs={{0,8},{8,16},{16,24},{1,9},{9,17},{17,25},{2,10},{10,18},{18,26},{... | collective-permute-start | bytes 688136 | tf_op jit(solution)/shard_map/ppermute | solution.py:156
  9.2 9.3 %collective-permute-start.1 = (bf16[14,32,256]{2,1,0:T(8,128)(2,1)S(1)}, bf16[14,32,256]{2,1,0:T(8,128)(2,1)S(1)}, u32[]{:S(2)}, u32[]{:S(2)}) collective-permute-start(bf16[14,32,256]{2,1,0:T(8,128)(2,1)S(1)} %pad_maximum_fusion.16), channel_id=1, source_target_pairs={{8,0},{16,8},{24,16},{9,1},{17,9},{25,17},{10,2},{18,10},{26,18},{... | collective-permute-start | bytes 688136 | tf_op jit(solution)/shard_map/ppermute | solution.py:157
  14.0 8.4 %collective-permute-start.2 = (bf16[14,32,256]{2,1,0:T(8,128)(2,1)S(1)}, bf16[14,32,256]{2,1,0:T(8,128)(2,1)S(1)}, u32[]{:S(2)}, u32[]{:S(2)}) collective-permute-start(bf16[14,32,256]{2,1,0:T(8,128)(2,1)S(1)} %collective-permute-done), channel_id=1, source_target_pairs={{0,8},{8,16},{16,24},{1,9},{9,17},{17,25},{2,10},{10,18},{18,26},{... | collective-permute-start | bytes 688136 | tf_op jit(solution)/shard_map/ppermute | solution.py:156
  18.5 8.3 %collective-permute-start.3 = (bf16[14,32,256]{2,1,0:T(8,128)(2,1)S(1)}, bf16[14,32,256]{2,1,0:T(8,128)(2,1)S(1)}, u32[]{:S(2)}, u32[]{:S(2)}) collective-permute-start(bf16[14,32,256]{2,1,0:T(8,128)(2,1)S(1)} %collective-permute-done.1), channel_id=1, source_target_pairs={{8,0},{16,8},{24,16},{9,1},{17,9},{25,17},{10,2},{18,10},{26,18},{... | collective-permute-start | bytes 688136 | tf_op jit(solution)/shard_map/ppermute | solution.py:157
  22.4 7.9 %collective-permute-start.4 = (bf16[14,32,256]{2,1,0:T(8,128)(2,1)S(1)}, bf16[14,32,256]{2,1,0:T(8,128)(2,1)S(1)}, u32[]{:S(2)}, u32[]{:S(2)}) collective-permute-start(bf16[14,32,256]{2,1,0:T(8,128)(2,1)S(1)} %collective-permute-done.2), channel_id=1, source_target_pairs={{0,8},{8,16},{16,24},{1,9},{9,17},{17,25},{2,10},{10,18},{18,26},{... | collective-permute-start | bytes 688136 | tf_op jit(solution)/shard_map/ppermute | solution.py:156
  26.8 7.9 %collective-permute-start.5 = (bf16[14,32,256]{2,1,0:T(8,128)(2,1)S(1)}, bf16[14,32,256]{2,1,0:T(8,128)(2,1)S(1)}, u32[]{:S(2)}, u32[]{:S(2)}) collective-permute-start(bf16[14,32,256]{2,1,0:T(8,128)(2,1)S(1)} %collective-permute-done.3), channel_id=1, source_target_pairs={{8,0},{16,8},{24,16},{9,1},{17,9},{25,17},{10,2},{18,10},{26,18},{... | collective-permute-start | bytes 688136 | tf_op jit(solution)/shard_map/ppermute | solution.py:157
  36.1 5.3 %collective-permute-start.6 = (bf16[8,256,12]{1,2,0:T(8,128)(2,1)S(1)}, bf16[8,256,12]{1,2,0:T(8,128)(2,1)S(1)}, u32[]{:S(2)}, u32[]{:S(2)}) collective-permute-start(bf16[8,256,12]{1,2,0:T(8,128)(2,1)S(1)} %get-tuple-element.9), channel_id=1, source_target_pairs={{0,2},{2,4},{4,6},{1,3},{3,5},{5,7},{8,10},{10,12},{12,14},{9,11},... | collective-permute-start | bytes 147464 | tf_op jit(solution)/shard_map/ppermute | solution.py:27
  39.5 6.2 %collective-permute-start.7 = (bf16[8,256,12]{1,2,0:T(8,128)(2,1)S(1)}, bf16[8,256,12]{1,2,0:T(8,128)(2,1)S(1)}, u32[]{:S(2)}, u32[]{:S(2)}) collective-permute-start(bf16[8,256,12]{1,2,0:T(8,128)(2,1)S(1)} %get-tuple-element.10), channel_id=1, source_target_pairs={{2,0},{4,2},{6,4},{3,1},{5,3},{7,5},{10,8},{12,10},{14,12},{11,9},... | collective-permute-start | bytes 147464 | tf_op jit(solution)/shard_map/ppermute | solution.py:29
  41.0 6.8 %copy-start.4 = (bf16[3,3,32,12]{2,3,1,0:T(8,128)(2,1)S(1)}, bf16[3,3,32,12]{2,3,1,0:T(8,128)(2,1)}, u32[]{:S(2)}) copy-start(bf16[3,3,32,12]{2,3,1,0:T(8,128)(2,1)} %param.14) | copy-start | bytes 20740
  45.9 1.5 %collective-permute-start.8 = (bf16[48,8,12]{1,2,0:T(8,128)(2,1)S(1)}, bf16[48,8,12]{1,2,0:T(8,128)(2,1)S(1)}, u32[]{:S(2)}, u32[]{:S(2)}) collective-permute-start(bf16[48,8,12]{1,2,0:T(8,128)(2,1)S(1)} %slice_select_fusion.1), channel_id=1, source_target_pairs={{0,1},{1,0},{2,3},{3,2},{4,5},{5,4},{6,7},{7,6},{8,9},{9,8},{10,11... | collective-permute-start | bytes 27656 | tf_op jit(solution)/shard_map/ppermute | solution.py:19
  51.9 1.3 %copy-start.2 = (bf16[3,3,32,32]{3,2,1,0:T(8,128)(2,1)S(1)}, bf16[3,3,32,32]{3,2,1,0:T(8,128)(2,1)}, u32[]{:S(2)}) copy-start(bf16[3,3,32,32]{3,2,1,0:T(8,128)(2,1)} %param.15) | copy-start | bytes 55300
  60.9 0.9 %copy-start.7 = (bf16[3,3,64,32]{2,3,1,0:T(8,128)(2,1)S(1)}, bf16[3,3,64,32]{2,3,1,0:T(8,128)(2,1)}, u32[]{:S(2)}) copy-start(bf16[3,3,64,32]{2,3,1,0:T(8,128)(2,1)} %param.16) | copy-start | bytes 110596
  60.9 0.9 %copy-start.9 = (pred[8,17]{0,1:T(8,128)(4,1)S(1)}, pred[8,17]{0,1:T(8,128)(4,1)}, u32[]{:S(2)}) copy-start(pred[8,17]{0,1:T(8,128)(4,1)} %constant.123) | copy-start | bytes 412
  64.0 0.7 copy-start.8
  68.0 0.9 %copy-start.3 = (bf16[3,3,32,96]{3,2,1,0:T(8,128)(2,1)S(1)}, bf16[3,3,32,96]{3,2,1,0:T(8,128)(2,1)}, u32[]{:S(2)}) copy-start(bf16[3,3,32,96]{3,2,1,0:T(8,128)(2,1)} %param.18) | copy-start | bytes 165892
  73.3 1.4 %copy-start.6 = (bf16[11,32]{1,0:T(8,128)(2,1)S(1)}, bf16[11,32]{1,0:T(8,128)(2,1)}, u32[]{:S(2)}) copy-start(bf16[11,32]{1,0:T(8,128)(2,1)} %param.19) | copy-start | bytes 2116

commit v13 on v10

--- a/solution.py
+++ b/solution.py
@@ -67,48 +67,43 @@
 
 
 def weight_kernel(score_ref, class_ref, quality_ref, weight_ref, shift_ref):
-    dates, rows, _ = class_ref.shape
+    dates = class_ref.shape[0]
     classes = score_ref.shape[0]
-    step = 16
-
-    def chunk(index, carry):
-        at = pl.ds(pl.multiple_of(index * step, step), step)
-
-        def score(date, top):
-            label = class_ref[date, at, :]
-            looked = jnp.zeros(label.shape, jnp.float32)
-            for k in range(classes):
-                looked = jnp.where(label == k, score_ref[k], looked)
-            value = looked + quality_ref[date, at, :]
-            weight_ref[date, at, :] = value
-            return jnp.maximum(top, value)
-
-        start = jnp.full((step, weight_ref.shape[2]), -jnp.inf, jnp.float32)
-        top = lax.fori_loop(0, dates, score, start)
-        shift = top.astype(jnp.bfloat16).astype(jnp.float32)
-        shift_ref[at, :] = shift
-
-        def one_date(date, inner):
-            weight_ref[date, at, :] = jnp.exp(weight_ref[date, at, :] - shift)
-            return inner
-
-        lax.fori_loop(0, dates, one_date, 0)
-        return carry
-
-    lax.fori_loop(0, rows // step, chunk, 0)
+
+    def score(date, top):
+        label = class_ref[date]
+        looked = jnp.zeros(label.shape, jnp.float32)
+        for k in range(classes):
+            looked = jnp.where(label == k, score_ref[k], looked)
+        value = looked + quality_ref[date]
+        weight_ref[date] = value
+        return jnp.maximum(top, value)
+
+    start = jnp.full(shift_ref.shape, -jnp.inf, jnp.float32)
+    top = lax.fori_loop(0, dates, score, start)
+    shift = top.astype(jnp.bfloat16).astype(jnp.float32)
+    shift_ref[...] = shift
+
+    def one_date(date, inner):
+        weight_ref[date] = jnp.exp(weight_ref[date] - shift)
+        return inner
+
+    lax.fori_loop(0, dates, one_date, 0)
 
 
 def shifted_weights(class_score, scene_class, quality):
     dates, rows, cols = quality.shape
-    vmem = pl.BlockSpec(memory_space=pltpu.VMEM)
+    step = 8
+    planes = pl.BlockSpec((dates, step, cols), lambda i: (0, i, 0))
     return pl.pallas_call(
         weight_kernel,
         out_shape=(
             jax.ShapeDtypeStruct((dates, rows, cols), jnp.float32),
             jax.ShapeDtypeStruct((rows, cols), jnp.float32),
         ),
-        in_specs=[pl.BlockSpec(memory_space=pltpu.SMEM), vmem, vmem],
-        out_specs=(vmem, vmem),
+        grid=(rows // step,),
+        in_specs=[pl.BlockSpec(memory_space=pltpu.SMEM), planes, planes],
+        out_specs=(planes, pl.BlockSpec((step, cols), lambda i: (i, 0))),
     )(class_score, scene_class, quality)
 
 

time: 69.5 us -> 70.8 us (1.019)
  Pallas kernels: 2.34 us -> 3.49 us
    pallas_call x1, Pallas kernels: 2.34 us -> 3.49 us  [shifted_weights(): pl.pallas_call(weight_kernel, out_shape=(jax.ShapeDtypeStruct((dates, row...]
where the time goes in v13:
time: 70.8 us; the launch traced here: 70.3 us
  blocking collectives  22.8 us (32%)
  matrix products  22.7 us (32%)
  waiting for transfers between devices  5.76 us (8%)
  local copies, waits for them, and re-layouts  5.46 us (8%)
  other arithmetic  4.83 us (7%)
  starting transfers between devices  4.76 us (7%)
  Pallas kernels  3.49 us (5%)
    all_gather x1, blocking collectives, shards(): gathered = lax.all_gather(packed, 'tm', axis=0).astype(jnp.float32)  22.8 us
    dot_general x26, matrix products, valid_conv(): jnp.einsum('hwc,oc->hwo', padded[a:a + height, e:e + width], kernel[a, e]...  16.6 us
    ppermute x1, waiting for transfers between devices, with_halo(): lax.ppermute(head, axis, [((i + 1) % count, i) for i in range(ends)])  4.27 us
    pallas_call x1, Pallas kernels, shifted_weights(): pl.pallas_call(weight_kernel, out_shape=(jax.ShapeDtypeStruct((dates, row...  3.49 us
    ppermute x1, starting transfers between devices, with_halo(): lax.ppermute(tail, axis, [(i, (i + 1) % count) for i in range(ends)])  3.4 us
    conv_general_dilated x2, matrix products, native_conv(): lax.conv_general_dilated(padded[None], kernel, (1, 1), 'VALID', dimension...  2.89 us
    unnamed x22, local copies, waits for them, and re-layouts  2.63 us
    dot_general x1, matrix products, shards(): jnp.einsum('oc,hwc->ohw', head_weight, decoded, preferred_element_type=jn...  2.15 us
  transfers between devices with their start and end apart: 3, of which 3 were waited for; matrix products, arithmetic and copies ran while one was open for 1% of the time, Pallas kernels for 0%

profile of v13, /device:TPU:0, one launch (start us, length us, event | category | flops | bytes accessed | tf_op | source)
XLA Modules:
  0.0 70.3 jit_solution(550271204004247416)
XLA Ops:
  0.0 3.5 %shard_map.100 = (f32[8,32,256]{2,1,0:T(8,128)}, f32[32,256]{1,0:T(8,128)}) custom-call(f32[12]{0:T(128)} %score_ref.1, s32[8,32,256]{2,1,0:T(8,128)} %class_ref.1, f32[8,32,256]{2,1,0:T(8,128)} %quality_ref.1), custom_call_target="tpu_custom_call" | custom-call | tf_op jit(solution)/shard_map/pallas_call | solution.py:98
  3.5 1.8 %multiply_reduce_fusion = bf16[12,32,256]{2,1,0:T(8,128)(2,1)S(1)} fusion(bf16[8,12,32,256]{3,2,1,0:T(8,128)(2,1)} %param.10, f32[8,32,256]{2,1,0:T(8,128)} %get-tuple-element.7), kind=kLoop, calls=%fused_computation.16 | loop fusion | flops 2260992 | bytes 2031616 | tf_op jit(solution)/shard_map/reduce_sum | solution.py:141
  5.4 22.8 %all_gather.4 = bf16[4,14,32,256]{3,2,1,0:T(8,128)(2,1)S(1)} all-gather(bf16[1,14,32,256]{3,2,1,0:T(8,128)(2,1)S(1)} %pad_maximum_fusion.16), channel_id=1, replica_groups=mesh['tm'=4,'row'=4,'col'=2] {'tm'}, dimensions={0}, use_global_device_ids=true | all-gather | bytes 1146880 | tf_op jit(solution)/shard_map/all_gather | solution.py:144
  28.2 0.2 convert_element_type.65
  28.5 0.2 fusion.28
  28.7 0.2 fusion.115
  28.9 3.4 %collective-permute-start = (bf16[8,256,12]{1,2,0:T(8,128)(2,1)S(1)}, bf16[8,256,12]{1,2,0:T(8,128)(2,1)S(1)}, u32[]{:S(2)}, u32[]{:S(2)}) collective-permute-start(bf16[8,256,12]{1,2,0:T(8,128)(2,1)S(1)} %get-tuple-element.9), channel_id=1, source_target_pairs={{0,2},{2,4},{4,6},{1,3},{3,5},{5,7},{8,10},{10,12},{12,14},{9,11},... | collective-permute-start | bytes 147464 | tf_op jit(solution)/shard_map/ppermute | solution.py:27
  32.3 1.3 %collective-permute-start.1 = (bf16[8,256,12]{1,2,0:T(8,128)(2,1)S(1)}, bf16[8,256,12]{1,2,0:T(8,128)(2,1)S(1)}, u32[]{:S(2)}, u32[]{:S(2)}) collective-permute-start(bf16[8,256,12]{1,2,0:T(8,128)(2,1)S(1)} %get-tuple-element.10), channel_id=1, source_target_pairs={{2,0},{4,2},{6,4},{3,1},{5,3},{7,5},{10,8},{12,10},{14,12},{11,9},... | collective-permute-start | bytes 147464 | tf_op jit(solution)/shard_map/ppermute | solution.py:29
  33.8 0.1 broadcast_and_fusion
  33.9 0.1 broadcast_and_fusion.1
  34.0 0.1 broadcast_and_fusion.2
  34.2 4.3 %collective-permute-done.1 = bf16[8,256,12]{1,2,0:T(8,128)(2,1)S(1)} collective-permute-done((bf16[8,256,12]{1,2,0:T(8,128)(2,1)S(1)}, bf16[8,256,12]{1,2,0:T(8,128)(2,1)S(1)}, u32[]{:S(2)}, u32[]{:S(2)}) %collective-permute-start.1) | collective-permute-done | bytes 49184 | tf_op jit(solution)/shard_map/ppermute | solution.py:29
  38.6 0.1 slice_select_fusion.1
  38.8 1.4 %collective-permute-done.2 = bf16[48,8,12]{1,2,0:T(8,128)(2,1)S(1)} collective-permute-done((bf16[48,8,12]{1,2,0:T(8,128)(2,1)S(1)}, bf16[48,8,12]{1,2,0:T(8,128)(2,1)S(1)}, u32[]{:S(2)}, u32[]{:S(2)}) %collective-permute-start.2) | collective-permute-done | bytes 9248 | tf_op jit(solution)/shard_map/ppermute | solution.py:19
  40.2 0.3 pad_maximum_fusion.14
  40.6 0.5 fusion.100
  41.1 0.5 fusion.102
  41.6 0.5 fusion.104
  42.1 0.5 fusion.106
  42.6 0.5 fusion.108
  43.1 0.5 fusion.94
  43.6 0.5 fusion.96
  44.2 0.5 fusion.98
  44.7 1.3 %select_convert_fusion = bf16[46,270,32]{1,2,0:T(8,128)(2,1)S(1)} fusion(f32[46,270,32]{1,2,0:T(8,128)S(1)} %fusion.94, f32[46,270,32]{1,2,0:T(8,128)S(1)} %fusion.96, f32[46,270,32]{1,2,0:T(8,128)S(1)} %fusion.98, f32[46,270,32]{1,2,0:T(8,128)S(1)} %fusion.100, f32[46,270,32]{1,2,0:T(8,128)S(1)} %fusion.102, f32[46,270,32]{1,2,0:T(8,128)S(1)} %fusion.104, ...), kind=kOutput, calls=%fused_computation.17 | convolution fusion | flops 13910400 | bytes 19470592 | tf_op jit(solution)/shard_map/hwc,oc->hwo/dot_general | solution.py:43
  46.0 0.5 fusion.62
  46.6 0.4 fusion.64
  47.0 0.5 fusion.66
  47.5 0.5 fusion.68
  48.1 0.4 fusion.70
  48.5 0.5 fusion.72
  49.0 0.5 fusion.74
  49.5 0.4 fusion.76
  50.0 1.6 %select_convert_fusion.1 = bf16[44,268,32]{1,2,0:T(8,128)(2,1)S(1)} fusion(f32[44,268,32]{1,2,0:T(8,128)S(1)} %fusion.62, f32[44,268,32]{1,2,0:T(8,128)S(1)} %fusion.64, f32[44,268,32]{1,2,0:T(8,128)S(1)} %fusion.66, f32[44,268,32]{1,2,0:T(8,128)S(1)} %fusion.68, f32[44,268,32]{1,2,0:T(8,128)S(1)} %fusion.70, f32[44,268,32]{1,2,0:T(8,128)S(1)} %fusion.72, ...), kind=kOutput, calls=%fused_computation.18 | convolution fusion | flops 28300800 | bytes 19164160 | tf_op jit(solution)/shard_map/hwc,oc->hwo/dot_general | solution.py:43
  51.6 0.4 slice.281
  52.0 0.6 fusion.117
  52.6 0.4 reduce_sum.49
  53.0 0.6 copy.60
  53.7 0.2 pad.clone
  53.9 0.1 copy.51
  54.0 0.5 copy-done.7
  54.5 1.3 %fusion.30 = bf16[20,8,17,64]{3,1,2,0:T(8,128)(2,1)S(1)} fusion(bf16[3,3,64,32]{2,3,1,0:T(8,128)(2,1)S(1)} %copy-done.7, bf16[22,1,7,2,32]{4,2,3,0,1:T(8,128)(2,1)S(1)} %slice.282, bf16[22,1,8,17,32]{4,2,3,0,1:T(8,128)(2,1)S(1)} %copy.51, pred[8,17]{0,1:T(8,128)(4,1)S(1)} %copy-done.9), kind=kOutput, calls=%fused_computation.47 | convolution fusion | flops 101434368 | bytes 596360 | tf_op jit(solution)/shard_map/conv_general_dilated | solution.py:54
  55.8 0.1 copy.52
  55.9 0.9 %fusion.1 = bf16[20,1,132,64]{3,0,2,1:T(8,128)(2,1)S(1)} fusion(bf16[20,1,136,64]{3,0,2,1:T(8,128)(2,1)S(1)} %bitcast.209, pred[20,132]{0,1:T(8,128)(4,1)S(1)} %broadcast_and_fusion.2), kind=kLoop, calls=%fused_computation.22 | loop fusion | flops 168960 | bytes 678480 | tf_op jit(solution)/shard_map/convert_element_type | solution.py:121
  56.8 0.2 pad.2
  57.0 0.1 copy.54
  57.2 0.3 copy-done.8
  57.5 1.6 %fusion.31 = bf16[18,8,17,64]{3,1,2,0:T(8,128)(2,1)S(1)} fusion(bf16[3,3,64,64]{3,2,1,0:T(8,128)(2,1)S(1)} %copy-done, bf16[20,1,7,2,64]{4,2,3,0,1:T(8,128)(2,1)S(1)} %slice.284, bf16[20,1,8,17,64]{4,2,3,0,1:T(8,128)(2,1)S(1)} %copy.54, pred[8,17]{0,1:T(8,128)(4,1)S(1)} %copy-done.8), kind=kOutput, calls=%fused_computation.50 | convolution fusion | flops 182123520 | bytes 771208 | tf_op jit(solution)/shard_map/conv_general_dilated | solution.py:54
  59.1 0.2 copy.55
  59.3 0.3 reshape.283
  59.6 0.4 copy.59
  60.0 0.5 fusion.55
  60.5 0.3 broadcast_in_dim.45
  60.8 0.2 slice.286
  61.0 0.7 copy-done.3
  61.7 0.3 fusion.6
  62.0 0.7 fusion.3
  62.7 0.7 %fusion.52 = f32[32,256,32]{1,2,0:T(8,128)S(1)} fusion(f32[32,256,32]{1,2,0:T(8,128)S(1)} %fusion.6, bf16[34,258,64]{1,2,0:T(8,128)(2,1)S(1)} %slice.286, bf16[34,258,32]{1,2,0:T(8,128)(2,1)S(1)} %slice.281, bf16[3,3,32,96]{3,2,1,0:T(8,128)(2,1)S(1)} %copy-done.3), kind=kOutput, calls=%fused_computation.59 | convolution fusion | flops 53739520 | bytes 4612096 | tf_op jit(solution)/shard_map/hwc,oc->hwo/dot_general | solution.py:43
  63.5 0.7 %fusion.49 = f32[32,256,32]{1,2,0:T(8,128)S(1)} fusion(f32[32,256,32]{1,2,0:T(8,128)S(1)} %fusion.52, bf16[34,258,64]{1,2,0:T(8,128)(2,1)S(1)} %slice.286, bf16[34,258,32]{1,2,0:T(8,128)(2,1)S(1)} %slice.281, bf16[3,3,32,96]{3,2,1,0:T(8,128)(2,1)S(1)} %copy-done.3), kind=kOutput, calls=%fused_computation.58 | convolution fusion | flops 53739520 | bytes 4612096 | tf_op jit(solution)/shard_map/hwc,oc->hwo/dot_general | solution.py:43
  64.2 0.4 fusion.46
  64.6 0.7 %fusion.43 = f32[32,256,32]{1,2,0:T(8,128)S(1)} fusion(f32[32,256,32]{1,2,0:T(8,128)S(1)} %fusion.46, bf16[34,258,64]{1,2,0:T(8,128)(2,1)S(1)} %slice.286, bf16[34,258,32]{1,2,0:T(8,128)(2,1)S(1)} %slice.281, bf16[3,3,32,96]{3,2,1,0:T(8,128)(2,1)S(1)} %copy-done.3), kind=kOutput, calls=%fused_computation.56 | convolution fusion | flops 53739520 | bytes 4612096 | tf_op jit(solution)/shard_map/hwc,oc->hwo/dot_general | solution.py:43
  65.3 0.7 %fusion.40 = f32[32,256,32]{1,2,0:T(8,128)S(1)} fusion(f32[32,256,32]{1,2,0:T(8,128)S(1)} %fusion.43, bf16[34,258,64]{1,2,0:T(8,128)(2,1)S(1)} %slice.286, bf16[34,258,32]{1,2,0:T(8,128)(2,1)S(1)} %slice.281, bf16[3,3,32,96]{3,2,1,0:T(8,128)(2,1)S(1)} %copy-done.3), kind=kOutput, calls=%fused_computation.55 | convolution fusion | flops 53739520 | bytes 4612096 | tf_op jit(solution)/shard_map/hwc,oc->hwo/dot_general | solution.py:43
  66.1 1.4 %fusion.37 = f32[32,256,32]{1,2,0:T(8,128)} fusion(f32[32,256,32]{1,2,0:T(8,128)S(1)} %fusion.3, f32[32,256,32]{1,2,0:T(8,128)S(1)} %fusion.40, bf16[34,258,64]{1,2,0:T(8,128)(2,1)S(1)} %slice.286, bf16[34,258,32]{1,2,0:T(8,128)(2,1)S(1)} %slice.281, bf16[3,3,32,96]{3,2,1,0:T(8,128)(2,1)S(1)} %copy-done.3), kind=kOutput, calls=%fused_computation.54 | convolution fusion | flops 54001664 | bytes 5660672 | tf_op jit(solution)/shard_map/hwc,oc->hwo/dot_general | solution.py:43
  67.4 2.2 %fusion.60 = bf16[11,32,256]{2,0,1:T(8,128)(2,1)S(1)} fusion(f32[32,256,32]{1,2,0:T(8,128)} %fusion.37, bf16[34,258,64]{1,2,0:T(8,128)(2,1)S(1)} %slice.286, bf16[34,258,32]{1,2,0:T(8,128)(2,1)S(1)} %slice.281, bf16[3,3,32,96]{3,2,1,0:T(8,128)(2,1)S(1)} %copy-done.3, bf16[11,32]{1,0:T(8,128)(2,1)S(1)} %copy-done.6), kind=kOutput, calls=%fused_computation.66 | convolution fusion | flops 60121088 | bytes 3747840 | tf_op jit(solution)/shard_map/oc,hwc->ohw/dot_general | solution.py:184
  69.6 0.7 %copy.57 = bf16[11,32,256]{2,1,0:T(8,128)(2,1)} copy(bf16[11,32,256]{2,0,1:T(8,128)(2,1)S(1)} %fusion.60) | data formatting | bytes 360448 | tf_op jit(solution)/shard_map/convert_element_type | solution.py:186
  (42 shorter events, 0.7 us)
Async XLA Ops:
  0.0 57.2 %copy-start = (bf16[3,3,64,64]{3,2,1,0:T(8,128)(2,1)S(1)}, bf16[3,3,64,64]{3,2,1,0:T(8,128)(2,1)}, u32[]{:S(2)}) copy-start(bf16[3,3,64,64]{3,2,1,0:T(8,128)(2,1)} %param.17) | copy-start | bytes 221188
  3.5 1.8 %copy-start.1 = (f32[8,32,256]{2,1,0:T(8,128)S(1)}, f32[8,32,256]{2,1,0:T(8,128)}, u32[]{:S(2)}) copy-start(f32[8,32,256]{2,1,0:T(8,128)} %get-tuple-element.7) | copy-start | bytes 786436
  3.5 1.8 %copy-start.5 = (f32[32,256]{1,0:T(8,128)S(1)}, f32[32,256]{1,0:T(8,128)}, u32[]{:S(2)}) copy-start(f32[32,256]{1,0:T(8,128)} %get-tuple-element.8) | copy-start | bytes 98308
  28.9 5.3 %collective-permute-start = (bf16[8,256,12]{1,2,0:T(8,128)(2,1)S(1)}, bf16[8,256,12]{1,2,0:T(8,128)(2,1)S(1)}, u32[]{:S(2)}, u32[]{:S(2)}) collective-permute-start(bf16[8,256,12]{1,2,0:T(8,128)(2,1)S(1)} %get-tuple-element.9), channel_id=1, source_target_pairs={{0,2},{2,4},{4,6},{1,3},{3,5},{5,7},{8,10},{10,12},{12,14},{9,11},... | collective-permute-start | bytes 147464 | tf_op jit(solution)/shard_map/ppermute | solution.py:27
  32.3 6.2 %collective-permute-start.1 = (bf16[8,256,12]{1,2,0:T(8,128)(2,1)S(1)}, bf16[8,256,12]{1,2,0:T(8,128)(2,1)S(1)}, u32[]{:S(2)}, u32[]{:S(2)}) collective-permute-start(bf16[8,256,12]{1,2,0:T(8,128)(2,1)S(1)} %get-tuple-element.10), channel_id=1, source_target_pairs={{2,0},{4,2},{6,4},{3,1},{5,3},{7,5},{10,8},{12,10},{14,12},{11,9},... | collective-permute-start | bytes 147464 | tf_op jit(solution)/shard_map/ppermute | solution.py:29
  33.7 6.8 %copy-start.4 = (bf16[3,3,32,12]{2,3,1,0:T(8,128)(2,1)S(1)}, bf16[3,3,32,12]{2,3,1,0:T(8,128)(2,1)}, u32[]{:S(2)}) copy-start(bf16[3,3,32,12]{2,3,1,0:T(8,128)(2,1)} %param.14) | copy-start | bytes 20740
  38.7 1.5 %collective-permute-start.2 = (bf16[48,8,12]{1,2,0:T(8,128)(2,1)S(1)}, bf16[48,8,12]{1,2,0:T(8,128)(2,1)S(1)}, u32[]{:S(2)}, u32[]{:S(2)}) collective-permute-start(bf16[48,8,12]{1,2,0:T(8,128)(2,1)S(1)} %slice_select_fusion.1), channel_id=1, source_target_pairs={{0,1},{1,0},{2,3},{3,2},{4,5},{5,4},{6,7},{7,6},{8,9},{9,8},{10,11... | collective-permute-start | bytes 27656 | tf_op jit(solution)/shard_map/ppermute | solution.py:19
  44.7 1.4 %copy-start.2 = (bf16[3,3,32,32]{3,2,1,0:T(8,128)(2,1)S(1)}, bf16[3,3,32,32]{3,2,1,0:T(8,128)(2,1)}, u32[]{:S(2)}) copy-start(bf16[3,3,32,32]{3,2,1,0:T(8,128)(2,1)} %param.15) | copy-start | bytes 55300
  53.6 0.9 %copy-start.7 = (bf16[3,3,64,32]{2,3,1,0:T(8,128)(2,1)S(1)}, bf16[3,3,64,32]{2,3,1,0:T(8,128)(2,1)}, u32[]{:S(2)}) copy-start(bf16[3,3,64,32]{2,3,1,0:T(8,128)(2,1)} %param.16) | copy-start | bytes 110596
  53.7 0.9 %copy-start.9 = (pred[8,17]{0,1:T(8,128)(4,1)S(1)}, pred[8,17]{0,1:T(8,128)(4,1)}, u32[]{:S(2)}) copy-start(pred[8,17]{0,1:T(8,128)(4,1)} %constant.114) | copy-start | bytes 412
  56.8 0.7 copy-start.8
  60.8 0.9 %copy-start.3 = (bf16[3,3,32,96]{3,2,1,0:T(8,128)(2,1)S(1)}, bf16[3,3,32,96]{3,2,1,0:T(8,128)(2,1)}, u32[]{:S(2)}) copy-start(bf16[3,3,32,96]{3,2,1,0:T(8,128)(2,1)} %param.18) | copy-start | bytes 165892
  66.0 1.4 %copy-start.6 = (bf16[11,32]{1,0:T(8,128)(2,1)S(1)}, bf16[11,32]{1,0:T(8,128)(2,1)}, u32[]{:S(2)}) copy-start(bf16[11,32]{1,0:T(8,128)(2,1)} %param.19) | copy-start | bytes 2116

commit v14 on v10

--- a/solution.py
+++ b/solution.py
@@ -155,7 +155,8 @@
 
     row0 = lax.axis_index("row") * block_rows
     col0 = lax.axis_index("col") * block_cols
-    widened = with_halo(composite.transpose(1, 2, 0), (("row", 0), ("col", 1)), HALO)
+    tall = with_halo(composite, (("row", 1),), HALO).transpose(1, 2, 0)
+    widened = with_halo(tall, (("col", 1),), HALO)
     first_map = masked_layer(widened, encode_first, row0 - HALO + 1, col0 - HALO + 1, total_rows, total_cols)
     skip_wide = masked_layer(first_map, encode_second, row0 - HALO + 2, col0 - HALO + 2, total_rows, total_cols)
     wide_rows, wide_cols, channels = skip_wide.shape

time: 69.5 us -> 69.5 us (level)
  no operation moved by 1% of the time
where the time goes in v14:
time: 69.5 us; the launch traced here: 69.1 us
  blocking collectives  22.8 us (33%)
  matrix products  22.6 us (33%)
  waiting for transfers between devices  5.76 us (8%)
  local copies, waits for them, and re-layouts  5.46 us (8%)
  other arithmetic  4.83 us (7%)
  starting transfers between devices  4.76 us (7%)
  Pallas kernels  2.34 us (3%)
    all_gather x1, blocking collectives, shards(): gathered = lax.all_gather(packed, 'tm', axis=0).astype(jnp.float32)  22.8 us
    dot_general x26, matrix products, valid_conv(): jnp.einsum('hwc,oc->hwo', padded[a:a + height, e:e + width], kernel[a, e]...  16.6 us
    ppermute x1, waiting for transfers between devices, with_halo(): lax.ppermute(head, axis, [((i + 1) % count, i) for i in range(ends)])  4.27 us
    ppermute x1, starting transfers between devices, with_halo(): lax.ppermute(tail, axis, [(i, (i + 1) % count) for i in range(ends)])  3.4 us
    conv_general_dilated x2, matrix products, native_conv(): lax.conv_general_dilated(padded[None], kernel, (1, 1), 'VALID', dimension...  2.89 us
    unnamed x22, local copies, waits for them, and re-layouts  2.63 us
    pallas_call x1, Pallas kernels, shifted_weights(): pl.pallas_call(weight_kernel, out_shape=(jax.ShapeDtypeStruct((dates, row...  2.34 us
    dot_general x1, matrix products, shards(): jnp.einsum('oc,hwc->ohw', head_weight, decoded, preferred_element_type=jn...  2.15 us
  transfers between devices with their start and end apart: 3, of which 3 were waited for; matrix products, arithmetic and copies ran while one was open for 1% of the time, Pallas kernels for 0%

profile of v14, /device:TPU:0, one launch (start us, length us, event | category | flops | bytes accessed | tf_op | source)
XLA Modules:
  0.0 69.1 jit_solution(9189375521811021132)
XLA Ops:
  0.0 2.3 %shard_map.100 = (f32[8,32,256]{2,1,0:T(8,128)}, f32[32,256]{1,0:T(8,128)}) custom-call(f32[12]{0:T(128)} %score_ref.1, s32[8,32,256]{2,1,0:T(8,128)} %class_ref.1, f32[8,32,256]{2,1,0:T(8,128)} %quality_ref.1), custom_call_target="tpu_custom_call" | custom-call | tf_op jit(solution)/shard_map/pallas_call | solution.py:104
  2.3 1.8 %multiply_reduce_fusion = bf16[12,32,256]{2,1,0:T(8,128)(2,1)S(1)} fusion(bf16[8,12,32,256]{3,2,1,0:T(8,128)(2,1)} %param.10, f32[8,32,256]{2,1,0:T(8,128)} %get-tuple-element.7), kind=kLoop, calls=%fused_computation.16 | loop fusion | flops 2260992 | bytes 2031616 | tf_op jit(solution)/shard_map/reduce_sum | solution.py:146
  4.2 22.8 %all_gather.4 = bf16[4,14,32,256]{3,2,1,0:T(8,128)(2,1)S(1)} all-gather(bf16[1,14,32,256]{3,2,1,0:T(8,128)(2,1)S(1)} %pad_maximum_fusion.15), channel_id=1, replica_groups=mesh['tm'=4,'row'=4,'col'=2] {'tm'}, dimensions={0}, use_global_device_ids=true | all-gather | bytes 1146880 | tf_op jit(solution)/shard_map/all_gather | solution.py:149
  27.0 0.2 convert_element_type.61
  27.3 0.2 fusion.28
  27.5 0.2 fusion.110
  27.8 3.4 %collective-permute-start = (bf16[12,8,256]{2,0,1:T(8,128)(2,1)S(1)}, bf16[12,8,256]{2,0,1:T(8,128)(2,1)S(1)}, u32[]{:S(2)}, u32[]{:S(2)}) collective-permute-start(bf16[12,8,256]{2,0,1:T(8,128)(2,1)S(1)} %get-tuple-element.9), channel_id=1, source_target_pairs={{0,2},{2,4},{4,6},{1,3},{3,5},{5,7},{8,10},{10,12},{12,14},{9,11},... | collective-permute-start | bytes 147464 | tf_op jit(solution)/shard_map/ppermute | solution.py:27
  31.2 1.3 %collective-permute-start.1 = (bf16[12,8,256]{2,0,1:T(8,128)(2,1)S(1)}, bf16[12,8,256]{2,0,1:T(8,128)(2,1)S(1)}, u32[]{:S(2)}, u32[]{:S(2)}) collective-permute-start(bf16[12,8,256]{2,0,1:T(8,128)(2,1)S(1)} %get-tuple-element.10), channel_id=1, source_target_pairs={{2,0},{4,2},{6,4},{3,1},{5,3},{7,5},{10,8},{12,10},{14,12},{11,9},... | collective-permute-start | bytes 147464 | tf_op jit(solution)/shard_map/ppermute | solution.py:29
  32.6 0.1 broadcast_and_fusion
  32.7 0.1 broadcast_and_fusion.1
  32.8 0.1 broadcast_and_fusion.2
  33.1 4.3 %collective-permute-done.1 = bf16[12,8,256]{2,0,1:T(8,128)(2,1)S(1)} collective-permute-done((bf16[12,8,256]{2,0,1:T(8,128)(2,1)S(1)}, bf16[12,8,256]{2,0,1:T(8,128)(2,1)S(1)}, u32[]{:S(2)}, u32[]{:S(2)}) %collective-permute-start.1) | collective-permute-done | bytes 49184 | tf_op jit(solution)/shard_map/ppermute | solution.py:29
  37.4 0.1 slice_select_fusion.1
  37.6 1.4 %collective-permute-done.2 = bf16[48,8,12]{1,2,0:T(8,128)(2,1)S(1)} collective-permute-done((bf16[48,8,12]{1,2,0:T(8,128)(2,1)S(1)}, bf16[48,8,12]{1,2,0:T(8,128)(2,1)S(1)}, u32[]{:S(2)}, u32[]{:S(2)}) %collective-permute-start.2) | collective-permute-done | bytes 9248 | tf_op jit(solution)/shard_map/ppermute | solution.py:19
  39.1 0.3 pad_maximum_fusion.14
  39.4 0.5 fusion.100
  39.9 0.5 fusion.102
  40.4 0.5 fusion.104
  40.9 0.5 fusion.106
  41.5 0.5 fusion.108
  41.9 0.5 fusion.94
  42.5 0.5 fusion.96
  43.0 0.5 fusion.98
  43.5 1.3 %select_convert_fusion = bf16[46,270,32]{1,2,0:T(8,128)(2,1)S(1)} fusion(f32[46,270,32]{1,2,0:T(8,128)S(1)} %fusion.94, f32[46,270,32]{1,2,0:T(8,128)S(1)} %fusion.96, f32[46,270,32]{1,2,0:T(8,128)S(1)} %fusion.98, f32[46,270,32]{1,2,0:T(8,128)S(1)} %fusion.100, f32[46,270,32]{1,2,0:T(8,128)S(1)} %fusion.102, f32[46,270,32]{1,2,0:T(8,128)S(1)} %fusion.104, ...), kind=kOutput, calls=%fused_computation.17 | convolution fusion | flops 13910400 | bytes 19470592 | tf_op jit(solution)/shard_map/hwc,oc->hwo/dot_general | solution.py:43
  44.8 0.5 fusion.62
  45.4 0.4 fusion.64
  45.8 0.5 fusion.66
  46.3 0.5 fusion.68
  46.9 0.4 fusion.70
  47.3 0.5 fusion.72
  47.8 0.5 fusion.74
  48.4 0.4 fusion.76
  48.8 1.6 %select_convert_fusion.1 = bf16[44,268,32]{1,2,0:T(8,128)(2,1)S(1)} fusion(f32[44,268,32]{1,2,0:T(8,128)S(1)} %fusion.62, f32[44,268,32]{1,2,0:T(8,128)S(1)} %fusion.64, f32[44,268,32]{1,2,0:T(8,128)S(1)} %fusion.66, f32[44,268,32]{1,2,0:T(8,128)S(1)} %fusion.68, f32[44,268,32]{1,2,0:T(8,128)S(1)} %fusion.70, f32[44,268,32]{1,2,0:T(8,128)S(1)} %fusion.72, ...), kind=kOutput, calls=%fused_computation.18 | convolution fusion | flops 28300800 | bytes 19164160 | tf_op jit(solution)/shard_map/hwc,oc->hwo/dot_general | solution.py:43
  50.4 0.4 slice.281
  50.8 0.6 fusion.116
  51.4 0.4 reduce_sum.49
  51.8 0.6 copy.60
  52.5 0.2 pad.clone
  52.7 0.1 copy.51
  52.8 0.5 copy-done.7
  53.4 1.3 %fusion.30 = bf16[20,8,17,64]{3,1,2,0:T(8,128)(2,1)S(1)} fusion(bf16[3,3,64,32]{2,3,1,0:T(8,128)(2,1)S(1)} %copy-done.7, bf16[22,1,7,2,32]{4,2,3,0,1:T(8,128)(2,1)S(1)} %slice.282, bf16[22,1,8,17,32]{4,2,3,0,1:T(8,128)(2,1)S(1)} %copy.51, pred[8,17]{0,1:T(8,128)(4,1)S(1)} %copy-done.9), kind=kOutput, calls=%fused_computation.47 | convolution fusion | flops 101434368 | bytes 596360 | tf_op jit(solution)/shard_map/conv_general_dilated | solution.py:54
  54.6 0.1 copy.52
  54.8 0.9 %fusion.1 = bf16[20,1,132,64]{3,0,2,1:T(8,128)(2,1)S(1)} fusion(bf16[20,1,136,64]{3,0,2,1:T(8,128)(2,1)S(1)} %bitcast.209, pred[20,132]{0,1:T(8,128)(4,1)S(1)} %broadcast_and_fusion.2), kind=kLoop, calls=%fused_computation.22 | loop fusion | flops 168960 | bytes 678480 | tf_op jit(solution)/shard_map/convert_element_type | solution.py:126
  55.7 0.2 pad.2
  55.8 0.1 copy.54
  56.0 0.3 copy-done.8
  56.3 1.6 %fusion.31 = bf16[18,8,17,64]{3,1,2,0:T(8,128)(2,1)S(1)} fusion(bf16[3,3,64,64]{3,2,1,0:T(8,128)(2,1)S(1)} %copy-done, bf16[20,1,7,2,64]{4,2,3,0,1:T(8,128)(2,1)S(1)} %slice.284, bf16[20,1,8,17,64]{4,2,3,0,1:T(8,128)(2,1)S(1)} %copy.54, pred[8,17]{0,1:T(8,128)(4,1)S(1)} %copy-done.8), kind=kOutput, calls=%fused_computation.50 | convolution fusion | flops 182123520 | bytes 771208 | tf_op jit(solution)/shard_map/conv_general_dilated | solution.py:54
  58.0 0.2 copy.55
  58.1 0.3 reshape.283
  58.5 0.4 copy.59
  58.9 0.5 fusion.55
  59.3 0.3 broadcast_in_dim.45
  59.6 0.2 slice.286
  59.8 0.7 %copy-done.3 = bf16[3,3,32,96]{3,2,1,0:T(8,128)(2,1)S(1)} copy-done((bf16[3,3,32,96]{3,2,1,0:T(8,128)(2,1)S(1)}, bf16[3,3,32,96]{3,2,1,0:T(8,128)(2,1)}, u32[]{:S(2)}) %copy-start.3) | copy-done | bytes 55320
  60.5 0.3 fusion.6
  60.9 0.7 %fusion.3 = f32[32,256,32]{1,2,0:T(8,128)S(1)} fusion(bf16[34,258,64]{1,2,0:T(8,128)(2,1)S(1)} %slice.286, bf16[34,258,32]{1,2,0:T(8,128)(2,1)S(1)} %slice.281, bf16[3,3,32,96]{3,2,1,0:T(8,128)(2,1)S(1)} %copy-done.3), kind=kOutput, calls=%fused_computation.24 | convolution fusion | flops 53477376 | bytes 3563520 | tf_op jit(solution)/shard_map/hwc,oc->hwo/dot_general | solution.py:43
  61.5 0.7 %fusion.52 = f32[32,256,32]{1,2,0:T(8,128)S(1)} fusion(f32[32,256,32]{1,2,0:T(8,128)S(1)} %fusion.6, bf16[34,258,64]{1,2,0:T(8,128)(2,1)S(1)} %slice.286, bf16[34,258,32]{1,2,0:T(8,128)(2,1)S(1)} %slice.281, bf16[3,3,32,96]{3,2,1,0:T(8,128)(2,1)S(1)} %copy-done.3), kind=kOutput, calls=%fused_computation.59 | convolution fusion | flops 53739520 | bytes 4612096 | tf_op jit(solution)/shard_map/hwc,oc->hwo/dot_general | solution.py:43
  62.3 0.7 %fusion.49 = f32[32,256,32]{1,2,0:T(8,128)S(1)} fusion(f32[32,256,32]{1,2,0:T(8,128)S(1)} %fusion.52, bf16[34,258,64]{1,2,0:T(8,128)(2,1)S(1)} %slice.286, bf16[34,258,32]{1,2,0:T(8,128)(2,1)S(1)} %slice.281, bf16[3,3,32,96]{3,2,1,0:T(8,128)(2,1)S(1)} %copy-done.3), kind=kOutput, calls=%fused_computation.58 | convolution fusion | flops 53739520 | bytes 4612096 | tf_op jit(solution)/shard_map/hwc,oc->hwo/dot_general | solution.py:43
  63.0 0.4 fusion.46
  63.4 0.7 %fusion.43 = f32[32,256,32]{1,2,0:T(8,128)S(1)} fusion(f32[32,256,32]{1,2,0:T(8,128)S(1)} %fusion.46, bf16[34,258,64]{1,2,0:T(8,128)(2,1)S(1)} %slice.286, bf16[34,258,32]{1,2,0:T(8,128)(2,1)S(1)} %slice.281, bf16[3,3,32,96]{3,2,1,0:T(8,128)(2,1)S(1)} %copy-done.3), kind=kOutput, calls=%fused_computation.56 | convolution fusion | flops 53739520 | bytes 4612096 | tf_op jit(solution)/shard_map/hwc,oc->hwo/dot_general | solution.py:43
  64.1 0.7 %fusion.40 = f32[32,256,32]{1,2,0:T(8,128)S(1)} fusion(f32[32,256,32]{1,2,0:T(8,128)S(1)} %fusion.43, bf16[34,258,64]{1,2,0:T(8,128)(2,1)S(1)} %slice.286, bf16[34,258,32]{1,2,0:T(8,128)(2,1)S(1)} %slice.281, bf16[3,3,32,96]{3,2,1,0:T(8,128)(2,1)S(1)} %copy-done.3), kind=kOutput, calls=%fused_computation.55 | convolution fusion | flops 53739520 | bytes 4612096 | tf_op jit(solution)/shard_map/hwc,oc->hwo/dot_general | solution.py:43
  64.9 1.4 %fusion.37 = f32[32,256,32]{1,2,0:T(8,128)} fusion(f32[32,256,32]{1,2,0:T(8,128)S(1)} %fusion.3, f32[32,256,32]{1,2,0:T(8,128)S(1)} %fusion.40, bf16[34,258,64]{1,2,0:T(8,128)(2,1)S(1)} %slice.286, bf16[34,258,32]{1,2,0:T(8,128)(2,1)S(1)} %slice.281, bf16[3,3,32,96]{3,2,1,0:T(8,128)(2,1)S(1)} %copy-done.3), kind=kOutput, calls=%fused_computation.54 | convolution fusion | flops 54001664 | bytes 5660672 | tf_op jit(solution)/shard_map/hwc,oc->hwo/dot_general | solution.py:43
  66.3 2.2 %fusion.60 = bf16[11,32,256]{2,0,1:T(8,128)(2,1)S(1)} fusion(f32[32,256,32]{1,2,0:T(8,128)} %fusion.37, bf16[34,258,64]{1,2,0:T(8,128)(2,1)S(1)} %slice.286, bf16[34,258,32]{1,2,0:T(8,128)(2,1)S(1)} %slice.281, bf16[3,3,32,96]{3,2,1,0:T(8,128)(2,1)S(1)} %copy-done.3, bf16[11,32]{1,0:T(8,128)(2,1)S(1)} %copy-done.6), kind=kOutput, calls=%fused_computation.66 | convolution fusion | flops 60121088 | bytes 3747840 | tf_op jit(solution)/shard_map/oc,hwc->ohw/dot_general | solution.py:190
  68.4 0.7 %copy.57 = bf16[11,32,256]{2,1,0:T(8,128)(2,1)} copy(bf16[11,32,256]{2,0,1:T(8,128)(2,1)S(1)} %fusion.60) | data formatting | bytes 360448 | tf_op jit(solution)/shard_map/convert_element_type | solution.py:192
  (42 shorter events, 0.7 us)
Async XLA Ops:
  0.0 56.0 %copy-start = (bf16[3,3,64,64]{3,2,1,0:T(8,128)(2,1)S(1)}, bf16[3,3,64,64]{3,2,1,0:T(8,128)(2,1)}, u32[]{:S(2)}) copy-start(bf16[3,3,64,64]{3,2,1,0:T(8,128)(2,1)} %param.17) | copy-start | bytes 221188
  2.3 1.8 %copy-start.1 = (f32[8,32,256]{2,1,0:T(8,128)S(1)}, f32[8,32,256]{2,1,0:T(8,128)}, u32[]{:S(2)}) copy-start(f32[8,32,256]{2,1,0:T(8,128)} %get-tuple-element.7) | copy-start | bytes 786436
  2.3 1.8 %copy-start.5 = (f32[32,256]{1,0:T(8,128)S(1)}, f32[32,256]{1,0:T(8,128)}, u32[]{:S(2)}) copy-start(f32[32,256]{1,0:T(8,128)} %get-tuple-element.8) | copy-start | bytes 98308
  27.8 5.3 %collective-permute-start = (bf16[12,8,256]{2,0,1:T(8,128)(2,1)S(1)}, bf16[12,8,256]{2,0,1:T(8,128)(2,1)S(1)}, u32[]{:S(2)}, u32[]{:S(2)}) collective-permute-start(bf16[12,8,256]{2,0,1:T(8,128)(2,1)S(1)} %get-tuple-element.9), channel_id=1, source_target_pairs={{0,2},{2,4},{4,6},{1,3},{3,5},{5,7},{8,10},{10,12},{12,14},{9,11},... | collective-permute-start | bytes 147464 | tf_op jit(solution)/shard_map/ppermute | solution.py:27
  31.2 6.2 %collective-permute-start.1 = (bf16[12,8,256]{2,0,1:T(8,128)(2,1)S(1)}, bf16[12,8,256]{2,0,1:T(8,128)(2,1)S(1)}, u32[]{:S(2)}, u32[]{:S(2)}) collective-permute-start(bf16[12,8,256]{2,0,1:T(8,128)(2,1)S(1)} %get-tuple-element.10), channel_id=1, source_target_pairs={{2,0},{4,2},{6,4},{3,1},{5,3},{7,5},{10,8},{12,10},{14,12},{11,9},... | collective-permute-start | bytes 147464 | tf_op jit(solution)/shard_map/ppermute | solution.py:29
  32.6 6.8 %copy-start.4 = (bf16[3,3,32,12]{2,3,1,0:T(8,128)(2,1)S(1)}, bf16[3,3,32,12]{2,3,1,0:T(8,128)(2,1)}, u32[]{:S(2)}) copy-start(bf16[3,3,32,12]{2,3,1,0:T(8,128)(2,1)} %param.14) | copy-start | bytes 20740
  37.5 1.5 %collective-permute-start.2 = (bf16[48,8,12]{1,2,0:T(8,128)(2,1)S(1)}, bf16[48,8,12]{1,2,0:T(8,128)(2,1)S(1)}, u32[]{:S(2)}, u32[]{:S(2)}) collective-permute-start(bf16[48,8,12]{1,2,0:T(8,128)(2,1)S(1)} %slice_select_fusion.1), channel_id=1, source_target_pairs={{0,1},{1,0},{2,3},{3,2},{4,5},{5,4},{6,7},{7,6},{8,9},{9,8},{10,11... | collective-permute-start | bytes 27656 | tf_op jit(solution)/shard_map/ppermute | solution.py:19
  43.5 1.4 %copy-start.2 = (bf16[3,3,32,32]{3,2,1,0:T(8,128)(2,1)S(1)}, bf16[3,3,32,32]{3,2,1,0:T(8,128)(2,1)}, u32[]{:S(2)}) copy-start(bf16[3,3,32,32]{3,2,1,0:T(8,128)(2,1)} %param.15) | copy-start | bytes 55300
  52.5 0.9 %copy-start.7 = (bf16[3,3,64,32]{2,3,1,0:T(8,128)(2,1)S(1)}, bf16[3,3,64,32]{2,3,1,0:T(8,128)(2,1)}, u32[]{:S(2)}) copy-start(bf16[3,3,64,32]{2,3,1,0:T(8,128)(2,1)} %param.16) | copy-start | bytes 110596
  52.5 0.9 %copy-start.9 = (pred[8,17]{0,1:T(8,128)(4,1)S(1)}, pred[8,17]{0,1:T(8,128)(4,1)}, u32[]{:S(2)}) copy-start(pred[8,17]{0,1:T(8,128)(4,1)} %constant.114) | copy-start | bytes 412
  55.6 0.7 copy-start.8
  59.6 0.9 %copy-start.3 = (bf16[3,3,32,96]{3,2,1,0:T(8,128)(2,1)S(1)}, bf16[3,3,32,96]{3,2,1,0:T(8,128)(2,1)}, u32[]{:S(2)}) copy-start(bf16[3,3,32,96]{3,2,1,0:T(8,128)(2,1)} %param.18) | copy-start | bytes 165892
  64.9 1.4 %copy-start.6 = (bf16[11,32]{1,0:T(8,128)(2,1)S(1)}, bf16[11,32]{1,0:T(8,128)(2,1)}, u32[]{:S(2)}) copy-start(bf16[11,32]{1,0:T(8,128)(2,1)} %param.19) | copy-start | bytes 2116

commit v15 on v10

--- a/solution.py
+++ b/solution.py
@@ -159,11 +159,14 @@
     first_map = masked_layer(widened, encode_first, row0 - HALO + 1, col0 - HALO + 1, total_rows, total_cols)
     skip_wide = masked_layer(first_map, encode_second, row0 - HALO + 2, col0 - HALO + 2, total_rows, total_cols)
     wide_rows, wide_cols, channels = skip_wide.shape
-    col_pairs = jnp.einsum(
-        "vw,hwc->hvc", pair_matrix(wide_cols // 2, wide_cols, 0), skip_wide, preferred_element_type=jnp.float32
-    )
     pooled = (
-        jnp.sum(col_pairs.reshape(wide_rows // 2, 2, wide_cols // 2, channels), axis=1) * 0.25
+        jnp.einsum(
+            "vw,hrwc->hvc",
+            pair_matrix(wide_cols // 2, wide_cols, 0),
+            skip_wide.reshape(wide_rows // 2, 2, wide_cols, channels),
+            preferred_element_type=jnp.float32,
+        )
+        * 0.25
     ).astype(jnp.bfloat16)
     coarse_halo = (HALO - 2) // 2
     crow0 = row0 // 2 - coarse_halo

time: 69.5 us -> 69.2 us (level)
  no operation moved by 1% of the time
where the time goes in v15:
time: 69.2 us; the launch traced here: 68.8 us
  blocking collectives  22.8 us (33%)
  matrix products  22.4 us (32%)
  waiting for transfers between devices  5.76 us (8%)
  local copies, waits for them, and re-layouts  5.63 us (8%)
  starting transfers between devices  4.76 us (7%)
  other arithmetic  4.57 us (7%)
  Pallas kernels  2.34 us (3%)
    all_gather x1, blocking collectives, shards(): gathered = lax.all_gather(packed, 'tm', axis=0).astype(jnp.float32)  22.8 us
    dot_general x26, matrix products, valid_conv(): jnp.einsum('hwc,oc->hwo', padded[a:a + height, e:e + width], kernel[a, e]...  16.6 us
    ppermute x1, waiting for transfers between devices, with_halo(): lax.ppermute(head, axis, [((i + 1) % count, i) for i in range(ends)])  4.27 us
    ppermute x1, starting transfers between devices, with_halo(): lax.ppermute(tail, axis, [(i, (i + 1) % count) for i in range(ends)])  3.4 us
    conv_general_dilated x2, matrix products, native_conv(): lax.conv_general_dilated(padded[None], kernel, (1, 1), 'VALID', dimension...  2.88 us
    unnamed x22, local copies, waits for them, and re-layouts  2.8 us
    pallas_call x1, Pallas kernels, shifted_weights(): pl.pallas_call(weight_kernel, out_shape=(jax.ShapeDtypeStruct((dates, row...  2.34 us
    dot_general x1, matrix products, shards(): jnp.einsum('oc,hwc->ohw', head_weight, decoded, preferred_element_type=jn...  2.15 us
  transfers between devices with their start and end apart: 3, of which 3 were waited for; matrix products, arithmetic and copies ran while one was open for 1% of the time, Pallas kernels for 0%

profile of v15, /device:TPU:0, one launch (start us, length us, event | category | flops | bytes accessed | tf_op | source)
XLA Modules:
  0.0 68.8 jit_solution(15087910447946520009)
XLA Ops:
  0.0 2.3 %shard_map.100 = (f32[8,32,256]{2,1,0:T(8,128)}, f32[32,256]{1,0:T(8,128)}) custom-call(f32[12]{0:T(128)} %score_ref.1, s32[8,32,256]{2,1,0:T(8,128)} %class_ref.1, f32[8,32,256]{2,1,0:T(8,128)} %quality_ref.1), custom_call_target="tpu_custom_call" | custom-call | tf_op jit(solution)/shard_map/pallas_call | solution.py:104
  2.3 1.8 %multiply_reduce_fusion = bf16[12,32,256]{2,1,0:T(8,128)(2,1)S(1)} fusion(bf16[8,12,32,256]{3,2,1,0:T(8,128)(2,1)} %param.10, f32[8,32,256]{2,1,0:T(8,128)} %get-tuple-element.7), kind=kLoop, calls=%fused_computation.16 | loop fusion | flops 2260992 | bytes 2031616 | tf_op jit(solution)/shard_map/reduce_sum | solution.py:146
  4.2 22.8 %all_gather.4 = bf16[4,14,32,256]{3,2,1,0:T(8,128)(2,1)S(1)} all-gather(bf16[1,14,32,256]{3,2,1,0:T(8,128)(2,1)S(1)} %pad_maximum_fusion.16), channel_id=1, replica_groups=mesh['tm'=4,'row'=4,'col'=2] {'tm'}, dimensions={0}, use_global_device_ids=true | all-gather | bytes 1146880 | tf_op jit(solution)/shard_map/all_gather | solution.py:149
  27.0 0.2 convert_element_type.64
  27.3 0.2 fusion.28
  27.5 0.2 fusion.116
  27.8 3.4 %collective-permute-start = (bf16[8,256,12]{1,2,0:T(8,128)(2,1)S(1)}, bf16[8,256,12]{1,2,0:T(8,128)(2,1)S(1)}, u32[]{:S(2)}, u32[]{:S(2)}) collective-permute-start(bf16[8,256,12]{1,2,0:T(8,128)(2,1)S(1)} %get-tuple-element.9), channel_id=1, source_target_pairs={{0,2},{2,4},{4,6},{1,3},{3,5},{5,7},{8,10},{10,12},{12,14},{9,11},... | collective-permute-start | bytes 147464 | tf_op jit(solution)/shard_map/ppermute | solution.py:27
  31.2 1.3 %collective-permute-start.1 = (bf16[8,256,12]{1,2,0:T(8,128)(2,1)S(1)}, bf16[8,256,12]{1,2,0:T(8,128)(2,1)S(1)}, u32[]{:S(2)}, u32[]{:S(2)}) collective-permute-start(bf16[8,256,12]{1,2,0:T(8,128)(2,1)S(1)} %get-tuple-element.10), channel_id=1, source_target_pairs={{2,0},{4,2},{6,4},{3,1},{5,3},{7,5},{10,8},{12,10},{14,12},{11,9},... | collective-permute-start | bytes 147464 | tf_op jit(solution)/shard_map/ppermute | solution.py:29
  32.6 0.1 broadcast_and_fusion
  32.7 0.1 broadcast_and_fusion.1
  32.8 0.1 broadcast_and_fusion.2
  33.1 4.3 %collective-permute-done.1 = bf16[8,256,12]{1,2,0:T(8,128)(2,1)S(1)} collective-permute-done((bf16[8,256,12]{1,2,0:T(8,128)(2,1)S(1)}, bf16[8,256,12]{1,2,0:T(8,128)(2,1)S(1)}, u32[]{:S(2)}, u32[]{:S(2)}) %collective-permute-start.1) | collective-permute-done | bytes 49184 | tf_op jit(solution)/shard_map/ppermute | solution.py:29
  37.4 0.1 slice_select_fusion.1
  37.6 1.4 %collective-permute-done.2 = bf16[48,8,12]{1,2,0:T(8,128)(2,1)S(1)} collective-permute-done((bf16[48,8,12]{1,2,0:T(8,128)(2,1)S(1)}, bf16[48,8,12]{1,2,0:T(8,128)(2,1)S(1)}, u32[]{:S(2)}, u32[]{:S(2)}) %collective-permute-start.2) | collective-permute-done | bytes 9248 | tf_op jit(solution)/shard_map/ppermute | solution.py:19
  39.1 0.3 pad_maximum_fusion.14
  39.4 0.5 fusion.100
  39.9 0.5 fusion.102
  40.5 0.5 fusion.104
  40.9 0.5 fusion.106
  41.5 0.5 fusion.108
  42.0 0.5 fusion.110
  42.5 0.5 fusion.96
  43.0 0.5 fusion.98
  43.5 1.3 %select_convert_fusion = bf16[46,270,32]{1,2,0:T(8,128)(2,1)S(1)} fusion(f32[46,270,32]{1,2,0:T(8,128)S(1)} %fusion.96, f32[46,270,32]{1,2,0:T(8,128)S(1)} %fusion.98, f32[46,270,32]{1,2,0:T(8,128)S(1)} %fusion.100, f32[46,270,32]{1,2,0:T(8,128)S(1)} %fusion.102, f32[46,270,32]{1,2,0:T(8,128)S(1)} %fusion.104, f32[46,270,32]{1,2,0:T(8,128)S(1)} %fusion.106, ...), kind=kOutput, calls=%fused_computation.17 | convolution fusion | flops 13910400 | bytes 19470592 | tf_op jit(solution)/shard_map/hwc,oc->hwo/dot_general | solution.py:43
  44.8 0.5 fusion.64
  45.4 0.4 fusion.66
  45.8 0.5 fusion.68
  46.3 0.5 fusion.70
  46.9 0.4 fusion.72
  47.3 0.5 fusion.74
  47.8 0.5 fusion.76
  48.4 0.4 fusion.78
  48.8 1.6 %select_convert_fusion.1 = bf16[44,268,32]{1,2,0:T(8,128)(2,1)S(1)} fusion(f32[44,268,32]{1,2,0:T(8,128)S(1)} %fusion.64, f32[44,268,32]{1,2,0:T(8,128)S(1)} %fusion.66, f32[44,268,32]{1,2,0:T(8,128)S(1)} %fusion.68, f32[44,268,32]{1,2,0:T(8,128)S(1)} %fusion.70, f32[44,268,32]{1,2,0:T(8,128)S(1)} %fusion.72, f32[44,268,32]{1,2,0:T(8,128)S(1)} %fusion.74, ...), kind=kOutput, calls=%fused_computation.19 | convolution fusion | flops 28300800 | bytes 19164160 | tf_op jit(solution)/shard_map/hwc,oc->hwo/dot_general | solution.py:43
  50.4 0.4 slice.281
  50.8 0.2 convert_reduce_fusion
  51.0 0.4 fusion.60
  51.4 0.8 %copy.63 = bf16[22,1,134,32]{3,0,2,1:T(8,128)(2,1)S(1)} copy(bf16[22,1,134,32]{2,3,0,1:T(8,128)(2,1)S(1)} %fusion.60) | data formatting | bytes 377344
  52.2 0.2 pad.clone
  52.4 0.1 copy.54
  52.5 0.5 copy-done.7
  53.1 1.3 %fusion.30 = bf16[20,8,17,64]{3,1,2,0:T(8,128)(2,1)S(1)} fusion(bf16[3,3,64,32]{2,3,1,0:T(8,128)(2,1)S(1)} %copy-done.7, bf16[22,1,7,2,32]{4,2,3,0,1:T(8,128)(2,1)S(1)} %slice.282, bf16[22,1,8,17,32]{4,2,3,0,1:T(8,128)(2,1)S(1)} %copy.54, pred[8,17]{0,1:T(8,128)(4,1)S(1)} %copy-done.9), kind=kOutput, calls=%fused_computation.48 | convolution fusion | flops 101434368 | bytes 596360 | tf_op jit(solution)/shard_map/conv_general_dilated | solution.py:54
  54.3 0.1 copy.55
  54.5 0.9 %fusion.1 = bf16[20,1,132,64]{3,0,2,1:T(8,128)(2,1)S(1)} fusion(bf16[20,1,136,64]{3,0,2,1:T(8,128)(2,1)S(1)} %bitcast.210, pred[20,132]{0,1:T(8,128)(4,1)S(1)} %broadcast_and_fusion.2), kind=kLoop, calls=%fused_computation.23 | loop fusion | flops 168960 | bytes 678480 | tf_op jit(solution)/shard_map/convert_element_type | solution.py:126
  55.4 0.2 pad.2
  55.5 0.1 copy.57
  55.7 0.3 copy-done.8
  56.0 1.6 %fusion.31 = bf16[18,8,17,64]{3,1,2,0:T(8,128)(2,1)S(1)} fusion(bf16[3,3,64,64]{3,2,1,0:T(8,128)(2,1)S(1)} %copy-done, bf16[20,1,7,2,64]{4,2,3,0,1:T(8,128)(2,1)S(1)} %slice.284, bf16[20,1,8,17,64]{4,2,3,0,1:T(8,128)(2,1)S(1)} %copy.57, pred[8,17]{0,1:T(8,128)(4,1)S(1)} %copy-done.8), kind=kOutput, calls=%fused_computation.51 | convolution fusion | flops 182123520 | bytes 771208 | tf_op jit(solution)/shard_map/conv_general_dilated | solution.py:54
  57.7 0.2 copy.58
  57.8 0.3 reshape.269
  58.1 0.4 copy.62
  58.6 0.5 fusion.55
  59.0 0.3 broadcast_in_dim.48
  59.3 0.2 slice.286
  59.5 0.7 %copy-done.3 = bf16[3,3,32,96]{3,2,1,0:T(8,128)(2,1)S(1)} copy-done((bf16[3,3,32,96]{3,2,1,0:T(8,128)(2,1)S(1)}, bf16[3,3,32,96]{3,2,1,0:T(8,128)(2,1)}, u32[]{:S(2)}) %copy-start.3) | copy-done | bytes 55320
  60.2 0.3 fusion.6
  60.6 0.7 %fusion.3 = f32[32,256,32]{1,2,0:T(8,128)S(1)} fusion(bf16[34,258,64]{1,2,0:T(8,128)(2,1)S(1)} %slice.286, bf16[34,258,32]{1,2,0:T(8,128)(2,1)S(1)} %slice.281, bf16[3,3,32,96]{3,2,1,0:T(8,128)(2,1)S(1)} %copy-done.3), kind=kOutput, calls=%fused_computation.25 | convolution fusion | flops 53477376 | bytes 3563520 | tf_op jit(solution)/shard_map/hwc,oc->hwo/dot_general | solution.py:43
  61.2 0.7 %fusion.52 = f32[32,256,32]{1,2,0:T(8,128)S(1)} fusion(f32[32,256,32]{1,2,0:T(8,128)S(1)} %fusion.6, bf16[34,258,64]{1,2,0:T(8,128)(2,1)S(1)} %slice.286, bf16[34,258,32]{1,2,0:T(8,128)(2,1)S(1)} %slice.281, bf16[3,3,32,96]{3,2,1,0:T(8,128)(2,1)S(1)} %copy-done.3), kind=kOutput, calls=%fused_computation.60 | convolution fusion | flops 53739520 | bytes 4612096 | tf_op jit(solution)/shard_map/hwc,oc->hwo/dot_general | solution.py:43
  62.0 0.7 %fusion.49 = f32[32,256,32]{1,2,0:T(8,128)S(1)} fusion(f32[32,256,32]{1,2,0:T(8,128)S(1)} %fusion.52, bf16[34,258,64]{1,2,0:T(8,128)(2,1)S(1)} %slice.286, bf16[34,258,32]{1,2,0:T(8,128)(2,1)S(1)} %slice.281, bf16[3,3,32,96]{3,2,1,0:T(8,128)(2,1)S(1)} %copy-done.3), kind=kOutput, calls=%fused_computation.59 | convolution fusion | flops 53739520 | bytes 4612096 | tf_op jit(solution)/shard_map/hwc,oc->hwo/dot_general | solution.py:43
  62.7 0.4 fusion.46
  63.1 0.7 %fusion.43 = f32[32,256,32]{1,2,0:T(8,128)S(1)} fusion(f32[32,256,32]{1,2,0:T(8,128)S(1)} %fusion.46, bf16[34,258,64]{1,2,0:T(8,128)(2,1)S(1)} %slice.286, bf16[34,258,32]{1,2,0:T(8,128)(2,1)S(1)} %slice.281, bf16[3,3,32,96]{3,2,1,0:T(8,128)(2,1)S(1)} %copy-done.3), kind=kOutput, calls=%fused_computation.57 | convolution fusion | flops 53739520 | bytes 4612096 | tf_op jit(solution)/shard_map/hwc,oc->hwo/dot_general | solution.py:43
  63.8 0.7 %fusion.40 = f32[32,256,32]{1,2,0:T(8,128)S(1)} fusion(f32[32,256,32]{1,2,0:T(8,128)S(1)} %fusion.43, bf16[34,258,64]{1,2,0:T(8,128)(2,1)S(1)} %slice.286, bf16[34,258,32]{1,2,0:T(8,128)(2,1)S(1)} %slice.281, bf16[3,3,32,96]{3,2,1,0:T(8,128)(2,1)S(1)} %copy-done.3), kind=kOutput, calls=%fused_computation.56 | convolution fusion | flops 53739520 | bytes 4612096 | tf_op jit(solution)/shard_map/hwc,oc->hwo/dot_general | solution.py:43
  64.6 1.4 %fusion.37 = f32[32,256,32]{1,2,0:T(8,128)} fusion(f32[32,256,32]{1,2,0:T(8,128)S(1)} %fusion.3, f32[32,256,32]{1,2,0:T(8,128)S(1)} %fusion.40, bf16[34,258,64]{1,2,0:T(8,128)(2,1)S(1)} %slice.286, bf16[34,258,32]{1,2,0:T(8,128)(2,1)S(1)} %slice.281, bf16[3,3,32,96]{3,2,1,0:T(8,128)(2,1)S(1)} %copy-done.3), kind=kOutput, calls=%fused_computation.55 | convolution fusion | flops 54001664 | bytes 5660672 | tf_op jit(solution)/shard_map/hwc,oc->hwo/dot_general | solution.py:43
  65.9 2.2 %fusion.62 = bf16[11,32,256]{2,0,1:T(8,128)(2,1)S(1)} fusion(f32[32,256,32]{1,2,0:T(8,128)} %fusion.37, bf16[34,258,64]{1,2,0:T(8,128)(2,1)S(1)} %slice.286, bf16[34,258,32]{1,2,0:T(8,128)(2,1)S(1)} %slice.281, bf16[3,3,32,96]{3,2,1,0:T(8,128)(2,1)S(1)} %copy-done.3, bf16[11,32]{1,0:T(8,128)(2,1)S(1)} %copy-done.6), kind=kOutput, calls=%fused_computation.70 | convolution fusion | flops 60121088 | bytes 3747840 | tf_op jit(solution)/shard_map/oc,hwc->ohw/dot_general | solution.py:192
  68.1 0.7 %copy.60 = bf16[11,32,256]{2,1,0:T(8,128)(2,1)} copy(bf16[11,32,256]{2,0,1:T(8,128)(2,1)S(1)} %fusion.62) | data formatting | bytes 360448 | tf_op jit(solution)/shard_map/convert_element_type | solution.py:194
  (41 shorter events, 0.6 us)
Async XLA Ops:
  0.0 55.7 %copy-start = (bf16[3,3,64,64]{3,2,1,0:T(8,128)(2,1)S(1)}, bf16[3,3,64,64]{3,2,1,0:T(8,128)(2,1)}, u32[]{:S(2)}) copy-start(bf16[3,3,64,64]{3,2,1,0:T(8,128)(2,1)} %param.17) | copy-start | bytes 221188
  2.3 1.8 %copy-start.1 = (f32[8,32,256]{2,1,0:T(8,128)S(1)}, f32[8,32,256]{2,1,0:T(8,128)}, u32[]{:S(2)}) copy-start(f32[8,32,256]{2,1,0:T(8,128)} %get-tuple-element.7) | copy-start | bytes 786436
  2.3 1.8 %copy-start.5 = (f32[32,256]{1,0:T(8,128)S(1)}, f32[32,256]{1,0:T(8,128)}, u32[]{:S(2)}) copy-start(f32[32,256]{1,0:T(8,128)} %get-tuple-element.8) | copy-start | bytes 98308
  27.8 5.3 %collective-permute-start = (bf16[8,256,12]{1,2,0:T(8,128)(2,1)S(1)}, bf16[8,256,12]{1,2,0:T(8,128)(2,1)S(1)}, u32[]{:S(2)}, u32[]{:S(2)}) collective-permute-start(bf16[8,256,12]{1,2,0:T(8,128)(2,1)S(1)} %get-tuple-element.9), channel_id=1, source_target_pairs={{0,2},{2,4},{4,6},{1,3},{3,5},{5,7},{8,10},{10,12},{12,14},{9,11},... | collective-permute-start | bytes 147464 | tf_op jit(solution)/shard_map/ppermute | solution.py:27
  31.2 6.2 %collective-permute-start.1 = (bf16[8,256,12]{1,2,0:T(8,128)(2,1)S(1)}, bf16[8,256,12]{1,2,0:T(8,128)(2,1)S(1)}, u32[]{:S(2)}, u32[]{:S(2)}) collective-permute-start(bf16[8,256,12]{1,2,0:T(8,128)(2,1)S(1)} %get-tuple-element.10), channel_id=1, source_target_pairs={{2,0},{4,2},{6,4},{3,1},{5,3},{7,5},{10,8},{12,10},{14,12},{11,9},... | collective-permute-start | bytes 147464 | tf_op jit(solution)/shard_map/ppermute | solution.py:29
  32.6 6.8 %copy-start.4 = (bf16[3,3,32,12]{2,3,1,0:T(8,128)(2,1)S(1)}, bf16[3,3,32,12]{2,3,1,0:T(8,128)(2,1)}, u32[]{:S(2)}) copy-start(bf16[3,3,32,12]{2,3,1,0:T(8,128)(2,1)} %param.14) | copy-start | bytes 20740
  37.5 1.5 %collective-permute-start.2 = (bf16[48,8,12]{1,2,0:T(8,128)(2,1)S(1)}, bf16[48,8,12]{1,2,0:T(8,128)(2,1)S(1)}, u32[]{:S(2)}, u32[]{:S(2)}) collective-permute-start(bf16[48,8,12]{1,2,0:T(8,128)(2,1)S(1)} %slice_select_fusion.1), channel_id=1, source_target_pairs={{0,1},{1,0},{2,3},{3,2},{4,5},{5,4},{6,7},{7,6},{8,9},{9,8},{10,11... | collective-permute-start | bytes 27656 | tf_op jit(solution)/shard_map/ppermute | solution.py:19
  43.5 1.4 %copy-start.2 = (bf16[3,3,32,32]{3,2,1,0:T(8,128)(2,1)S(1)}, bf16[3,3,32,32]{3,2,1,0:T(8,128)(2,1)}, u32[]{:S(2)}) copy-start(bf16[3,3,32,32]{3,2,1,0:T(8,128)(2,1)} %param.15) | copy-start | bytes 55300
  52.2 0.9 %copy-start.7 = (bf16[3,3,64,32]{2,3,1,0:T(8,128)(2,1)S(1)}, bf16[3,3,64,32]{2,3,1,0:T(8,128)(2,1)}, u32[]{:S(2)}) copy-start(bf16[3,3,64,32]{2,3,1,0:T(8,128)(2,1)} %param.16) | copy-start | bytes 110596
  52.2 0.9 %copy-start.9 = (pred[8,17]{0,1:T(8,128)(4,1)S(1)}, pred[8,17]{0,1:T(8,128)(4,1)}, u32[]{:S(2)}) copy-start(pred[8,17]{0,1:T(8,128)(4,1)} %constant.114) | copy-start | bytes 412
  55.3 0.7 copy-start.8
  59.3 0.9 %copy-start.3 = (bf16[3,3,32,96]{3,2,1,0:T(8,128)(2,1)S(1)}, bf16[3,3,32,96]{3,2,1,0:T(8,128)(2,1)}, u32[]{:S(2)}) copy-start(bf16[3,3,32,96]{3,2,1,0:T(8,128)(2,1)} %param.18) | copy-start | bytes 165892
  64.6 1.4 %copy-start.6 = (bf16[11,32]{1,0:T(8,128)(2,1)S(1)}, bf16[11,32]{1,0:T(8,128)(2,1)}, u32[]{:S(2)}) copy-start(bf16[11,32]{1,0:T(8,128)(2,1)} %param.19) | copy-start | bytes 2116

commit v16 on v15

--- a/solution.py
+++ b/solution.py
@@ -66,10 +66,10 @@
     return (jnp.arange(narrow, dtype=jnp.int32)[:, None] == pick[None, :]).astype(jnp.bfloat16)
 
 
-def weight_kernel(score_ref, class_ref, quality_ref, weight_ref, shift_ref):
+def weight_kernel(score_ref, class_ref, quality_ref, weight_ref, shift_ref, value_ref):
     dates, rows, _ = class_ref.shape
     classes = score_ref.shape[0]
-    step = 16
+    step = value_ref.shape[1]
 
     def chunk(index, carry):
         at = pl.ds(pl.multiple_of(index * step, step), step)
@@ -80,16 +80,16 @@
             for k in range(classes):
                 looked = jnp.where(label == k, score_ref[k], looked)
             value = looked + quality_ref[date, at, :]
-            weight_ref[date, at, :] = value
+            value_ref[date] = value
             return jnp.maximum(top, value)
 
-        start = jnp.full((step, weight_ref.shape[2]), -jnp.inf, jnp.float32)
+        start = jnp.full((step, value_ref.shape[2]), -jnp.inf, jnp.float32)
         top = lax.fori_loop(0, dates, score, start)
         shift = top.astype(jnp.bfloat16).astype(jnp.float32)
         shift_ref[at, :] = shift
 
         def one_date(date, inner):
-            weight_ref[date, at, :] = jnp.exp(weight_ref[date, at, :] - shift)
+            weight_ref[date, at, :] = jnp.exp(value_ref[date] - shift).astype(weight_ref.dtype)
             return inner
 
         lax.fori_loop(0, dates, one_date, 0)
@@ -104,11 +104,12 @@
     return pl.pallas_call(
         weight_kernel,
         out_shape=(
-            jax.ShapeDtypeStruct((dates, rows, cols), jnp.float32),
+            jax.ShapeDtypeStruct((dates, rows, cols), jnp.bfloat16),
             jax.ShapeDtypeStruct((rows, cols), jnp.float32),
         ),
         in_specs=[pl.BlockSpec(memory_space=pltpu.SMEM), vmem, vmem],
         out_specs=(vmem, vmem),
+        scratch_shapes=[pltpu.VMEM((dates, 16, cols), jnp.float32)],
     )(class_score, scene_class, quality)
 
 
@@ -143,7 +144,8 @@
     total_rows = block_rows * lax.axis_size("row")
     total_cols = block_cols * lax.axis_size("col")
     weights, shift = shifted_weights(class_score, scene_class, quality)
-    part_sums = jnp.sum(weights[:, None] * reflectance, axis=0)
+    weights = weights.astype(jnp.float32)
+    part_sums = jnp.sum(weights[:, None] * reflectance.astype(jnp.float32), axis=0)
     part_total = jnp.sum(weights, axis=0)
     packed = jnp.concatenate([part_sums, part_total[None], shift[None]], axis=0).astype(jnp.bfloat16)
     gathered = lax.all_gather(packed, "tm", axis=0).astype(jnp.float32)

time: 69.2 us -> 70.9 us (1.025)
  other arithmetic: 4.57 us -> 6.26 us
    convert_element_type x0 -> x1, other arithmetic: none -> 1.01 us  [shards(): weights = weights.astype(jnp.float32)]
    concatenate x2, other arithmetic: 0.04 us -> 0.8 us  [shards(): jnp.concatenate([part_sums, part_total[None], shift[None]], axis=0)]
    reduce_sum x2 -> x1, other arithmetic: 1.82 us -> 1.74 us  [shards(): jnp.sum(weights[:, None] * reflectance.astype(jnp.float32), axis=0)]
    unnamed x22 -> x18, local copies, waits for them, and re-layouts: 2.8 us -> 2.79 us
where the time goes in v16:
time: 70.9 us; the launch traced here: 70.5 us
  blocking collectives  22.8 us (32%)
  matrix products  22.5 us (32%)
  other arithmetic  6.26 us (9%)
  waiting for transfers between devices  5.76 us (8%)
  local copies, waits for them, and re-layouts  5.63 us (8%)
  starting transfers between devices  4.76 us (7%)
  Pallas kernels  2.3 us (3%)
    all_gather x1, blocking collectives, shards(): gathered = lax.all_gather(packed, 'tm', axis=0).astype(jnp.float32)  22.8 us
    dot_general x26, matrix products, valid_conv(): jnp.einsum('hwc,oc->hwo', padded[a:a + height, e:e + width], kernel[a, e]...  16.6 us
    ppermute x1, waiting for transfers between devices, with_halo(): lax.ppermute(head, axis, [((i + 1) % count, i) for i in range(ends)])  4.27 us
    ppermute x1, starting transfers between devices, with_halo(): lax.ppermute(tail, axis, [(i, (i + 1) % count) for i in range(ends)])  3.4 us
    conv_general_dilated x2, matrix products, native_conv(): lax.conv_general_dilated(padded[None], kernel, (1, 1), 'VALID', dimension...  2.88 us
    unnamed x18, local copies, waits for them, and re-layouts  2.79 us
    pallas_call x1, Pallas kernels, shifted_weights(): pl.pallas_call(weight_kernel, out_shape=(jax.ShapeDtypeStruct((dates, row...  2.3 us
    dot_general x1, matrix products, shards(): jnp.einsum('oc,hwc->ohw', head_weight, decoded, preferred_element_type=jn...  2.15 us
  transfers between devices with their start and end apart: 3, of which 3 were waited for; matrix products, arithmetic and copies ran while one was open for 1% of the time, Pallas kernels for 0%

profile of v16, /device:TPU:0, one launch (start us, length us, event | category | flops | bytes accessed | tf_op | source)
XLA Modules:
  0.0 70.5 jit_solution(17137063868411169773)
XLA Ops:
  0.0 2.3 %shard_map.100 = (bf16[8,32,256]{2,1,0:T(8,128)(2,1)}, f32[32,256]{1,0:T(8,128)}) custom-call(f32[12]{0:T(128)} %score_ref.1, s32[8,32,256]{2,1,0:T(8,128)} %class_ref.1, f32[8,32,256]{2,1,0:T(8,128)} %quality_ref.1), custom_call_target="tpu_custom_call" | custom-call | tf_op jit(solution)/shard_map/pallas_call | solution.py:104
  2.3 1.0 %fusion.216 = (f32[8,32,256]{2,1,0:T(8,128)S(1)}, bf16[32,256]{1,0:T(8,128)(2,1)S(1)}) fusion(bf16[8,32,256]{2,1,0:T(8,128)(2,1)} %get-tuple-element.7), kind=kLoop, calls=%fused_computation.253 | loop fusion | flops 122880 | bytes 409600 | tf_op jit(solution)/shard_map/convert_element_type | solution.py:147
  3.3 0.8 %convert_bitcast_fusion.1 = bf16[1,1,32,256]{3,2,1,0:T(8,128)(2,1)S(1)} fusion(f32[32,256]{1,0:T(8,128)} %get-tuple-element.8), kind=kLoop, calls=%fused_computation.148 | loop fusion | flops 8192 | bytes 49152 | tf_op jit(solution)/shard_map/concatenate | solution.py:150
  4.1 1.7 %multiply_reduce_fusion = bf16[12,32,256]{2,1,0:T(8,128)(2,1)S(1)} fusion(bf16[8,12,32,256]{3,2,1,0:T(8,128)(2,1)} %param.10, f32[8,32,256]{2,1,0:T(8,128)S(1)} %get-tuple-element.13), kind=kLoop, calls=%fused_computation.16 | loop fusion | flops 2260992 | bytes 2031616 | tf_op jit(solution)/shard_map/reduce_sum | solution.py:148
  5.9 22.8 %all_gather.4 = bf16[4,14,32,256]{3,2,1,0:T(8,128)(2,1)S(1)} all-gather(bf16[1,14,32,256]{3,2,1,0:T(8,128)(2,1)S(1)} %pad_maximum_fusion.16), channel_id=1, replica_groups=mesh['tm'=4,'row'=4,'col'=2] {'tm'}, dimensions={0}, use_global_device_ids=true | all-gather | bytes 1146880 | tf_op jit(solution)/shard_map/all_gather | solution.py:151
  28.6 0.2 convert_element_type.68
  28.9 0.2 fusion.28
  29.1 0.2 fusion.116
  29.4 3.4 %collective-permute-start = (bf16[8,256,12]{1,2,0:T(8,128)(2,1)S(1)}, bf16[8,256,12]{1,2,0:T(8,128)(2,1)S(1)}, u32[]{:S(2)}, u32[]{:S(2)}) collective-permute-start(bf16[8,256,12]{1,2,0:T(8,128)(2,1)S(1)} %get-tuple-element.9), channel_id=1, source_target_pairs={{0,2},{2,4},{4,6},{1,3},{3,5},{5,7},{8,10},{10,12},{12,14},{9,11},... | collective-permute-start | bytes 147464 | tf_op jit(solution)/shard_map/ppermute | solution.py:27
  32.8 1.3 %collective-permute-start.1 = (bf16[8,256,12]{1,2,0:T(8,128)(2,1)S(1)}, bf16[8,256,12]{1,2,0:T(8,128)(2,1)S(1)}, u32[]{:S(2)}, u32[]{:S(2)}) collective-permute-start(bf16[8,256,12]{1,2,0:T(8,128)(2,1)S(1)} %get-tuple-element.10), channel_id=1, source_target_pairs={{2,0},{4,2},{6,4},{3,1},{5,3},{7,5},{10,8},{12,10},{14,12},{11,9},... | collective-permute-start | bytes 147464 | tf_op jit(solution)/shard_map/ppermute | solution.py:29
  34.4 0.1 broadcast_and_fusion.2
  34.7 4.3 %collective-permute-done.1 = bf16[8,256,12]{1,2,0:T(8,128)(2,1)S(1)} collective-permute-done((bf16[8,256,12]{1,2,0:T(8,128)(2,1)S(1)}, bf16[8,256,12]{1,2,0:T(8,128)(2,1)S(1)}, u32[]{:S(2)}, u32[]{:S(2)}) %collective-permute-start.1) | collective-permute-done | bytes 49184 | tf_op jit(solution)/shard_map/ppermute | solution.py:29
  39.0 0.1 slice_select_fusion.1
  39.2 1.4 %collective-permute-done.2 = bf16[48,8,12]{1,2,0:T(8,128)(2,1)S(1)} collective-permute-done((bf16[48,8,12]{1,2,0:T(8,128)(2,1)S(1)}, bf16[48,8,12]{1,2,0:T(8,128)(2,1)S(1)}, u32[]{:S(2)}, u32[]{:S(2)}) %collective-permute-start.2) | collective-permute-done | bytes 9248 | tf_op jit(solution)/shard_map/ppermute | solution.py:19
  40.7 0.3 pad_maximum_fusion.14
  41.0 0.5 fusion.100
  41.5 0.5 fusion.102
  42.1 0.5 fusion.104
  42.6 0.5 fusion.106
  43.1 0.5 fusion.108
  43.6 0.5 fusion.110
  44.1 0.5 fusion.96
  44.6 0.5 fusion.98
  45.1 1.3 %select_convert_fusion = bf16[46,270,32]{1,2,0:T(8,128)(2,1)S(1)} fusion(f32[46,270,32]{1,2,0:T(8,128)S(1)} %fusion.96, f32[46,270,32]{1,2,0:T(8,128)S(1)} %fusion.98, f32[46,270,32]{1,2,0:T(8,128)S(1)} %fusion.100, f32[46,270,32]{1,2,0:T(8,128)S(1)} %fusion.102, f32[46,270,32]{1,2,0:T(8,128)S(1)} %fusion.104, f32[46,270,32]{1,2,0:T(8,128)S(1)} %fusion.106, ...), kind=kOutput, calls=%fused_computation.17 | convolution fusion | flops 13910400 | bytes 19470592 | tf_op jit(solution)/shard_map/hwc,oc->hwo/dot_general | solution.py:43
  46.5 0.5 fusion.64
  47.0 0.4 fusion.66
  47.4 0.5 fusion.68
  48.0 0.5 fusion.70
  48.5 0.4 fusion.72
  48.9 0.5 fusion.74
  49.5 0.5 fusion.76
  50.0 0.4 fusion.78
  50.4 1.6 %select_convert_fusion.1 = bf16[44,268,32]{1,2,0:T(8,128)(2,1)S(1)} fusion(f32[44,268,32]{1,2,0:T(8,128)S(1)} %fusion.64, f32[44,268,32]{1,2,0:T(8,128)S(1)} %fusion.66, f32[44,268,32]{1,2,0:T(8,128)S(1)} %fusion.68, f32[44,268,32]{1,2,0:T(8,128)S(1)} %fusion.70, f32[44,268,32]{1,2,0:T(8,128)S(1)} %fusion.72, f32[44,268,32]{1,2,0:T(8,128)S(1)} %fusion.74, ...), kind=kOutput, calls=%fused_computation.19 | convolution fusion | flops 28300800 | bytes 19164160 | tf_op jit(solution)/shard_map/hwc,oc->hwo/dot_general | solution.py:43
  52.0 0.4 slice.281
  52.4 0.2 convert_reduce_fusion
  52.6 0.4 fusion.60
  53.0 0.8 %copy.63 = bf16[22,1,134,32]{3,0,2,1:T(8,128)(2,1)S(1)} copy(bf16[22,1,134,32]{2,3,0,1:T(8,128)(2,1)S(1)} %fusion.60) | data formatting | bytes 377344
  53.8 0.2 pad.clone
  54.0 0.1 copy.54
  54.2 0.5 copy-done.5
  54.7 1.3 %fusion.30 = bf16[20,8,17,64]{3,1,2,0:T(8,128)(2,1)S(1)} fusion(bf16[3,3,64,32]{2,3,1,0:T(8,128)(2,1)S(1)} %copy-done.5, bf16[22,1,7,2,32]{4,2,3,0,1:T(8,128)(2,1)S(1)} %slice.282, bf16[22,1,8,17,32]{4,2,3,0,1:T(8,128)(2,1)S(1)} %copy.54, pred[8,17]{0,1:T(8,128)(4,1)S(1)} %copy-done.7), kind=kOutput, calls=%fused_computation.48 | convolution fusion | flops 101434368 | bytes 596360 | tf_op jit(solution)/shard_map/conv_general_dilated | solution.py:54
  56.0 0.1 copy.55
  56.1 0.9 %fusion.1 = bf16[20,1,132,64]{3,0,2,1:T(8,128)(2,1)S(1)} fusion(bf16[20,1,136,64]{3,0,2,1:T(8,128)(2,1)S(1)} %bitcast.208, pred[20,132]{0,1:T(8,128)(4,1)S(1)} %broadcast_and_fusion.2), kind=kLoop, calls=%fused_computation.23 | loop fusion | flops 168960 | bytes 678480 | tf_op jit(solution)/shard_map/convert_element_type | solution.py:127
  57.0 0.2 pad.2
  57.2 0.1 copy.57
  57.3 0.3 copy-done.6
  57.7 1.6 %fusion.31 = bf16[18,8,17,64]{3,1,2,0:T(8,128)(2,1)S(1)} fusion(bf16[3,3,64,64]{3,2,1,0:T(8,128)(2,1)S(1)} %copy-done, bf16[20,1,7,2,64]{4,2,3,0,1:T(8,128)(2,1)S(1)} %slice.284, bf16[20,1,8,17,64]{4,2,3,0,1:T(8,128)(2,1)S(1)} %copy.57, pred[8,17]{0,1:T(8,128)(4,1)S(1)} %copy-done.6), kind=kOutput, calls=%fused_computation.51 | convolution fusion | flops 182123520 | bytes 771208 | tf_op jit(solution)/shard_map/conv_general_dilated | solution.py:54
  59.3 0.2 copy.58
  59.5 0.3 reshape.269
  59.8 0.4 copy.62
  60.2 0.5 fusion.55
  60.7 0.3 broadcast_in_dim.48
  61.0 0.2 slice.286
  61.1 0.7 copy-done.2
  61.8 0.3 fusion.6
  62.2 0.7 fusion.3
  62.9 0.7 %fusion.52 = f32[32,256,32]{1,2,0:T(8,128)S(1)} fusion(f32[32,256,32]{1,2,0:T(8,128)S(1)} %fusion.6, bf16[34,258,64]{1,2,0:T(8,128)(2,1)S(1)} %slice.286, bf16[34,258,32]{1,2,0:T(8,128)(2,1)S(1)} %slice.281, bf16[3,3,32,96]{3,2,1,0:T(8,128)(2,1)S(1)} %copy-done.2), kind=kOutput, calls=%fused_computation.60 | convolution fusion | flops 53739520 | bytes 4612096 | tf_op jit(solution)/shard_map/hwc,oc->hwo/dot_general | solution.py:43
  63.6 0.7 %fusion.49 = f32[32,256,32]{1,2,0:T(8,128)S(1)} fusion(f32[32,256,32]{1,2,0:T(8,128)S(1)} %fusion.52, bf16[34,258,64]{1,2,0:T(8,128)(2,1)S(1)} %slice.286, bf16[34,258,32]{1,2,0:T(8,128)(2,1)S(1)} %slice.281, bf16[3,3,32,96]{3,2,1,0:T(8,128)(2,1)S(1)} %copy-done.2), kind=kOutput, calls=%fused_computation.59 | convolution fusion | flops 53739520 | bytes 4612096 | tf_op jit(solution)/shard_map/hwc,oc->hwo/dot_general | solution.py:43
  64.4 0.4 fusion.46
  64.7 0.7 %fusion.43 = f32[32,256,32]{1,2,0:T(8,128)S(1)} fusion(f32[32,256,32]{1,2,0:T(8,128)S(1)} %fusion.46, bf16[34,258,64]{1,2,0:T(8,128)(2,1)S(1)} %slice.286, bf16[34,258,32]{1,2,0:T(8,128)(2,1)S(1)} %slice.281, bf16[3,3,32,96]{3,2,1,0:T(8,128)(2,1)S(1)} %copy-done.2), kind=kOutput, calls=%fused_computation.57 | convolution fusion | flops 53739520 | bytes 4612096 | tf_op jit(solution)/shard_map/hwc,oc->hwo/dot_general | solution.py:43
  65.5 0.7 %fusion.40 = f32[32,256,32]{1,2,0:T(8,128)S(1)} fusion(f32[32,256,32]{1,2,0:T(8,128)S(1)} %fusion.43, bf16[34,258,64]{1,2,0:T(8,128)(2,1)S(1)} %slice.286, bf16[34,258,32]{1,2,0:T(8,128)(2,1)S(1)} %slice.281, bf16[3,3,32,96]{3,2,1,0:T(8,128)(2,1)S(1)} %copy-done.2), kind=kOutput, calls=%fused_computation.56 | convolution fusion | flops 53739520 | bytes 4612096 | tf_op jit(solution)/shard_map/hwc,oc->hwo/dot_general | solution.py:43
  66.2 1.4 %fusion.37 = f32[32,256,32]{1,2,0:T(8,128)} fusion(f32[32,256,32]{1,2,0:T(8,128)S(1)} %fusion.3, f32[32,256,32]{1,2,0:T(8,128)S(1)} %fusion.40, bf16[34,258,64]{1,2,0:T(8,128)(2,1)S(1)} %slice.286, bf16[34,258,32]{1,2,0:T(8,128)(2,1)S(1)} %slice.281, bf16[3,3,32,96]{3,2,1,0:T(8,128)(2,1)S(1)} %copy-done.2), kind=kOutput, calls=%fused_computation.55 | convolution fusion | flops 54001664 | bytes 5660672 | tf_op jit(solution)/shard_map/hwc,oc->hwo/dot_general | solution.py:43
  67.6 2.2 %fusion.62 = bf16[11,32,256]{2,0,1:T(8,128)(2,1)S(1)} fusion(f32[32,256,32]{1,2,0:T(8,128)} %fusion.37, bf16[34,258,64]{1,2,0:T(8,128)(2,1)S(1)} %slice.286, bf16[34,258,32]{1,2,0:T(8,128)(2,1)S(1)} %slice.281, bf16[3,3,32,96]{3,2,1,0:T(8,128)(2,1)S(1)} %copy-done.2, bf16[11,32]{1,0:T(8,128)(2,1)S(1)} %copy-done.4), kind=kOutput, calls=%fused_computation.70 | convolution fusion | flops 60121088 | bytes 3747840 | tf_op jit(solution)/shard_map/oc,hwc->ohw/dot_general | solution.py:194
  69.7 0.7 %copy.60 = bf16[11,32,256]{2,1,0:T(8,128)(2,1)} copy(bf16[11,32,256]{2,0,1:T(8,128)(2,1)S(1)} %fusion.62) | data formatting | bytes 360448 | tf_op jit(solution)/shard_map/convert_element_type | solution.py:196
  (37 shorter events, 0.8 us)
Async XLA Ops:
  0.0 57.3 %copy-start = (bf16[3,3,64,64]{3,2,1,0:T(8,128)(2,1)S(1)}, bf16[3,3,64,64]{3,2,1,0:T(8,128)(2,1)}, u32[]{:S(2)}) copy-start(bf16[3,3,64,64]{3,2,1,0:T(8,128)(2,1)} %param.17) | copy-start | bytes 221188
  29.4 5.3 %collective-permute-start = (bf16[8,256,12]{1,2,0:T(8,128)(2,1)S(1)}, bf16[8,256,12]{1,2,0:T(8,128)(2,1)S(1)}, u32[]{:S(2)}, u32[]{:S(2)}) collective-permute-start(bf16[8,256,12]{1,2,0:T(8,128)(2,1)S(1)} %get-tuple-element.9), channel_id=1, source_target_pairs={{0,2},{2,4},{4,6},{1,3},{3,5},{5,7},{8,10},{10,12},{12,14},{9,11},... | collective-permute-start | bytes 147464 | tf_op jit(solution)/shard_map/ppermute | solution.py:27
  32.8 6.2 %collective-permute-start.1 = (bf16[8,256,12]{1,2,0:T(8,128)(2,1)S(1)}, bf16[8,256,12]{1,2,0:T(8,128)(2,1)S(1)}, u32[]{:S(2)}, u32[]{:S(2)}) collective-permute-start(bf16[8,256,12]{1,2,0:T(8,128)(2,1)S(1)} %get-tuple-element.10), channel_id=1, source_target_pairs={{2,0},{4,2},{6,4},{3,1},{5,3},{7,5},{10,8},{12,10},{14,12},{11,9},... | collective-permute-start | bytes 147464 | tf_op jit(solution)/shard_map/ppermute | solution.py:29
  34.2 6.8 %copy-start.3 = (bf16[3,3,32,12]{2,3,1,0:T(8,128)(2,1)S(1)}, bf16[3,3,32,12]{2,3,1,0:T(8,128)(2,1)}, u32[]{:S(2)}) copy-start(bf16[3,3,32,12]{2,3,1,0:T(8,128)(2,1)} %param.14) | copy-start | bytes 20740
  39.1 1.5 %collective-permute-start.2 = (bf16[48,8,12]{1,2,0:T(8,128)(2,1)S(1)}, bf16[48,8,12]{1,2,0:T(8,128)(2,1)S(1)}, u32[]{:S(2)}, u32[]{:S(2)}) collective-permute-start(bf16[48,8,12]{1,2,0:T(8,128)(2,1)S(1)} %slice_select_fusion.1), channel_id=1, source_target_pairs={{0,1},{1,0},{2,3},{3,2},{4,5},{5,4},{6,7},{7,6},{8,9},{9,8},{10,11... | collective-permute-start | bytes 27656 | tf_op jit(solution)/shard_map/ppermute | solution.py:19
  45.1 1.4 %copy-start.1 = (bf16[3,3,32,32]{3,2,1,0:T(8,128)(2,1)S(1)}, bf16[3,3,32,32]{3,2,1,0:T(8,128)(2,1)}, u32[]{:S(2)}) copy-start(bf16[3,3,32,32]{3,2,1,0:T(8,128)(2,1)} %param.15) | copy-start | bytes 55300
  53.8 0.9 %copy-start.5 = (bf16[3,3,64,32]{2,3,1,0:T(8,128)(2,1)S(1)}, bf16[3,3,64,32]{2,3,1,0:T(8,128)(2,1)}, u32[]{:S(2)}) copy-start(bf16[3,3,64,32]{2,3,1,0:T(8,128)(2,1)} %param.16) | copy-start | bytes 110596
  53.8 0.9 %copy-start.7 = (pred[8,17]{0,1:T(8,128)(4,1)S(1)}, pred[8,17]{0,1:T(8,128)(4,1)}, u32[]{:S(2)}) copy-start(pred[8,17]{0,1:T(8,128)(4,1)} %constant.114) | copy-start | bytes 412
  57.0 0.7 copy-start.6
  61.0 0.9 %copy-start.2 = (bf16[3,3,32,96]{3,2,1,0:T(8,128)(2,1)S(1)}, bf16[3,3,32,96]{3,2,1,0:T(8,128)(2,1)}, u32[]{:S(2)}) copy-start(bf16[3,3,32,96]{3,2,1,0:T(8,128)(2,1)} %param.18) | copy-start | bytes 165892
  66.2 1.4 %copy-start.4 = (bf16[11,32]{1,0:T(8,128)(2,1)S(1)}, bf16[11,32]{1,0:T(8,128)(2,1)}, u32[]{:S(2)}) copy-start(bf16[11,32]{1,0:T(8,128)(2,1)} %param.19) | copy-start | bytes 2116

commit v17 on v15

--- a/solution.py
+++ b/solution.py
@@ -76,10 +76,16 @@
 
         def score(date, top):
             label = class_ref[date, at, :]
-            looked = jnp.zeros(label.shape, jnp.float32)
-            for k in range(classes):
-                looked = jnp.where(label == k, score_ref[k], looked)
-            value = looked + quality_ref[date, at, :]
+            options = [score_ref[k] for k in range(classes)]
+            level = 0
+            while len(options) > 1:
+                bit = (label & (1 << level)) != 0
+                options = [
+                    jnp.where(bit, options[j + 1], options[j]) if j + 1 < len(options) else options[j]
+                    for j in range(0, len(options), 2)
+                ]
+                level += 1
+            value = options[0] + quality_ref[date, at, :]
             weight_ref[date, at, :] = value
             return jnp.maximum(top, value)
 

time: 69.2 us -> 69.1 us (level)
  no operation moved by 1% of the time
where the time goes in v17:
time: 69.1 us; the launch traced here: 68.8 us
  blocking collectives  22.8 us (33%)
  matrix products  22.4 us (32%)
  waiting for transfers between devices  5.76 us (8%)
  local copies, waits for them, and re-layouts  5.63 us (8%)
  starting transfers between devices  4.76 us (7%)
  other arithmetic  4.57 us (7%)
  Pallas kernels  2.27 us (3%)
    all_gather x1, blocking collectives, shards(): gathered = lax.all_gather(packed, 'tm', axis=0).astype(jnp.float32)  22.8 us
    dot_general x26, matrix products, valid_conv(): jnp.einsum('hwc,oc->hwo', padded[a:a + height, e:e + width], kernel[a, e]...  16.6 us
    ppermute x1, waiting for transfers between devices, with_halo(): lax.ppermute(head, axis, [((i + 1) % count, i) for i in range(ends)])  4.27 us
    ppermute x1, starting transfers between devices, with_halo(): lax.ppermute(tail, axis, [(i, (i + 1) % count) for i in range(ends)])  3.4 us
    conv_general_dilated x2, matrix products, native_conv(): lax.conv_general_dilated(padded[None], kernel, (1, 1), 'VALID', dimension...  2.88 us
    unnamed x22, local copies, waits for them, and re-layouts  2.8 us
    pallas_call x1, Pallas kernels, shifted_weights(): pl.pallas_call(weight_kernel, out_shape=(jax.ShapeDtypeStruct((dates, row...  2.27 us
    dot_general x1, matrix products, shards(): jnp.einsum('oc,hwc->ohw', head_weight, decoded, preferred_element_type=jn...  2.15 us
  transfers between devices with their start and end apart: 3, of which 3 were waited for; matrix products, arithmetic and copies ran while one was open for 1% of the time, Pallas kernels for 0%

profile of v17, /device:TPU:0, one launch (start us, length us, event | category | flops | bytes accessed | tf_op | source)
XLA Modules:
  0.0 68.8 jit_solution(7024399283175370895)
XLA Ops:
  0.0 2.3 %shard_map.100 = (f32[8,32,256]{2,1,0:T(8,128)}, f32[32,256]{1,0:T(8,128)}) custom-call(f32[12]{0:T(128)} %score_ref.1, s32[8,32,256]{2,1,0:T(8,128)} %class_ref.1, f32[8,32,256]{2,1,0:T(8,128)} %quality_ref.1), custom_call_target="tpu_custom_call" | custom-call | tf_op jit(solution)/shard_map/pallas_call | solution.py:110
  2.3 1.8 %multiply_reduce_fusion = bf16[12,32,256]{2,1,0:T(8,128)(2,1)S(1)} fusion(bf16[8,12,32,256]{3,2,1,0:T(8,128)(2,1)} %param.10, f32[8,32,256]{2,1,0:T(8,128)} %get-tuple-element.7), kind=kLoop, calls=%fused_computation.16 | loop fusion | flops 2260992 | bytes 2031616 | tf_op jit(solution)/shard_map/reduce_sum | solution.py:152
  4.2 22.8 %all_gather.4 = bf16[4,14,32,256]{3,2,1,0:T(8,128)(2,1)S(1)} all-gather(bf16[1,14,32,256]{3,2,1,0:T(8,128)(2,1)S(1)} %pad_maximum_fusion.16), channel_id=1, replica_groups=mesh['tm'=4,'row'=4,'col'=2] {'tm'}, dimensions={0}, use_global_device_ids=true | all-gather | bytes 1146880 | tf_op jit(solution)/shard_map/all_gather | solution.py:155
  26.9 0.2 convert_element_type.64
  27.2 0.2 fusion.28
  27.4 0.2 fusion.116
  27.7 3.4 %collective-permute-start = (bf16[8,256,12]{1,2,0:T(8,128)(2,1)S(1)}, bf16[8,256,12]{1,2,0:T(8,128)(2,1)S(1)}, u32[]{:S(2)}, u32[]{:S(2)}) collective-permute-start(bf16[8,256,12]{1,2,0:T(8,128)(2,1)S(1)} %get-tuple-element.9), channel_id=1, source_target_pairs={{0,2},{2,4},{4,6},{1,3},{3,5},{5,7},{8,10},{10,12},{12,14},{9,11},... | collective-permute-start | bytes 147464 | tf_op jit(solution)/shard_map/ppermute | solution.py:27
  31.1 1.3 %collective-permute-start.1 = (bf16[8,256,12]{1,2,0:T(8,128)(2,1)S(1)}, bf16[8,256,12]{1,2,0:T(8,128)(2,1)S(1)}, u32[]{:S(2)}, u32[]{:S(2)}) collective-permute-start(bf16[8,256,12]{1,2,0:T(8,128)(2,1)S(1)} %get-tuple-element.10), channel_id=1, source_target_pairs={{2,0},{4,2},{6,4},{3,1},{5,3},{7,5},{10,8},{12,10},{14,12},{11,9},... | collective-permute-start | bytes 147464 | tf_op jit(solution)/shard_map/ppermute | solution.py:29
  32.6 0.1 broadcast_and_fusion
  32.7 0.1 broadcast_and_fusion.1
  32.7 0.1 broadcast_and_fusion.2
  33.0 4.3 %collective-permute-done.1 = bf16[8,256,12]{1,2,0:T(8,128)(2,1)S(1)} collective-permute-done((bf16[8,256,12]{1,2,0:T(8,128)(2,1)S(1)}, bf16[8,256,12]{1,2,0:T(8,128)(2,1)S(1)}, u32[]{:S(2)}, u32[]{:S(2)}) %collective-permute-start.1) | collective-permute-done | bytes 49184 | tf_op jit(solution)/shard_map/ppermute | solution.py:29
  37.3 0.1 slice_select_fusion.1
  37.5 1.4 %collective-permute-done.2 = bf16[48,8,12]{1,2,0:T(8,128)(2,1)S(1)} collective-permute-done((bf16[48,8,12]{1,2,0:T(8,128)(2,1)S(1)}, bf16[48,8,12]{1,2,0:T(8,128)(2,1)S(1)}, u32[]{:S(2)}, u32[]{:S(2)}) %collective-permute-start.2) | collective-permute-done | bytes 9248 | tf_op jit(solution)/shard_map/ppermute | solution.py:19
  39.0 0.3 pad_maximum_fusion.14
  39.4 0.5 fusion.100
  39.9 0.5 fusion.102
  40.4 0.5 fusion.104
  40.9 0.5 fusion.106
  41.4 0.5 fusion.108
  41.9 0.5 fusion.110
  42.4 0.5 fusion.96
  42.9 0.5 fusion.98
  43.4 1.3 %select_convert_fusion = bf16[46,270,32]{1,2,0:T(8,128)(2,1)S(1)} fusion(f32[46,270,32]{1,2,0:T(8,128)S(1)} %fusion.96, f32[46,270,32]{1,2,0:T(8,128)S(1)} %fusion.98, f32[46,270,32]{1,2,0:T(8,128)S(1)} %fusion.100, f32[46,270,32]{1,2,0:T(8,128)S(1)} %fusion.102, f32[46,270,32]{1,2,0:T(8,128)S(1)} %fusion.104, f32[46,270,32]{1,2,0:T(8,128)S(1)} %fusion.106, ...), kind=kOutput, calls=%fused_computation.17 | convolution fusion | flops 13910400 | bytes 19470592 | tf_op jit(solution)/shard_map/hwc,oc->hwo/dot_general | solution.py:43
  44.8 0.5 fusion.64
  45.3 0.4 fusion.66
  45.7 0.5 fusion.68
  46.3 0.5 fusion.70
  46.8 0.4 fusion.72
  47.2 0.5 fusion.74
  47.7 0.5 fusion.76
  48.3 0.4 fusion.78
  48.7 1.6 %select_convert_fusion.1 = bf16[44,268,32]{1,2,0:T(8,128)(2,1)S(1)} fusion(f32[44,268,32]{1,2,0:T(8,128)S(1)} %fusion.64, f32[44,268,32]{1,2,0:T(8,128)S(1)} %fusion.66, f32[44,268,32]{1,2,0:T(8,128)S(1)} %fusion.68, f32[44,268,32]{1,2,0:T(8,128)S(1)} %fusion.70, f32[44,268,32]{1,2,0:T(8,128)S(1)} %fusion.72, f32[44,268,32]{1,2,0:T(8,128)S(1)} %fusion.74, ...), kind=kOutput, calls=%fused_computation.19 | convolution fusion | flops 28300800 | bytes 19164160 | tf_op jit(solution)/shard_map/hwc,oc->hwo/dot_general | solution.py:43
  50.3 0.4 slice.281
  50.7 0.2 convert_reduce_fusion
  50.9 0.4 fusion.60
  51.3 0.8 %copy.63 = bf16[22,1,134,32]{3,0,2,1:T(8,128)(2,1)S(1)} copy(bf16[22,1,134,32]{2,3,0,1:T(8,128)(2,1)S(1)} %fusion.60) | data formatting | bytes 377344
  52.1 0.2 pad.clone
  52.3 0.1 copy.54
  52.5 0.5 copy-done.7
  53.0 1.3 %fusion.30 = bf16[20,8,17,64]{3,1,2,0:T(8,128)(2,1)S(1)} fusion(bf16[3,3,64,32]{2,3,1,0:T(8,128)(2,1)S(1)} %copy-done.7, bf16[22,1,7,2,32]{4,2,3,0,1:T(8,128)(2,1)S(1)} %slice.282, bf16[22,1,8,17,32]{4,2,3,0,1:T(8,128)(2,1)S(1)} %copy.54, pred[8,17]{0,1:T(8,128)(4,1)S(1)} %copy-done.9), kind=kOutput, calls=%fused_computation.48 | convolution fusion | flops 101434368 | bytes 596360 | tf_op jit(solution)/shard_map/conv_general_dilated | solution.py:54
  54.3 0.1 copy.55
  54.4 0.9 %fusion.1 = bf16[20,1,132,64]{3,0,2,1:T(8,128)(2,1)S(1)} fusion(bf16[20,1,136,64]{3,0,2,1:T(8,128)(2,1)S(1)} %bitcast.210, pred[20,132]{0,1:T(8,128)(4,1)S(1)} %broadcast_and_fusion.2), kind=kLoop, calls=%fused_computation.23 | loop fusion | flops 168960 | bytes 678480 | tf_op jit(solution)/shard_map/convert_element_type | solution.py:132
  55.3 0.2 pad.2
  55.5 0.1 copy.57
  55.6 0.3 copy-done.8
  56.0 1.6 %fusion.31 = bf16[18,8,17,64]{3,1,2,0:T(8,128)(2,1)S(1)} fusion(bf16[3,3,64,64]{3,2,1,0:T(8,128)(2,1)S(1)} %copy-done, bf16[20,1,7,2,64]{4,2,3,0,1:T(8,128)(2,1)S(1)} %slice.284, bf16[20,1,8,17,64]{4,2,3,0,1:T(8,128)(2,1)S(1)} %copy.57, pred[8,17]{0,1:T(8,128)(4,1)S(1)} %copy-done.8), kind=kOutput, calls=%fused_computation.51 | convolution fusion | flops 182123520 | bytes 771208 | tf_op jit(solution)/shard_map/conv_general_dilated | solution.py:54
  57.6 0.2 copy.58
  57.8 0.3 reshape.269
  58.1 0.4 copy.62
  58.5 0.5 fusion.55
  59.0 0.3 broadcast_in_dim.48
  59.3 0.2 slice.286
  59.4 0.7 %copy-done.3 = bf16[3,3,32,96]{3,2,1,0:T(8,128)(2,1)S(1)} copy-done((bf16[3,3,32,96]{3,2,1,0:T(8,128)(2,1)S(1)}, bf16[3,3,32,96]{3,2,1,0:T(8,128)(2,1)}, u32[]{:S(2)}) %copy-start.3) | copy-done | bytes 55320
  60.1 0.3 fusion.6
  60.5 0.7 %fusion.3 = f32[32,256,32]{1,2,0:T(8,128)S(1)} fusion(bf16[34,258,64]{1,2,0:T(8,128)(2,1)S(1)} %slice.286, bf16[34,258,32]{1,2,0:T(8,128)(2,1)S(1)} %slice.281, bf16[3,3,32,96]{3,2,1,0:T(8,128)(2,1)S(1)} %copy-done.3), kind=kOutput, calls=%fused_computation.25 | convolution fusion | flops 53477376 | bytes 3563520 | tf_op jit(solution)/shard_map/hwc,oc->hwo/dot_general | solution.py:43
  61.2 0.7 %fusion.52 = f32[32,256,32]{1,2,0:T(8,128)S(1)} fusion(f32[32,256,32]{1,2,0:T(8,128)S(1)} %fusion.6, bf16[34,258,64]{1,2,0:T(8,128)(2,1)S(1)} %slice.286, bf16[34,258,32]{1,2,0:T(8,128)(2,1)S(1)} %slice.281, bf16[3,3,32,96]{3,2,1,0:T(8,128)(2,1)S(1)} %copy-done.3), kind=kOutput, calls=%fused_computation.60 | convolution fusion | flops 53739520 | bytes 4612096 | tf_op jit(solution)/shard_map/hwc,oc->hwo/dot_general | solution.py:43
  61.9 0.7 %fusion.49 = f32[32,256,32]{1,2,0:T(8,128)S(1)} fusion(f32[32,256,32]{1,2,0:T(8,128)S(1)} %fusion.52, bf16[34,258,64]{1,2,0:T(8,128)(2,1)S(1)} %slice.286, bf16[34,258,32]{1,2,0:T(8,128)(2,1)S(1)} %slice.281, bf16[3,3,32,96]{3,2,1,0:T(8,128)(2,1)S(1)} %copy-done.3), kind=kOutput, calls=%fused_computation.59 | convolution fusion | flops 53739520 | bytes 4612096 | tf_op jit(solution)/shard_map/hwc,oc->hwo/dot_general | solution.py:43
  62.7 0.4 fusion.46
  63.0 0.7 %fusion.43 = f32[32,256,32]{1,2,0:T(8,128)S(1)} fusion(f32[32,256,32]{1,2,0:T(8,128)S(1)} %fusion.46, bf16[34,258,64]{1,2,0:T(8,128)(2,1)S(1)} %slice.286, bf16[34,258,32]{1,2,0:T(8,128)(2,1)S(1)} %slice.281, bf16[3,3,32,96]{3,2,1,0:T(8,128)(2,1)S(1)} %copy-done.3), kind=kOutput, calls=%fused_computation.57 | convolution fusion | flops 53739520 | bytes 4612096 | tf_op jit(solution)/shard_map/hwc,oc->hwo/dot_general | solution.py:43
  63.8 0.7 %fusion.40 = f32[32,256,32]{1,2,0:T(8,128)S(1)} fusion(f32[32,256,32]{1,2,0:T(8,128)S(1)} %fusion.43, bf16[34,258,64]{1,2,0:T(8,128)(2,1)S(1)} %slice.286, bf16[34,258,32]{1,2,0:T(8,128)(2,1)S(1)} %slice.281, bf16[3,3,32,96]{3,2,1,0:T(8,128)(2,1)S(1)} %copy-done.3), kind=kOutput, calls=%fused_computation.56 | convolution fusion | flops 53739520 | bytes 4612096 | tf_op jit(solution)/shard_map/hwc,oc->hwo/dot_general | solution.py:43
  64.5 1.4 %fusion.37 = f32[32,256,32]{1,2,0:T(8,128)} fusion(f32[32,256,32]{1,2,0:T(8,128)S(1)} %fusion.3, f32[32,256,32]{1,2,0:T(8,128)S(1)} %fusion.40, bf16[34,258,64]{1,2,0:T(8,128)(2,1)S(1)} %slice.286, bf16[34,258,32]{1,2,0:T(8,128)(2,1)S(1)} %slice.281, bf16[3,3,32,96]{3,2,1,0:T(8,128)(2,1)S(1)} %copy-done.3), kind=kOutput, calls=%fused_computation.55 | convolution fusion | flops 54001664 | bytes 5660672 | tf_op jit(solution)/shard_map/hwc,oc->hwo/dot_general | solution.py:43
  65.9 2.2 %fusion.62 = bf16[11,32,256]{2,0,1:T(8,128)(2,1)S(1)} fusion(f32[32,256,32]{1,2,0:T(8,128)} %fusion.37, bf16[34,258,64]{1,2,0:T(8,128)(2,1)S(1)} %slice.286, bf16[34,258,32]{1,2,0:T(8,128)(2,1)S(1)} %slice.281, bf16[3,3,32,96]{3,2,1,0:T(8,128)(2,1)S(1)} %copy-done.3, bf16[11,32]{1,0:T(8,128)(2,1)S(1)} %copy-done.6), kind=kOutput, calls=%fused_computation.70 | convolution fusion | flops 60121088 | bytes 3747840 | tf_op jit(solution)/shard_map/oc,hwc->ohw/dot_general | solution.py:198
  68.0 0.7 %copy.60 = bf16[11,32,256]{2,1,0:T(8,128)(2,1)} copy(bf16[11,32,256]{2,0,1:T(8,128)(2,1)S(1)} %fusion.62) | data formatting | bytes 360448 | tf_op jit(solution)/shard_map/convert_element_type | solution.py:200
  (41 shorter events, 0.6 us)
Async XLA Ops:
  0.0 55.6 %copy-start = (bf16[3,3,64,64]{3,2,1,0:T(8,128)(2,1)S(1)}, bf16[3,3,64,64]{3,2,1,0:T(8,128)(2,1)}, u32[]{:S(2)}) copy-start(bf16[3,3,64,64]{3,2,1,0:T(8,128)(2,1)} %param.17) | copy-start | bytes 221188
  2.3 1.8 %copy-start.1 = (f32[8,32,256]{2,1,0:T(8,128)S(1)}, f32[8,32,256]{2,1,0:T(8,128)}, u32[]{:S(2)}) copy-start(f32[8,32,256]{2,1,0:T(8,128)} %get-tuple-element.7) | copy-start | bytes 786436
  2.3 1.8 %copy-start.5 = (f32[32,256]{1,0:T(8,128)S(1)}, f32[32,256]{1,0:T(8,128)}, u32[]{:S(2)}) copy-start(f32[32,256]{1,0:T(8,128)} %get-tuple-element.8) | copy-start | bytes 98308
  27.7 5.3 %collective-permute-start = (bf16[8,256,12]{1,2,0:T(8,128)(2,1)S(1)}, bf16[8,256,12]{1,2,0:T(8,128)(2,1)S(1)}, u32[]{:S(2)}, u32[]{:S(2)}) collective-permute-start(bf16[8,256,12]{1,2,0:T(8,128)(2,1)S(1)} %get-tuple-element.9), channel_id=1, source_target_pairs={{0,2},{2,4},{4,6},{1,3},{3,5},{5,7},{8,10},{10,12},{12,14},{9,11},... | collective-permute-start | bytes 147464 | tf_op jit(solution)/shard_map/ppermute | solution.py:27
  31.1 6.2 %collective-permute-start.1 = (bf16[8,256,12]{1,2,0:T(8,128)(2,1)S(1)}, bf16[8,256,12]{1,2,0:T(8,128)(2,1)S(1)}, u32[]{:S(2)}, u32[]{:S(2)}) collective-permute-start(bf16[8,256,12]{1,2,0:T(8,128)(2,1)S(1)} %get-tuple-element.10), channel_id=1, source_target_pairs={{2,0},{4,2},{6,4},{3,1},{5,3},{7,5},{10,8},{12,10},{14,12},{11,9},... | collective-permute-start | bytes 147464 | tf_op jit(solution)/shard_map/ppermute | solution.py:29
  32.5 6.8 %copy-start.4 = (bf16[3,3,32,12]{2,3,1,0:T(8,128)(2,1)S(1)}, bf16[3,3,32,12]{2,3,1,0:T(8,128)(2,1)}, u32[]{:S(2)}) copy-start(bf16[3,3,32,12]{2,3,1,0:T(8,128)(2,1)} %param.14) | copy-start | bytes 20740
  37.5 1.5 %collective-permute-start.2 = (bf16[48,8,12]{1,2,0:T(8,128)(2,1)S(1)}, bf16[48,8,12]{1,2,0:T(8,128)(2,1)S(1)}, u32[]{:S(2)}, u32[]{:S(2)}) collective-permute-start(bf16[48,8,12]{1,2,0:T(8,128)(2,1)S(1)} %slice_select_fusion.1), channel_id=1, source_target_pairs={{0,1},{1,0},{2,3},{3,2},{4,5},{5,4},{6,7},{7,6},{8,9},{9,8},{10,11... | collective-permute-start | bytes 27656 | tf_op jit(solution)/shard_map/ppermute | solution.py:19
  43.4 1.4 %copy-start.2 = (bf16[3,3,32,32]{3,2,1,0:T(8,128)(2,1)S(1)}, bf16[3,3,32,32]{3,2,1,0:T(8,128)(2,1)}, u32[]{:S(2)}) copy-start(bf16[3,3,32,32]{3,2,1,0:T(8,128)(2,1)} %param.15) | copy-start | bytes 55300
  52.1 0.9 %copy-start.7 = (bf16[3,3,64,32]{2,3,1,0:T(8,128)(2,1)S(1)}, bf16[3,3,64,32]{2,3,1,0:T(8,128)(2,1)}, u32[]{:S(2)}) copy-start(bf16[3,3,64,32]{2,3,1,0:T(8,128)(2,1)} %param.16) | copy-start | bytes 110596
  52.1 0.9 %copy-start.9 = (pred[8,17]{0,1:T(8,128)(4,1)S(1)}, pred[8,17]{0,1:T(8,128)(4,1)}, u32[]{:S(2)}) copy-start(pred[8,17]{0,1:T(8,128)(4,1)} %constant.114) | copy-start | bytes 412
  55.3 0.7 %copy-start.8 = (pred[8,17]{0,1:T(8,128)(4,1)S(1)}, pred[8,17]{0,1:T(8,128)(4,1)}, u32[]{:S(2)}) copy-start(pred[8,17]{0,1:T(8,128)(4,1)} %constant.113) | copy-start | bytes 412
  59.2 0.9 %copy-start.3 = (bf16[3,3,32,96]{3,2,1,0:T(8,128)(2,1)S(1)}, bf16[3,3,32,96]{3,2,1,0:T(8,128)(2,1)}, u32[]{:S(2)}) copy-start(bf16[3,3,32,96]{3,2,1,0:T(8,128)(2,1)} %param.18) | copy-start | bytes 165892
  64.5 1.4 %copy-start.6 = (bf16[11,32]{1,0:T(8,128)(2,1)S(1)}, bf16[11,32]{1,0:T(8,128)(2,1)}, u32[]{:S(2)}) copy-start(bf16[11,32]{1,0:T(8,128)(2,1)} %param.19) | copy-start | bytes 2116

commit v18 on v17

--- a/solution.py
+++ b/solution.py
@@ -69,7 +69,7 @@
 def weight_kernel(score_ref, class_ref, quality_ref, weight_ref, shift_ref):
     dates, rows, _ = class_ref.shape
     classes = score_ref.shape[0]
-    step = 16
+    step = 32 if rows % 32 == 0 else 16
 
     def chunk(index, carry):
         at = pl.ds(pl.multiple_of(index * step, step), step)

time: 69.1 us -> 69 us (level)
  no operation moved by 1% of the time
where the time goes in v18:
time: 69 us; the launch traced here: 68.6 us
  blocking collectives  22.8 us (33%)
  matrix products  22.4 us (32%)
  waiting for transfers between devices  5.76 us (8%)
  local copies, waits for them, and re-layouts  5.63 us (8%)
  starting transfers between devices  4.76 us (7%)
  other arithmetic  4.57 us (7%)
  Pallas kernels  2.14 us (3%)
    all_gather x1, blocking collectives, shards(): gathered = lax.all_gather(packed, 'tm', axis=0).astype(jnp.float32)  22.8 us
    dot_general x26, matrix products, valid_conv(): jnp.einsum('hwc,oc->hwo', padded[a:a + height, e:e + width], kernel[a, e]...  16.6 us
    ppermute x1, waiting for transfers between devices, with_halo(): lax.ppermute(head, axis, [((i + 1) % count, i) for i in range(ends)])  4.27 us
    ppermute x1, starting transfers between devices, with_halo(): lax.ppermute(tail, axis, [(i, (i + 1) % count) for i in range(ends)])  3.4 us
    conv_general_dilated x2, matrix products, native_conv(): lax.conv_general_dilated(padded[None], kernel, (1, 1), 'VALID', dimension...  2.88 us
    unnamed x22, local copies, waits for them, and re-layouts  2.8 us
    dot_general x1, matrix products, shards(): jnp.einsum('oc,hwc->ohw', head_weight, decoded, preferred_element_type=jn...  2.15 us
    pallas_call x1, Pallas kernels, shifted_weights(): pl.pallas_call(weight_kernel, out_shape=(jax.ShapeDtypeStruct((dates, row...  2.14 us
  transfers between devices with their start and end apart: 3, of which 3 were waited for; matrix products, arithmetic and copies ran while one was open for 1% of the time, Pallas kernels for 0%

profile of v18, /device:TPU:0, one launch (start us, length us, event | category | flops | bytes accessed | tf_op | source)
XLA Modules:
  0.0 68.6 jit_solution(6048235431385686172)
XLA Ops:
  0.0 2.1 %shard_map.100 = (f32[8,32,256]{2,1,0:T(8,128)}, f32[32,256]{1,0:T(8,128)}) custom-call(f32[12]{0:T(128)} %score_ref.1, s32[8,32,256]{2,1,0:T(8,128)} %class_ref.1, f32[8,32,256]{2,1,0:T(8,128)} %quality_ref.1), custom_call_target="tpu_custom_call" | custom-call | tf_op jit(solution)/shard_map/pallas_call | solution.py:110
  2.1 1.8 %multiply_reduce_fusion = bf16[12,32,256]{2,1,0:T(8,128)(2,1)S(1)} fusion(bf16[8,12,32,256]{3,2,1,0:T(8,128)(2,1)} %param.10, f32[8,32,256]{2,1,0:T(8,128)} %get-tuple-element.7), kind=kLoop, calls=%fused_computation.16 | loop fusion | flops 2260992 | bytes 2031616 | tf_op jit(solution)/shard_map/reduce_sum | solution.py:152
  4.0 22.8 %all_gather.4 = bf16[4,14,32,256]{3,2,1,0:T(8,128)(2,1)S(1)} all-gather(bf16[1,14,32,256]{3,2,1,0:T(8,128)(2,1)S(1)} %pad_maximum_fusion.16), channel_id=1, replica_groups=mesh['tm'=4,'row'=4,'col'=2] {'tm'}, dimensions={0}, use_global_device_ids=true | all-gather | bytes 1146880 | tf_op jit(solution)/shard_map/all_gather | solution.py:155
  26.8 0.2 convert_element_type.64
  27.1 0.2 fusion.28
  27.3 0.2 fusion.116
  27.6 3.4 %collective-permute-start = (bf16[8,256,12]{1,2,0:T(8,128)(2,1)S(1)}, bf16[8,256,12]{1,2,0:T(8,128)(2,1)S(1)}, u32[]{:S(2)}, u32[]{:S(2)}) collective-permute-start(bf16[8,256,12]{1,2,0:T(8,128)(2,1)S(1)} %get-tuple-element.9), channel_id=1, source_target_pairs={{0,2},{2,4},{4,6},{1,3},{3,5},{5,7},{8,10},{10,12},{12,14},{9,11},... | collective-permute-start | bytes 147464 | tf_op jit(solution)/shard_map/ppermute | solution.py:27
  31.0 1.3 %collective-permute-start.1 = (bf16[8,256,12]{1,2,0:T(8,128)(2,1)S(1)}, bf16[8,256,12]{1,2,0:T(8,128)(2,1)S(1)}, u32[]{:S(2)}, u32[]{:S(2)}) collective-permute-start(bf16[8,256,12]{1,2,0:T(8,128)(2,1)S(1)} %get-tuple-element.10), channel_id=1, source_target_pairs={{2,0},{4,2},{6,4},{3,1},{5,3},{7,5},{10,8},{12,10},{14,12},{11,9},... | collective-permute-start | bytes 147464 | tf_op jit(solution)/shard_map/ppermute | solution.py:29
  32.4 0.1 broadcast_and_fusion
  32.5 0.1 broadcast_and_fusion.1
  32.6 0.1 broadcast_and_fusion.2
  32.8 4.3 %collective-permute-done.1 = bf16[8,256,12]{1,2,0:T(8,128)(2,1)S(1)} collective-permute-done((bf16[8,256,12]{1,2,0:T(8,128)(2,1)S(1)}, bf16[8,256,12]{1,2,0:T(8,128)(2,1)S(1)}, u32[]{:S(2)}, u32[]{:S(2)}) %collective-permute-start.1) | collective-permute-done | bytes 49184 | tf_op jit(solution)/shard_map/ppermute | solution.py:29
  37.2 0.1 slice_select_fusion.1
  37.4 1.4 %collective-permute-done.2 = bf16[48,8,12]{1,2,0:T(8,128)(2,1)S(1)} collective-permute-done((bf16[48,8,12]{1,2,0:T(8,128)(2,1)S(1)}, bf16[48,8,12]{1,2,0:T(8,128)(2,1)S(1)}, u32[]{:S(2)}, u32[]{:S(2)}) %collective-permute-start.2) | collective-permute-done | bytes 9248 | tf_op jit(solution)/shard_map/ppermute | solution.py:19
  38.9 0.3 pad_maximum_fusion.14
  39.2 0.5 fusion.100
  39.7 0.5 fusion.102
  40.2 0.5 fusion.104
  40.7 0.5 fusion.106
  41.3 0.5 fusion.108
  41.8 0.5 fusion.110
  42.3 0.5 fusion.96
  42.8 0.5 fusion.98
  43.3 1.3 %select_convert_fusion = bf16[46,270,32]{1,2,0:T(8,128)(2,1)S(1)} fusion(f32[46,270,32]{1,2,0:T(8,128)S(1)} %fusion.96, f32[46,270,32]{1,2,0:T(8,128)S(1)} %fusion.98, f32[46,270,32]{1,2,0:T(8,128)S(1)} %fusion.100, f32[46,270,32]{1,2,0:T(8,128)S(1)} %fusion.102, f32[46,270,32]{1,2,0:T(8,128)S(1)} %fusion.104, f32[46,270,32]{1,2,0:T(8,128)S(1)} %fusion.106, ...), kind=kOutput, calls=%fused_computation.17 | convolution fusion | flops 13910400 | bytes 19470592 | tf_op jit(solution)/shard_map/hwc,oc->hwo/dot_general | solution.py:43
  44.6 0.5 fusion.64
  45.2 0.4 fusion.66
  45.6 0.5 fusion.68
  46.1 0.5 fusion.70
  46.7 0.4 fusion.72
  47.1 0.5 fusion.74
  47.6 0.5 fusion.76
  48.2 0.4 fusion.78
  48.6 1.6 %select_convert_fusion.1 = bf16[44,268,32]{1,2,0:T(8,128)(2,1)S(1)} fusion(f32[44,268,32]{1,2,0:T(8,128)S(1)} %fusion.64, f32[44,268,32]{1,2,0:T(8,128)S(1)} %fusion.66, f32[44,268,32]{1,2,0:T(8,128)S(1)} %fusion.68, f32[44,268,32]{1,2,0:T(8,128)S(1)} %fusion.70, f32[44,268,32]{1,2,0:T(8,128)S(1)} %fusion.72, f32[44,268,32]{1,2,0:T(8,128)S(1)} %fusion.74, ...), kind=kOutput, calls=%fused_computation.19 | convolution fusion | flops 28300800 | bytes 19164160 | tf_op jit(solution)/shard_map/hwc,oc->hwo/dot_general | solution.py:43
  50.2 0.4 slice.281
  50.6 0.2 convert_reduce_fusion
  50.8 0.4 fusion.60
  51.2 0.8 %copy.63 = bf16[22,1,134,32]{3,0,2,1:T(8,128)(2,1)S(1)} copy(bf16[22,1,134,32]{2,3,0,1:T(8,128)(2,1)S(1)} %fusion.60) | data formatting | bytes 377344
  52.0 0.2 pad.clone
  52.2 0.1 copy.54
  52.3 0.5 copy-done.7
  52.8 1.3 %fusion.30 = bf16[20,8,17,64]{3,1,2,0:T(8,128)(2,1)S(1)} fusion(bf16[3,3,64,32]{2,3,1,0:T(8,128)(2,1)S(1)} %copy-done.7, bf16[22,1,7,2,32]{4,2,3,0,1:T(8,128)(2,1)S(1)} %slice.282, bf16[22,1,8,17,32]{4,2,3,0,1:T(8,128)(2,1)S(1)} %copy.54, pred[8,17]{0,1:T(8,128)(4,1)S(1)} %copy-done.9), kind=kOutput, calls=%fused_computation.48 | convolution fusion | flops 101434368 | bytes 596360 | tf_op jit(solution)/shard_map/conv_general_dilated | solution.py:54
  54.1 0.1 copy.55
  54.3 0.9 %fusion.1 = bf16[20,1,132,64]{3,0,2,1:T(8,128)(2,1)S(1)} fusion(bf16[20,1,136,64]{3,0,2,1:T(8,128)(2,1)S(1)} %bitcast.210, pred[20,132]{0,1:T(8,128)(4,1)S(1)} %broadcast_and_fusion.2), kind=kLoop, calls=%fused_computation.23 | loop fusion | flops 168960 | bytes 678480 | tf_op jit(solution)/shard_map/convert_element_type | solution.py:132
  55.2 0.2 pad.2
  55.3 0.1 copy.57
  55.5 0.3 copy-done.8
  55.8 1.6 %fusion.31 = bf16[18,8,17,64]{3,1,2,0:T(8,128)(2,1)S(1)} fusion(bf16[3,3,64,64]{3,2,1,0:T(8,128)(2,1)S(1)} %copy-done, bf16[20,1,7,2,64]{4,2,3,0,1:T(8,128)(2,1)S(1)} %slice.284, bf16[20,1,8,17,64]{4,2,3,0,1:T(8,128)(2,1)S(1)} %copy.57, pred[8,17]{0,1:T(8,128)(4,1)S(1)} %copy-done.8), kind=kOutput, calls=%fused_computation.51 | convolution fusion | flops 182123520 | bytes 771208 | tf_op jit(solution)/shard_map/conv_general_dilated | solution.py:54
  57.5 0.2 copy.58
  57.6 0.3 reshape.269
  57.9 0.4 copy.62
  58.4 0.5 fusion.55
  58.8 0.3 broadcast_in_dim.48
  59.1 0.2 slice.286
  59.3 0.7 %copy-done.3 = bf16[3,3,32,96]{3,2,1,0:T(8,128)(2,1)S(1)} copy-done((bf16[3,3,32,96]{3,2,1,0:T(8,128)(2,1)S(1)}, bf16[3,3,32,96]{3,2,1,0:T(8,128)(2,1)}, u32[]{:S(2)}) %copy-start.3) | copy-done | bytes 55320
  60.0 0.3 fusion.6
  60.3 0.7 %fusion.3 = f32[32,256,32]{1,2,0:T(8,128)S(1)} fusion(bf16[34,258,64]{1,2,0:T(8,128)(2,1)S(1)} %slice.286, bf16[34,258,32]{1,2,0:T(8,128)(2,1)S(1)} %slice.281, bf16[3,3,32,96]{3,2,1,0:T(8,128)(2,1)S(1)} %copy-done.3), kind=kOutput, calls=%fused_computation.25 | convolution fusion | flops 53477376 | bytes 3563520 | tf_op jit(solution)/shard_map/hwc,oc->hwo/dot_general | solution.py:43
  61.0 0.7 %fusion.52 = f32[32,256,32]{1,2,0:T(8,128)S(1)} fusion(f32[32,256,32]{1,2,0:T(8,128)S(1)} %fusion.6, bf16[34,258,64]{1,2,0:T(8,128)(2,1)S(1)} %slice.286, bf16[34,258,32]{1,2,0:T(8,128)(2,1)S(1)} %slice.281, bf16[3,3,32,96]{3,2,1,0:T(8,128)(2,1)S(1)} %copy-done.3), kind=kOutput, calls=%fused_computation.60 | convolution fusion | flops 53739520 | bytes 4612096 | tf_op jit(solution)/shard_map/hwc,oc->hwo/dot_general | solution.py:43
  61.8 0.7 %fusion.49 = f32[32,256,32]{1,2,0:T(8,128)S(1)} fusion(f32[32,256,32]{1,2,0:T(8,128)S(1)} %fusion.52, bf16[34,258,64]{1,2,0:T(8,128)(2,1)S(1)} %slice.286, bf16[34,258,32]{1,2,0:T(8,128)(2,1)S(1)} %slice.281, bf16[3,3,32,96]{3,2,1,0:T(8,128)(2,1)S(1)} %copy-done.3), kind=kOutput, calls=%fused_computation.59 | convolution fusion | flops 53739520 | bytes 4612096 | tf_op jit(solution)/shard_map/hwc,oc->hwo/dot_general | solution.py:43
  62.5 0.4 fusion.46
  62.9 0.7 %fusion.43 = f32[32,256,32]{1,2,0:T(8,128)S(1)} fusion(f32[32,256,32]{1,2,0:T(8,128)S(1)} %fusion.46, bf16[34,258,64]{1,2,0:T(8,128)(2,1)S(1)} %slice.286, bf16[34,258,32]{1,2,0:T(8,128)(2,1)S(1)} %slice.281, bf16[3,3,32,96]{3,2,1,0:T(8,128)(2,1)S(1)} %copy-done.3), kind=kOutput, calls=%fused_computation.57 | convolution fusion | flops 53739520 | bytes 4612096 | tf_op jit(solution)/shard_map/hwc,oc->hwo/dot_general | solution.py:43
  63.6 0.7 %fusion.40 = f32[32,256,32]{1,2,0:T(8,128)S(1)} fusion(f32[32,256,32]{1,2,0:T(8,128)S(1)} %fusion.43, bf16[34,258,64]{1,2,0:T(8,128)(2,1)S(1)} %slice.286, bf16[34,258,32]{1,2,0:T(8,128)(2,1)S(1)} %slice.281, bf16[3,3,32,96]{3,2,1,0:T(8,128)(2,1)S(1)} %copy-done.3), kind=kOutput, calls=%fused_computation.56 | convolution fusion | flops 53739520 | bytes 4612096 | tf_op jit(solution)/shard_map/hwc,oc->hwo/dot_general | solution.py:43
  64.4 1.4 %fusion.37 = f32[32,256,32]{1,2,0:T(8,128)} fusion(f32[32,256,32]{1,2,0:T(8,128)S(1)} %fusion.3, f32[32,256,32]{1,2,0:T(8,128)S(1)} %fusion.40, bf16[34,258,64]{1,2,0:T(8,128)(2,1)S(1)} %slice.286, bf16[34,258,32]{1,2,0:T(8,128)(2,1)S(1)} %slice.281, bf16[3,3,32,96]{3,2,1,0:T(8,128)(2,1)S(1)} %copy-done.3), kind=kOutput, calls=%fused_computation.55 | convolution fusion | flops 54001664 | bytes 5660672 | tf_op jit(solution)/shard_map/hwc,oc->hwo/dot_general | solution.py:43
  65.7 2.2 %fusion.62 = bf16[11,32,256]{2,0,1:T(8,128)(2,1)S(1)} fusion(f32[32,256,32]{1,2,0:T(8,128)} %fusion.37, bf16[34,258,64]{1,2,0:T(8,128)(2,1)S(1)} %slice.286, bf16[34,258,32]{1,2,0:T(8,128)(2,1)S(1)} %slice.281, bf16[3,3,32,96]{3,2,1,0:T(8,128)(2,1)S(1)} %copy-done.3, bf16[11,32]{1,0:T(8,128)(2,1)S(1)} %copy-done.6), kind=kOutput, calls=%fused_computation.70 | convolution fusion | flops 60121088 | bytes 3747840 | tf_op jit(solution)/shard_map/oc,hwc->ohw/dot_general | solution.py:198
  67.9 0.7 %copy.60 = bf16[11,32,256]{2,1,0:T(8,128)(2,1)} copy(bf16[11,32,256]{2,0,1:T(8,128)(2,1)S(1)} %fusion.62) | data formatting | bytes 360448 | tf_op jit(solution)/shard_map/convert_element_type | solution.py:200
  (41 shorter events, 0.6 us)
Async XLA Ops:
  0.0 55.5 %copy-start = (bf16[3,3,64,64]{3,2,1,0:T(8,128)(2,1)S(1)}, bf16[3,3,64,64]{3,2,1,0:T(8,128)(2,1)}, u32[]{:S(2)}) copy-start(bf16[3,3,64,64]{3,2,1,0:T(8,128)(2,1)} %param.17) | copy-start | bytes 221188
  2.1 1.8 %copy-start.1 = (f32[8,32,256]{2,1,0:T(8,128)S(1)}, f32[8,32,256]{2,1,0:T(8,128)}, u32[]{:S(2)}) copy-start(f32[8,32,256]{2,1,0:T(8,128)} %get-tuple-element.7) | copy-start | bytes 786436
  2.1 1.8 %copy-start.5 = (f32[32,256]{1,0:T(8,128)S(1)}, f32[32,256]{1,0:T(8,128)}, u32[]{:S(2)}) copy-start(f32[32,256]{1,0:T(8,128)} %get-tuple-element.8) | copy-start | bytes 98308
  27.6 5.3 %collective-permute-start = (bf16[8,256,12]{1,2,0:T(8,128)(2,1)S(1)}, bf16[8,256,12]{1,2,0:T(8,128)(2,1)S(1)}, u32[]{:S(2)}, u32[]{:S(2)}) collective-permute-start(bf16[8,256,12]{1,2,0:T(8,128)(2,1)S(1)} %get-tuple-element.9), channel_id=1, source_target_pairs={{0,2},{2,4},{4,6},{1,3},{3,5},{5,7},{8,10},{10,12},{12,14},{9,11},... | collective-permute-start | bytes 147464 | tf_op jit(solution)/shard_map/ppermute | solution.py:27
  31.0 6.2 %collective-permute-start.1 = (bf16[8,256,12]{1,2,0:T(8,128)(2,1)S(1)}, bf16[8,256,12]{1,2,0:T(8,128)(2,1)S(1)}, u32[]{:S(2)}, u32[]{:S(2)}) collective-permute-start(bf16[8,256,12]{1,2,0:T(8,128)(2,1)S(1)} %get-tuple-element.10), channel_id=1, source_target_pairs={{2,0},{4,2},{6,4},{3,1},{5,3},{7,5},{10,8},{12,10},{14,12},{11,9},... | collective-permute-start | bytes 147464 | tf_op jit(solution)/shard_map/ppermute | solution.py:29
  32.4 6.8 %copy-start.4 = (bf16[3,3,32,12]{2,3,1,0:T(8,128)(2,1)S(1)}, bf16[3,3,32,12]{2,3,1,0:T(8,128)(2,1)}, u32[]{:S(2)}) copy-start(bf16[3,3,32,12]{2,3,1,0:T(8,128)(2,1)} %param.14) | copy-start | bytes 20740
  37.3 1.5 %collective-permute-start.2 = (bf16[48,8,12]{1,2,0:T(8,128)(2,1)S(1)}, bf16[48,8,12]{1,2,0:T(8,128)(2,1)S(1)}, u32[]{:S(2)}, u32[]{:S(2)}) collective-permute-start(bf16[48,8,12]{1,2,0:T(8,128)(2,1)S(1)} %slice_select_fusion.1), channel_id=1, source_target_pairs={{0,1},{1,0},{2,3},{3,2},{4,5},{5,4},{6,7},{7,6},{8,9},{9,8},{10,11... | collective-permute-start | bytes 27656 | tf_op jit(solution)/shard_map/ppermute | solution.py:19
  43.3 1.4 %copy-start.2 = (bf16[3,3,32,32]{3,2,1,0:T(8,128)(2,1)S(1)}, bf16[3,3,32,32]{3,2,1,0:T(8,128)(2,1)}, u32[]{:S(2)}) copy-start(bf16[3,3,32,32]{3,2,1,0:T(8,128)(2,1)} %param.15) | copy-start | bytes 55300
  52.0 0.9 %copy-start.7 = (bf16[3,3,64,32]{2,3,1,0:T(8,128)(2,1)S(1)}, bf16[3,3,64,32]{2,3,1,0:T(8,128)(2,1)}, u32[]{:S(2)}) copy-start(bf16[3,3,64,32]{2,3,1,0:T(8,128)(2,1)} %param.16) | copy-start | bytes 110596
  52.0 0.9 %copy-start.9 = (pred[8,17]{0,1:T(8,128)(4,1)S(1)}, pred[8,17]{0,1:T(8,128)(4,1)}, u32[]{:S(2)}) copy-start(pred[8,17]{0,1:T(8,128)(4,1)} %constant.114) | copy-start | bytes 412
  55.1 0.7 %copy-start.8 = (pred[8,17]{0,1:T(8,128)(4,1)S(1)}, pred[8,17]{0,1:T(8,128)(4,1)}, u32[]{:S(2)}) copy-start(pred[8,17]{0,1:T(8,128)(4,1)} %constant.113) | copy-start | bytes 412
  59.1 0.9 %copy-start.3 = (bf16[3,3,32,96]{3,2,1,0:T(8,128)(2,1)S(1)}, bf16[3,3,32,96]{3,2,1,0:T(8,128)(2,1)}, u32[]{:S(2)}) copy-start(bf16[3,3,32,96]{3,2,1,0:T(8,128)(2,1)} %param.18) | copy-start | bytes 165892
  64.4 1.4 %copy-start.6 = (bf16[11,32]{1,0:T(8,128)(2,1)S(1)}, bf16[11,32]{1,0:T(8,128)(2,1)}, u32[]{:S(2)}) copy-start(bf16[11,32]{1,0:T(8,128)(2,1)} %param.19) | copy-start | bytes 2116
